TPU v7x, 32 devices: a whole 2x2x4 slice. The times are simulated.
32 devices in a mesh: grp: 2 (over y), gx: 4 (over z), gy: 2 (over x), col: 2 (over core).
Axes of the slice: x: 2, y: 2, z: 4, core: 2. Of those that a mesh axis runs over, the one named last changes fastest.
Arguments:
- x_act: bfloat16 [32, 32, 32, 128], P(('grp', 'gx'), 'gy'), parts along dimension 0, may hold values from -6 to 6
- grad_out: bfloat16 [32, 32, 32, 128], P(('grp', 'gx'), 'gy'), parts along dimension 0, may hold values from -6 to 6
- weight: bfloat16 [27, 128, 128], replicated, may hold values from -0.109375 to 0.109375
Outputs:
- grad_in: bfloat16 [32, 32, 32, 128], P(('grp', 'gx'), 'gy'), parts along dimension 0
- grad_weight: float32 [6912, 128], P(('grp', 'gx', 'gy'), 'col'), parts along dimension 0
There are 2 independent parts, one for each index of `grp`. A program takes and returns all parts, laid end to end along the dimension named above; an argument that names none is the same for every part. Nothing has to cross between parts.
All inputs are finite; a program needn't handle non-finite values.
Results may differ from a plain program's by a relative error of at most 0.001.
Values may be sent and summed in bfloat16 or wider, within the bound.
No kernel may reach another device: no remote copies, remote signals or barrier semaphores. Data moves between devices by JAX's collectives and lax.ppermute only.
A program may use at most 64 MiB of HBM per device.

v0:
```python
import jax
import jax.numpy as jnp
from jax import lax
from jax.sharding import PartitionSpec as P


def with_halo(cells, sides, width):
    for axis, dim in sides:
        count = lax.axis_size(axis)
        ends = count - 1
        head = lax.slice_in_dim(cells, 0, width, axis=dim)
        tail = lax.slice_in_dim(cells, cells.shape[dim] - width, cells.shape[dim], axis=dim)
        cells = jnp.concatenate(
            [
                lax.ppermute(tail, axis, [(i, (i + 1) % count) for i in range(ends)]),
                cells,
                lax.ppermute(head, axis, [((i + 1) % count, i) for i in range(ends)]),
            ],
            axis=dim,
        )
    return cells


def depth_taps(block, starts, depth):
    return jnp.concatenate([lax.slice_in_dim(block, s, s + depth, axis=2) for s in starts], axis=3)


def kernel_rows(weight, a, b):
    first = a * 9 + b * 3
    three = weight[first : first + 3]
    return jnp.transpose(three, (0, 2, 1)).reshape(3 * weight.shape[2], weight.shape[1])


def local_terms(gslab, x_rows, weight_part, size_x, size_y, depth):
    chans = x_rows.shape[3]
    width = weight_part.shape[2]
    cells = size_x * size_y * depth
    xflat = x_rows.reshape(cells, chans)
    contract_rows = (((0,), (0,)), ((), ()))
    accum = jnp.zeros((cells, chans), jnp.float32)
    pieces = []
    for a in range(3):
        for b in range(3):
            block = gslab[2 - a : 2 - a + size_x, 2 - b : 2 - b + size_y]
            stacked = depth_taps(block, (2, 1, 0), depth).reshape(cells, 3 * width)
            accum = accum + jnp.dot(
                stacked, kernel_rows(weight_part, a, b), preferred_element_type=jnp.float32
            )
            term = lax.dot_general(
                xflat, stacked, contract_rows, preferred_element_type=jnp.float32
            )
            pieces.append(
                jnp.transpose(term.reshape(chans, 3, width), (1, 0, 2)).reshape(3 * chans, width)
            )
    return (accum.reshape(size_x, size_y, depth, chans), jnp.concatenate(pieces, axis=0))


def on_device(x_act, grad_out, weight):
    size_x, size_y, depth, chans = x_act.shape
    ncores = lax.axis_size("col")
    half = chans // ncores
    offset = lax.axis_index("col") * half
    grad_share = lax.dynamic_slice_in_dim(grad_out, offset, half, 3)
    weight_share = lax.dynamic_slice_in_dim(weight, offset, half, 2)
    grim = with_halo(grad_share, (("gx", 0), ("gy", 1)), 1)
    gdeep = jnp.pad(grim, ((0, 0), (0, 0), (1, 1), (0, 0)))
    inner, weight_terms = local_terms(gdeep, x_act, weight_share, size_x, size_y, depth)
    grad_in = lax.psum(inner, "col").astype(jnp.bfloat16)
    owned = lax.psum_scatter(weight_terms, ("gx", "gy"), scatter_dimension=0, tiled=True)
    total_cells = size_x * lax.axis_size("gx") * size_y * lax.axis_size("gy") * depth
    grad_weight = owned / jnp.sqrt(jnp.float32(total_cells))
    return (grad_in, grad_weight)


def solution(mesh):
    return jax.shard_map(
        on_device,
        mesh=mesh,
        in_specs=(P(("grp", "gx"), "gy", None, None), P(("grp", "gx"), "gy", None, None), P()),
        out_specs=(P(("grp", "gx"), "gy", None, None), P(("grp", "gx", "gy"), "col")),
        check_vma=False,
    )
```

profile of v0, /device:TPU:0, one launch (start us, length us, event | category | flops | bytes accessed | tf_op | source)
XLA Modules:
  0.0 125.0 jit_solution(10722042512559907340)
XLA Ops:
  7.2 1.2 constant_dynamic-slice_fusion.9
  8.5 4.9 %collective-permute-start = (bf16[1,16,32,64]{3,2,1,0:T(8,128)(2,1)S(1)}, bf16[1,16,32,64]{3,2,1,0:T(8,128)(2,1)S(1)}, u32[]{:S(2)}, u32[]{:S(2)}) collective-permute-start(bf16[1,16,32,64]{3,2,1,0:T(8,128)(2,1)S(1)} %get-tuple-element.42), channel_id=1, source_target_pairs={{0,4},{4,8},{8,12},{1,5},{5,9},{9,13},{2,6},{6,10},{10,14},{3,7},{... | collective-permute-start | bytes 196616 | tf_op jit(solution)/shard_map/ppermute | solution.py:15
  13.4 1.3 %collective-permute-start.1 = (bf16[1,16,32,64]{3,2,1,0:T(8,128)(2,1)S(1)}, bf16[1,16,32,64]{3,2,1,0:T(8,128)(2,1)S(1)}, u32[]{:S(2)}, u32[]{:S(2)}) collective-permute-start(bf16[1,16,32,64]{3,2,1,0:T(8,128)(2,1)S(1)} %get-tuple-element.43), channel_id=1, source_target_pairs={{4,0},{8,4},{12,8},{5,1},{9,5},{13,9},{6,2},{10,6},{14,10},{7,3},{... | collective-permute-start | bytes 196616 | tf_op jit(solution)/shard_map/ppermute | solution.py:17
  14.7 1.3 %constant_dynamic-slice_fusion.11 = bf16[4,16,32,64]{3,2,1,0:T(8,128)(2,1)S(1)} fusion(bf16[4,16,32,128]{3,2,1,0:T(8,128)(2,1)} %param.4, s32[]{:T(128)S(6)} %select_n.4), kind=kLoop, calls=%fused_computation.57 | loop fusion | bytes 524292 | tf_op jit(solution)/shard_map/dynamic_slice | solution.py:63
  16.1 4.1 %collective-permute-done.1 = bf16[1,16,32,64]{3,2,1,0:T(8,128)(2,1)S(1)} collective-permute-done((bf16[1,16,32,64]{3,2,1,0:T(8,128)(2,1)S(1)}, bf16[1,16,32,64]{3,2,1,0:T(8,128)(2,1)S(1)}, u32[]{:S(2)}, u32[]{:S(2)}) %collective-permute-start.1) | collective-permute-done | bytes 65568 | tf_op jit(solution)/shard_map/ppermute | solution.py:17
  20.3 3.4 %collective-permute-start.2 = (bf16[6,1,32,64]{3,2,1,0:T(8,128)(2,1)S(1)}, bf16[6,1,32,64]{3,2,1,0:T(8,128)(2,1)S(1)}, u32[]{:S(2)}, u32[]{:S(2)}) collective-permute-start(bf16[6,1,32,64]{3,2,1,0:T(8,128)(2,1)S(1)} %get-tuple-element.37), channel_id=1, source_target_pairs={{0,2},{1,3},{4,6},{5,7},{8,10},{9,11},{12,14},{13,15},{16,18},{17,... | collective-permute-start | bytes 73736 | tf_op jit(solution)/shard_map/ppermute | solution.py:15
  23.7 1.3 %collective-permute-start.3 = (bf16[6,1,32,64]{3,2,1,0:T(8,128)(2,1)S(1)}, bf16[6,1,32,64]{3,2,1,0:T(8,128)(2,1)S(1)}, u32[]{:S(2)}, u32[]{:S(2)}) collective-permute-start(bf16[6,1,32,64]{3,2,1,0:T(8,128)(2,1)S(1)} %get-tuple-element.38), channel_id=1, source_target_pairs={{2,0},{3,1},{6,4},{7,5},{10,8},{11,9},{14,12},{15,13},{18,16},{19,... | collective-permute-start | bytes 73736 | tf_op jit(solution)/shard_map/ppermute | solution.py:17
  25.3 0.7 copy.46
  26.1 0.7 copy.47
  26.8 0.7 copy.48
  27.5 0.7 copy.49
  28.2 0.7 copy.50
  28.9 0.7 copy.51
  29.6 0.7 copy.52
  30.3 0.7 copy.53
  31.1 0.5 select_maximum_fusion
  31.7 2.8 %fusion.10 = (bf16[4,16,32,64]{3,2,1,0:T(8,128)(2,1)S(1)}, bf16[4,16,32,64]{3,2,1,0:T(8,128)(2,1)S(1)}, bf16[4,16,32,64]{3,2,1,0:T(8,128)(2,1)S(1)}, bf16[4,16,3...) fusion(bf16[6,18,34,64]{3,2,1,0:T(8,128)(2,1)S(1)} %select_maxi, ...), kind=kLoop, calls=%fused_computation.58 | loop fusion | bytes 9437184 | tf_op jit(solution)/shard_map/slice | solution.py:25
  34.4 2.0 %fusion.7 = (bf16[4,16,32,192]{3,2,1,0:T(8,128)(2,1)S(1)}, bf16[4,16,32,192]{3,2,1,0:T(8,128)(2,1)S(1)}, bf16[4,16,32,192]{3,2,1,0:T(8,128)(2,1)S(1)}) fusion(bf16[4,16,32,64]{3,2,1,0:T(8,128)(2,1)S(1)} %constant_dynamic-slice_fusion.11, bf16[1,16,32,64]{3,2,1,0:T(8,128)(2,1)S(1)} %collective-permute-done, bf16[4,16,32,64]{3,2,1,0:T(8,128)(2,1)S(1)} %get-tuple-element.3, ...), kind=kLoop, calls=%fused_computation.20 | loop fusion | flops 8650752 | bytes 4325376 | tf_op jit(solution)/shard_map/concatenate | solution.py:25
  36.4 0.5 fusion.15
  36.9 0.5 copy-done.1
  38.3 1.1 pad_maximum_fusion.2
  39.4 0.5 fusion.14
  40.0 0.5 fusion.16
  40.9 1.1 pad_maximum_fusion.4
  42.0 0.5 fusion.17
  42.5 0.5 fusion.18
  43.3 0.5 fusion.19
  43.9 1.1 pad_maximum_fusion.7
  45.0 0.5 fusion.20
  45.5 0.5 fusion.21
  46.3 0.5 fusion.22
  47.0 1.8 %copy.43 = f32[3456,64]{1,0:T(8,128)} copy(f32[3456,64]{0,1:T(8,128)S(1)} %bitcast_dynamic-update-slice_fusion) | data formatting | bytes 1769472
  48.8 0.8 copy-done.22
  49.6 1.6 %fusion.13 = f32[2048,128]{1,0:T(8,128)S(1)} fusion(bf16[2048,192]{1,0:T(8,128)(2,1)} %bitcast.199, bf16[192,128]{1,0:T(8,128)(2,1)S(1)} %bitcast.218), kind=kOutput, calls=%fused_computation.61 | convolution fusion | flops 100663296 | bytes 1884160 | tf_op jit(solution)/shard_map/dot_general | solution.py:46
  51.3 0.4 convolution_add_fusion.7
  51.7 0.8 copy-done.4
  52.5 0.4 convolution_add_fusion.6
  53.0 0.4 convolution_add_fusion.5
  53.7 0.4 convolution_add_fusion.4
  54.2 0.5 copy-done.6
  54.7 0.4 convolution_add_fusion.3
  55.5 0.4 convolution_add_fusion.2
  56.0 0.4 convolution_add_fusion.1
  56.4 0.7 copy-done.10
  57.5 6.6 %all-reduce.2 = bf16[4,16,32,128]{3,2,1,0:T(8,128)(2,1)} all-reduce(f32[4,16,32,128]{3,2,1,0:T(8,128)S(1)} %bitcast.200), channel_id=1, replica_groups=mesh['grp'=2,'gx'=4,'gy'=2,'col'=2] {'col'}, use_global_device_ids=true, to_apply=%region_0.1 | all-reduce | flops 262144 | bytes 1572864 | tf_op jit(solution)/shard_map/psum | solution.py:68
  64.1 52.3 %reduce-scatter.4.cloned.1.call-done = f32[432,64]{1,0:T(8,128)} async-done(((f32[3456,64]{1,0:T(8,128)}), f32[432,64]{1,0:T(8,128)}) %reduce-scatter.4.cloned.1.call-update) | async-done | bytes 110608
  116.4 1.0 copy.44
  117.5 0.7 broadcast_multiply_fusion
  (71 shorter events, 4.3 us)
Async XLA Ops:
  7.2 29.3 %copy-start = (bf16[4,16,32,128]{3,2,1,0:T(8,128)(2,1)S(1)}, bf16[4,16,32,128]{3,2,1,0:T(8,128)(2,1)}, u32[]{:S(2)}) copy-start(bf16[4,16,32,128]{3,2,1,0:T(8,128)(2,1)} %param.3) | copy-start | bytes 1572868
  7.2 17.8 %copy-start.14 = (bf16[27,128,128]{2,1,0:T(8,128)(2,1)S(1)}, bf16[27,128,128]{2,1,0:T(8,128)(2,1)}, u32[]{:S(2)}) copy-start(bf16[27,128,128]{2,1,0:T(8,128)(2,1)} %param.5) | copy-start | bytes 2654212
  7.2 109.2 %reduce-scatter.4.cloned.1.call-start = ((), (), s32[]{:S(2)}) async-start(), calls=%async_computation.1 | async-start | bytes 1990656
  8.5 7.7 %collective-permute-start = (bf16[1,16,32,64]{3,2,1,0:T(8,128)(2,1)S(1)}, bf16[1,16,32,64]{3,2,1,0:T(8,128)(2,1)S(1)}, u32[]{:S(2)}, u32[]{:S(2)}) collective-permute-start(bf16[1,16,32,64]{3,2,1,0:T(8,128)(2,1)S(1)} %get-tuple-element.42), channel_id=1, source_target_pairs={{0,4},{4,8},{8,12},{1,5},{5,9},{9,13},{2,6},{6,10},{10,14},{3,7},{... | collective-permute-start | bytes 196616 | tf_op jit(solution)/shard_map/ppermute | solution.py:15
  13.4 6.9 %collective-permute-start.1 = (bf16[1,16,32,64]{3,2,1,0:T(8,128)(2,1)S(1)}, bf16[1,16,32,64]{3,2,1,0:T(8,128)(2,1)S(1)}, u32[]{:S(2)}, u32[]{:S(2)}) collective-permute-start(bf16[1,16,32,64]{3,2,1,0:T(8,128)(2,1)S(1)} %get-tuple-element.43), channel_id=1, source_target_pairs={{4,0},{8,4},{12,8},{5,1},{9,5},{13,9},{6,2},{10,6},{14,10},{7,3},{... | collective-permute-start | bytes 196616 | tf_op jit(solution)/shard_map/ppermute | solution.py:17
  20.3 10.8 %collective-permute-start.2 = (bf16[6,1,32,64]{3,2,1,0:T(8,128)(2,1)S(1)}, bf16[6,1,32,64]{3,2,1,0:T(8,128)(2,1)S(1)}, u32[]{:S(2)}, u32[]{:S(2)}) collective-permute-start(bf16[6,1,32,64]{3,2,1,0:T(8,128)(2,1)S(1)} %get-tuple-element.37), channel_id=1, source_target_pairs={{0,2},{1,3},{4,6},{5,7},{8,10},{9,11},{12,14},{13,15},{16,18},{17,... | collective-permute-start | bytes 73736 | tf_op jit(solution)/shard_map/ppermute | solution.py:15
  23.7 7.5 %collective-permute-start.3 = (bf16[6,1,32,64]{3,2,1,0:T(8,128)(2,1)S(1)}, bf16[6,1,32,64]{3,2,1,0:T(8,128)(2,1)S(1)}, u32[]{:S(2)}, u32[]{:S(2)}) collective-permute-start(bf16[6,1,32,64]{3,2,1,0:T(8,128)(2,1)S(1)} %get-tuple-element.38), channel_id=1, source_target_pairs={{2,0},{3,1},{6,4},{7,5},{10,8},{11,9},{14,12},{15,13},{18,16},{19,... | collective-permute-start | bytes 73736 | tf_op jit(solution)/shard_map/ppermute | solution.py:17
  36.4 1.0 copy-start.1
  39.4 1.1 copy-start.3
  39.4 1.4 %copy-start.13 = (bf16[4,16,32,192]{3,2,1,0:T(8,128)(2,1)}, bf16[4,16,32,192]{3,2,1,0:T(8,128)(2,1)S(1)}, u32[]{:S(2)}) copy-start(bf16[4,16,32,192]{3,2,1,0:T(8,128)(2,1)S(1)} %get-tuple-element.44) | copy-start | bytes 2359300
  42.0 1.0 copy-start.7
  42.0 1.4 %copy-start.5 = (bf16[4,16,32,192]{3,2,1,0:T(8,128)(2,1)}, bf16[4,16,32,192]{3,2,1,0:T(8,128)(2,1)S(1)}, u32[]{:S(2)}) copy-start(bf16[4,16,32,192]{3,2,1,0:T(8,128)(2,1)S(1)} %get-tuple-element.47) | copy-start | bytes 2359300
  45.0 1.0 copy-start.11
  45.0 1.3 %copy-start.9 = (bf16[4,16,32,192]{3,2,1,0:T(8,128)(2,1)}, bf16[4,16,32,192]{3,2,1,0:T(8,128)(2,1)S(1)}, u32[]{:S(2)}) copy-start(bf16[4,16,32,192]{3,2,1,0:T(8,128)(2,1)S(1)} %get-tuple-element.49) | copy-start | bytes 2359300
  48.8 0.8 copy-start.22
  48.8 2.5 %copy-start.21 = (bf16[3,128,64]{1,2,0:T(8,128)(2,1)S(1)}, bf16[3,128,64]{1,2,0:T(8,128)(2,1)}, u32[]{:S(2)}) copy-start(bf16[3,128,64]{1,2,0:T(8,128)(2,1)} %copy.47) | copy-start | bytes 147460
  48.8 2.4 %copy-start.2 = (bf16[4,16,32,192]{3,2,1,0:T(8,128)(2,1)S(1)}, bf16[4,16,32,192]{3,2,1,0:T(8,128)(2,1)}, u32[]{:S(2)}) copy-start(bf16[4,16,32,192]{3,2,1,0:T(8,128)(2,1)} %copy-done.1) | copy-start | bytes 2359300
  51.2 1.2 copy-start.4
  51.2 1.2 copy-start.20
  51.7 1.3 %copy-start.8 = (bf16[4,16,32,192]{3,2,1,0:T(8,128)(2,1)S(1)}, bf16[4,16,32,192]{3,2,1,0:T(8,128)(2,1)}, u32[]{:S(2)}) copy-start(bf16[4,16,32,192]{3,2,1,0:T(8,128)(2,1)} %copy-done.7) | copy-start | bytes 2359300
  51.7 1.3 %copy-start.19 = (bf16[3,128,64]{1,2,0:T(8,128)(2,1)S(1)}, bf16[3,128,64]{1,2,0:T(8,128)(2,1)}, u32[]{:S(2)}) copy-start(bf16[3,128,64]{1,2,0:T(8,128)(2,1)} %copy.49) | copy-start | bytes 147460
  52.9 0.8 copy-start.18
  53.4 1.2 copy-start.6
  53.4 1.2 copy-start.17
  54.1 1.3 %copy-start.12 = (bf16[4,16,32,192]{3,2,1,0:T(8,128)(2,1)S(1)}, bf16[4,16,32,192]{3,2,1,0:T(8,128)(2,1)}, u32[]{:S(2)}) copy-start(bf16[4,16,32,192]{3,2,1,0:T(8,128)(2,1)} %copy-done.11) | copy-start | bytes 2359300
  54.1 1.3 %copy-start.16 = (bf16[3,128,64]{1,2,0:T(8,128)(2,1)S(1)}, bf16[3,128,64]{1,2,0:T(8,128)(2,1)}, u32[]{:S(2)}) copy-start(bf16[3,128,64]{1,2,0:T(8,128)(2,1)} %copy.52) | copy-start | bytes 147460
  55.1 0.9 copy-start.15
  55.9 1.2 copy-start.10
Sparse Core Ops, SparseCore 0:
  48.9 67.4 reduce-scatter.3
where the time goes:
time: 125 us
  waiting for transfers between devices  56.6 us (45%)
  local copies, waits for them, and re-layouts  20.4 us (16%)
  between operations  14.6 us (12%)
  starting transfers between devices  11 us (9%)
  matrix products  9.23 us (7%)
  blocking collectives  6.63 us (5%)
  other arithmetic  6.59 us (5%)
    unnamed x2, waiting for transfers between devices  52.3 us
    unnamed x65, local copies, waits for them, and re-layouts  13.6 us
    ppermute x2, starting transfers between devices, with_halo(): lax.ppermute(tail, axis, [(i, (i + 1) % count) for i in range(ends)])  8.33 us
    psum x1, blocking collectives, on_device(): grad_in = lax.psum(inner, 'col').astype(jnp.bfloat16)  6.63 us
    concatenate x4, other arithmetic, depth_taps(): jnp.concatenate([lax.slice_in_dim(block, s, s + depth, axis=2) for s in s...  5.16 us
    dot_general x9, matrix products, local_terms(): jnp.dot(stacked, kernel_rows(weight_part, a, b), preferred_element_type=j...  4.99 us
    dot_general x9, matrix products, local_terms(): lax.dot_general(xflat, stacked, contract_rows, preferred_element_type=jnp...  4.23 us
    ppermute x2, waiting for transfers between devices, with_halo(): lax.ppermute(head, axis, [((i + 1) % count, i) for i in range(ends)])  4.13 us
  transfers between devices with their start and end apart: 5, of which 3 were waited for; matrix products, arithmetic and copies ran while one was open for 10% of the time, Pallas kernels for 0%

commit v1 on v0

--- a/solution.py
+++ b/solution.py
@@ -55,6 +55,24 @@
     return (accum.reshape(size_x, size_y, depth, chans), jnp.concatenate(pieces, axis=0))
 
 
+def scatter_sum(blocks, axis, dim):
+    count = lax.axis_size(axis)
+    if count == 1:
+        return lax.index_in_dim(blocks, 0, dim, keepdims=False)
+    if count > 4:
+        return lax.psum_scatter(blocks, axis, scatter_dimension=dim, tiled=False)
+    me = lax.axis_index(axis)
+    total = lax.dynamic_index_in_dim(blocks, me, dim, keepdims=False)
+    for shift in range(1, count):
+        for sign in (1, -1):
+            step = sign * shift
+            pairs = [(j, j + step) for j in range(count) if 0 <= j + step < count]
+            target = jnp.clip(me + step, 0, count - 1)
+            part = lax.dynamic_index_in_dim(blocks, target, dim, keepdims=False)
+            total = total + lax.ppermute(part, axis, pairs)
+    return total
+
+
 def on_device(x_act, grad_out, weight):
     size_x, size_y, depth, chans = x_act.shape
     ncores = lax.axis_size("col")
@@ -66,7 +84,10 @@
     gdeep = jnp.pad(grim, ((0, 0), (0, 0), (1, 1), (0, 0)))
     inner, weight_terms = local_terms(gdeep, x_act, weight_share, size_x, size_y, depth)
     grad_in = lax.psum(inner, "col").astype(jnp.bfloat16)
-    owned = lax.psum_scatter(weight_terms, ("gx", "gy"), scatter_dimension=0, tiled=True)
+    nx = lax.axis_size("gx")
+    ny = lax.axis_size("gy")
+    blocks = weight_terms.reshape(nx, ny, weight_terms.shape[0] // (nx * ny), weight_terms.shape[1])
+    owned = scatter_sum(scatter_sum(blocks, "gy", 1), "gx", 0)
     total_cells = size_x * lax.axis_size("gx") * size_y * lax.axis_size("gy") * depth
     grad_weight = owned / jnp.sqrt(jnp.float32(total_cells))
     return (grad_in, grad_weight)

time: 125 us -> 90.2 us (0.72)
  waiting for transfers between devices: 56.6 us -> 8.25 us
  starting transfers between devices: 11 us -> 34.5 us
  between operations: 14.6 us -> 1.42 us
  local copies, waits for them, and re-layouts: 20.4 us -> 23.3 us
    unnamed x2 -> x0, waiting for transfers between devices: 52.3 us -> none
    ppermute x0 -> x8, starting transfers between devices: none -> 23.5 us  [scatter_sum(): total = total + lax.ppermute(part, axis, pairs)]
    ppermute x0 -> x8, waiting for transfers between devices: none -> 3.94 us  [scatter_sum(): total = total + lax.ppermute(part, axis, pairs)]
    dynamic_slice x0 -> x2, local copies, waits for them, and re-layouts: none -> 2.41 us  [scatter_sum(): total = lax.dynamic_index_in_dim(blocks, me, dim, keepdims=False)]
    reshape x0 -> x1, local copies, waits for them, and re-layouts: none -> 1.37 us  [on_device(): weight_terms.reshape(nx, ny, weight_terms.shape[0] // (nx * ny), weight_t...]
    unnamed x65 -> x77, local copies, waits for them, and re-layouts: 13.6 us -> 12.8 us
  transfers between devices with their start and end apart: 5 -> 12, of which waited for: 3 -> 3; matrix products, arithmetic and copies ran while one was open for 10% -> 13% of each run, Pallas kernels for 0% -> 0%
where the time goes in v1:
time: 90.2 us; the launch traced here: 89.1 us
  starting transfers between devices  34.5 us (38%)
  local copies, waits for them, and re-layouts  23.3 us (26%)
  waiting for transfers between devices  8.25 us (9%)
  matrix products  8.01 us (9%)
  other arithmetic  6.93 us (8%)
  blocking collectives  6.63 us (7%)
  between operations  1.42 us (2%)
    ppermute x8, starting transfers between devices, scatter_sum(): total = total + lax.ppermute(part, axis, pairs)  23.5 us
    unnamed x77, local copies, waits for them, and re-layouts  12.8 us
    ppermute x2, starting transfers between devices, with_halo(): lax.ppermute(tail, axis, [(i, (i + 1) % count) for i in range(ends)])  8.46 us
    psum x1, blocking collectives, on_device(): grad_in = lax.psum(inner, 'col').astype(jnp.bfloat16)  6.63 us
    concatenate x4, other arithmetic, depth_taps(): jnp.concatenate([lax.slice_in_dim(block, s, s + depth, axis=2) for s in s...  5.17 us
    dot_general x9, matrix products, local_terms(): lax.dot_general(xflat, stacked, contract_rows, preferred_element_type=jnp...  4.21 us
    ppermute x2, waiting for transfers between devices, with_halo(): lax.ppermute(head, axis, [((i + 1) % count, i) for i in range(ends)])  4.13 us
    ppermute x8, waiting for transfers between devices, scatter_sum(): total = total + lax.ppermute(part, axis, pairs)  3.94 us
  transfers between devices with their start and end apart: 12, of which 3 were waited for; matrix products, arithmetic and copies ran while one was open for 13% of the time, Pallas kernels for 0%

profile of v1, /device:TPU:0, one launch (start us, length us, event | category | flops | bytes accessed | tf_op | source)
XLA Modules:
  0.0 89.1 jit_solution(15799991133731236435)
XLA Ops:
  0.6 1.2 %constant_dynamic-slice_fusion.9 = (bf16[1,16,32,64]{3,2,1,0:T(8,128)(2,1)S(1)}, bf16[1,16,32,64]{3,2,1,0:T(8,128)(2,1)S(1)}) fusion(bf16[4,16,32,128]{3,2,1,0:T(8,128)(2,1)} %param.4, s32[]{:T(128)S(6)} %add.123, s32[]{:T(128)S(6)} %select_n.20), kind=kLoop, calls=%fused_computation.71 | loop fusion | bytes 262152 | tf_op jit(solution)/shard_map/slice | solution.py:12
  1.8 5.1 %collective-permute-start = (bf16[1,16,32,64]{3,2,1,0:T(8,128)(2,1)S(1)}, bf16[1,16,32,64]{3,2,1,0:T(8,128)(2,1)S(1)}, u32[]{:S(2)}, u32[]{:S(2)}) collective-permute-start(bf16[1,16,32,64]{3,2,1,0:T(8,128)(2,1)S(1)} %get-tuple-element.52), channel_id=1, source_target_pairs={{0,4},{4,8},{8,12},{1,5},{5,9},{9,13},{2,6},{6,10},{10,14},{3,7},{... | collective-permute-start | bytes 196616 | tf_op jit(solution)/shard_map/ppermute | solution.py:15
  6.9 1.3 %collective-permute-start.1 = (bf16[1,16,32,64]{3,2,1,0:T(8,128)(2,1)S(1)}, bf16[1,16,32,64]{3,2,1,0:T(8,128)(2,1)S(1)}, u32[]{:S(2)}, u32[]{:S(2)}) collective-permute-start(bf16[1,16,32,64]{3,2,1,0:T(8,128)(2,1)S(1)} %get-tuple-element.53), channel_id=1, source_target_pairs={{4,0},{8,4},{12,8},{5,1},{9,5},{13,9},{6,2},{10,6},{14,10},{7,3},{... | collective-permute-start | bytes 196616 | tf_op jit(solution)/shard_map/ppermute | solution.py:17
  8.2 1.3 %constant_dynamic-slice_fusion.21 = bf16[4,16,32,64]{3,2,1,0:T(8,128)(2,1)S(1)} fusion(bf16[4,16,32,128]{3,2,1,0:T(8,128)(2,1)} %param.4, s32[]{:T(128)S(6)} %select_n.20), kind=kLoop, calls=%fused_computation.83 | loop fusion | bytes 524292 | tf_op jit(solution)/shard_map/dynamic_slice | solution.py:81
  9.6 4.1 %collective-permute-done.1 = bf16[1,16,32,64]{3,2,1,0:T(8,128)(2,1)S(1)} collective-permute-done((bf16[1,16,32,64]{3,2,1,0:T(8,128)(2,1)S(1)}, bf16[1,16,32,64]{3,2,1,0:T(8,128)(2,1)S(1)}, u32[]{:S(2)}, u32[]{:S(2)}) %collective-permute-start.1) | collective-permute-done | bytes 65568 | tf_op jit(solution)/shard_map/ppermute | solution.py:17
  13.8 3.4 %collective-permute-start.2 = (bf16[6,1,32,64]{3,2,1,0:T(8,128)(2,1)S(1)}, bf16[6,1,32,64]{3,2,1,0:T(8,128)(2,1)S(1)}, u32[]{:S(2)}, u32[]{:S(2)}) collective-permute-start(bf16[6,1,32,64]{3,2,1,0:T(8,128)(2,1)S(1)} %get-tuple-element.40), channel_id=1, source_target_pairs={{0,2},{1,3},{4,6},{5,7},{8,10},{9,11},{12,14},{13,15},{16,18},{17,... | collective-permute-start | bytes 73736 | tf_op jit(solution)/shard_map/ppermute | solution.py:15
  17.2 1.3 %collective-permute-start.3 = (bf16[6,1,32,64]{3,2,1,0:T(8,128)(2,1)S(1)}, bf16[6,1,32,64]{3,2,1,0:T(8,128)(2,1)S(1)}, u32[]{:S(2)}, u32[]{:S(2)}) collective-permute-start(bf16[6,1,32,64]{3,2,1,0:T(8,128)(2,1)S(1)} %get-tuple-element.41), channel_id=1, source_target_pairs={{2,0},{3,1},{6,4},{7,5},{10,8},{11,9},{14,12},{15,13},{18,16},{19,... | collective-permute-start | bytes 73736 | tf_op jit(solution)/shard_map/ppermute | solution.py:17
  18.9 0.7 copy.35
  19.6 0.7 copy.36
  20.3 0.7 copy.37
  21.0 0.7 copy.38
  21.7 0.7 copy.39
  22.4 0.7 copy.40
  23.2 0.7 copy.41
  23.9 0.7 copy.42
  24.7 0.5 select_maximum_fusion
  25.2 2.8 %fusion.17 = (bf16[4,16,32,64]{3,2,1,0:T(8,128)(2,1)S(1)}, bf16[4,16,32,64]{3,2,1,0:T(8,128)(2,1)S(1)}, bf16[4,16,32,64]{3,2,1,0:T(8,128)(2,1)S(1)}, bf16[4,16,3...) fusion(bf16[6,18,34,64]{3,2,1,0:T(8,128)(2,1)S(1)} %select_maxi, ...), kind=kLoop, calls=%fused_computation.84 | loop fusion | bytes 9437184 | tf_op jit(solution)/shard_map/slice | solution.py:25
  28.0 2.0 %fusion.7 = (bf16[4,16,32,192]{3,2,1,0:T(8,128)(2,1)S(1)}, bf16[4,16,32,192]{3,2,1,0:T(8,128)(2,1)S(1)}, bf16[4,16,32,192]{3,2,1,0:T(8,128)(2,1)S(1)}) fusion(bf16[4,16,32,64]{3,2,1,0:T(8,128)(2,1)S(1)} %constant_dynamic-slice_fusion.21, bf16[1,16,32,64]{3,2,1,0:T(8,128)(2,1)S(1)} %collective-permute-done, bf16[4,16,32,64]{3,2,1,0:T(8,128)(2,1)S(1)} %get-tuple-element.3, ...), kind=kLoop, calls=%fused_computation.20 | loop fusion | flops 8650752 | bytes 4325376 | tf_op jit(solution)/shard_map/concatenate | solution.py:25
  30.0 0.5 fusion.22
  30.5 0.5 copy-done.3
  31.8 1.1 %pad_maximum_fusion.2 = (bf16[4,16,32,192]{3,2,1,0:T(8,128)(2,1)S(1)}, bf16[4,16,32,192]{3,2,1,0:T(8,128)(2,1)S(1)}) fusion(bf16[4,16,32,64]{3,2,1,0:T(8,128)(2,1)S(1)} %get-tuple-element.17, bf16[4,16,32,64]{3,2,1,0:T(8,128)(2,1)S(1)} %get-tuple-element.37, bf16[4,16,32,64]{3,2,1,0:T(8,128)(2,1)S(1)} %get-tuple-element.18, ...), kind=kLoop, calls=%fused_computation.24 | loop fusion | flops 4718592 | bytes 3145728 | tf_op jit(solution)/shard_map/concatenate | solution.py:25
  32.9 0.5 fusion.21
  33.4 0.5 copy-done.15
  34.8 1.1 %pad_maximum_fusion.4 = (bf16[4,16,32,192]{3,2,1,0:T(8,128)(2,1)S(1)}, bf16[4,16,32,192]{3,2,1,0:T(8,128)(2,1)S(1)}) fusion(bf16[4,16,32,64]{3,2,1,0:T(8,128)(2,1)S(1)} %get-tuple-element.11, bf16[4,16,32,64]{3,2,1,0:T(8,128)(2,1)S(1)} %get-tuple-element.36, bf16[4,16,32,64]{3,2,1,0:T(8,128)(2,1)S(1)} %get-tuple-element.12, ...), kind=kLoop, calls=%fused_computation.26 | loop fusion | flops 4718592 | bytes 3145728 | tf_op jit(solution)/shard_map/concatenate | solution.py:25
  35.9 0.5 fusion.24
  36.9 0.5 fusion.25
  38.0 1.1 %pad_maximum_fusion.7 = (bf16[4,16,32,192]{3,2,1,0:T(8,128)(2,1)S(1)}, bf16[4,16,32,192]{3,2,1,0:T(8,128)(2,1)S(1)}) fusion(bf16[4,16,32,64]{3,2,1,0:T(8,128)(2,1)S(1)} %get-tuple-element.5, bf16[4,16,32,64]{3,2,1,0:T(8,128)(2,1)S(1)} %get-tuple-element.35, bf16[4,16,32,64]{3,2,1,0:T(8,128)(2,1)S(1)} %get-tuple-element.6, ...), kind=kLoop, calls=%fused_computation.29 | loop fusion | flops 4718592 | bytes 3145728 | tf_op jit(solution)/shard_map/concatenate | solution.py:25
  39.1 0.5 fusion.27
  39.6 0.5 copy-done.13
  41.4 1.4 %reshape.156 = f32[4,2,432,64]{2,1,0,3:T(2,128)S(1)} reshape(f32[3456,64]{0,1:T(8,128)S(1)} %bitcast_dynamic-update-slice_fusion) | data formatting | bytes 1769472 | tf_op jit(solution)/shard_map/reshape | solution.py:89
  42.7 1.6 %constant_dynamic-slice_fusion.19 = (f32[4,1,432,64]{2,1,0,3:T(1,128)S(1)}, f32[4,1,432,64]{2,1,0,3:T(1,128)S(1)}, f32[4,1,432,64]{2,1,0,3:T(1,128)S(1)}) fusion(f32[4,2,432,64]{2,1,0,3:T(2,128)S(1)} %reshape.156, s32[]{:T(128)S(6)} %select_n.21, s32[]{:T(128)S(6)} %min.26, s32[]{:T(128)S(6)} %min.25), kind=kLoop, calls=%fused_computation.81 | loop fusion | bytes 2654220 | tf_op jit(solution)/shard_map/jit(dynamic_index_in_dim)/dynamic_slice | solution.py:65
  44.5 4.7 %collective-permute-start.4 = (f32[4,432,64]{1,0,2:T(4,128)S(1)}, f32[4,432,64]{1,0,2:T(4,128)S(1)}, u32[]{:S(2)}, u32[]{:S(2)}) collective-permute-start(f32[4,432,64]{1,0,2:T(4,128)S(1)} %bitcast.253), channel_id=1, source_target_pairs={{0,2},{1,3},{4,6},{5,7},{8,10},{9,11},{12,14},{13,15},{16,18},{17,... | collective-permute-start | bytes 1327112 | tf_op jit(solution)/shard_map/ppermute | solution.py:72
  49.4 1.6 %collective-permute-start.5 = (f32[4,432,64]{1,0,2:T(4,128)S(1)}, f32[4,432,64]{1,0,2:T(4,128)S(1)}, u32[]{:S(2)}, u32[]{:S(2)}) collective-permute-start(f32[4,432,64]{1,0,2:T(4,128)S(1)} %bitcast.254), channel_id=1, source_target_pairs={{2,0},{3,1},{6,4},{7,5},{10,8},{11,9},{14,12},{15,13},{18,16},{19,... | collective-permute-start | bytes 1327112 | tf_op jit(solution)/shard_map/ppermute | solution.py:72
  52.0 0.8 copy-done.8
  53.2 0.8 copy-done.12
  54.4 0.8 copy-done.2
  55.6 0.8 copy-done.10
  56.9 0.8 copy-done.14
  58.9 3.9 %collective-permute-done.5 = f32[4,432,64]{1,0,2:T(4,128)S(1)} collective-permute-done((f32[4,432,64]{1,0,2:T(4,128)S(1)}, f32[4,432,64]{1,0,2:T(4,128)S(1)}, u32[]{:S(2)}, u32[]{:S(2)}) %collective-permute-start.5) | collective-permute-done | bytes 442400 | tf_op jit(solution)/shard_map/ppermute | solution.py:72
  63.1 0.8 constant_dynamic-slice_fusion.16
  63.9 3.8 %collective-permute-start.10 = (f32[432,64]{0,1:T(8,128)S(1)}, f32[432,64]{0,1:T(8,128)S(1)}, u32[]{:S(2)}, u32[]{:S(2)}) collective-permute-start(f32[432,64]{0,1:T(8,128)S(1)} %bitcast.264), channel_id=1, source_target_pairs={{0,12},{1,13},{2,14},{3,15},{16,28},{17,29},{18,30},{19,31}} | collective-permute-start | bytes 331784 | tf_op jit(solution)/shard_map/ppermute | solution.py:72
  68.2 1.3 %collective-permute-start.11 = (f32[432,64]{0,1:T(8,128)S(1)}, f32[432,64]{0,1:T(8,128)S(1)}, u32[]{:S(2)}, u32[]{:S(2)}) collective-permute-start(f32[432,64]{0,1:T(8,128)S(1)} %bitcast.265), channel_id=1, source_target_pairs={{12,0},{13,1},{14,2},{15,3},{28,16},{29,17},{30,18},{31,19}} | collective-permute-start | bytes 331784 | tf_op jit(solution)/shard_map/ppermute | solution.py:72
  69.5 1.3 %collective-permute-start.6 = (f32[432,64]{0,1:T(8,128)S(1)}, f32[432,64]{0,1:T(8,128)S(1)}, u32[]{:S(2)}, u32[]{:S(2)}) collective-permute-start(f32[432,64]{0,1:T(8,128)S(1)} %bitcast.266), channel_id=1, source_target_pairs={{0,4},{4,8},{8,12},{1,5},{5,9},{9,13},{2,6},{6,10},{10,14},{3,7},{... | collective-permute-start | bytes 331784 | tf_op jit(solution)/shard_map/ppermute | solution.py:72
  70.9 1.3 %collective-permute-start.7 = (f32[432,64]{0,1:T(8,128)S(1)}, f32[432,64]{0,1:T(8,128)S(1)}, u32[]{:S(2)}, u32[]{:S(2)}) collective-permute-start(f32[432,64]{0,1:T(8,128)S(1)} %bitcast.267), channel_id=1, source_target_pairs={{4,0},{8,4},{12,8},{5,1},{9,5},{13,9},{6,2},{10,6},{14,10},{7,3},{... | collective-permute-start | bytes 331784 | tf_op jit(solution)/shard_map/ppermute | solution.py:72
  72.2 8.2 %collective-permute-start.8 = (f32[432,64]{0,1:T(8,128)S(1)}, f32[432,64]{0,1:T(8,128)S(1)}, u32[]{:S(2)}, u32[]{:S(2)}) collective-permute-start(f32[432,64]{0,1:T(8,128)S(1)} %bitcast.268), channel_id=1, source_target_pairs={{0,8},{4,12},{1,9},{5,13},{2,10},{6,14},{3,11},{7,15},{16,24},{20,... | collective-permute-start | bytes 331784 | tf_op jit(solution)/shard_map/ppermute | solution.py:72
  80.4 1.3 %collective-permute-start.9 = (f32[432,64]{0,1:T(8,128)S(1)}, f32[432,64]{0,1:T(8,128)S(1)}, u32[]{:S(2)}, u32[]{:S(2)}) collective-permute-start(f32[432,64]{0,1:T(8,128)S(1)} %bitcast.269), channel_id=1, source_target_pairs={{8,0},{12,4},{9,1},{13,5},{10,2},{14,6},{11,3},{15,7},{24,16},{28,... | collective-permute-start | bytes 331784 | tf_op jit(solution)/shard_map/ppermute | solution.py:72
  81.7 6.6 %all-reduce.2 = bf16[4,16,32,128]{3,2,1,0:T(8,128)(2,1)} all-reduce(f32[4,16,32,128]{3,2,1,0:T(8,128)S(1)} %bitcast.243), channel_id=1, replica_groups=mesh['grp'=2,'gx'=4,'gy'=2,'col'=2] {'col'}, use_global_device_ids=true, to_apply=%region_0.1 | all-reduce | flops 262144 | bytes 1572864 | tf_op jit(solution)/shard_map/psum | solution.py:86
  88.3 0.7 fusion.16
  (100 shorter events, 9.5 us)
Async XLA Ops:
  0.6 29.4 %copy-start = (bf16[4,16,32,128]{3,2,1,0:T(8,128)(2,1)S(1)}, bf16[4,16,32,128]{3,2,1,0:T(8,128)(2,1)}, u32[]{:S(2)}) copy-start(bf16[4,16,32,128]{3,2,1,0:T(8,128)(2,1)} %param.3) | copy-start | bytes 1572868
  1.8 16.7 %copy-start.17 = (bf16[27,128,128]{2,1,0:T(8,128)(2,1)S(1)}, bf16[27,128,128]{2,1,0:T(8,128)(2,1)}, u32[]{:S(2)}) copy-start(bf16[27,128,128]{2,1,0:T(8,128)(2,1)} %param.5) | copy-start | bytes 2654212
  1.8 7.8 %collective-permute-start = (bf16[1,16,32,64]{3,2,1,0:T(8,128)(2,1)S(1)}, bf16[1,16,32,64]{3,2,1,0:T(8,128)(2,1)S(1)}, u32[]{:S(2)}, u32[]{:S(2)}) collective-permute-start(bf16[1,16,32,64]{3,2,1,0:T(8,128)(2,1)S(1)} %get-tuple-element.52), channel_id=1, source_target_pairs={{0,4},{4,8},{8,12},{1,5},{5,9},{9,13},{2,6},{6,10},{10,14},{3,7},{... | collective-permute-start | bytes 196616 | tf_op jit(solution)/shard_map/ppermute | solution.py:15
  6.9 6.9 %collective-permute-start.1 = (bf16[1,16,32,64]{3,2,1,0:T(8,128)(2,1)S(1)}, bf16[1,16,32,64]{3,2,1,0:T(8,128)(2,1)S(1)}, u32[]{:S(2)}, u32[]{:S(2)}) collective-permute-start(bf16[1,16,32,64]{3,2,1,0:T(8,128)(2,1)S(1)} %get-tuple-element.53), channel_id=1, source_target_pairs={{4,0},{8,4},{12,8},{5,1},{9,5},{13,9},{6,2},{10,6},{14,10},{7,3},{... | collective-permute-start | bytes 196616 | tf_op jit(solution)/shard_map/ppermute | solution.py:17
  13.8 10.9 %collective-permute-start.2 = (bf16[6,1,32,64]{3,2,1,0:T(8,128)(2,1)S(1)}, bf16[6,1,32,64]{3,2,1,0:T(8,128)(2,1)S(1)}, u32[]{:S(2)}, u32[]{:S(2)}) collective-permute-start(bf16[6,1,32,64]{3,2,1,0:T(8,128)(2,1)S(1)} %get-tuple-element.40), channel_id=1, source_target_pairs={{0,2},{1,3},{4,6},{5,7},{8,10},{9,11},{12,14},{13,15},{16,18},{17,... | collective-permute-start | bytes 73736 | tf_op jit(solution)/shard_map/ppermute | solution.py:15
  17.2 7.5 %collective-permute-start.3 = (bf16[6,1,32,64]{3,2,1,0:T(8,128)(2,1)S(1)}, bf16[6,1,32,64]{3,2,1,0:T(8,128)(2,1)S(1)}, u32[]{:S(2)}, u32[]{:S(2)}) collective-permute-start(bf16[6,1,32,64]{3,2,1,0:T(8,128)(2,1)S(1)} %get-tuple-element.41), channel_id=1, source_target_pairs={{2,0},{3,1},{6,4},{7,5},{10,8},{11,9},{14,12},{15,13},{18,16},{19,... | collective-permute-start | bytes 73736 | tf_op jit(solution)/shard_map/ppermute | solution.py:17
  30.0 1.0 %copy-start.3 = (bf16[4,16,32,192]{3,2,1,0:T(8,128)(2,1)}, bf16[4,16,32,192]{3,2,1,0:T(8,128)(2,1)S(1)}, u32[]{:S(2)}) copy-start(bf16[4,16,32,192]{3,2,1,0:T(8,128)(2,1)S(1)} %get-tuple-element.51) | copy-start | bytes 2359300
  30.0 6.9 %copy-start.1 = (bf16[4,16,32,192]{3,2,1,0:T(8,128)(2,1)}, bf16[4,16,32,192]{3,2,1,0:T(8,128)(2,1)S(1)}, u32[]{:S(2)}) copy-start(bf16[4,16,32,192]{3,2,1,0:T(8,128)(2,1)S(1)} %get-tuple-element.50) | copy-start | bytes 2359300
  32.9 1.0 %copy-start.15 = (bf16[4,16,32,192]{3,2,1,0:T(8,128)(2,1)}, bf16[4,16,32,192]{3,2,1,0:T(8,128)(2,1)S(1)}, u32[]{:S(2)}) copy-start(bf16[4,16,32,192]{3,2,1,0:T(8,128)(2,1)S(1)} %get-tuple-element.54) | copy-start | bytes 2359300
  32.9 1.3 %copy-start.7 = (bf16[4,16,32,192]{3,2,1,0:T(8,128)(2,1)}, bf16[4,16,32,192]{3,2,1,0:T(8,128)(2,1)S(1)}, u32[]{:S(2)}) copy-start(bf16[4,16,32,192]{3,2,1,0:T(8,128)(2,1)S(1)} %get-tuple-element.55) | copy-start | bytes 2359300
  35.8 1.0 %copy-start.11 = (bf16[4,16,32,192]{3,2,1,0:T(8,128)(2,1)}, bf16[4,16,32,192]{3,2,1,0:T(8,128)(2,1)S(1)}, u32[]{:S(2)}) copy-start(bf16[4,16,32,192]{3,2,1,0:T(8,128)(2,1)S(1)} %get-tuple-element.56) | copy-start | bytes 2359300
  35.9 1.6 %copy-start.9 = (bf16[4,16,32,192]{3,2,1,0:T(8,128)(2,1)}, bf16[4,16,32,192]{3,2,1,0:T(8,128)(2,1)S(1)}, u32[]{:S(2)}) copy-start(bf16[4,16,32,192]{3,2,1,0:T(8,128)(2,1)S(1)} %get-tuple-element.57) | copy-start | bytes 2359300
  39.1 1.0 %copy-start.13 = (bf16[4,16,32,192]{3,2,1,0:T(8,128)(2,1)}, bf16[4,16,32,192]{3,2,1,0:T(8,128)(2,1)S(1)}, u32[]{:S(2)}) copy-start(bf16[4,16,32,192]{3,2,1,0:T(8,128)(2,1)S(1)} %get-tuple-element.58) | copy-start | bytes 2359300
  39.1 1.6 %copy-start.5 = (bf16[4,16,32,192]{3,2,1,0:T(8,128)(2,1)}, bf16[4,16,32,192]{3,2,1,0:T(8,128)(2,1)S(1)}, u32[]{:S(2)}) copy-start(bf16[4,16,32,192]{3,2,1,0:T(8,128)(2,1)S(1)} %get-tuple-element.59) | copy-start | bytes 2359300
  44.4 6.7 %copy-start.16 = (bf16[4,16,32,192]{3,2,1,0:T(8,128)(2,1)S(1)}, bf16[4,16,32,192]{3,2,1,0:T(8,128)(2,1)}, u32[]{:S(2)}) copy-start(bf16[4,16,32,192]{3,2,1,0:T(8,128)(2,1)} %copy-done.15) | copy-start | bytes 2359300
  44.4 6.7 %copy-start.25 = (bf16[3,128,64]{1,2,0:T(8,128)(2,1)S(1)}, bf16[3,128,64]{1,2,0:T(8,128)(2,1)}, u32[]{:S(2)}) copy-start(bf16[3,128,64]{1,2,0:T(8,128)(2,1)} %copy.35) | copy-start | bytes 147460
  44.5 14.4 %collective-permute-start.4 = (f32[4,432,64]{1,0,2:T(4,128)S(1)}, f32[4,432,64]{1,0,2:T(4,128)S(1)}, u32[]{:S(2)}, u32[]{:S(2)}) collective-permute-start(f32[4,432,64]{1,0,2:T(4,128)S(1)} %bitcast.253), channel_id=1, source_target_pairs={{0,2},{1,3},{4,6},{5,7},{8,10},{9,11},{12,14},{13,15},{16,18},{17,... | collective-permute-start | bytes 1327112 | tf_op jit(solution)/shard_map/ppermute | solution.py:72
  49.4 2.1 %copy-start.4 = (bf16[4,16,32,192]{3,2,1,0:T(8,128)(2,1)S(1)}, bf16[4,16,32,192]{3,2,1,0:T(8,128)(2,1)}, u32[]{:S(2)}) copy-start(bf16[4,16,32,192]{3,2,1,0:T(8,128)(2,1)} %copy-done.3) | copy-start | bytes 2359300
  49.4 2.1 %copy-start.24 = (bf16[3,128,64]{1,2,0:T(8,128)(2,1)S(1)}, bf16[3,128,64]{1,2,0:T(8,128)(2,1)}, u32[]{:S(2)}) copy-start(bf16[3,128,64]{1,2,0:T(8,128)(2,1)} %copy.36) | copy-start | bytes 147460
  49.4 13.4 %collective-permute-start.5 = (f32[4,432,64]{1,0,2:T(4,128)S(1)}, f32[4,432,64]{1,0,2:T(4,128)S(1)}, u32[]{:S(2)}, u32[]{:S(2)}) collective-permute-start(f32[4,432,64]{1,0,2:T(4,128)S(1)} %bitcast.254), channel_id=1, source_target_pairs={{2,0},{3,1},{6,4},{7,5},{10,8},{11,9},{14,12},{15,13},{18,16},{19,... | collective-permute-start | bytes 1327112 | tf_op jit(solution)/shard_map/ppermute | solution.py:72
  51.5 1.2 %copy-start.8 = (bf16[4,16,32,192]{3,2,1,0:T(8,128)(2,1)S(1)}, bf16[4,16,32,192]{3,2,1,0:T(8,128)(2,1)}, u32[]{:S(2)}) copy-start(bf16[4,16,32,192]{3,2,1,0:T(8,128)(2,1)} %copy-done.7) | copy-start | bytes 2359300
  51.5 1.2 %copy-start.23 = (bf16[3,128,64]{1,2,0:T(8,128)(2,1)S(1)}, bf16[3,128,64]{1,2,0:T(8,128)(2,1)}, u32[]{:S(2)}) copy-start(bf16[3,128,64]{1,2,0:T(8,128)(2,1)} %copy.37) | copy-start | bytes 147460
  52.8 1.2 %copy-start.12 = (bf16[4,16,32,192]{3,2,1,0:T(8,128)(2,1)S(1)}, bf16[4,16,32,192]{3,2,1,0:T(8,128)(2,1)}, u32[]{:S(2)}) copy-start(bf16[4,16,32,192]{3,2,1,0:T(8,128)(2,1)} %copy-done.11) | copy-start | bytes 2359300
  52.8 1.2 %copy-start.22 = (bf16[3,128,64]{1,2,0:T(8,128)(2,1)S(1)}, bf16[3,128,64]{1,2,0:T(8,128)(2,1)}, u32[]{:S(2)}) copy-start(bf16[3,128,64]{1,2,0:T(8,128)(2,1)} %copy.38) | copy-start | bytes 147460
  54.0 1.2 %copy-start.2 = (bf16[4,16,32,192]{3,2,1,0:T(8,128)(2,1)S(1)}, bf16[4,16,32,192]{3,2,1,0:T(8,128)(2,1)}, u32[]{:S(2)}) copy-start(bf16[4,16,32,192]{3,2,1,0:T(8,128)(2,1)} %copy-done.1) | copy-start | bytes 2359300
  54.0 1.2 %copy-start.21 = (bf16[3,128,64]{1,2,0:T(8,128)(2,1)S(1)}, bf16[3,128,64]{1,2,0:T(8,128)(2,1)}, u32[]{:S(2)}) copy-start(bf16[3,128,64]{1,2,0:T(8,128)(2,1)} %copy.39) | copy-start | bytes 147460
  55.2 1.2 %copy-start.10 = (bf16[4,16,32,192]{3,2,1,0:T(8,128)(2,1)S(1)}, bf16[4,16,32,192]{3,2,1,0:T(8,128)(2,1)}, u32[]{:S(2)}) copy-start(bf16[4,16,32,192]{3,2,1,0:T(8,128)(2,1)} %copy-done.9) | copy-start | bytes 2359300
  55.2 1.2 %copy-start.20 = (bf16[3,128,64]{1,2,0:T(8,128)(2,1)S(1)}, bf16[3,128,64]{1,2,0:T(8,128)(2,1)}, u32[]{:S(2)}) copy-start(bf16[3,128,64]{1,2,0:T(8,128)(2,1)} %copy.40) | copy-start | bytes 147460
  56.4 1.2 %copy-start.14 = (bf16[4,16,32,192]{3,2,1,0:T(8,128)(2,1)S(1)}, bf16[4,16,32,192]{3,2,1,0:T(8,128)(2,1)}, u32[]{:S(2)}) copy-start(bf16[4,16,32,192]{3,2,1,0:T(8,128)(2,1)} %copy-done.13) | copy-start | bytes 2359300
  56.5 1.2 %copy-start.19 = (bf16[3,128,64]{1,2,0:T(8,128)(2,1)S(1)}, bf16[3,128,64]{1,2,0:T(8,128)(2,1)}, u32[]{:S(2)}) copy-start(bf16[3,128,64]{1,2,0:T(8,128)(2,1)} %copy.41) | copy-start | bytes 147460
  57.7 0.8 copy-start.18
  63.1 4.6 %copy-start.6 = (bf16[4,16,32,192]{3,2,1,0:T(8,128)(2,1)S(1)}, bf16[4,16,32,192]{3,2,1,0:T(8,128)(2,1)}, u32[]{:S(2)}) copy-start(bf16[4,16,32,192]{3,2,1,0:T(8,128)(2,1)} %copy-done.5) | copy-start | bytes 2359300
  63.9 16.4 %collective-permute-start.10 = (f32[432,64]{0,1:T(8,128)S(1)}, f32[432,64]{0,1:T(8,128)S(1)}, u32[]{:S(2)}, u32[]{:S(2)}) collective-permute-start(f32[432,64]{0,1:T(8,128)S(1)} %bitcast.264), channel_id=1, source_target_pairs={{0,12},{1,13},{2,14},{3,15},{16,28},{17,29},{18,30},{19,31}} | collective-permute-start | bytes 331784 | tf_op jit(solution)/shard_map/ppermute | solution.py:72
  68.2 20.1 %collective-permute-start.11 = (f32[432,64]{0,1:T(8,128)S(1)}, f32[432,64]{0,1:T(8,128)S(1)}, u32[]{:S(2)}, u32[]{:S(2)}) collective-permute-start(f32[432,64]{0,1:T(8,128)S(1)} %bitcast.265), channel_id=1, source_target_pairs={{12,0},{13,1},{14,2},{15,3},{28,16},{29,17},{30,18},{31,19}} | collective-permute-start | bytes 331784 | tf_op jit(solution)/shard_map/ppermute | solution.py:72
  69.5 18.8 %collective-permute-start.6 = (f32[432,64]{0,1:T(8,128)S(1)}, f32[432,64]{0,1:T(8,128)S(1)}, u32[]{:S(2)}, u32[]{:S(2)}) collective-permute-start(f32[432,64]{0,1:T(8,128)S(1)} %bitcast.266), channel_id=1, source_target_pairs={{0,4},{4,8},{8,12},{1,5},{5,9},{9,13},{2,6},{6,10},{10,14},{3,7},{... | collective-permute-start | bytes 331784 | tf_op jit(solution)/shard_map/ppermute | solution.py:72
  70.9 17.4 %collective-permute-start.7 = (f32[432,64]{0,1:T(8,128)S(1)}, f32[432,64]{0,1:T(8,128)S(1)}, u32[]{:S(2)}, u32[]{:S(2)}) collective-permute-start(f32[432,64]{0,1:T(8,128)S(1)} %bitcast.267), channel_id=1, source_target_pairs={{4,0},{8,4},{12,8},{5,1},{9,5},{13,9},{6,2},{10,6},{14,10},{7,3},{... | collective-permute-start | bytes 331784 | tf_op jit(solution)/shard_map/ppermute | solution.py:72
  72.2 16.1 %collective-permute-start.8 = (f32[432,64]{0,1:T(8,128)S(1)}, f32[432,64]{0,1:T(8,128)S(1)}, u32[]{:S(2)}, u32[]{:S(2)}) collective-permute-start(f32[432,64]{0,1:T(8,128)S(1)} %bitcast.268), channel_id=1, source_target_pairs={{0,8},{4,12},{1,9},{5,13},{2,10},{6,14},{3,11},{7,15},{16,24},{20,... | collective-permute-start | bytes 331784 | tf_op jit(solution)/shard_map/ppermute | solution.py:72
  80.4 8.0 %collective-permute-start.9 = (f32[432,64]{0,1:T(8,128)S(1)}, f32[432,64]{0,1:T(8,128)S(1)}, u32[]{:S(2)}, u32[]{:S(2)}) collective-permute-start(f32[432,64]{0,1:T(8,128)S(1)} %bitcast.269), channel_id=1, source_target_pairs={{8,0},{12,4},{9,1},{13,5},{10,2},{14,6},{11,3},{15,7},{24,16},{28,... | collective-permute-start | bytes 331784 | tf_op jit(solution)/shard_map/ppermute | solution.py:72

commit v2 on v1

v2 whole, which is shorter than its diff:
```python
import jax
import jax.numpy as jnp
from jax import lax
from jax.sharding import PartitionSpec as P


def with_halo(cells, sides, width):
    for axis, dim in sides:
        count = lax.axis_size(axis)
        ends = count - 1
        head = lax.slice_in_dim(cells, 0, width, axis=dim)
        tail = lax.slice_in_dim(cells, cells.shape[dim] - width, cells.shape[dim], axis=dim)
        cells = jnp.concatenate(
            [
                lax.ppermute(tail, axis, [(i, (i + 1) % count) for i in range(ends)]),
                cells,
                lax.ppermute(head, axis, [((i + 1) % count, i) for i in range(ends)]),
            ],
            axis=dim,
        )
    return cells


def scatter_sum(blocks, axis, dim):
    count = lax.axis_size(axis)
    if count == 1:
        return lax.index_in_dim(blocks, 0, dim, keepdims=False)
    if count > 4:
        return lax.psum_scatter(blocks, axis, scatter_dimension=dim, tiled=False)
    me = lax.axis_index(axis)
    total = lax.dynamic_index_in_dim(blocks, me, dim, keepdims=False)
    for shift in range(1, count):
        up = [(j, j + shift) for j in range(count) if j + shift < count]
        down = [(j, j - shift) for j in range(count) if j - shift >= 0]
        if {s for s, _ in up} & {s for s, _ in down}:
            groups = [(up, me + shift), (down, me - shift)]
        else:
            groups = [(up + down, jnp.where(me + shift < count, me + shift, me - shift))]
        for pairs, target in groups:
            part = lax.dynamic_index_in_dim(blocks, jnp.clip(target, 0, count - 1), dim, keepdims=False)
            total = total + lax.ppermute(part, axis, pairs)
    return total


def on_device(x_act, grad_out, weight):
    size_x, size_y, depth, chans = x_act.shape
    ncores = lax.axis_size("col")
    half = weight.shape[2] // ncores
    offset = lax.axis_index("col") * half
    gh = with_halo(grad_out, (("gx", 0), ("gy", 1)), 1)
    taps = weight.reshape(3, 3, 3, chans, weight.shape[2])
    kflip = jnp.transpose(taps[::-1, ::-1, ::-1], (0, 1, 2, 4, 3))
    pad = [(0, 0), (0, 0), (1, 1)]
    inner = lax.conv_general_dilated(
        gh[None], kflip, (1, 1, 1), pad,
        dimension_numbers=("NDHWC", "DHWIO", "NDHWC"),
        preferred_element_type=jnp.float32,
    )[0]
    grad_in = inner.astype(jnp.bfloat16)
    gshare = lax.dynamic_slice_in_dim(gh, offset, half, 3)
    filter_dims = lax.ConvDimensionNumbers(
        lhs_spec=(4, 0, 1, 2, 3), rhs_spec=(4, 0, 1, 2, 3), out_spec=(3, 4, 0, 1, 2)
    )
    kgrad = lax.conv_general_dilated(
        gshare[None], x_act[None], (1, 1, 1), pad,
        dimension_numbers=filter_dims,
        preferred_element_type=jnp.float32,
    )
    weight_terms = jnp.transpose(kgrad[::-1, ::-1, ::-1], (0, 1, 2, 4, 3)).reshape(27 * chans, half)
    nx = lax.axis_size("gx")
    ny = lax.axis_size("gy")
    blocks = weight_terms.reshape(nx, ny, weight_terms.shape[0] // (nx * ny), half)
    owned = scatter_sum(scatter_sum(blocks, "gy", 1), "gx", 0)
    total_cells = size_x * lax.axis_size("gx") * size_y * lax.axis_size("gy") * depth
    grad_weight = owned / jnp.sqrt(jnp.float32(total_cells))
    return (grad_in, grad_weight)


def solution(mesh):
    return jax.shard_map(
        on_device,
        mesh=mesh,
        in_specs=(P(("grp", "gx"), "gy", None, None), P(("grp", "gx"), "gy", None, None), P()),
        out_specs=(P(("grp", "gx"), "gy", None, None), P(("grp", "gx", "gy"), "col")),
        check_vma=False,
    )
```

time: 90.2 us -> 71.6 us (0.79)
  local copies, waits for them, and re-layouts: 23.3 us -> 9.96 us
  starting transfers between devices: 34.5 us -> 22.7 us
  waiting for transfers between devices: 8.25 us -> 18.1 us
  matrix products: 8.01 us -> 17.5 us
  blocking collectives: 6.63 us -> 0 us
  other arithmetic: 6.93 us -> 1.93 us
    conv_general_dilated x0 -> x2, matrix products: none -> 17.5 us  [the longest x1 12.8 us: on_device(): lax.conv_general_dilated(gshare[None], x_act[None], (1, 1, 1), pad, dimen...]
    ppermute x8 -> x5, starting transfers between devices: 23.5 us -> 11.8 us  [scatter_sum(): total = total + lax.ppermute(part, axis, pairs)]
    unnamed x77 -> x17, local copies, waits for them, and re-layouts: 12.8 us -> 3.74 us
    dot_general x18 -> x0, matrix products: 8.01 us -> none  [the longest x9 4.21 us: local_terms(): lax.dot_general(xflat, stacked, contract_rows, preferred_element_type=jnp...]
    psum x1 -> x0, blocking collectives: 6.63 us -> none  [on_device(): grad_in = lax.psum(inner, 'col').astype(jnp.bfloat16)]
    concatenate x4 -> x0, other arithmetic: 5.17 us -> none  [depth_taps(): jnp.concatenate([lax.slice_in_dim(block, s, s + depth, axis=2) for s in s...]
    ppermute x8 -> x5, waiting for transfers between devices: 3.94 us -> 9.02 us  [scatter_sum(): total = total + lax.ppermute(part, axis, pairs)]
    ppermute x2, waiting for transfers between devices: 4.13 us -> 7.25 us  [with_halo(): lax.ppermute(head, axis, [((i + 1) % count, i) for i in range(ends)])]
  transfers between devices with their start and end apart: 12 -> 9, of which waited for: 3 -> 7; matrix products, arithmetic and copies ran while one was open for 13% -> 11% of each run, Pallas kernels for 0% -> 0%
where the time goes in v2:
time: 71.6 us; the launch traced here: 71.2 us
  starting transfers between devices  22.7 us (32%)
  waiting for transfers between devices  18.1 us (25%)
  matrix products  17.5 us (24%)
  local copies, waits for them, and re-layouts  9.96 us (14%)
  other arithmetic  1.93 us (3%)
  between operations  0.95 us (1%)
    conv_general_dilated x1, matrix products, on_device(): lax.conv_general_dilated(gshare[None], x_act[None], (1, 1, 1), pad, dimen...  12.8 us
    ppermute x5, starting transfers between devices, scatter_sum(): total = total + lax.ppermute(part, axis, pairs)  11.8 us
    ppermute x5, waiting for transfers between devices, scatter_sum(): total = total + lax.ppermute(part, axis, pairs)  9.02 us
    ppermute x2, starting transfers between devices, with_halo(): lax.ppermute(tail, axis, [(i, (i + 1) % count) for i in range(ends)])  8.33 us
    ppermute x2, waiting for transfers between devices, with_halo(): lax.ppermute(head, axis, [((i + 1) % count, i) for i in range(ends)])  7.25 us
    conv_general_dilated x1, matrix products, on_device(): lax.conv_general_dilated(gh[None], kflip, (1, 1, 1), pad, dimension_numbe...  4.74 us
    unnamed x17, local copies, waits for them, and re-layouts  3.74 us
    ppermute x2, starting transfers between devices, with_halo(): lax.ppermute(head, axis, [((i + 1) % count, i) for i in range(ends)])  2.58 us
  transfers between devices with their start and end apart: 9, of which 7 were waited for; matrix products, arithmetic and copies ran while one was open for 11% of the time, Pallas kernels for 0%

profile of v2, /device:TPU:0, one launch (start us, length us, event | category | flops | bytes accessed | tf_op | source)
XLA Modules:
  0.0 71.2 jit_solution(4849685658210531606)
XLA Ops:
  0.6 0.0 copy-start
  0.6 1.1 %fusion.27 = (bf16[1,16,32,128]{3,2,1,0:T(8,128)(2,1)S(1)}, bf16[1,16,32,128]{3,2,1,0:T(8,128)(2,1)S(1)}) fusion(bf16[4,16,32,128]{3,2,1,0:T(8,128)(2,1)} %param.4), kind=kLoop, calls=%fused_computation.44 | loop fusion | bytes 524288 | tf_op jit(solution)/shard_map/slice | solution.py:11
  1.7 4.9 %collective-permute-start = (bf16[1,16,32,128]{3,2,1,0:T(8,128)(2,1)S(1)}, bf16[1,16,32,128]{3,2,1,0:T(8,128)(2,1)S(1)}, u32[]{:S(2)}, u32[]{:S(2)}) collective-permute-start(bf16[1,16,32,128]{3,2,1,0:T(8,128)(2,1)S(1)} %get-tuple-element.16), channel_id=1, source_target_pairs={{0,4},{4,8},{8,12},{1,5},{5,9},{9,13},{2,6},{6,10},{10,14},{3,7},{... | collective-permute-start | bytes 393224 | tf_op jit(solution)/shard_map/ppermute | solution.py:15
  6.7 1.3 %collective-permute-start.1 = (bf16[1,16,32,128]{3,2,1,0:T(8,128)(2,1)S(1)}, bf16[1,16,32,128]{3,2,1,0:T(8,128)(2,1)S(1)}, u32[]{:S(2)}, u32[]{:S(2)}) collective-permute-start(bf16[1,16,32,128]{3,2,1,0:T(8,128)(2,1)S(1)} %get-tuple-element.15), channel_id=1, source_target_pairs={{4,0},{8,4},{12,8},{5,1},{9,5},{13,9},{6,2},{10,6},{14,10},{7,3},{... | collective-permute-start | bytes 393224 | tf_op jit(solution)/shard_map/ppermute | solution.py:17
  8.0 1.4 %collective-permute-done = bf16[1,16,32,128]{3,2,1,0:T(8,128)(2,1)S(1)} collective-permute-done((bf16[1,16,32,128]{3,2,1,0:T(8,128)(2,1)S(1)}, bf16[1,16,32,128]{3,2,1,0:T(8,128)(2,1)S(1)}, u32[]{:S(2)}, u32[]{:S(2)}) %collective-permute-start) | collective-permute-done | bytes 131104 | tf_op jit(solution)/shard_map/ppermute | solution.py:15
  9.4 1.1 %constant_dynamic-update-slice_fusion.1 = bf16[6,16,32,128]{3,2,1,0:T(8,128)(2,1)S(1)} fusion(bf16[6,16,32,128]{3,2,1,0:T(8,128)(2,1)S(1)} %constant_dynamic-update-slice_fusion.2, bf16[4,16,32,128]{3,2,1,0:T(8,128)(2,1)} %param.4), kind=kLoop, calls=%fused_computation.30 | loop fusion | bytes 1048576
  10.5 3.0 %collective-permute-done.1 = bf16[1,16,32,128]{3,2,1,0:T(8,128)(2,1)S(1)} collective-permute-done((bf16[1,16,32,128]{3,2,1,0:T(8,128)(2,1)S(1)}, bf16[1,16,32,128]{3,2,1,0:T(8,128)(2,1)S(1)}, u32[]{:S(2)}, u32[]{:S(2)}) %collective-permute-start.1) | collective-permute-done | bytes 131104 | tf_op jit(solution)/shard_map/ppermute | solution.py:17
  13.6 3.4 %collective-permute-start.2 = (bf16[6,1,32,128]{3,2,1,0:T(8,128)(2,1)S(1)}, bf16[6,1,32,128]{3,2,1,0:T(8,128)(2,1)S(1)}, u32[]{:S(2)}, u32[]{:S(2)}) collective-permute-start(bf16[6,1,32,128]{3,2,1,0:T(8,128)(2,1)S(1)} %get-tuple-element.8), channel_id=1, source_target_pairs={{0,2},{1,3},{4,6},{5,7},{8,10},{9,11},{12,14},{13,15},{16,18},{17,... | collective-permute-start | bytes 147464 | tf_op jit(solution)/shard_map/ppermute | solution.py:15
  17.0 1.3 %collective-permute-start.3 = (bf16[6,1,32,128]{3,2,1,0:T(8,128)(2,1)S(1)}, bf16[6,1,32,128]{3,2,1,0:T(8,128)(2,1)S(1)}, u32[]{:S(2)}, u32[]{:S(2)}) collective-permute-start(bf16[6,1,32,128]{3,2,1,0:T(8,128)(2,1)S(1)} %get-tuple-element.9), channel_id=1, source_target_pairs={{2,0},{3,1},{6,4},{7,5},{10,8},{11,9},{14,12},{15,13},{18,16},{19,... | collective-permute-start | bytes 147464 | tf_op jit(solution)/shard_map/ppermute | solution.py:17
  18.3 0.4 collective-permute-done.2
  18.7 4.3 %collective-permute-done.3 = bf16[6,1,32,128]{3,2,1,0:T(8,128)(2,1)S(1)} collective-permute-done((bf16[6,1,32,128]{3,2,1,0:T(8,128)(2,1)S(1)}, bf16[6,1,32,128]{3,2,1,0:T(8,128)(2,1)S(1)}, u32[]{:S(2)}, u32[]{:S(2)}) %collective-permute-start.3) | collective-permute-done | bytes 49184 | tf_op jit(solution)/shard_map/ppermute | solution.py:17
  22.9 1.0 %pad_maximum_fusion = (bf16[6,18,32,128]{3,2,1,0:T(8,128)(2,1)S(1)}, bf16[6,18,1,32,128]{4,3,1,0,2:T(8,128)(2,1)}) fusion(bf16[6,1,32,128]{3,2,1,0:T(8,128)(2,1)S(1)} %collective-permute-done.3, bf16[6,16,32,128]{3,2,1,0:T(8,128)(2,1)S(1)} %constant_dynamic-update-slice_fusion, bf16[6,1,32,128]{3,2,1,0:T(8,128)(2,1)S(1)} %collective-permute-done.2), kind=kLoop, calls=%fused_computation.13 | loop fusion | flops 884736 | bytes 2654208 | tf_op jit(solution)/shard_map/concatenate | solution.py:13
  24.0 0.0 copy-start.2
  24.0 0.3 dynamic-slice_bitcast_fusion
  24.3 0.7 %copy-done.2 = bf16[4,16,32,128]{3,2,1,0:T(8,128)(2,1)S(1)} copy-done((bf16[4,16,32,128]{3,2,1,0:T(8,128)(2,1)S(1)}, bf16[4,16,32,128]{3,2,1,0:T(8,128)(2,1)}, u32[]{:S(2)}) %copy-start.2) | copy-done | bytes 524312
  25.0 12.8 %fusion.1 = f32[3,3,3,64,128]{4,3,2,1,0:T(8,128)S(1)} fusion(bf16[1,6,18,32,64]{4,3,2,1,0:T(8,128)(2,1)S(1)} %dynamic-slice_bitcast_fusion, bf16[1,4,16,32,128]{4,3,2,1,0:T(8,128)(2,1)S(1)} %bitcast.57), kind=kOutput, calls=%fused_computation.2 | convolution fusion | flops 887095296 | bytes 1851392 | tf_op jit(solution)/shard_map/conv_general_dilated | solution.py:64
  37.8 0.1 reverse_bitcast_fusion
  37.9 0.8 %copy.12 = f32[3,3,3,128,64]{3,2,1,0,4:T(4,128)S(1)} copy(f32[3,3,3,128,64]{3,4,2,1,0:T(8,128)S(1)} %reverse_bitcast_fusion) | data formatting | bytes 1769472 | tf_op jit(solution)/shard_map/transpose | solution.py:69
  38.7 1.7 %reshape_reshape.3 = f32[4,2,432,64]{2,1,0,3:T(2,128)S(1)} reshape(f32[3,3,3,128,64]{3,2,1,0,4:T(4,128)S(1)} %copy.12) | data formatting | bytes 1769472 | tf_op jit(solution)/shard_map/reshape;reshape | solution.py:72
  40.4 0.0 copy-start.1
  40.4 1.1 %constant_dynamic-slice_fusion.6 = (f32[4,1,432,64]{2,1,0,3:T(1,128)S(1)}, f32[4,1,432,64]{2,1,0,3:T(1,128)S(1)}) fusion(f32[4,2,432,64]{2,1,0,3:T(2,128)S(1)} %reshape_reshape.3, s32[]{:T(128)S(6)} %select_n.27, s32[]{:T(128)S(6)} %min.16), kind=kLoop, calls=%fused_computation.39 | loop fusion | bytes 1769480 | tf_op jit(solution)/shard_map/jit(dynamic_index_in_dim)/dynamic_slice | solution.py:31
  41.5 0.1 copy.33
  41.6 0.1 collective-permute-start.4
  41.7 0.0 copy-done.1
  41.7 0.4 copy.21
  42.1 0.2 pad.clone
  42.4 0.0 copy-start.3
  42.4 0.1 copy.8
  42.5 0.1 slice.20
  42.6 0.0 copy-done
  42.7 0.4 copy-done.3
  43.0 4.7 %fusion.13 = bf16[4,16,8,5,128]{4,2,3,1,0:T(8,128)(2,1)S(1)} fusion(bf16[3,3,3,128,128]{4,3,2,1,0:T(8,128)(2,1)S(1)} %bitcast.49, bf16[6,18,1,7,2,128]{5,3,4,1,0,2:T(8,128)(2,1)S(1)} %slice.20, bf16[6,18,1,8,5,128]{5,3,4,1,0,2:T(8,128)(2,1)S(1)} %copy.8, pred[8,5]{0,1:T(8,128)(4,1)S(1)} %copy-done.3), kind=kOutput, calls=%fused_computation.11 | convolution fusion | flops 2270224384 | bytes 3033128 | tf_op jit(solution)/shard_map/conv_general_dilated | solution.py:54
  47.8 0.1 copy.9
  47.9 4.6 %collective-permute-done.4 = f32[4,432,64]{1,0,2:T(4,128)S(1)} collective-permute-done((f32[4,432,64]{1,0,2:T(4,128)S(1)}, f32[4,432,64]{1,0,2:T(4,128)S(1)}, u32[]{:S(2)}, u32[]{:S(2)}) %collective-permute-start.4) | collective-permute-done | bytes 442400 | tf_op jit(solution)/shard_map/ppermute | solution.py:41
  52.5 0.2 bitcast_add_fusion
  52.7 0.6 constant_dynamic-slice_fusion.4
  53.3 3.5 %collective-permute-start.5 = (f32[432,64]{0,1:T(8,128)S(1)}, f32[432,64]{0,1:T(8,128)S(1)}, u32[]{:S(2)}, u32[]{:S(2)}) collective-permute-start(f32[432,64]{0,1:T(8,128)S(1)} %bitcast.53), channel_id=1, source_target_pairs={{0,4},{4,8},{8,12},{1,5},{5,9},{9,13},{2,6},{6,10},{10,14},{3,7},{... | collective-permute-start | bytes 331784 | tf_op jit(solution)/shard_map/ppermute | solution.py:41
  56.8 1.3 %collective-permute-start.6 = (f32[432,64]{0,1:T(8,128)S(1)}, f32[432,64]{0,1:T(8,128)S(1)}, u32[]{:S(2)}, u32[]{:S(2)}) collective-permute-start(f32[432,64]{0,1:T(8,128)S(1)} %bitcast.54), channel_id=1, source_target_pairs={{4,0},{8,4},{12,8},{5,1},{9,5},{13,9},{6,2},{10,6},{14,10},{7,3},{... | collective-permute-start | bytes 331784 | tf_op jit(solution)/shard_map/ppermute | solution.py:41
  58.1 3.7 %collective-permute-start.7 = (f32[432,64]{0,1:T(8,128)S(1)}, f32[432,64]{0,1:T(8,128)S(1)}, u32[]{:S(2)}, u32[]{:S(2)}) collective-permute-start(f32[432,64]{0,1:T(8,128)S(1)} %bitcast.55), channel_id=1, source_target_pairs={{0,8},{4,12},{8,0},{12,4},{1,9},{5,13},{9,1},{13,5},{2,10},{6,14},... | collective-permute-start | bytes 331784 | tf_op jit(solution)/shard_map/ppermute | solution.py:41
  61.8 3.3 %collective-permute-start.8 = (f32[432,64]{0,1:T(8,128)S(1)}, f32[432,64]{0,1:T(8,128)S(1)}, u32[]{:S(2)}, u32[]{:S(2)}) collective-permute-start(f32[432,64]{0,1:T(8,128)S(1)} %bitcast.56), channel_id=1, source_target_pairs={{0,12},{12,0},{1,13},{13,1},{2,14},{14,2},{3,15},{15,3},{16,28},{2... | collective-permute-start | bytes 331784 | tf_op jit(solution)/shard_map/ppermute | solution.py:41
  65.1 0.9 %copy.13 = bf16[4,16,32,128]{3,2,1,0:T(8,128)(2,1)} copy(bf16[4,16,32,128]{3,1,2,0:T(8,128)(2,1)S(1)} %slice_bitcast_fusion) | data formatting | bytes 1048576
  66.1 0.0 collective-permute-done.5
  66.1 0.0 collective-permute-done.6
  66.1 2.8 %collective-permute-done.7 = f32[432,64]{0,1:T(8,128)S(1)} collective-permute-done((f32[432,64]{0,1:T(8,128)S(1)}, f32[432,64]{0,1:T(8,128)S(1)}, u32[]{:S(2)}, u32[]{:S(2)}) %collective-permute-start.7) | collective-permute-done | bytes 110624 | tf_op jit(solution)/shard_map/ppermute | solution.py:41
  68.9 1.6 %collective-permute-done.8 = f32[432,64]{0,1:T(8,128)S(1)} collective-permute-done((f32[432,64]{0,1:T(8,128)S(1)}, f32[432,64]{0,1:T(8,128)S(1)}, u32[]{:S(2)}, u32[]{:S(2)}) %collective-permute-start.8) | collective-permute-done | bytes 110624 | tf_op jit(solution)/shard_map/ppermute | solution.py:41
  70.5 0.7 fusion.21
  (8 shorter events, 0.1 us)
Async XLA Ops:
  0.6 42.0 %copy-start = (bf16[27,128,128]{2,1,0:T(8,128)(2,1)S(1)}, bf16[27,128,128]{2,1,0:T(8,128)(2,1)}, u32[]{:S(2)}) copy-start(bf16[27,128,128]{2,1,0:T(8,128)(2,1)} %param.5) | copy-start | bytes 2654212
  1.7 7.7 %collective-permute-start = (bf16[1,16,32,128]{3,2,1,0:T(8,128)(2,1)S(1)}, bf16[1,16,32,128]{3,2,1,0:T(8,128)(2,1)S(1)}, u32[]{:S(2)}, u32[]{:S(2)}) collective-permute-start(bf16[1,16,32,128]{3,2,1,0:T(8,128)(2,1)S(1)} %get-tuple-element.16), channel_id=1, source_target_pairs={{0,4},{4,8},{8,12},{1,5},{5,9},{9,13},{2,6},{6,10},{10,14},{3,7},{... | collective-permute-start | bytes 393224 | tf_op jit(solution)/shard_map/ppermute | solution.py:15
  6.7 6.9 %collective-permute-start.1 = (bf16[1,16,32,128]{3,2,1,0:T(8,128)(2,1)S(1)}, bf16[1,16,32,128]{3,2,1,0:T(8,128)(2,1)S(1)}, u32[]{:S(2)}, u32[]{:S(2)}) collective-permute-start(bf16[1,16,32,128]{3,2,1,0:T(8,128)(2,1)S(1)} %get-tuple-element.15), channel_id=1, source_target_pairs={{4,0},{8,4},{12,8},{5,1},{9,5},{13,9},{6,2},{10,6},{14,10},{7,3},{... | collective-permute-start | bytes 393224 | tf_op jit(solution)/shard_map/ppermute | solution.py:17
  13.6 5.1 %collective-permute-start.2 = (bf16[6,1,32,128]{3,2,1,0:T(8,128)(2,1)S(1)}, bf16[6,1,32,128]{3,2,1,0:T(8,128)(2,1)S(1)}, u32[]{:S(2)}, u32[]{:S(2)}) collective-permute-start(bf16[6,1,32,128]{3,2,1,0:T(8,128)(2,1)S(1)} %get-tuple-element.8), channel_id=1, source_target_pairs={{0,2},{1,3},{4,6},{5,7},{8,10},{9,11},{12,14},{13,15},{16,18},{17,... | collective-permute-start | bytes 147464 | tf_op jit(solution)/shard_map/ppermute | solution.py:15
  17.0 6.0 %collective-permute-start.3 = (bf16[6,1,32,128]{3,2,1,0:T(8,128)(2,1)S(1)}, bf16[6,1,32,128]{3,2,1,0:T(8,128)(2,1)S(1)}, u32[]{:S(2)}, u32[]{:S(2)}) collective-permute-start(bf16[6,1,32,128]{3,2,1,0:T(8,128)(2,1)S(1)} %get-tuple-element.9), channel_id=1, source_target_pairs={{2,0},{3,1},{6,4},{7,5},{10,8},{11,9},{14,12},{15,13},{18,16},{19,... | collective-permute-start | bytes 147464 | tf_op jit(solution)/shard_map/ppermute | solution.py:17
  24.0 1.0 %copy-start.2 = (bf16[4,16,32,128]{3,2,1,0:T(8,128)(2,1)S(1)}, bf16[4,16,32,128]{3,2,1,0:T(8,128)(2,1)}, u32[]{:S(2)}) copy-start(bf16[4,16,32,128]{3,2,1,0:T(8,128)(2,1)} %param.3) | copy-start | bytes 1572868
  40.4 1.3 %copy-start.1 = (bf16[6,18,1,32,128]{4,3,1,0,2:T(8,128)(2,1)S(1)}, bf16[6,18,1,32,128]{4,3,1,0,2:T(8,128)(2,1)}, u32[]{:S(2)}) copy-start(bf16[6,18,1,32,128]{4,3,1,0,2:T(8,128)(2,1)} %get-tuple-element.7) | copy-start | bytes 2654212
  41.6 10.9 %collective-permute-start.4 = (f32[4,432,64]{1,0,2:T(4,128)S(1)}, f32[4,432,64]{1,0,2:T(4,128)S(1)}, u32[]{:S(2)}, u32[]{:S(2)}) collective-permute-start(f32[4,432,64]{1,0,2:T(4,128)S(1)} %bitcast.52), channel_id=1, source_target_pairs={{0,2},{2,0},{1,3},{3,1},{4,6},{6,4},{5,7},{7,5},{8,10},{10,8},{9,1... | collective-permute-start | bytes 1327112 | tf_op jit(solution)/shard_map/ppermute | solution.py:41
  42.4 0.7 copy-start.3
  53.3 12.8 %collective-permute-start.5 = (f32[432,64]{0,1:T(8,128)S(1)}, f32[432,64]{0,1:T(8,128)S(1)}, u32[]{:S(2)}, u32[]{:S(2)}) collective-permute-start(f32[432,64]{0,1:T(8,128)S(1)} %bitcast.53), channel_id=1, source_target_pairs={{0,4},{4,8},{8,12},{1,5},{5,9},{9,13},{2,6},{6,10},{10,14},{3,7},{... | collective-permute-start | bytes 331784 | tf_op jit(solution)/shard_map/ppermute | solution.py:41
  56.8 9.3 %collective-permute-start.6 = (f32[432,64]{0,1:T(8,128)S(1)}, f32[432,64]{0,1:T(8,128)S(1)}, u32[]{:S(2)}, u32[]{:S(2)}) collective-permute-start(f32[432,64]{0,1:T(8,128)S(1)} %bitcast.54), channel_id=1, source_target_pairs={{4,0},{8,4},{12,8},{5,1},{9,5},{13,9},{6,2},{10,6},{14,10},{7,3},{... | collective-permute-start | bytes 331784 | tf_op jit(solution)/shard_map/ppermute | solution.py:41
  58.1 10.8 %collective-permute-start.7 = (f32[432,64]{0,1:T(8,128)S(1)}, f32[432,64]{0,1:T(8,128)S(1)}, u32[]{:S(2)}, u32[]{:S(2)}) collective-permute-start(f32[432,64]{0,1:T(8,128)S(1)} %bitcast.55), channel_id=1, source_target_pairs={{0,8},{4,12},{8,0},{12,4},{1,9},{5,13},{9,1},{13,5},{2,10},{6,14},... | collective-permute-start | bytes 331784 | tf_op jit(solution)/shard_map/ppermute | solution.py:41
  61.8 8.7 %collective-permute-start.8 = (f32[432,64]{0,1:T(8,128)S(1)}, f32[432,64]{0,1:T(8,128)S(1)}, u32[]{:S(2)}, u32[]{:S(2)}) collective-permute-start(f32[432,64]{0,1:T(8,128)S(1)} %bitcast.56), channel_id=1, source_target_pairs={{0,12},{12,0},{1,13},{13,1},{2,14},{14,2},{3,15},{15,3},{16,28},{2... | collective-permute-start | bytes 331784 | tf_op jit(solution)/shard_map/ppermute | solution.py:41

commit v3 on v2

--- a/solution.py
+++ b/solution.py
@@ -7,17 +7,20 @@
 def with_halo(cells, sides, width):
     for axis, dim in sides:
         count = lax.axis_size(axis)
-        ends = count - 1
         head = lax.slice_in_dim(cells, 0, width, axis=dim)
         tail = lax.slice_in_dim(cells, cells.shape[dim] - width, cells.shape[dim], axis=dim)
-        cells = jnp.concatenate(
-            [
-                lax.ppermute(tail, axis, [(i, (i + 1) % count) for i in range(ends)]),
-                cells,
-                lax.ppermute(head, axis, [((i + 1) % count, i) for i in range(ends)]),
-            ],
-            axis=dim,
-        )
+        if count == 1:
+            low = jnp.zeros_like(tail)
+            high = jnp.zeros_like(head)
+        elif count == 2:
+            me = lax.axis_index(axis)
+            got = lax.ppermute(jnp.where(me == 0, tail, head), axis, [(0, 1), (1, 0)])
+            low = jnp.where(me == 1, got, jnp.zeros_like(got))
+            high = jnp.where(me == 0, got, jnp.zeros_like(got))
+        else:
+            low = lax.ppermute(tail, axis, [(i, i + 1) for i in range(count - 1)])
+            high = lax.ppermute(head, axis, [(i + 1, i) for i in range(count - 1)])
+        cells = jnp.concatenate([low, cells, high], axis=dim)
     return cells
 
 
@@ -47,7 +50,7 @@
     ncores = lax.axis_size("col")
     half = weight.shape[2] // ncores
     offset = lax.axis_index("col") * half
-    gh = with_halo(grad_out, (("gx", 0), ("gy", 1)), 1)
+    gh = with_halo(grad_out, (("gy", 1), ("gx", 0)), 1)
     taps = weight.reshape(3, 3, 3, chans, weight.shape[2])
     kflip = jnp.transpose(taps[::-1, ::-1, ::-1], (0, 1, 2, 4, 3))
     pad = [(0, 0), (0, 0), (1, 1)]
@@ -58,15 +61,17 @@
     )[0]
     grad_in = inner.astype(jnp.bfloat16)
     gshare = lax.dynamic_slice_in_dim(gh, offset, half, 3)
-    filter_dims = lax.ConvDimensionNumbers(
-        lhs_spec=(4, 0, 1, 2, 3), rhs_spec=(4, 0, 1, 2, 3), out_spec=(3, 4, 0, 1, 2)
-    )
-    kgrad = lax.conv_general_dilated(
-        gshare[None], x_act[None], (1, 1, 1), pad,
-        dimension_numbers=filter_dims,
-        preferred_element_type=jnp.float32,
-    )
-    weight_terms = jnp.transpose(kgrad[::-1, ::-1, ::-1], (0, 1, 2, 4, 3)).reshape(27 * chans, half)
+    gdeep = jnp.pad(gshare, ((0, 0), (0, 0), (1, 1), (0, 0)))
+    stack = jnp.concatenate([lax.slice_in_dim(gdeep, 2 - c, 2 - c + depth, axis=2) for c in range(3)], axis=3)
+    pieces = []
+    for a in range(3):
+        for b in range(3):
+            window = stack[2 - a : 2 - a + size_x, 2 - b : 2 - b + size_y]
+            term = lax.dot_general(
+                x_act, window, (((0, 1, 2), (0, 1, 2)), ((), ())), preferred_element_type=jnp.float32
+            )
+            pieces.append(jnp.transpose(term.reshape(chans, 3, half), (1, 0, 2)).reshape(3 * chans, half))
+    weight_terms = jnp.concatenate(pieces, axis=0)
     nx = lax.axis_size("gx")
     ny = lax.axis_size("gy")
     blocks = weight_terms.reshape(nx, ny, weight_terms.shape[0] // (nx * ny), half)

time: 71.6 us -> 59.8 us (0.84)
  matrix products: 17.5 us -> 9.21 us
  other arithmetic: 1.93 us -> 4.96 us
  waiting for transfers between devices: 18.1 us -> 15.1 us
  local copies, waits for them, and re-layouts: 9.96 us -> 7.52 us
  starting transfers between devices: 22.7 us -> 21.6 us
    conv_general_dilated x1 -> x0, matrix products: 12.8 us -> none  [on_device(): lax.conv_general_dilated(gshare[None], x_act[None], (1, 1, 1), pad, dimen...]
    dot_general x0 -> x9, matrix products: none -> 4.26 us  [on_device(): lax.dot_general(x_act, window, (((0, 1, 2), (0, 1, 2)), ((), ())), prefer...]
    ppermute x4 -> x3, starting transfers between devices: 10.9 us -> 8.25 us  [the longest x1 4.02 us: with_halo(): low = lax.ppermute(tail, axis, [(i, i + 1) for i in range(count - 1)])]
    reshape x0 -> x10, local copies, waits for them, and re-layouts: none -> 2.01 us  [the longest x1 1.37 us: on_device(): weight_terms.reshape(nx, ny, weight_terms.shape[0] // (nx * ny), half)]
    another operation x1 -> x0, local copies, waits for them, and re-layouts: 1.68 us -> none  [on_device(): weight_terms.reshape(nx, ny, weight_terms.shape[0] // (nx * ny), half)]
    unnamed x17 -> x23, local copies, waits for them, and re-layouts: 3.74 us -> 2.14 us
    ppermute x5, waiting for transfers between devices: 9.02 us -> 7.47 us  [scatter_sum(): total = total + lax.ppermute(part, axis, pairs)]
    ppermute x4 -> x3, waiting for transfers between devices: 9.06 us -> 7.58 us  [the longest x1 4.39 us: with_halo(): high = lax.ppermute(head, axis, [(i + 1, i) for i in range(count - 1)])]
  transfers between devices with their start and end apart: 9 -> 8, of which waited for: 7 -> 6; matrix products, arithmetic and copies ran while one was open for 11% -> 12% of each run, Pallas kernels for 0% -> 0%
where the time goes in v3:
time: 59.8 us; the launch traced here: 59.4 us
  starting transfers between devices  21.6 us (36%)
  waiting for transfers between devices  15.1 us (25%)
  matrix products  9.21 us (15%)
  local copies, waits for them, and re-layouts  7.52 us (13%)
  other arithmetic  4.96 us (8%)
  between operations  1.12 us (2%)
    ppermute x5, starting transfers between devices, scatter_sum(): total = total + lax.ppermute(part, axis, pairs)  13.3 us
    ppermute x5, waiting for transfers between devices, scatter_sum(): total = total + lax.ppermute(part, axis, pairs)  7.47 us
    conv_general_dilated x1, matrix products, on_device(): lax.conv_general_dilated(gh[None], kflip, (1, 1, 1), pad, dimension_numbe...  4.94 us
    ppermute x1, waiting for transfers between devices, with_halo(): high = lax.ppermute(head, axis, [(i + 1, i) for i in range(count - 1)])  4.39 us
    dot_general x9, matrix products, on_device(): lax.dot_general(x_act, window, (((0, 1, 2), (0, 1, 2)), ((), ())), prefer...  4.26 us
    ppermute x1, starting transfers between devices, with_halo(): low = lax.ppermute(tail, axis, [(i, i + 1) for i in range(count - 1)])  4.02 us
    ppermute x1, starting transfers between devices, with_halo(): got = lax.ppermute(jnp.where(me == 0, tail, head), axis, [(0, 1), (1, 0)])  2.94 us
    unnamed x23, local copies, waits for them, and re-layouts  2.14 us
  transfers between devices with their start and end apart: 8, of which 6 were waited for; matrix products, arithmetic and copies ran while one was open for 12% of the time, Pallas kernels for 0%

profile of v3, /device:TPU:0, one launch (start us, length us, event | category | flops | bytes accessed | tf_op | source)
XLA Modules:
  0.0 59.4 jit_solution(14567762441352081526)
XLA Ops:
  0.7 0.9 %slice_select_fusion = bf16[4,1,32,128]{3,2,1,0:T(8,128)(2,1)S(1)} fusion(bf16[4,16,32,128]{3,2,1,0:T(8,128)(2,1)} %param.4, pred[]{:T(512)S(6)} %eq.8), kind=kLoop, calls=%fused_computation.39 | loop fusion | flops 16384 | bytes 98305 | tf_op jit(solution)/shard_map/jit(_where)/select_n | solution.py:17
  1.5 2.9 %collective-permute-start = (bf16[4,1,32,128]{3,2,1,0:T(8,128)(2,1)S(1)}, bf16[4,1,32,128]{3,2,1,0:T(8,128)(2,1)S(1)}, u32[]{:S(2)}, u32[]{:S(2)}) collective-permute-start(bf16[4,1,32,128]{3,2,1,0:T(8,128)(2,1)S(1)} %slice_select_fusion), channel_id=1, source_target_pairs={{0,2},{2,0},{1,3},{3,1},{4,6},{6,4},{5,7},{7,5},{8,10},{10,8},{9,1... | collective-permute-start | bytes 98312 | tf_op jit(solution)/shard_map/ppermute | solution.py:17
  4.5 1.9 %collective-permute-done = bf16[4,1,32,128]{3,2,1,0:T(8,128)(2,1)S(1)} collective-permute-done((bf16[4,1,32,128]{3,2,1,0:T(8,128)(2,1)S(1)}, bf16[4,1,32,128]{3,2,1,0:T(8,128)(2,1)S(1)}, u32[]{:S(2)}, u32[]{:S(2)}) %collective-permute-start) | collective-permute-done | bytes 32800 | tf_op jit(solution)/shard_map/ppermute | solution.py:17
  6.4 1.0 %pad_maximum_fusion.4 = (bf16[1,18,32,128]{3,2,1,0:T(8,128)(2,1)S(1)}, bf16[1,18,32,128]{3,2,1,0:T(8,128)(2,1)S(1)}) fusion(bf16[4,1,32,128]{3,2,1,0:T(8,128)(2,1)S(1)} %get-tuple-element.16, bf16[4,16,32,128]{3,2,1,0:T(8,128)(2,1)} %param.4, bf16[4,1,32,128]{3,2,1,0:T(8,128)(2,1)S(1)} %get-tuple-element.15), kind=kLoop, calls=%fused_computation.20 | loop fusion | flops 294912 | bytes 884736 | tf_op jit(solution)/shard_map/slice | solution.py:11
  7.4 4.0 %collective-permute-start.1 = (bf16[1,18,32,128]{3,2,1,0:T(8,128)(2,1)S(1)}, bf16[1,18,32,128]{3,2,1,0:T(8,128)(2,1)S(1)}, u32[]{:S(2)}, u32[]{:S(2)}) collective-permute-start(bf16[1,18,32,128]{3,2,1,0:T(8,128)(2,1)S(1)} %get-tuple-element.8), channel_id=1, source_target_pairs={{0,4},{4,8},{8,12},{1,5},{5,9},{9,13},{2,6},{6,10},{10,14},{3,7},{... | collective-permute-start | bytes 442376 | tf_op jit(solution)/shard_map/ppermute | solution.py:21
  11.4 1.3 %collective-permute-start.2 = (bf16[1,18,32,128]{3,2,1,0:T(8,128)(2,1)S(1)}, bf16[1,18,32,128]{3,2,1,0:T(8,128)(2,1)S(1)}, u32[]{:S(2)}, u32[]{:S(2)}) collective-permute-start(bf16[1,18,32,128]{3,2,1,0:T(8,128)(2,1)S(1)} %get-tuple-element.9), channel_id=1, source_target_pairs={{4,0},{8,4},{12,8},{5,1},{9,5},{13,9},{6,2},{10,6},{14,10},{7,3},{... | collective-permute-start | bytes 442376 | tf_op jit(solution)/shard_map/ppermute | solution.py:22
  12.7 1.3 %collective-permute-done.1 = bf16[1,18,32,128]{3,2,1,0:T(8,128)(2,1)S(1)} collective-permute-done((bf16[1,18,32,128]{3,2,1,0:T(8,128)(2,1)S(1)}, bf16[1,18,32,128]{3,2,1,0:T(8,128)(2,1)S(1)}, u32[]{:S(2)}, u32[]{:S(2)}) %collective-permute-start.1) | collective-permute-done | bytes 147488 | tf_op jit(solution)/shard_map/ppermute | solution.py:21
  14.1 4.4 %collective-permute-done.2 = bf16[1,18,32,128]{3,2,1,0:T(8,128)(2,1)S(1)} collective-permute-done((bf16[1,18,32,128]{3,2,1,0:T(8,128)(2,1)S(1)}, bf16[1,18,32,128]{3,2,1,0:T(8,128)(2,1)S(1)}, u32[]{:S(2)}, u32[]{:S(2)}) %collective-permute-start.2) | collective-permute-done | bytes 147488 | tf_op jit(solution)/shard_map/ppermute | solution.py:22
  18.4 1.2 %pad_maximum_fusion.1 = bf16[6,18,32,128]{3,2,1,0:T(8,128)(2,1)S(1)} fusion(bf16[1,18,32,128]{3,2,1,0:T(8,128)(2,1)S(1)} %collective-permute-done.2, bf16[4,1,32,128]{3,2,1,0:T(8,128)(2,1)S(1)} %get-tuple-element.16, bf16[4,16,32,128]{3,2,1,0:T(8,128)(2,1)} %param.4, bf16[4,1,32,128]{3,2,1,0:T(8,128)(2,1)S(1)} %get-tuple-element.15, ...), kind=kLoop, calls=%fused_computation.13 | loop fusion | flops 1769472 | bytes 1769472 | tf_op jit(solution)/shard_map/concatenate | solution.py:23
  19.6 0.3 constant_dynamic-slice_fusion.7
  19.9 0.8 %pad_slice_fusion.1 = (bf16[6,18,32,64]{3,2,1,0:T(8,128)(2,1)S(1)}, bf16[6,18,32,64]{3,2,1,0:T(8,128)(2,1)S(1)}) fusion(bf16[6,18,32,64]{3,2,1,0:T(8,128)(2,1)S(1)} %constant_dynamic-slice_fusion.7), kind=kLoop, calls=%fused_computation.12 | loop fusion | bytes 1327104 | tf_op jit(solution)/shard_map/slice | solution.py:65
  20.7 0.9 %pad_maximum_fusion = bf16[6,18,32,192]{3,2,1,0:T(8,128)(2,1)S(1)} fusion(bf16[6,18,32,64]{3,2,1,0:T(8,128)(2,1)S(1)} %get-tuple-element.7, bf16[6,18,32,64]{3,2,1,0:T(8,128)(2,1)S(1)} %constant_dynamic-slice_fusion.7, bf16[6,18,32,64]{3,2,1,0:T(8,128)(2,1)S(1)} %get-tuple-element.6), kind=kLoop, calls=%fused_computation.2 | loop fusion | flops 3981312 | bytes 2654208 | tf_op jit(solution)/shard_map/concatenate | solution.py:65
  21.6 0.2 copy-done.2
  21.8 0.5 fusion.22
  22.2 0.5 fusion.23
  22.7 0.5 fusion.24
  23.2 0.5 fusion.25
  23.7 0.5 fusion.26
  24.2 0.5 fusion.27
  24.6 0.5 fusion.28
  25.1 0.5 fusion.29
  25.6 0.5 fusion.30
  26.2 0.1 copy.11
  26.5 0.1 copy.14
  26.6 0.1 copy.15
  26.9 1.4 %reshape.84 = f32[4,2,432,64]{2,1,0,3:T(2,128)S(1)} reshape(f32[3456,64]{0,1:T(8,128)S(1)} %bitcast_dynamic-update-slice_fusion) | data formatting | bytes 1769472 | tf_op jit(solution)/shard_map/reshape | solution.py:77
  28.3 1.1 %constant_dynamic-slice_fusion.6 = (f32[4,1,432,64]{2,1,0,3:T(1,128)S(1)}, f32[4,1,432,64]{2,1,0,3:T(1,128)S(1)}) fusion(f32[4,2,432,64]{2,1,0,3:T(2,128)S(1)} %reshape.84, s32[]{:T(128)S(6)} %select_n.50, s32[]{:T(128)S(6)} %min.16), kind=kLoop, calls=%fused_computation.48 | loop fusion | bytes 1769480 | tf_op jit(solution)/shard_map/jit(dynamic_index_in_dim)/dynamic_slice | solution.py:34
  29.4 0.1 copy.61
  29.6 1.6 %collective-permute-start.3 = (f32[4,432,64]{1,0,2:T(4,128)S(1)}, f32[4,432,64]{1,0,2:T(4,128)S(1)}, u32[]{:S(2)}, u32[]{:S(2)}) collective-permute-start(f32[4,432,64]{1,0,2:T(4,128)S(1)} %bitcast.191), channel_id=1, source_target_pairs={{0,2},{2,0},{1,3},{3,1},{4,6},{6,4},{5,7},{7,5},{8,10},{10,8},{9,1... | collective-permute-start | bytes 1327112 | tf_op jit(solution)/shard_map/ppermute | solution.py:44
  31.1 0.2 fusion.50
  31.3 0.4 copy.35
  31.7 0.2 pad.5.clone
  31.9 0.1 copy.7
  32.1 0.1 slice.63
  32.2 0.4 copy-done.3
  32.6 4.9 %fusion.11 = bf16[4,16,8,5,128]{4,2,3,1,0:T(8,128)(2,1)S(1)} fusion(bf16[3,3,3,128,128]{4,3,2,1,0:T(8,128)(2,1)S(1)} %bitcast.179, bf16[6,18,1,7,2,128]{5,3,4,1,0,2:T(8,128)(2,1)S(1)} %slice.63, bf16[6,18,1,8,5,128]{5,3,4,1,0,2:T(8,128)(2,1)S(1)} %copy.7, pred[8,5]{0,1:T(8,128)(4,1)S(1)} %copy-done.3), kind=kOutput, calls=%fused_computation.10 | convolution fusion | flops 2270224384 | bytes 3033128 | tf_op jit(solution)/shard_map/conv_general_dilated | solution.py:57
  37.5 0.1 copy.8
  37.7 3.1 %collective-permute-done.3 = f32[4,432,64]{1,0,2:T(4,128)S(1)} collective-permute-done((f32[4,432,64]{1,0,2:T(4,128)S(1)}, f32[4,432,64]{1,0,2:T(4,128)S(1)}, u32[]{:S(2)}, u32[]{:S(2)}) %collective-permute-start.3) | collective-permute-done | bytes 442400 | tf_op jit(solution)/shard_map/ppermute | solution.py:44
  40.7 0.2 bitcast_add_fusion
  40.9 0.6 constant_dynamic-slice_fusion.4
  41.5 3.5 %collective-permute-start.4 = (f32[432,64]{0,1:T(8,128)S(1)}, f32[432,64]{0,1:T(8,128)S(1)}, u32[]{:S(2)}, u32[]{:S(2)}) collective-permute-start(f32[432,64]{0,1:T(8,128)S(1)} %bitcast.192), channel_id=1, source_target_pairs={{0,4},{4,8},{8,12},{1,5},{5,9},{9,13},{2,6},{6,10},{10,14},{3,7},{... | collective-permute-start | bytes 331784 | tf_op jit(solution)/shard_map/ppermute | solution.py:44
  45.0 1.3 %collective-permute-start.5 = (f32[432,64]{0,1:T(8,128)S(1)}, f32[432,64]{0,1:T(8,128)S(1)}, u32[]{:S(2)}, u32[]{:S(2)}) collective-permute-start(f32[432,64]{0,1:T(8,128)S(1)} %bitcast.193), channel_id=1, source_target_pairs={{4,0},{8,4},{12,8},{5,1},{9,5},{13,9},{6,2},{10,6},{14,10},{7,3},{... | collective-permute-start | bytes 331784 | tf_op jit(solution)/shard_map/ppermute | solution.py:44
  46.3 3.7 %collective-permute-start.6 = (f32[432,64]{0,1:T(8,128)S(1)}, f32[432,64]{0,1:T(8,128)S(1)}, u32[]{:S(2)}, u32[]{:S(2)}) collective-permute-start(f32[432,64]{0,1:T(8,128)S(1)} %bitcast.194), channel_id=1, source_target_pairs={{0,8},{4,12},{8,0},{12,4},{1,9},{5,13},{9,1},{13,5},{2,10},{6,14},... | collective-permute-start | bytes 331784 | tf_op jit(solution)/shard_map/ppermute | solution.py:44
  50.0 3.3 %collective-permute-start.7 = (f32[432,64]{0,1:T(8,128)S(1)}, f32[432,64]{0,1:T(8,128)S(1)}, u32[]{:S(2)}, u32[]{:S(2)}) collective-permute-start(f32[432,64]{0,1:T(8,128)S(1)} %bitcast.195), channel_id=1, source_target_pairs={{0,12},{12,0},{1,13},{13,1},{2,14},{14,2},{3,15},{15,3},{16,28},{2... | collective-permute-start | bytes 331784 | tf_op jit(solution)/shard_map/ppermute | solution.py:44
  53.4 0.9 %copy.18 = bf16[4,16,32,128]{3,2,1,0:T(8,128)(2,1)} copy(bf16[4,16,32,128]{3,1,2,0:T(8,128)(2,1)S(1)} %slice_bitcast_fusion) | data formatting | bytes 1048576
  54.3 2.8 %collective-permute-done.6 = f32[432,64]{0,1:T(8,128)S(1)} collective-permute-done((f32[432,64]{0,1:T(8,128)S(1)}, f32[432,64]{0,1:T(8,128)S(1)}, u32[]{:S(2)}, u32[]{:S(2)}) %collective-permute-start.6) | collective-permute-done | bytes 110624 | tf_op jit(solution)/shard_map/ppermute | solution.py:44
  57.1 1.6 %collective-permute-done.7 = f32[432,64]{0,1:T(8,128)S(1)} collective-permute-done((f32[432,64]{0,1:T(8,128)S(1)}, f32[432,64]{0,1:T(8,128)S(1)}, u32[]{:S(2)}, u32[]{:S(2)}) %collective-permute-start.7) | collective-permute-done | bytes 110624 | tf_op jit(solution)/shard_map/ppermute | solution.py:44
  58.7 0.7 %fusion.18 = f32[432,64]{0,1:T(8,128)} fusion(f32[432,64]{0,1:T(8,128)S(1)} %collective-permute-done.7, f32[432,64]{0,1:T(8,128)S(1)} %collective-permute-done.6, f32[432,64]{0,1:T(8,128)S(1)} %collective-permute-done.5, f32[432,64]{0,1:T(8,128)S(1)} %collective-permute-done.4, f32[1,432,64]{1,0,2:T(1,128)S(1)} %get-tuple-element.10), kind=kLoop, calls=%fused_computation.29 | loop fusion | flops 138240 | bytes 663552 | tf_op jit(solution)/shard_map/div | solution.py:80
  (29 shorter events, 0.6 us)
Async XLA Ops:
  0.6 31.6 %copy-start = (bf16[27,128,128]{2,1,0:T(8,128)(2,1)S(1)}, bf16[27,128,128]{2,1,0:T(8,128)(2,1)}, u32[]{:S(2)}) copy-start(bf16[27,128,128]{2,1,0:T(8,128)(2,1)} %param.5) | copy-start | bytes 2654212
  1.5 4.8 %collective-permute-start = (bf16[4,1,32,128]{3,2,1,0:T(8,128)(2,1)S(1)}, bf16[4,1,32,128]{3,2,1,0:T(8,128)(2,1)S(1)}, u32[]{:S(2)}, u32[]{:S(2)}) collective-permute-start(bf16[4,1,32,128]{3,2,1,0:T(8,128)(2,1)S(1)} %slice_select_fusion), channel_id=1, source_target_pairs={{0,2},{2,0},{1,3},{3,1},{4,6},{6,4},{5,7},{7,5},{8,10},{10,8},{9,1... | collective-permute-start | bytes 98312 | tf_op jit(solution)/shard_map/ppermute | solution.py:17
  7.4 6.7 %collective-permute-start.1 = (bf16[1,18,32,128]{3,2,1,0:T(8,128)(2,1)S(1)}, bf16[1,18,32,128]{3,2,1,0:T(8,128)(2,1)S(1)}, u32[]{:S(2)}, u32[]{:S(2)}) collective-permute-start(bf16[1,18,32,128]{3,2,1,0:T(8,128)(2,1)S(1)} %get-tuple-element.8), channel_id=1, source_target_pairs={{0,4},{4,8},{8,12},{1,5},{5,9},{9,13},{2,6},{6,10},{10,14},{3,7},{... | collective-permute-start | bytes 442376 | tf_op jit(solution)/shard_map/ppermute | solution.py:21
  11.4 7.0 %collective-permute-start.2 = (bf16[1,18,32,128]{3,2,1,0:T(8,128)(2,1)S(1)}, bf16[1,18,32,128]{3,2,1,0:T(8,128)(2,1)S(1)}, u32[]{:S(2)}, u32[]{:S(2)}) collective-permute-start(bf16[1,18,32,128]{3,2,1,0:T(8,128)(2,1)S(1)} %get-tuple-element.9), channel_id=1, source_target_pairs={{4,0},{8,4},{12,8},{5,1},{9,5},{13,9},{6,2},{10,6},{14,10},{7,3},{... | collective-permute-start | bytes 442376 | tf_op jit(solution)/shard_map/ppermute | solution.py:22
  20.7 1.0 %copy-start.2 = (bf16[4,16,32,128]{3,2,1,0:T(8,128)(2,1)S(1)}, bf16[4,16,32,128]{3,2,1,0:T(8,128)(2,1)}, u32[]{:S(2)}) copy-start(bf16[4,16,32,128]{3,2,1,0:T(8,128)(2,1)} %param.3) | copy-start | bytes 1572868
  28.3 2.8 %copy-start.1 = (bf16[4,16,32,128]{3,2,1,0:T(8,128)(2,1)S(1)}, bf16[4,16,32,128]{3,2,1,0:T(8,128)(2,1)}, u32[]{:S(2)}) copy-start(bf16[4,16,32,128]{3,2,1,0:T(8,128)(2,1)} %param.4) | copy-start | bytes 1572868
  29.6 11.1 %collective-permute-start.3 = (f32[4,432,64]{1,0,2:T(4,128)S(1)}, f32[4,432,64]{1,0,2:T(4,128)S(1)}, u32[]{:S(2)}, u32[]{:S(2)}) collective-permute-start(f32[4,432,64]{1,0,2:T(4,128)S(1)} %bitcast.191), channel_id=1, source_target_pairs={{0,2},{2,0},{1,3},{3,1},{4,6},{6,4},{5,7},{7,5},{8,10},{10,8},{9,1... | collective-permute-start | bytes 1327112 | tf_op jit(solution)/shard_map/ppermute | solution.py:44
  31.9 0.7 %copy-start.3 = (pred[8,5]{0,1:T(8,128)(4,1)S(1)}, pred[8,5]{0,1:T(8,128)(4,1)}, u32[]{:S(2)}) copy-start(pred[8,5]{0,1:T(8,128)(4,1)} %constant.69) | copy-start | bytes 124
  41.5 12.8 %collective-permute-start.4 = (f32[432,64]{0,1:T(8,128)S(1)}, f32[432,64]{0,1:T(8,128)S(1)}, u32[]{:S(2)}, u32[]{:S(2)}) collective-permute-start(f32[432,64]{0,1:T(8,128)S(1)} %bitcast.192), channel_id=1, source_target_pairs={{0,4},{4,8},{8,12},{1,5},{5,9},{9,13},{2,6},{6,10},{10,14},{3,7},{... | collective-permute-start | bytes 331784 | tf_op jit(solution)/shard_map/ppermute | solution.py:44
  45.0 9.3 %collective-permute-start.5 = (f32[432,64]{0,1:T(8,128)S(1)}, f32[432,64]{0,1:T(8,128)S(1)}, u32[]{:S(2)}, u32[]{:S(2)}) collective-permute-start(f32[432,64]{0,1:T(8,128)S(1)} %bitcast.193), channel_id=1, source_target_pairs={{4,0},{8,4},{12,8},{5,1},{9,5},{13,9},{6,2},{10,6},{14,10},{7,3},{... | collective-permute-start | bytes 331784 | tf_op jit(solution)/shard_map/ppermute | solution.py:44
  46.3 10.8 %collective-permute-start.6 = (f32[432,64]{0,1:T(8,128)S(1)}, f32[432,64]{0,1:T(8,128)S(1)}, u32[]{:S(2)}, u32[]{:S(2)}) collective-permute-start(f32[432,64]{0,1:T(8,128)S(1)} %bitcast.194), channel_id=1, source_target_pairs={{0,8},{4,12},{8,0},{12,4},{1,9},{5,13},{9,1},{13,5},{2,10},{6,14},... | collective-permute-start | bytes 331784 | tf_op jit(solution)/shard_map/ppermute | solution.py:44
  50.0 8.7 %collective-permute-start.7 = (f32[432,64]{0,1:T(8,128)S(1)}, f32[432,64]{0,1:T(8,128)S(1)}, u32[]{:S(2)}, u32[]{:S(2)}) collective-permute-start(f32[432,64]{0,1:T(8,128)S(1)} %bitcast.195), channel_id=1, source_target_pairs={{0,12},{12,0},{1,13},{13,1},{2,14},{14,2},{3,15},{15,3},{16,28},{2... | collective-permute-start | bytes 331784 | tf_op jit(solution)/shard_map/ppermute | solution.py:44

commit v4 on v3

--- a/solution.py
+++ b/solution.py
@@ -33,15 +33,8 @@
     me = lax.axis_index(axis)
     total = lax.dynamic_index_in_dim(blocks, me, dim, keepdims=False)
     for shift in range(1, count):
-        up = [(j, j + shift) for j in range(count) if j + shift < count]
-        down = [(j, j - shift) for j in range(count) if j - shift >= 0]
-        if {s for s, _ in up} & {s for s, _ in down}:
-            groups = [(up, me + shift), (down, me - shift)]
-        else:
-            groups = [(up + down, jnp.where(me + shift < count, me + shift, me - shift))]
-        for pairs, target in groups:
-            part = lax.dynamic_index_in_dim(blocks, jnp.clip(target, 0, count - 1), dim, keepdims=False)
-            total = total + lax.ppermute(part, axis, pairs)
+        part = lax.dynamic_index_in_dim(blocks, (me + shift) % count, dim, keepdims=False)
+        total = total + lax.ppermute(part, axis, [(j, (j + shift) % count) for j in range(count)])
     return total
 
 

time: 59.8 us -> 53 us (0.89)
  starting transfers between devices: 21.6 us -> 15.5 us
  waiting for transfers between devices: 15.1 us -> 14.5 us
    ppermute x5 -> x4, starting transfers between devices: 13.3 us -> 7.24 us  [scatter_sum(): lax.ppermute(part, axis, [(j, (j + shift) % count) for j in range(count)])]
    ppermute x5 -> x4, waiting for transfers between devices: 7.47 us -> 6.97 us  [scatter_sum(): lax.ppermute(part, axis, [(j, (j + shift) % count) for j in range(count)])]
    unnamed x23 -> x22, local copies, waits for them, and re-layouts: 2.14 us -> 2.13 us
  transfers between devices with their start and end apart: 8 -> 7, of which waited for: 6 -> 6; matrix products, arithmetic and copies ran while one was open for 12% -> 13% of each run, Pallas kernels for 0% -> 0%
where the time goes in v4:
time: 53 us; the launch traced here: 52.7 us
  starting transfers between devices  15.5 us (29%)
  waiting for transfers between devices  14.5 us (27%)
  matrix products  9.22 us (17%)
  local copies, waits for them, and re-layouts  7.39 us (14%)
  other arithmetic  4.95 us (9%)
  between operations  1.09 us (2%)
    ppermute x4, starting transfers between devices, scatter_sum(): lax.ppermute(part, axis, [(j, (j + shift) % count) for j in range(count)])  7.24 us
    ppermute x4, waiting for transfers between devices, scatter_sum(): lax.ppermute(part, axis, [(j, (j + shift) % count) for j in range(count)])  6.97 us
    conv_general_dilated x1, matrix products, on_device(): lax.conv_general_dilated(gh[None], kflip, (1, 1, 1), pad, dimension_numbe...  4.96 us
    ppermute x1, waiting for transfers between devices, with_halo(): high = lax.ppermute(head, axis, [(i + 1, i) for i in range(count - 1)])  4.39 us
    dot_general x9, matrix products, on_device(): lax.dot_general(x_act, window, (((0, 1, 2), (0, 1, 2)), ((), ())), prefer...  4.26 us
    ppermute x1, starting transfers between devices, with_halo(): low = lax.ppermute(tail, axis, [(i, i + 1) for i in range(count - 1)])  4.02 us
    ppermute x1, starting transfers between devices, with_halo(): got = lax.ppermute(jnp.where(me == 0, tail, head), axis, [(0, 1), (1, 0)])  2.94 us
    unnamed x22, local copies, waits for them, and re-layouts  2.13 us
  transfers between devices with their start and end apart: 7, of which 6 were waited for; matrix products, arithmetic and copies ran while one was open for 13% of the time, Pallas kernels for 0%

profile of v4, /device:TPU:0, one launch (start us, length us, event | category | flops | bytes accessed | tf_op | source)
XLA Modules:
  0.0 52.7 jit_solution(17198076634365194511)
XLA Ops:
  0.7 0.9 %slice_select_fusion = bf16[4,1,32,128]{3,2,1,0:T(8,128)(2,1)S(1)} fusion(bf16[4,16,32,128]{3,2,1,0:T(8,128)(2,1)} %param.4, pred[]{:T(512)S(6)} %eq.13), kind=kLoop, calls=%fused_computation.37 | loop fusion | flops 16384 | bytes 98305 | tf_op jit(solution)/shard_map/jit(_where)/select_n | solution.py:17
  1.5 2.9 %collective-permute-start = (bf16[4,1,32,128]{3,2,1,0:T(8,128)(2,1)S(1)}, bf16[4,1,32,128]{3,2,1,0:T(8,128)(2,1)S(1)}, u32[]{:S(2)}, u32[]{:S(2)}) collective-permute-start(bf16[4,1,32,128]{3,2,1,0:T(8,128)(2,1)S(1)} %slice_select_fusion), channel_id=1, source_target_pairs={{0,2},{2,0},{1,3},{3,1},{4,6},{6,4},{5,7},{7,5},{8,10},{10,8},{9,1... | collective-permute-start | bytes 98312 | tf_op jit(solution)/shard_map/ppermute | solution.py:17
  4.5 1.9 %collective-permute-done = bf16[4,1,32,128]{3,2,1,0:T(8,128)(2,1)S(1)} collective-permute-done((bf16[4,1,32,128]{3,2,1,0:T(8,128)(2,1)S(1)}, bf16[4,1,32,128]{3,2,1,0:T(8,128)(2,1)S(1)}, u32[]{:S(2)}, u32[]{:S(2)}) %collective-permute-start) | collective-permute-done | bytes 32800 | tf_op jit(solution)/shard_map/ppermute | solution.py:17
  6.4 1.0 %pad_maximum_fusion.4 = (bf16[1,18,32,128]{3,2,1,0:T(8,128)(2,1)S(1)}, bf16[1,18,32,128]{3,2,1,0:T(8,128)(2,1)S(1)}) fusion(bf16[4,1,32,128]{3,2,1,0:T(8,128)(2,1)S(1)} %get-tuple-element.15, bf16[4,16,32,128]{3,2,1,0:T(8,128)(2,1)} %param.4, bf16[4,1,32,128]{3,2,1,0:T(8,128)(2,1)S(1)} %get-tuple-element.14), kind=kLoop, calls=%fused_computation.20 | loop fusion | flops 294912 | bytes 884736 | tf_op jit(solution)/shard_map/slice | solution.py:11
  7.4 4.0 %collective-permute-start.1 = (bf16[1,18,32,128]{3,2,1,0:T(8,128)(2,1)S(1)}, bf16[1,18,32,128]{3,2,1,0:T(8,128)(2,1)S(1)}, u32[]{:S(2)}, u32[]{:S(2)}) collective-permute-start(bf16[1,18,32,128]{3,2,1,0:T(8,128)(2,1)S(1)} %get-tuple-element.8), channel_id=1, source_target_pairs={{0,4},{4,8},{8,12},{1,5},{5,9},{9,13},{2,6},{6,10},{10,14},{3,7},{... | collective-permute-start | bytes 442376 | tf_op jit(solution)/shard_map/ppermute | solution.py:21
  11.4 1.3 %collective-permute-start.2 = (bf16[1,18,32,128]{3,2,1,0:T(8,128)(2,1)S(1)}, bf16[1,18,32,128]{3,2,1,0:T(8,128)(2,1)S(1)}, u32[]{:S(2)}, u32[]{:S(2)}) collective-permute-start(bf16[1,18,32,128]{3,2,1,0:T(8,128)(2,1)S(1)} %get-tuple-element.9), channel_id=1, source_target_pairs={{4,0},{8,4},{12,8},{5,1},{9,5},{13,9},{6,2},{10,6},{14,10},{7,3},{... | collective-permute-start | bytes 442376 | tf_op jit(solution)/shard_map/ppermute | solution.py:22
  12.8 1.3 %collective-permute-done.1 = bf16[1,18,32,128]{3,2,1,0:T(8,128)(2,1)S(1)} collective-permute-done((bf16[1,18,32,128]{3,2,1,0:T(8,128)(2,1)S(1)}, bf16[1,18,32,128]{3,2,1,0:T(8,128)(2,1)S(1)}, u32[]{:S(2)}, u32[]{:S(2)}) %collective-permute-start.1) | collective-permute-done | bytes 147488 | tf_op jit(solution)/shard_map/ppermute | solution.py:21
  14.1 4.4 %collective-permute-done.2 = bf16[1,18,32,128]{3,2,1,0:T(8,128)(2,1)S(1)} collective-permute-done((bf16[1,18,32,128]{3,2,1,0:T(8,128)(2,1)S(1)}, bf16[1,18,32,128]{3,2,1,0:T(8,128)(2,1)S(1)}, u32[]{:S(2)}, u32[]{:S(2)}) %collective-permute-start.2) | collective-permute-done | bytes 147488 | tf_op jit(solution)/shard_map/ppermute | solution.py:22
  18.4 1.2 %pad_maximum_fusion.1 = bf16[6,18,32,128]{3,2,1,0:T(8,128)(2,1)S(1)} fusion(bf16[1,18,32,128]{3,2,1,0:T(8,128)(2,1)S(1)} %collective-permute-done.2, bf16[4,1,32,128]{3,2,1,0:T(8,128)(2,1)S(1)} %get-tuple-element.15, bf16[4,16,32,128]{3,2,1,0:T(8,128)(2,1)} %param.4, bf16[4,1,32,128]{3,2,1,0:T(8,128)(2,1)S(1)} %get-tuple-element.14, ...), kind=kLoop, calls=%fused_computation.13 | loop fusion | flops 1769472 | bytes 1769472 | tf_op jit(solution)/shard_map/concatenate | solution.py:23
  19.6 0.3 constant_dynamic-slice_fusion.6
  19.9 0.8 %pad_slice_fusion.1 = (bf16[6,18,32,64]{3,2,1,0:T(8,128)(2,1)S(1)}, bf16[6,18,32,64]{3,2,1,0:T(8,128)(2,1)S(1)}) fusion(bf16[6,18,32,64]{3,2,1,0:T(8,128)(2,1)S(1)} %constant_dynamic-slice_fusion.6), kind=kLoop, calls=%fused_computation.12 | loop fusion | bytes 1327104 | tf_op jit(solution)/shard_map/slice | solution.py:58
  20.7 0.9 %pad_maximum_fusion = bf16[6,18,32,192]{3,2,1,0:T(8,128)(2,1)S(1)} fusion(bf16[6,18,32,64]{3,2,1,0:T(8,128)(2,1)S(1)} %get-tuple-element.7, bf16[6,18,32,64]{3,2,1,0:T(8,128)(2,1)S(1)} %constant_dynamic-slice_fusion.6, bf16[6,18,32,64]{3,2,1,0:T(8,128)(2,1)S(1)} %get-tuple-element.6), kind=kLoop, calls=%fused_computation.2 | loop fusion | flops 3981312 | bytes 2654208 | tf_op jit(solution)/shard_map/concatenate | solution.py:58
  21.6 0.2 copy-done.2
  21.8 0.5 fusion.21
  22.2 0.5 fusion.22
  22.7 0.5 fusion.23
  23.2 0.5 fusion.24
  23.7 0.5 fusion.25
  24.2 0.5 fusion.26
  24.6 0.5 fusion.27
  25.1 0.5 fusion.28
  25.6 0.5 fusion.29
  26.1 0.1 copy.9
  26.2 0.1 copy.10
  26.5 0.1 copy.14
  26.7 0.1 copy.17
  26.9 1.4 %reshape.84 = f32[4,2,432,64]{2,1,0,3:T(2,128)S(1)} reshape(f32[3456,64]{0,1:T(8,128)S(1)} %bitcast_dynamic-update-slice_fusion) | data formatting | bytes 1769472 | tf_op jit(solution)/shard_map/reshape | solution.py:70
  28.3 1.1 %constant_dynamic-slice_fusion.5 = (f32[4,1,432,64]{2,1,0,3:T(1,128)S(1)}, f32[4,1,432,64]{2,1,0,3:T(1,128)S(1)}) fusion(f32[4,2,432,64]{2,1,0,3:T(2,128)S(1)} %reshape.84, s32[]{:T(128)S(6)} %select_n.66, s32[]{:T(128)S(6)} %select_n.68), kind=kLoop, calls=%fused_computation.45 | loop fusion | bytes 1769480 | tf_op jit(solution)/shard_map/jit(dynamic_index_in_dim)/dynamic_slice | solution.py:34
  29.4 0.1 copy.59
  29.6 1.6 %collective-permute-start.3 = (f32[4,432,64]{1,0,2:T(4,128)S(1)}, f32[4,432,64]{1,0,2:T(4,128)S(1)}, u32[]{:S(2)}, u32[]{:S(2)}) collective-permute-start(f32[4,432,64]{1,0,2:T(4,128)S(1)} %bitcast.186), channel_id=1, source_target_pairs={{0,2},{2,0},{1,3},{3,1},{4,6},{6,4},{5,7},{7,5},{8,10},{10,8},{9,1... | collective-permute-start | bytes 1327112 | tf_op jit(solution)/shard_map/ppermute | solution.py:37
  31.1 0.2 fusion.49
  31.3 0.4 copy.34
  31.7 0.2 pad.5.clone
  31.9 0.1 copy.7
  32.1 0.1 slice.63
  32.2 0.4 copy-done.3
  32.6 5.0 %fusion.11 = bf16[4,16,8,5,128]{4,2,3,1,0:T(8,128)(2,1)S(1)} fusion(bf16[3,3,3,128,128]{4,3,2,1,0:T(8,128)(2,1)S(1)} %bitcast.174, bf16[6,18,1,7,2,128]{5,3,4,1,0,2:T(8,128)(2,1)S(1)} %slice.63, bf16[6,18,1,8,5,128]{5,3,4,1,0,2:T(8,128)(2,1)S(1)} %copy.7, pred[8,5]{0,1:T(8,128)(4,1)S(1)} %copy-done.3), kind=kOutput, calls=%fused_computation.10 | convolution fusion | flops 2270224384 | bytes 3033128 | tf_op jit(solution)/shard_map/conv_general_dilated | solution.py:50
  37.6 0.1 copy.8
  37.7 3.0 %collective-permute-done.3 = f32[4,432,64]{1,0,2:T(4,128)S(1)} collective-permute-done((f32[4,432,64]{1,0,2:T(4,128)S(1)}, f32[4,432,64]{1,0,2:T(4,128)S(1)}, u32[]{:S(2)}, u32[]{:S(2)}) %collective-permute-start.3) | collective-permute-done | bytes 442400 | tf_op jit(solution)/shard_map/ppermute | solution.py:37
  40.7 0.2 bitcast_add_fusion
  40.9 0.5 constant_dynamic-slice_fusion.3
  41.4 1.6 %collective-permute-start.4 = (f32[432,64]{0,1:T(8,128)S(1)}, f32[432,64]{0,1:T(8,128)S(1)}, u32[]{:S(2)}, u32[]{:S(2)}) collective-permute-start(f32[432,64]{0,1:T(8,128)S(1)} %bitcast.187), channel_id=1, source_target_pairs={{0,4},{4,8},{8,12},{12,0},{1,5},{5,9},{9,13},{13,1},{2,6},{6,10},{... | collective-permute-start | bytes 331784 | tf_op jit(solution)/shard_map/ppermute | solution.py:37
  43.0 1.1 %collective-permute-start.5 = (f32[432,64]{0,1:T(8,128)S(1)}, f32[432,64]{0,1:T(8,128)S(1)}, u32[]{:S(2)}, u32[]{:S(2)}) collective-permute-start(f32[432,64]{0,1:T(8,128)S(1)} %bitcast.188), channel_id=1, source_target_pairs={{0,8},{4,12},{8,0},{12,4},{1,9},{5,13},{9,1},{13,5},{2,10},{6,14},... | collective-permute-start | bytes 331784 | tf_op jit(solution)/shard_map/ppermute | solution.py:37
  44.1 3.0 %collective-permute-start.6 = (f32[432,64]{0,1:T(8,128)S(1)}, f32[432,64]{0,1:T(8,128)S(1)}, u32[]{:S(2)}, u32[]{:S(2)}) collective-permute-start(f32[432,64]{0,1:T(8,128)S(1)} %bitcast.189), channel_id=1, source_target_pairs={{0,12},{4,0},{8,4},{12,8},{1,13},{5,1},{9,5},{13,9},{2,14},{6,2},{... | collective-permute-start | bytes 331784 | tf_op jit(solution)/shard_map/ppermute | solution.py:37
  47.1 0.9 %copy.18 = bf16[4,16,32,128]{3,2,1,0:T(8,128)(2,1)} copy(bf16[4,16,32,128]{3,1,2,0:T(8,128)(2,1)S(1)} %slice_bitcast_fusion) | data formatting | bytes 1048576
  48.0 0.3 collective-permute-done.4
  48.3 3.6 %collective-permute-done.5 = f32[432,64]{0,1:T(8,128)S(1)} collective-permute-done((f32[432,64]{0,1:T(8,128)S(1)}, f32[432,64]{0,1:T(8,128)S(1)}, u32[]{:S(2)}, u32[]{:S(2)}) %collective-permute-start.5) | collective-permute-done | bytes 110624 | tf_op jit(solution)/shard_map/ppermute | solution.py:37
  52.0 0.7 %fusion.17 = f32[432,64]{0,1:T(8,128)} fusion(f32[432,64]{0,1:T(8,128)S(1)} %collective-permute-done.6, f32[432,64]{0,1:T(8,128)S(1)} %collective-permute-done.5, f32[432,64]{0,1:T(8,128)S(1)} %collective-permute-done.4, f32[1,432,64]{1,0,2:T(1,128)S(1)} %get-tuple-element.10), kind=kLoop, calls=%fused_computation.27 | loop fusion | flops 110592 | bytes 552960 | tf_op jit(solution)/shard_map/div | solution.py:73
  (26 shorter events, 0.5 us)
Async XLA Ops:
  0.6 31.6 %copy-start = (bf16[27,128,128]{2,1,0:T(8,128)(2,1)S(1)}, bf16[27,128,128]{2,1,0:T(8,128)(2,1)}, u32[]{:S(2)}) copy-start(bf16[27,128,128]{2,1,0:T(8,128)(2,1)} %param.5) | copy-start | bytes 2654212
  1.5 4.8 %collective-permute-start = (bf16[4,1,32,128]{3,2,1,0:T(8,128)(2,1)S(1)}, bf16[4,1,32,128]{3,2,1,0:T(8,128)(2,1)S(1)}, u32[]{:S(2)}, u32[]{:S(2)}) collective-permute-start(bf16[4,1,32,128]{3,2,1,0:T(8,128)(2,1)S(1)} %slice_select_fusion), channel_id=1, source_target_pairs={{0,2},{2,0},{1,3},{3,1},{4,6},{6,4},{5,7},{7,5},{8,10},{10,8},{9,1... | collective-permute-start | bytes 98312 | tf_op jit(solution)/shard_map/ppermute | solution.py:17
  7.4 6.7 %collective-permute-start.1 = (bf16[1,18,32,128]{3,2,1,0:T(8,128)(2,1)S(1)}, bf16[1,18,32,128]{3,2,1,0:T(8,128)(2,1)S(1)}, u32[]{:S(2)}, u32[]{:S(2)}) collective-permute-start(bf16[1,18,32,128]{3,2,1,0:T(8,128)(2,1)S(1)} %get-tuple-element.8), channel_id=1, source_target_pairs={{0,4},{4,8},{8,12},{1,5},{5,9},{9,13},{2,6},{6,10},{10,14},{3,7},{... | collective-permute-start | bytes 442376 | tf_op jit(solution)/shard_map/ppermute | solution.py:21
  11.4 7.0 %collective-permute-start.2 = (bf16[1,18,32,128]{3,2,1,0:T(8,128)(2,1)S(1)}, bf16[1,18,32,128]{3,2,1,0:T(8,128)(2,1)S(1)}, u32[]{:S(2)}, u32[]{:S(2)}) collective-permute-start(bf16[1,18,32,128]{3,2,1,0:T(8,128)(2,1)S(1)} %get-tuple-element.9), channel_id=1, source_target_pairs={{4,0},{8,4},{12,8},{5,1},{9,5},{13,9},{6,2},{10,6},{14,10},{7,3},{... | collective-permute-start | bytes 442376 | tf_op jit(solution)/shard_map/ppermute | solution.py:22
  20.7 1.0 %copy-start.2 = (bf16[4,16,32,128]{3,2,1,0:T(8,128)(2,1)S(1)}, bf16[4,16,32,128]{3,2,1,0:T(8,128)(2,1)}, u32[]{:S(2)}) copy-start(bf16[4,16,32,128]{3,2,1,0:T(8,128)(2,1)} %param.3) | copy-start | bytes 1572868
  28.3 2.8 %copy-start.1 = (bf16[4,16,32,128]{3,2,1,0:T(8,128)(2,1)S(1)}, bf16[4,16,32,128]{3,2,1,0:T(8,128)(2,1)}, u32[]{:S(2)}) copy-start(bf16[4,16,32,128]{3,2,1,0:T(8,128)(2,1)} %param.4) | copy-start | bytes 1572868
  29.6 11.1 %collective-permute-start.3 = (f32[4,432,64]{1,0,2:T(4,128)S(1)}, f32[4,432,64]{1,0,2:T(4,128)S(1)}, u32[]{:S(2)}, u32[]{:S(2)}) collective-permute-start(f32[4,432,64]{1,0,2:T(4,128)S(1)} %bitcast.186), channel_id=1, source_target_pairs={{0,2},{2,0},{1,3},{3,1},{4,6},{6,4},{5,7},{7,5},{8,10},{10,8},{9,1... | collective-permute-start | bytes 1327112 | tf_op jit(solution)/shard_map/ppermute | solution.py:37
  31.9 0.7 %copy-start.3 = (pred[8,5]{0,1:T(8,128)(4,1)S(1)}, pred[8,5]{0,1:T(8,128)(4,1)}, u32[]{:S(2)}) copy-start(pred[8,5]{0,1:T(8,128)(4,1)} %constant.79) | copy-start | bytes 124
  41.4 7.0 %collective-permute-start.4 = (f32[432,64]{0,1:T(8,128)S(1)}, f32[432,64]{0,1:T(8,128)S(1)}, u32[]{:S(2)}, u32[]{:S(2)}) collective-permute-start(f32[432,64]{0,1:T(8,128)S(1)} %bitcast.187), channel_id=1, source_target_pairs={{0,4},{4,8},{8,12},{12,0},{1,5},{5,9},{9,13},{13,1},{2,6},{6,10},{... | collective-permute-start | bytes 331784 | tf_op jit(solution)/shard_map/ppermute | solution.py:37
  43.0 9.0 %collective-permute-start.5 = (f32[432,64]{0,1:T(8,128)S(1)}, f32[432,64]{0,1:T(8,128)S(1)}, u32[]{:S(2)}, u32[]{:S(2)}) collective-permute-start(f32[432,64]{0,1:T(8,128)S(1)} %bitcast.188), channel_id=1, source_target_pairs={{0,8},{4,12},{8,0},{12,4},{1,9},{5,13},{9,1},{13,5},{2,10},{6,14},... | collective-permute-start | bytes 331784 | tf_op jit(solution)/shard_map/ppermute | solution.py:37
  44.1 7.9 %collective-permute-start.6 = (f32[432,64]{0,1:T(8,128)S(1)}, f32[432,64]{0,1:T(8,128)S(1)}, u32[]{:S(2)}, u32[]{:S(2)}) collective-permute-start(f32[432,64]{0,1:T(8,128)S(1)} %bitcast.189), channel_id=1, source_target_pairs={{0,12},{4,0},{8,4},{12,8},{1,13},{5,1},{9,5},{13,9},{2,14},{6,2},{... | collective-permute-start | bytes 331784 | tf_op jit(solution)/shard_map/ppermute | solution.py:37

commit v5 on v4

--- a/solution.py
+++ b/solution.py
@@ -24,6 +24,44 @@
     return cells
 
 
+def edge_pair(head, tail, axis):
+    count = lax.axis_size(axis)
+    if count == 1:
+        return jnp.zeros_like(tail), jnp.zeros_like(head)
+    if count == 2:
+        me = lax.axis_index(axis)
+        got = lax.ppermute(jnp.where(me == 0, tail, head), axis, [(0, 1), (1, 0)])
+        return jnp.where(me == 1, got, jnp.zeros_like(got)), jnp.where(me == 0, got, jnp.zeros_like(got))
+    low = lax.ppermute(tail, axis, [(i, i + 1) for i in range(count - 1)])
+    high = lax.ppermute(head, axis, [(i + 1, i) for i in range(count - 1)])
+    return low, high
+
+
+def with_halo_one_stage(cells):
+    nx = lax.axis_size("gx")
+    ix = lax.axis_index("gx")
+    iy = lax.axis_index("gy")
+    low_r, high_r = edge_pair(cells[:1], cells[-1:], "gx")
+    low_c, high_c = edge_pair(cells[:, :1], cells[:, -1:], "gy")
+    both = ("gx", "gy")
+    zero = jnp.zeros_like(cells[:1, :1])
+    if nx > 1:
+        ahead = [(x * 2 + y, (x + 1) * 2 + 1 - y) for x in range(nx - 1) for y in range(2)]
+        behind = [((x + 1) * 2 + y, x * 2 + 1 - y) for x in range(nx - 1) for y in range(2)]
+        from_low = lax.ppermute(jnp.where(iy == 0, cells[-1:, -1:], cells[-1:, :1]), both, ahead)
+        from_high = lax.ppermute(jnp.where(iy == 0, cells[:1, -1:], cells[:1, :1]), both, behind)
+    else:
+        from_low = from_high = zero
+    top = jnp.concatenate(
+        [jnp.where(iy == 1, from_low, zero), low_r, jnp.where(iy == 0, from_low, zero)], axis=1
+    )
+    bottom = jnp.concatenate(
+        [jnp.where(iy == 1, from_high, zero), high_r, jnp.where(iy == 0, from_high, zero)], axis=1
+    )
+    middle = jnp.concatenate([low_c, cells, high_c], axis=1)
+    return jnp.concatenate([top, middle, bottom], axis=0)
+
+
 def scatter_sum(blocks, axis, dim):
     count = lax.axis_size(axis)
     if count == 1:
@@ -43,7 +81,10 @@
     ncores = lax.axis_size("col")
     half = weight.shape[2] // ncores
     offset = lax.axis_index("col") * half
-    gh = with_halo(grad_out, (("gy", 1), ("gx", 0)), 1)
+    if lax.axis_size("gy") == 2:
+        gh = with_halo_one_stage(grad_out)
+    else:
+        gh = with_halo(grad_out, (("gy", 1), ("gx", 0)), 1)
     taps = weight.reshape(3, 3, 3, chans, weight.shape[2])
     kflip = jnp.transpose(taps[::-1, ::-1, ::-1], (0, 1, 2, 4, 3))
     pad = [(0, 0), (0, 0), (1, 1)]

time: 53 us -> 58.5 us (1.10)
  starting transfers between devices: 15.5 us -> 20.7 us
  local copies, waits for them, and re-layouts: 7.39 us -> 8.38 us
    ppermute x3 -> x5, starting transfers between devices: 8.25 us -> 14.4 us  [the longest x1 5.84 us: with_halo_one_stage(): lax.ppermute(jnp.where(iy == 0, cells[-1:, -1:], cells[-1:, :1]), both, a...]
    ppermute x3 -> x5, waiting for transfers between devices: 7.56 us -> 5.43 us  [the longest x1 4.36 us: edge_pair(): high = lax.ppermute(head, axis, [(i + 1, i) for i in range(count - 1)])]
    ppermute x4, waiting for transfers between devices: 6.97 us -> 8.59 us  [scatter_sum(): lax.ppermute(part, axis, [(j, (j + shift) % count) for j in range(count)])]
    slice x1 -> x0, other arithmetic: 1.01 us -> none  [with_halo(): lax.slice_in_dim(cells, cells.shape[dim] - width, cells.shape[dim], axis=...]
    slice x0 -> x1, local copies, waits for them, and re-layouts: none -> 0.99 us  [with_halo_one_stage(): low_r, high_r = edge_pair(cells[:1], cells[-1:], 'gx')]
    ppermute x4, starting transfers between devices: 7.24 us -> 6.29 us  [scatter_sum(): lax.ppermute(part, axis, [(j, (j + shift) % count) for j in range(count)])]
    select_n x2 -> x5, other arithmetic: 0.87 us -> 1.65 us  [the longest x1 0.83 us: with_halo_one_stage(): jnp.where(iy == 0, cells[-1:, -1:], cells[-1:, :1])]
  transfers between devices with their start and end apart: 7 -> 9, of which waited for: 6 -> 5; matrix products, arithmetic and copies ran while one was open for 13% -> 15% of each run, Pallas kernels for 0% -> 0%
where the time goes in v5:
time: 58.5 us; the launch traced here: 58.1 us
  starting transfers between devices  20.7 us (35%)
  waiting for transfers between devices  14 us (24%)
  matrix products  9.21 us (16%)
  local copies, waits for them, and re-layouts  8.38 us (14%)
  other arithmetic  4.64 us (8%)
  between operations  1.15 us (2%)
    ppermute x4, waiting for transfers between devices, scatter_sum(): lax.ppermute(part, axis, [(j, (j + shift) % count) for j in range(count)])  8.59 us
    ppermute x4, starting transfers between devices, scatter_sum(): lax.ppermute(part, axis, [(j, (j + shift) % count) for j in range(count)])  6.29 us
    ppermute x1, starting transfers between devices, with_halo_one_stage(): lax.ppermute(jnp.where(iy == 0, cells[-1:, -1:], cells[-1:, :1]), both, a...  5.84 us
    ppermute x1, starting transfers between devices, edge_pair(): low = lax.ppermute(tail, axis, [(i, i + 1) for i in range(count - 1)])  5.48 us
    conv_general_dilated x1, matrix products, on_device(): lax.conv_general_dilated(gh[None], kflip, (1, 1, 1), pad, dimension_numbe...  4.94 us
    ppermute x1, waiting for transfers between devices, edge_pair(): high = lax.ppermute(head, axis, [(i + 1, i) for i in range(count - 1)])  4.36 us
    dot_general x9, matrix products, on_device(): lax.dot_general(x_act, window, (((0, 1, 2), (0, 1, 2)), ((), ())), prefer...  4.26 us
    unnamed x22, local copies, waits for them, and re-layouts  2.13 us
  transfers between devices with their start and end apart: 9, of which 5 were waited for; matrix products, arithmetic and copies ran while one was open for 15% of the time, Pallas kernels for 0%

profile of v5, /device:TPU:0, one launch (start us, length us, event | category | flops | bytes accessed | tf_op | source)
XLA Modules:
  0.0 58.1 jit_solution(8755838581292629101)
XLA Ops:
  0.7 0.8 %slice_select_fusion.2 = (bf16[1,1,32,128]{3,2,1,0:T(8,128)(2,1)S(1)}, bf16[1,1,32,128]{3,2,1,0:T(8,128)(2,1)S(1)}) fusion(bf16[4,16,32,128]{3,2,1,0:T(8,128)(2,1)} %param.4, pred[]{:T(512)S(6)} %eq.9), kind=kLoop, calls=%fused_computation.38 | loop fusion | flops 8192 | bytes 49153 | tf_op jit(solution)/shard_map/jit(_where)/select_n | solution.py:51
  1.5 5.8 %collective-permute-start = (bf16[1,1,32,128]{3,2,1,0:T(8,128)(2,1)S(1)}, bf16[1,1,32,128]{3,2,1,0:T(8,128)(2,1)S(1)}, u32[]{:S(2)}, u32[]{:S(2)}) collective-permute-start(bf16[1,1,32,128]{3,2,1,0:T(8,128)(2,1)S(1)} %get-tuple-element.14), channel_id=1, source_target_pairs={{0,6},{2,4},{4,10},{6,8},{8,14},{10,12},{1,7},{3,5},{5,11},{7,9},{... | collective-permute-start | bytes 24584 | tf_op jit(solution)/shard_map/ppermute | solution.py:51
  7.3 1.3 %collective-permute-start.3 = (bf16[1,1,32,128]{3,2,1,0:T(8,128)(2,1)S(1)}, bf16[1,1,32,128]{3,2,1,0:T(8,128)(2,1)S(1)}, u32[]{:S(2)}, u32[]{:S(2)}) collective-permute-start(bf16[1,1,32,128]{3,2,1,0:T(8,128)(2,1)S(1)} %get-tuple-element.15), channel_id=1, source_target_pairs={{4,2},{6,0},{8,6},{10,4},{12,10},{14,8},{5,3},{7,1},{9,7},{11,5},{... | collective-permute-start | bytes 24584 | tf_op jit(solution)/shard_map/ppermute | solution.py:52
  8.6 0.8 %slice_select_fusion = bf16[4,1,32,128]{3,2,1,0:T(8,128)(2,1)S(1)} fusion(bf16[4,16,32,128]{3,2,1,0:T(8,128)(2,1)} %param.4, pred[]{:T(512)S(6)} %eq.9), kind=kLoop, calls=%fused_computation.34 | loop fusion | flops 16384 | bytes 98305 | tf_op jit(solution)/shard_map/jit(_where)/select_n | solution.py:33
  9.4 0.5 collective-permute-start.2
  10.0 1.0 %fusion.21 = (bf16[1,16,32,128]{3,2,1,0:T(8,128)(2,1)S(1)}, bf16[1,16,32,128]{3,2,1,0:T(8,128)(2,1)S(1)}) fusion(bf16[4,16,32,128]{3,2,1,0:T(8,128)(2,1)} %param.4), kind=kLoop, calls=%fused_computation.53 | loop fusion | bytes 524288 | tf_op jit(solution)/shard_map/slice | solution.py:44
  10.9 5.5 %collective-permute-start.1 = (bf16[1,16,32,128]{3,2,1,0:T(8,128)(2,1)S(1)}, bf16[1,16,32,128]{3,2,1,0:T(8,128)(2,1)S(1)}, u32[]{:S(2)}, u32[]{:S(2)}) collective-permute-start(bf16[1,16,32,128]{3,2,1,0:T(8,128)(2,1)S(1)} %get-tuple-element.12), channel_id=1, source_target_pairs={{0,4},{4,8},{8,12},{1,5},{5,9},{9,13},{2,6},{6,10},{10,14},{3,7},{... | collective-permute-start | bytes 393224 | tf_op jit(solution)/shard_map/ppermute | solution.py:35
  16.4 1.3 %collective-permute-start.4 = (bf16[1,16,32,128]{3,2,1,0:T(8,128)(2,1)S(1)}, bf16[1,16,32,128]{3,2,1,0:T(8,128)(2,1)S(1)}, u32[]{:S(2)}, u32[]{:S(2)}) collective-permute-start(bf16[1,16,32,128]{3,2,1,0:T(8,128)(2,1)S(1)} %get-tuple-element.13), channel_id=1, source_target_pairs={{4,0},{8,4},{12,8},{5,1},{9,5},{13,9},{6,2},{10,6},{14,10},{7,3},{... | collective-permute-start | bytes 393224 | tf_op jit(solution)/shard_map/ppermute | solution.py:36
  17.9 1.1 %collective-permute-done.1 = bf16[1,16,32,128]{3,2,1,0:T(8,128)(2,1)S(1)} collective-permute-done((bf16[1,16,32,128]{3,2,1,0:T(8,128)(2,1)S(1)}, bf16[1,16,32,128]{3,2,1,0:T(8,128)(2,1)S(1)}, u32[]{:S(2)}, u32[]{:S(2)}) %collective-permute-start.1) | collective-permute-done | bytes 131104 | tf_op jit(solution)/shard_map/ppermute | solution.py:35
  18.9 4.4 %collective-permute-done.4 = bf16[1,16,32,128]{3,2,1,0:T(8,128)(2,1)S(1)} collective-permute-done((bf16[1,16,32,128]{3,2,1,0:T(8,128)(2,1)S(1)}, bf16[1,16,32,128]{3,2,1,0:T(8,128)(2,1)S(1)}, u32[]{:S(2)}, u32[]{:S(2)}) %collective-permute-start.4) | collective-permute-done | bytes 131104 | tf_op jit(solution)/shard_map/ppermute | solution.py:36
  23.3 1.2 %maximum_maximum_fusion = bf16[6,18,32,128]{3,2,1,0:T(8,128)(2,1)S(1)} fusion(bf16[1,1,32,128]{3,2,1,0:T(8,128)(2,1)S(1)} %get-tuple-element.21, bf16[1,16,32,128]{3,2,1,0:T(8,128)(2,1)S(1)} %collective-permute-done.4, bf16[1,1,32,128]{3,2,1,0:T(8,128)(2,1)S(1)} %get-tuple-element.20, bf16[4,1,32,128]{3,2,1,0:T(8,128)(2,1)S(1)} %get-tuple-element.17, ...), kind=kLoop, calls=%fused_computation.13 | loop fusion | flops 3538944 | bytes 1769472 | tf_op jit(solution)/shard_map/concatenate | solution.py:62
  24.5 0.3 constant_dynamic-slice_fusion.6
  24.8 0.8 %pad_slice_fusion.1 = (bf16[6,18,32,64]{3,2,1,0:T(8,128)(2,1)S(1)}, bf16[6,18,32,64]{3,2,1,0:T(8,128)(2,1)S(1)}) fusion(bf16[6,18,32,64]{3,2,1,0:T(8,128)(2,1)S(1)} %constant_dynamic-slice_fusion.6), kind=kLoop, calls=%fused_computation.12 | loop fusion | bytes 1327104 | tf_op jit(solution)/shard_map/slice | solution.py:99
  25.5 0.9 %pad_maximum_fusion = bf16[6,18,32,192]{3,2,1,0:T(8,128)(2,1)S(1)} fusion(bf16[6,18,32,64]{3,2,1,0:T(8,128)(2,1)S(1)} %get-tuple-element.7, bf16[6,18,32,64]{3,2,1,0:T(8,128)(2,1)S(1)} %constant_dynamic-slice_fusion.6, bf16[6,18,32,64]{3,2,1,0:T(8,128)(2,1)S(1)} %get-tuple-element.6), kind=kLoop, calls=%fused_computation.2 | loop fusion | flops 3981312 | bytes 2654208 | tf_op jit(solution)/shard_map/concatenate | solution.py:99
  26.4 0.2 copy-done.2
  26.6 0.5 fusion.22
  27.1 0.5 fusion.23
  27.5 0.5 fusion.24
  28.0 0.5 fusion.25
  28.5 0.5 fusion.26
  29.0 0.5 fusion.27
  29.5 0.5 fusion.28
  29.9 0.5 fusion.29
  30.4 0.5 fusion.30
  31.2 0.1 copy.13
  31.5 0.1 copy.17
  31.8 1.4 %reshape.84 = f32[4,2,432,64]{2,1,0,3:T(2,128)S(1)} reshape(f32[3456,64]{0,1:T(8,128)S(1)} %bitcast_dynamic-update-slice_fusion) | data formatting | bytes 1769472 | tf_op jit(solution)/shard_map/reshape | solution.py:111
  33.2 1.1 %constant_dynamic-slice_fusion.5 = (f32[4,1,432,64]{2,1,0,3:T(1,128)S(1)}, f32[4,1,432,64]{2,1,0,3:T(1,128)S(1)}) fusion(f32[4,2,432,64]{2,1,0,3:T(2,128)S(1)} %reshape.84, s32[]{:T(128)S(6)} %select_n.104, s32[]{:T(128)S(6)} %select_n.106), kind=kLoop, calls=%fused_computation.48 | loop fusion | bytes 1769480 | tf_op jit(solution)/shard_map/jit(dynamic_index_in_dim)/dynamic_slice | solution.py:72
  34.2 0.1 copy.59
  34.4 0.6 %collective-permute-start.5 = (f32[4,432,64]{1,0,2:T(4,128)S(1)}, f32[4,432,64]{1,0,2:T(4,128)S(1)}, u32[]{:S(2)}, u32[]{:S(2)}) collective-permute-start(f32[4,432,64]{1,0,2:T(4,128)S(1)} %bitcast.186), channel_id=1, source_target_pairs={{0,2},{2,0},{1,3},{3,1},{4,6},{6,4},{5,7},{7,5},{8,10},{10,8},{9,1... | collective-permute-start | bytes 1327112 | tf_op jit(solution)/shard_map/ppermute | solution.py:75
  35.0 0.1 fusion.50
  35.1 0.4 copy.34
  35.5 0.2 pad.5.clone
  35.8 0.1 copy.7
  35.9 0.1 slice.79
  36.1 0.4 copy-done.3
  36.4 4.9 %fusion.11 = bf16[4,16,8,5,128]{4,2,3,1,0:T(8,128)(2,1)S(1)} fusion(bf16[3,3,3,128,128]{4,3,2,1,0:T(8,128)(2,1)S(1)} %bitcast.174, bf16[6,18,1,7,2,128]{5,3,4,1,0,2:T(8,128)(2,1)S(1)} %slice.79, bf16[6,18,1,8,5,128]{5,3,4,1,0,2:T(8,128)(2,1)S(1)} %copy.7, pred[8,5]{0,1:T(8,128)(4,1)S(1)} %copy-done.3), kind=kOutput, calls=%fused_computation.10 | convolution fusion | flops 2270224384 | bytes 3033128 | tf_op jit(solution)/shard_map/conv_general_dilated | solution.py:91
  41.4 0.1 copy.8
  41.5 4.4 %collective-permute-done.5 = f32[4,432,64]{1,0,2:T(4,128)S(1)} collective-permute-done((f32[4,432,64]{1,0,2:T(4,128)S(1)}, f32[4,432,64]{1,0,2:T(4,128)S(1)}, u32[]{:S(2)}, u32[]{:S(2)}) %collective-permute-start.5) | collective-permute-done | bytes 442400 | tf_op jit(solution)/shard_map/ppermute | solution.py:75
  45.8 0.2 bitcast_add_fusion
  46.0 0.5 constant_dynamic-slice_fusion.3
  46.5 1.6 %collective-permute-start.6 = (f32[432,64]{0,1:T(8,128)S(1)}, f32[432,64]{0,1:T(8,128)S(1)}, u32[]{:S(2)}, u32[]{:S(2)}) collective-permute-start(f32[432,64]{0,1:T(8,128)S(1)} %bitcast.187), channel_id=1, source_target_pairs={{0,4},{4,8},{8,12},{12,0},{1,5},{5,9},{9,13},{13,1},{2,6},{6,10},{... | collective-permute-start | bytes 331784 | tf_op jit(solution)/shard_map/ppermute | solution.py:75
  48.1 1.1 %collective-permute-start.7 = (f32[432,64]{0,1:T(8,128)S(1)}, f32[432,64]{0,1:T(8,128)S(1)}, u32[]{:S(2)}, u32[]{:S(2)}) collective-permute-start(f32[432,64]{0,1:T(8,128)S(1)} %bitcast.188), channel_id=1, source_target_pairs={{0,8},{4,12},{8,0},{12,4},{1,9},{5,13},{9,1},{13,5},{2,10},{6,14},... | collective-permute-start | bytes 331784 | tf_op jit(solution)/shard_map/ppermute | solution.py:75
  49.3 3.0 %collective-permute-start.8 = (f32[432,64]{0,1:T(8,128)S(1)}, f32[432,64]{0,1:T(8,128)S(1)}, u32[]{:S(2)}, u32[]{:S(2)}) collective-permute-start(f32[432,64]{0,1:T(8,128)S(1)} %bitcast.189), channel_id=1, source_target_pairs={{0,12},{4,0},{8,4},{12,8},{1,13},{5,1},{9,5},{13,9},{2,14},{6,2},{... | collective-permute-start | bytes 331784 | tf_op jit(solution)/shard_map/ppermute | solution.py:75
  52.3 0.9 %copy.18 = bf16[4,16,32,128]{3,2,1,0:T(8,128)(2,1)} copy(bf16[4,16,32,128]{3,1,2,0:T(8,128)(2,1)S(1)} %slice_bitcast_fusion) | data formatting | bytes 1048576
  53.2 0.3 collective-permute-done.6
  53.5 3.9 %collective-permute-done.7 = f32[432,64]{0,1:T(8,128)S(1)} collective-permute-done((f32[432,64]{0,1:T(8,128)S(1)}, f32[432,64]{0,1:T(8,128)S(1)}, u32[]{:S(2)}, u32[]{:S(2)}) %collective-permute-start.7) | collective-permute-done | bytes 110624 | tf_op jit(solution)/shard_map/ppermute | solution.py:75
  57.4 0.7 %fusion.17 = f32[432,64]{0,1:T(8,128)} fusion(f32[432,64]{0,1:T(8,128)S(1)} %collective-permute-done.8, f32[432,64]{0,1:T(8,128)S(1)} %collective-permute-done.7, f32[432,64]{0,1:T(8,128)S(1)} %collective-permute-done.6, f32[1,432,64]{1,0,2:T(1,128)S(1)} %get-tuple-element.8), kind=kLoop, calls=%fused_computation.24 | loop fusion | flops 110592 | bytes 552960 | tf_op jit(solution)/shard_map/div | solution.py:114
  (33 shorter events, 0.7 us)
Async XLA Ops:
  0.6 35.4 %copy-start = (bf16[27,128,128]{2,1,0:T(8,128)(2,1)S(1)}, bf16[27,128,128]{2,1,0:T(8,128)(2,1)}, u32[]{:S(2)}) copy-start(bf16[27,128,128]{2,1,0:T(8,128)(2,1)} %param.5) | copy-start | bytes 2654212
  1.5 16.3 %collective-permute-start = (bf16[1,1,32,128]{3,2,1,0:T(8,128)(2,1)S(1)}, bf16[1,1,32,128]{3,2,1,0:T(8,128)(2,1)S(1)}, u32[]{:S(2)}, u32[]{:S(2)}) collective-permute-start(bf16[1,1,32,128]{3,2,1,0:T(8,128)(2,1)S(1)} %get-tuple-element.14), channel_id=1, source_target_pairs={{0,6},{2,4},{4,10},{6,8},{8,14},{10,12},{1,7},{3,5},{5,11},{7,9},{... | collective-permute-start | bytes 24584 | tf_op jit(solution)/shard_map/ppermute | solution.py:51
  7.3 10.5 %collective-permute-start.3 = (bf16[1,1,32,128]{3,2,1,0:T(8,128)(2,1)S(1)}, bf16[1,1,32,128]{3,2,1,0:T(8,128)(2,1)S(1)}, u32[]{:S(2)}, u32[]{:S(2)}) collective-permute-start(bf16[1,1,32,128]{3,2,1,0:T(8,128)(2,1)S(1)} %get-tuple-element.15), channel_id=1, source_target_pairs={{4,2},{6,0},{8,6},{10,4},{12,10},{14,8},{5,3},{7,1},{9,7},{11,5},{... | collective-permute-start | bytes 24584 | tf_op jit(solution)/shard_map/ppermute | solution.py:52
  9.4 8.4 %collective-permute-start.2 = (bf16[4,1,32,128]{3,2,1,0:T(8,128)(2,1)S(1)}, bf16[4,1,32,128]{3,2,1,0:T(8,128)(2,1)S(1)}, u32[]{:S(2)}, u32[]{:S(2)}) collective-permute-start(bf16[4,1,32,128]{3,2,1,0:T(8,128)(2,1)S(1)} %slice_select_fusion), channel_id=1, source_target_pairs={{0,2},{2,0},{1,3},{3,1},{4,6},{6,4},{5,7},{7,5},{8,10},{10,8},{9,1... | collective-permute-start | bytes 98312 | tf_op jit(solution)/shard_map/ppermute | solution.py:33
  10.9 8.0 %collective-permute-start.1 = (bf16[1,16,32,128]{3,2,1,0:T(8,128)(2,1)S(1)}, bf16[1,16,32,128]{3,2,1,0:T(8,128)(2,1)S(1)}, u32[]{:S(2)}, u32[]{:S(2)}) collective-permute-start(bf16[1,16,32,128]{3,2,1,0:T(8,128)(2,1)S(1)} %get-tuple-element.12), channel_id=1, source_target_pairs={{0,4},{4,8},{8,12},{1,5},{5,9},{9,13},{2,6},{6,10},{10,14},{3,7},{... | collective-permute-start | bytes 393224 | tf_op jit(solution)/shard_map/ppermute | solution.py:35
  16.4 6.9 %collective-permute-start.4 = (bf16[1,16,32,128]{3,2,1,0:T(8,128)(2,1)S(1)}, bf16[1,16,32,128]{3,2,1,0:T(8,128)(2,1)S(1)}, u32[]{:S(2)}, u32[]{:S(2)}) collective-permute-start(bf16[1,16,32,128]{3,2,1,0:T(8,128)(2,1)S(1)} %get-tuple-element.13), channel_id=1, source_target_pairs={{4,0},{8,4},{12,8},{5,1},{9,5},{13,9},{6,2},{10,6},{14,10},{7,3},{... | collective-permute-start | bytes 393224 | tf_op jit(solution)/shard_map/ppermute | solution.py:36
  25.5 1.0 %copy-start.2 = (bf16[4,16,32,128]{3,2,1,0:T(8,128)(2,1)S(1)}, bf16[4,16,32,128]{3,2,1,0:T(8,128)(2,1)}, u32[]{:S(2)}) copy-start(bf16[4,16,32,128]{3,2,1,0:T(8,128)(2,1)} %param.3) | copy-start | bytes 1572868
  33.1 1.9 %copy-start.1 = (bf16[4,16,32,128]{3,2,1,0:T(8,128)(2,1)S(1)}, bf16[4,16,32,128]{3,2,1,0:T(8,128)(2,1)}, u32[]{:S(2)}) copy-start(bf16[4,16,32,128]{3,2,1,0:T(8,128)(2,1)} %param.4) | copy-start | bytes 1572868
  34.4 11.5 %collective-permute-start.5 = (f32[4,432,64]{1,0,2:T(4,128)S(1)}, f32[4,432,64]{1,0,2:T(4,128)S(1)}, u32[]{:S(2)}, u32[]{:S(2)}) collective-permute-start(f32[4,432,64]{1,0,2:T(4,128)S(1)} %bitcast.186), channel_id=1, source_target_pairs={{0,2},{2,0},{1,3},{3,1},{4,6},{6,4},{5,7},{7,5},{8,10},{10,8},{9,1... | collective-permute-start | bytes 1327112 | tf_op jit(solution)/shard_map/ppermute | solution.py:75
  35.8 0.7 %copy-start.3 = (pred[8,5]{0,1:T(8,128)(4,1)S(1)}, pred[8,5]{0,1:T(8,128)(4,1)}, u32[]{:S(2)}) copy-start(pred[8,5]{0,1:T(8,128)(4,1)} %constant.80) | copy-start | bytes 124
  46.5 7.0 %collective-permute-start.6 = (f32[432,64]{0,1:T(8,128)S(1)}, f32[432,64]{0,1:T(8,128)S(1)}, u32[]{:S(2)}, u32[]{:S(2)}) collective-permute-start(f32[432,64]{0,1:T(8,128)S(1)} %bitcast.187), channel_id=1, source_target_pairs={{0,4},{4,8},{8,12},{12,0},{1,5},{5,9},{9,13},{13,1},{2,6},{6,10},{... | collective-permute-start | bytes 331784 | tf_op jit(solution)/shard_map/ppermute | solution.py:75
  48.1 9.3 %collective-permute-start.7 = (f32[432,64]{0,1:T(8,128)S(1)}, f32[432,64]{0,1:T(8,128)S(1)}, u32[]{:S(2)}, u32[]{:S(2)}) collective-permute-start(f32[432,64]{0,1:T(8,128)S(1)} %bitcast.188), channel_id=1, source_target_pairs={{0,8},{4,12},{8,0},{12,4},{1,9},{5,13},{9,1},{13,5},{2,10},{6,14},... | collective-permute-start | bytes 331784 | tf_op jit(solution)/shard_map/ppermute | solution.py:75
  49.3 8.2 %collective-permute-start.8 = (f32[432,64]{0,1:T(8,128)S(1)}, f32[432,64]{0,1:T(8,128)S(1)}, u32[]{:S(2)}, u32[]{:S(2)}) collective-permute-start(f32[432,64]{0,1:T(8,128)S(1)} %bitcast.189), channel_id=1, source_target_pairs={{0,12},{4,0},{8,4},{12,8},{1,13},{5,1},{9,5},{13,9},{2,14},{6,2},{... | collective-permute-start | bytes 331784 | tf_op jit(solution)/shard_map/ppermute | solution.py:75

commit v6 on v4

--- a/solution.py
+++ b/solution.py
@@ -4,7 +4,8 @@
 from jax.sharding import PartitionSpec as P
 
 
-def with_halo(cells, sides, width):
+def halo_pieces(cells, sides, width):
+    got = []
     for axis, dim in sides:
         count = lax.axis_size(axis)
         head = lax.slice_in_dim(cells, 0, width, axis=dim)
@@ -14,13 +15,25 @@
             high = jnp.zeros_like(head)
         elif count == 2:
             me = lax.axis_index(axis)
-            got = lax.ppermute(jnp.where(me == 0, tail, head), axis, [(0, 1), (1, 0)])
-            low = jnp.where(me == 1, got, jnp.zeros_like(got))
-            high = jnp.where(me == 0, got, jnp.zeros_like(got))
+            recv = lax.ppermute(jnp.where(me == 0, tail, head), axis, [(0, 1), (1, 0)])
+            low = jnp.where(me == 1, recv, jnp.zeros_like(recv))
+            high = jnp.where(me == 0, recv, jnp.zeros_like(recv))
         else:
             low = lax.ppermute(tail, axis, [(i, i + 1) for i in range(count - 1)])
             high = lax.ppermute(head, axis, [(i + 1, i) for i in range(count - 1)])
+        got.append((dim, low, high))
         cells = jnp.concatenate([low, cells, high], axis=dim)
+    return got
+
+
+def assemble(cells, got, channels):
+    cells = lax.slice_in_dim(cells, channels[0], channels[1], axis=3)
+    for dim, low, high in got:
+        cells = jnp.concatenate(
+            [lax.slice_in_dim(low, channels[0], channels[1], axis=3), cells,
+             lax.slice_in_dim(high, channels[0], channels[1], axis=3)],
+            axis=dim,
+        )
     return cells
 
 
@@ -43,7 +56,8 @@
     ncores = lax.axis_size("col")
     half = weight.shape[2] // ncores
     offset = lax.axis_index("col") * half
-    gh = with_halo(grad_out, (("gy", 1), ("gx", 0)), 1)
+    got = halo_pieces(grad_out, (("gy", 1), ("gx", 0)), 1)
+    gh = assemble(grad_out, got, (0, chans))
     taps = weight.reshape(3, 3, 3, chans, weight.shape[2])
     kflip = jnp.transpose(taps[::-1, ::-1, ::-1], (0, 1, 2, 4, 3))
     pad = [(0, 0), (0, 0), (1, 1)]
@@ -53,7 +67,14 @@
         preferred_element_type=jnp.float32,
     )[0]
     grad_in = inner.astype(jnp.bfloat16)
-    gshare = lax.dynamic_slice_in_dim(gh, offset, half, 3)
+    if ncores == 1:
+        gshare = assemble(grad_out, got, (0, half))
+    else:
+        gshare = jnp.where(
+            lax.axis_index("col") == 0,
+            assemble(grad_out, got, (0, half)),
+            assemble(grad_out, got, (half, 2 * half)),
+        )
     gdeep = jnp.pad(gshare, ((0, 0), (0, 0), (1, 1), (0, 0)))
     stack = jnp.concatenate([lax.slice_in_dim(gdeep, 2 - c, 2 - c + depth, axis=2) for c in range(3)], axis=3)
     pieces = []

time: 53 us -> 58 us (1.094)
  local copies, waits for them, and re-layouts: 7.39 us -> 15.8 us
  other arithmetic: 4.95 us -> 3.34 us
  waiting for transfers between devices: 14.5 us -> 12.9 us
    unnamed x22, local copies, waits for them, and re-layouts: 2.13 us -> 7.26 us
    slice x0 -> x4, local copies, waits for them, and re-layouts: none -> 1.74 us  [the longest x1 1.43 us: assemble(): cells = lax.slice_in_dim(cells, channels[0], channels[1], axis=3)]
    ppermute x3, waiting for transfers between devices: 7.56 us -> 5.92 us  [the longest x1 4.27 us: halo_pieces(): high = lax.ppermute(head, axis, [(i + 1, i) for i in range(count - 1)])]
    reshape x1, local copies, waits for them, and re-layouts: 1.37 us -> 2.57 us  [on_device(): weight_terms.reshape(nx, ny, weight_terms.shape[0] // (nx * ny), half)]
    concatenate x1 -> x0, other arithmetic: 1.19 us -> none  [with_halo(): cells = jnp.concatenate([low, cells, high], axis=dim)]
    slice x1, other arithmetic: 1.01 us -> 0.04 us  [halo_pieces(): lax.slice_in_dim(cells, cells.shape[dim] - width, cells.shape[dim], axis=...]
    concatenate x1, local copies, waits for them, and re-layouts: 0.01 us -> 0.65 us  [on_device(): weight_terms = jnp.concatenate(pieces, axis=0)]
    select_n x2 -> x3, other arithmetic: 0.87 us -> 1.43 us  [the longest x1 0.89 us: halo_pieces(): recv = lax.ppermute(jnp.where(me == 0, tail, head), axis, [(0, 1), (1, 0)])]
  transfers between devices with their start and end apart: 7 -> 7, of which waited for: 6 -> 6; matrix products, arithmetic and copies ran while one was open for 13% -> 15% of each run, Pallas kernels for 0% -> 0%
where the time goes in v6:
time: 58 us; the launch traced here: 57.7 us
  local copies, waits for them, and re-layouts  15.8 us (27%)
  starting transfers between devices  15.5 us (27%)
  waiting for transfers between devices  12.9 us (22%)
  matrix products  9.08 us (16%)
  other arithmetic  3.34 us (6%)
  between operations  1.05 us (2%)
    unnamed x22, local copies, waits for them, and re-layouts  7.26 us
    ppermute x4, starting transfers between devices, scatter_sum(): lax.ppermute(part, axis, [(j, (j + shift) % count) for j in range(count)])  7.23 us
    ppermute x4, waiting for transfers between devices, scatter_sum(): lax.ppermute(part, axis, [(j, (j + shift) % count) for j in range(count)])  7 us
    conv_general_dilated x1, matrix products, on_device(): lax.conv_general_dilated(gh[None], kflip, (1, 1, 1), pad, dimension_numbe...  4.94 us
    ppermute x1, waiting for transfers between devices, halo_pieces(): high = lax.ppermute(head, axis, [(i + 1, i) for i in range(count - 1)])  4.27 us
    dot_general x9, matrix products, on_device(): lax.dot_general(x_act, window, (((0, 1, 2), (0, 1, 2)), ((), ())), prefer...  4.14 us
    ppermute x1, starting transfers between devices, halo_pieces(): low = lax.ppermute(tail, axis, [(i, i + 1) for i in range(count - 1)])  4.02 us
    ppermute x1, starting transfers between devices, halo_pieces(): recv = lax.ppermute(jnp.where(me == 0, tail, head), axis, [(0, 1), (1, 0)])  2.94 us
  transfers between devices with their start and end apart: 7, of which 6 were waited for; matrix products, arithmetic and copies ran while one was open for 15% of the time, Pallas kernels for 0%

profile of v6, /device:TPU:0, one launch (start us, length us, event | category | flops | bytes accessed | tf_op | source)
XLA Modules:
  0.0 57.7 jit_solution(3652493328626641874)
XLA Ops:
  0.7 0.9 %slice_select_fusion = bf16[4,1,32,128]{3,2,1,0:T(8,128)(2,1)S(1)} fusion(bf16[4,16,32,128]{3,2,1,0:T(8,128)(2,1)} %param.4, pred[]{:T(512)S(6)} %eq.16), kind=kLoop, calls=%fused_computation.38 | loop fusion | flops 16384 | bytes 98305 | tf_op jit(solution)/shard_map/jit(_where)/select_n | solution.py:18
  1.6 2.9 %collective-permute-start = (bf16[4,1,32,128]{3,2,1,0:T(8,128)(2,1)S(1)}, bf16[4,1,32,128]{3,2,1,0:T(8,128)(2,1)S(1)}, u32[]{:S(2)}, u32[]{:S(2)}) collective-permute-start(bf16[4,1,32,128]{3,2,1,0:T(8,128)(2,1)S(1)} %slice_select_fusion), channel_id=1, source_target_pairs={{0,2},{2,0},{1,3},{3,1},{4,6},{6,4},{5,7},{7,5},{8,10},{10,8},{9,1... | collective-permute-start | bytes 98312 | tf_op jit(solution)/shard_map/ppermute | solution.py:18
  4.5 1.4 %fusion.21 = (bf16[4,16,32,64]{3,2,1,0:T(8,128)(2,1)S(1)}, bf16[4,16,32,64]{3,2,1,0:T(8,128)(2,1)S(1)}) fusion(bf16[4,16,32,128]{3,2,1,0:T(8,128)(2,1)} %param.4), kind=kLoop, calls=%fused_computation.50 | loop fusion | bytes 1048576 | tf_op jit(solution)/shard_map/slice | solution.py:30
  6.0 0.4 collective-permute-done
  6.5 4.0 %collective-permute-start.1 = (bf16[1,18,32,128]{3,2,1,0:T(8,128)(2,1)S(1)}, bf16[1,18,32,128]{3,2,1,0:T(8,128)(2,1)S(1)}, u32[]{:S(2)}, u32[]{:S(2)}) collective-permute-start(bf16[1,18,32,128]{3,2,1,0:T(8,128)(2,1)S(1)} %get-tuple-element.8), channel_id=1, source_target_pairs={{0,4},{4,8},{8,12},{1,5},{5,9},{9,13},{2,6},{6,10},{10,14},{3,7},{... | collective-permute-start | bytes 442376 | tf_op jit(solution)/shard_map/ppermute | solution.py:22
  10.5 1.3 %collective-permute-start.2 = (bf16[1,18,32,128]{3,2,1,0:T(8,128)(2,1)S(1)}, bf16[1,18,32,128]{3,2,1,0:T(8,128)(2,1)S(1)}, u32[]{:S(2)}, u32[]{:S(2)}) collective-permute-start(bf16[1,18,32,128]{3,2,1,0:T(8,128)(2,1)S(1)} %get-tuple-element.9), channel_id=1, source_target_pairs={{4,0},{8,4},{12,8},{5,1},{9,5},{13,9},{6,2},{10,6},{14,10},{7,3},{... | collective-permute-start | bytes 442376 | tf_op jit(solution)/shard_map/ppermute | solution.py:23
  11.9 1.3 %collective-permute-done.1 = bf16[1,18,32,128]{3,2,1,0:T(8,128)(2,1)S(1)} collective-permute-done((bf16[1,18,32,128]{3,2,1,0:T(8,128)(2,1)S(1)}, bf16[1,18,32,128]{3,2,1,0:T(8,128)(2,1)S(1)}, u32[]{:S(2)}, u32[]{:S(2)}) %collective-permute-start.1) | collective-permute-done | bytes 147488 | tf_op jit(solution)/shard_map/ppermute | solution.py:22
  13.2 4.3 %collective-permute-done.2 = bf16[1,18,32,128]{3,2,1,0:T(8,128)(2,1)S(1)} collective-permute-done((bf16[1,18,32,128]{3,2,1,0:T(8,128)(2,1)S(1)}, bf16[1,18,32,128]{3,2,1,0:T(8,128)(2,1)S(1)}, u32[]{:S(2)}, u32[]{:S(2)}) %collective-permute-start.2) | collective-permute-done | bytes 147488 | tf_op jit(solution)/shard_map/ppermute | solution.py:23
  17.6 0.5 maximum_select_fusion
  18.2 0.8 %pad_slice_fusion.1 = (bf16[6,18,32,64]{3,2,1,0:T(8,128)(2,1)S(1)}, bf16[6,18,32,64]{3,2,1,0:T(8,128)(2,1)S(1)}) fusion(bf16[6,18,32,64]{3,2,1,0:T(8,128)(2,1)S(1)} %maximum_select_fusion), kind=kLoop, calls=%fused_computation.12 | loop fusion | bytes 1327104 | tf_op jit(solution)/shard_map/slice | solution.py:79
  18.9 0.9 %pad_maximum_fusion = bf16[6,18,32,192]{3,2,1,0:T(8,128)(2,1)S(1)} fusion(bf16[6,18,32,64]{3,2,1,0:T(8,128)(2,1)S(1)} %get-tuple-element.7, bf16[6,18,32,64]{3,2,1,0:T(8,128)(2,1)S(1)} %maximum_select_fusion, bf16[6,18,32,64]{3,2,1,0:T(8,128)(2,1)S(1)} %get-tuple-element.6), kind=kLoop, calls=%fused_computation.2 | loop fusion | flops 3981312 | bytes 2654208 | tf_op jit(solution)/shard_map/concatenate | solution.py:79
  19.8 0.2 copy-done.2
  20.0 0.5 fusion.26
  20.4 0.5 fusion.27
  20.9 0.5 fusion.28
  21.4 0.5 fusion.29
  21.8 0.5 fusion.30
  22.3 0.5 fusion.31
  22.8 0.5 fusion.32
  23.2 0.5 fusion.33
  23.7 0.5 fusion.34
  24.2 0.7 %bitcast_dynamic-update-slice_fusion.8 = f32[3456,64]{0,1:T(8,128)} fusion(f32[8,8,3,128]{3,2,1,0:T(4,128)S(1)} %bitcast.185), kind=kLoop, calls=%fused_computation.37 | loop fusion | bytes 196608
  25.5 0.7 %bitcast_dynamic-update-slice_fusion.7 = f32[3456,64]{0,1:T(8,128)} fusion(f32[3456,64]{0,1:T(8,128)} %bitcast_dynamic-update-slice_fusion.8, f32[8,8,3,128]{3,2,1,0:T(4,128)S(1)} %bitcast.183), kind=kLoop, calls=%fused_computation.36 | loop fusion | bytes 196608
  26.2 0.6 %bitcast_dynamic-update-slice_fusion.6 = f32[3456,64]{0,1:T(8,128)} fusion(f32[3456,64]{0,1:T(8,128)} %bitcast_dynamic-update-slice_fusion.7, f32[8,8,3,128]{3,2,1,0:T(4,128)S(1)} %bitcast.184), kind=kLoop, calls=%fused_computation.35 | loop fusion | bytes 196608
  26.8 0.6 %bitcast_dynamic-update-slice_fusion.5 = f32[3456,64]{0,1:T(8,128)} fusion(f32[3456,64]{0,1:T(8,128)} %bitcast_dynamic-update-slice_fusion.6, f32[8,8,3,128]{3,2,1,0:T(4,128)S(1)} %bitcast.182), kind=kLoop, calls=%fused_computation.34 | loop fusion | bytes 196608
  27.5 0.6 %bitcast_dynamic-update-slice_fusion.4 = f32[3456,64]{0,1:T(8,128)} fusion(f32[3456,64]{0,1:T(8,128)} %bitcast_dynamic-update-slice_fusion.5, f32[8,8,3,128]{3,2,1,0:T(4,128)S(1)} %bitcast.181), kind=kLoop, calls=%fused_computation.33 | loop fusion | bytes 196608
  28.1 0.6 %bitcast_dynamic-update-slice_fusion.3 = f32[3456,64]{0,1:T(8,128)} fusion(f32[3456,64]{0,1:T(8,128)} %bitcast_dynamic-update-slice_fusion.4, f32[8,8,3,128]{3,2,1,0:T(4,128)S(1)} %bitcast.180), kind=kLoop, calls=%fused_computation.32 | loop fusion | bytes 196608
  28.8 0.7 %bitcast_dynamic-update-slice_fusion.2 = f32[3456,64]{0,1:T(8,128)} fusion(f32[3456,64]{0,1:T(8,128)} %bitcast_dynamic-update-slice_fusion.3, f32[8,8,3,128]{3,2,1,0:T(4,128)S(1)} %bitcast.179), kind=kLoop, calls=%fused_computation.31 | loop fusion | bytes 196608
  29.4 0.7 %bitcast_dynamic-update-slice_fusion.1 = f32[3456,64]{0,1:T(8,128)} fusion(f32[3456,64]{0,1:T(8,128)} %bitcast_dynamic-update-slice_fusion.2, f32[8,8,3,128]{3,2,1,0:T(4,128)S(1)} %bitcast.178), kind=kLoop, calls=%fused_computation.30 | loop fusion | bytes 196608
  30.1 0.6 %bitcast_dynamic-update-slice_fusion = f32[3456,64]{0,1:T(8,128)} fusion(f32[3456,64]{0,1:T(8,128)} %bitcast_dynamic-update-slice_fusion.1, f32[8,8,3,128]{3,2,1,0:T(4,128)S(1)} %bitcast.177), kind=kLoop, calls=%fused_computation.29 | loop fusion | bytes 196608 | tf_op jit(solution)/shard_map/concatenate | solution.py:88
  30.7 2.6 %reshape.84 = f32[4,2,432,64]{2,1,0,3:T(2,128)S(1)} reshape(f32[3456,64]{0,1:T(8,128)} %bitcast_dynamic-update-slice_fusion) | data formatting | bytes 1769472 | tf_op jit(solution)/shard_map/reshape | solution.py:91
  33.3 1.1 %constant_dynamic-slice_fusion.5 = (f32[4,1,432,64]{2,1,0,3:T(1,128)S(1)}, f32[4,1,432,64]{2,1,0,3:T(1,128)S(1)}) fusion(f32[4,2,432,64]{2,1,0,3:T(2,128)S(1)} %reshape.84, s32[]{:T(128)S(6)} %select_n.72, s32[]{:T(128)S(6)} %select_n.74), kind=kLoop, calls=%fused_computation.46 | loop fusion | bytes 1769480 | tf_op jit(solution)/shard_map/jit(dynamic_index_in_dim)/dynamic_slice | solution.py:47
  34.5 1.6 %collective-permute-start.3 = (f32[4,432,64]{1,0,2:T(4,128)S(1)}, f32[4,432,64]{1,0,2:T(4,128)S(1)}, u32[]{:S(2)}, u32[]{:S(2)}) collective-permute-start(f32[4,432,64]{1,0,2:T(4,128)S(1)} %bitcast.186), channel_id=1, source_target_pairs={{0,2},{2,0},{1,3},{3,1},{4,6},{6,4},{5,7},{7,5},{8,10},{10,8},{9,1... | collective-permute-start | bytes 1327112 | tf_op jit(solution)/shard_map/ppermute | solution.py:50
  36.1 0.2 maximum_bitcast_fusion
  36.2 0.4 copy.34
  36.6 0.2 pad.5.clone
  37.2 0.4 copy-done.3
  37.6 4.9 %fusion.11 = bf16[4,16,8,5,128]{4,2,3,1,0:T(8,128)(2,1)S(1)} fusion(bf16[3,3,3,128,128]{4,3,2,1,0:T(8,128)(2,1)S(1)} %bitcast.174, bf16[6,18,1,7,2,128]{5,3,4,1,0,2:T(8,128)(2,1)S(1)} %slice.103, bf16[6,18,1,8,5,128]{5,3,4,1,0,2:T(8,128)(2,1)S(1)} %copy.7, pred[8,5]{0,1:T(8,128)(4,1)S(1)} %copy-done.3), kind=kOutput, calls=%fused_computation.10 | convolution fusion | flops 2270224384 | bytes 3033128 | tf_op jit(solution)/shard_map/conv_general_dilated | solution.py:64
  42.6 3.1 %collective-permute-done.3 = f32[4,432,64]{1,0,2:T(4,128)S(1)} collective-permute-done((f32[4,432,64]{1,0,2:T(4,128)S(1)}, f32[4,432,64]{1,0,2:T(4,128)S(1)}, u32[]{:S(2)}, u32[]{:S(2)}) %collective-permute-start.3) | collective-permute-done | bytes 442400 | tf_op jit(solution)/shard_map/ppermute | solution.py:50
  45.7 0.2 bitcast_add_fusion
  45.9 0.5 constant_dynamic-slice_fusion.3
  46.3 1.6 %collective-permute-start.4 = (f32[432,64]{0,1:T(8,128)S(1)}, f32[432,64]{0,1:T(8,128)S(1)}, u32[]{:S(2)}, u32[]{:S(2)}) collective-permute-start(f32[432,64]{0,1:T(8,128)S(1)} %bitcast.187), channel_id=1, source_target_pairs={{0,4},{4,8},{8,12},{12,0},{1,5},{5,9},{9,13},{13,1},{2,6},{6,10},{... | collective-permute-start | bytes 331784 | tf_op jit(solution)/shard_map/ppermute | solution.py:50
  48.0 1.1 %collective-permute-start.5 = (f32[432,64]{0,1:T(8,128)S(1)}, f32[432,64]{0,1:T(8,128)S(1)}, u32[]{:S(2)}, u32[]{:S(2)}) collective-permute-start(f32[432,64]{0,1:T(8,128)S(1)} %bitcast.188), channel_id=1, source_target_pairs={{0,8},{4,12},{8,0},{12,4},{1,9},{5,13},{9,1},{13,5},{2,10},{6,14},... | collective-permute-start | bytes 331784 | tf_op jit(solution)/shard_map/ppermute | solution.py:50
  49.1 3.0 %collective-permute-start.6 = (f32[432,64]{0,1:T(8,128)S(1)}, f32[432,64]{0,1:T(8,128)S(1)}, u32[]{:S(2)}, u32[]{:S(2)}) collective-permute-start(f32[432,64]{0,1:T(8,128)S(1)} %bitcast.189), channel_id=1, source_target_pairs={{0,12},{4,0},{8,4},{12,8},{1,13},{5,1},{9,5},{13,9},{2,14},{6,2},{... | collective-permute-start | bytes 331784 | tf_op jit(solution)/shard_map/ppermute | solution.py:50
  52.1 0.9 %copy.18 = bf16[4,16,32,128]{3,2,1,0:T(8,128)(2,1)} copy(bf16[4,16,32,128]{3,1,2,0:T(8,128)(2,1)S(1)} %slice_bitcast_fusion) | data formatting | bytes 1048576
  53.0 0.3 collective-permute-done.4
  53.3 3.6 %collective-permute-done.5 = f32[432,64]{0,1:T(8,128)S(1)} collective-permute-done((f32[432,64]{0,1:T(8,128)S(1)}, f32[432,64]{0,1:T(8,128)S(1)}, u32[]{:S(2)}, u32[]{:S(2)}) %collective-permute-start.5) | collective-permute-done | bytes 110624 | tf_op jit(solution)/shard_map/ppermute | solution.py:50
  57.0 0.7 %fusion.17 = f32[432,64]{0,1:T(8,128)} fusion(f32[432,64]{0,1:T(8,128)S(1)} %collective-permute-done.6, f32[432,64]{0,1:T(8,128)S(1)} %collective-permute-done.5, f32[432,64]{0,1:T(8,128)S(1)} %collective-permute-done.4, f32[1,432,64]{1,0,2:T(1,128)S(1)} %get-tuple-element.10), kind=kLoop, calls=%fused_computation.28 | loop fusion | flops 110592 | bytes 552960 | tf_op jit(solution)/shard_map/div | solution.py:94
  (29 shorter events, 1.6 us)
Async XLA Ops:
  0.6 36.5 %copy-start = (bf16[27,128,128]{2,1,0:T(8,128)(2,1)S(1)}, bf16[27,128,128]{2,1,0:T(8,128)(2,1)}, u32[]{:S(2)}) copy-start(bf16[27,128,128]{2,1,0:T(8,128)(2,1)} %param.5) | copy-start | bytes 2654212
  0.6 5.8 %copy-start.1 = (bf16[4,16,32,128]{3,2,1,0:T(8,128)(2,1)S(1)}, bf16[4,16,32,128]{3,2,1,0:T(8,128)(2,1)}, u32[]{:S(2)}) copy-start(bf16[4,16,32,128]{3,2,1,0:T(8,128)(2,1)} %param.4) | copy-start | bytes 1572868
  1.6 4.8 %collective-permute-start = (bf16[4,1,32,128]{3,2,1,0:T(8,128)(2,1)S(1)}, bf16[4,1,32,128]{3,2,1,0:T(8,128)(2,1)S(1)}, u32[]{:S(2)}, u32[]{:S(2)}) collective-permute-start(bf16[4,1,32,128]{3,2,1,0:T(8,128)(2,1)S(1)} %slice_select_fusion), channel_id=1, source_target_pairs={{0,2},{2,0},{1,3},{3,1},{4,6},{6,4},{5,7},{7,5},{8,10},{10,8},{9,1... | collective-permute-start | bytes 98312 | tf_op jit(solution)/shard_map/ppermute | solution.py:18
  6.5 6.7 %collective-permute-start.1 = (bf16[1,18,32,128]{3,2,1,0:T(8,128)(2,1)S(1)}, bf16[1,18,32,128]{3,2,1,0:T(8,128)(2,1)S(1)}, u32[]{:S(2)}, u32[]{:S(2)}) collective-permute-start(bf16[1,18,32,128]{3,2,1,0:T(8,128)(2,1)S(1)} %get-tuple-element.8), channel_id=1, source_target_pairs={{0,4},{4,8},{8,12},{1,5},{5,9},{9,13},{2,6},{6,10},{10,14},{3,7},{... | collective-permute-start | bytes 442376 | tf_op jit(solution)/shard_map/ppermute | solution.py:22
  10.5 7.0 %collective-permute-start.2 = (bf16[1,18,32,128]{3,2,1,0:T(8,128)(2,1)S(1)}, bf16[1,18,32,128]{3,2,1,0:T(8,128)(2,1)S(1)}, u32[]{:S(2)}, u32[]{:S(2)}) collective-permute-start(bf16[1,18,32,128]{3,2,1,0:T(8,128)(2,1)S(1)} %get-tuple-element.9), channel_id=1, source_target_pairs={{4,0},{8,4},{12,8},{5,1},{9,5},{13,9},{6,2},{10,6},{14,10},{7,3},{... | collective-permute-start | bytes 442376 | tf_op jit(solution)/shard_map/ppermute | solution.py:23
  18.9 1.0 %copy-start.2 = (bf16[4,16,32,128]{3,2,1,0:T(8,128)(2,1)S(1)}, bf16[4,16,32,128]{3,2,1,0:T(8,128)(2,1)}, u32[]{:S(2)}) copy-start(bf16[4,16,32,128]{3,2,1,0:T(8,128)(2,1)} %param.3) | copy-start | bytes 1572868
  34.5 11.2 %collective-permute-start.3 = (f32[4,432,64]{1,0,2:T(4,128)S(1)}, f32[4,432,64]{1,0,2:T(4,128)S(1)}, u32[]{:S(2)}, u32[]{:S(2)}) collective-permute-start(f32[4,432,64]{1,0,2:T(4,128)S(1)} %bitcast.186), channel_id=1, source_target_pairs={{0,2},{2,0},{1,3},{3,1},{4,6},{6,4},{5,7},{7,5},{8,10},{10,8},{9,1... | collective-permute-start | bytes 1327112 | tf_op jit(solution)/shard_map/ppermute | solution.py:50
  36.9 0.7 %copy-start.3 = (pred[8,5]{0,1:T(8,128)(4,1)S(1)}, pred[8,5]{0,1:T(8,128)(4,1)}, u32[]{:S(2)}) copy-start(pred[8,5]{0,1:T(8,128)(4,1)} %constant.75) | copy-start | bytes 124
  46.3 7.0 %collective-permute-start.4 = (f32[432,64]{0,1:T(8,128)S(1)}, f32[432,64]{0,1:T(8,128)S(1)}, u32[]{:S(2)}, u32[]{:S(2)}) collective-permute-start(f32[432,64]{0,1:T(8,128)S(1)} %bitcast.187), channel_id=1, source_target_pairs={{0,4},{4,8},{8,12},{12,0},{1,5},{5,9},{9,13},{13,1},{2,6},{6,10},{... | collective-permute-start | bytes 331784 | tf_op jit(solution)/shard_map/ppermute | solution.py:50
  48.0 9.0 %collective-permute-start.5 = (f32[432,64]{0,1:T(8,128)S(1)}, f32[432,64]{0,1:T(8,128)S(1)}, u32[]{:S(2)}, u32[]{:S(2)}) collective-permute-start(f32[432,64]{0,1:T(8,128)S(1)} %bitcast.188), channel_id=1, source_target_pairs={{0,8},{4,12},{8,0},{12,4},{1,9},{5,13},{9,1},{13,5},{2,10},{6,14},... | collective-permute-start | bytes 331784 | tf_op jit(solution)/shard_map/ppermute | solution.py:50
  49.1 7.9 %collective-permute-start.6 = (f32[432,64]{0,1:T(8,128)S(1)}, f32[432,64]{0,1:T(8,128)S(1)}, u32[]{:S(2)}, u32[]{:S(2)}) collective-permute-start(f32[432,64]{0,1:T(8,128)S(1)} %bitcast.189), channel_id=1, source_target_pairs={{0,12},{4,0},{8,4},{12,8},{1,13},{5,1},{9,5},{13,9},{2,14},{6,2},{... | collective-permute-start | bytes 331784 | tf_op jit(solution)/shard_map/ppermute | solution.py:50

commit v7 on v6

--- a/solution.py
+++ b/solution.py
@@ -1,6 +1,7 @@
 import jax
 import jax.numpy as jnp
 from jax import lax
+from jax.experimental.layout import Layout, with_layout_constraint
 from jax.sharding import PartitionSpec as P
 
 
@@ -85,11 +86,14 @@
                 x_act, window, (((0, 1, 2), (0, 1, 2)), ((), ())), preferred_element_type=jnp.float32
             )
             pieces.append(jnp.transpose(term.reshape(chans, 3, half), (1, 0, 2)).reshape(3 * chans, half))
-    weight_terms = jnp.concatenate(pieces, axis=0)
+    weight_terms = with_layout_constraint(jnp.concatenate(pieces, axis=0), Layout(major_to_minor=(0, 1)))
     nx = lax.axis_size("gx")
     ny = lax.axis_size("gy")
     blocks = weight_terms.reshape(nx, ny, weight_terms.shape[0] // (nx * ny), half)
-    owned = scatter_sum(scatter_sum(blocks, "gy", 1), "gx", 0)
+    rows_major = Layout(major_to_minor=(0, 1, 2, 3))
+    blocks = with_layout_constraint(blocks, rows_major)
+    partial = with_layout_constraint(scatter_sum(blocks, "gy", 1), Layout(major_to_minor=(0, 1, 2)))
+    owned = with_layout_constraint(scatter_sum(partial, "gx", 0), Layout(major_to_minor=(0, 1)))
     total_cells = size_x * lax.axis_size("gx") * size_y * lax.axis_size("gy") * depth
     grad_weight = owned / jnp.sqrt(jnp.float32(total_cells))
     return (grad_in, grad_weight)

time: 58 us -> 70.7 us (1.22)
  the two profiles are of different devices: /device:TPU:0 before, /device:TPU:13 now
where the time goes in v7:
time: 70.7 us; the launch traced here: 70.2 us
  waiting for transfers between devices  24.9 us (35%)
  local copies, waits for them, and re-layouts  21.1 us (30%)
  starting transfers between devices  10.3 us (15%)
  matrix products  10.3 us (15%)
  other arithmetic  2.63 us (4%)
  between operations  1.03 us (1%)
    ppermute x4, waiting for transfers between devices, scatter_sum(): lax.ppermute(part, axis, [(j, (j + shift) % count) for j in range(count)])  21.2 us
    unnamed x21, local copies, waits for them, and re-layouts  7.04 us
    conv_general_dilated x1, matrix products, on_device(): lax.conv_general_dilated(gh[None], kflip, (1, 1, 1), pad, dimension_numbe...  6.12 us
    reshape x9, local copies, waits for them, and re-layouts, on_device(): term.reshape(chans, 3, half)  4.62 us
    dot_general x9, matrix products, on_device(): lax.dot_general(x_act, window, (((0, 1, 2), (0, 1, 2)), ((), ())), prefer...  4.14 us
    ppermute x4, starting transfers between devices, scatter_sum(): lax.ppermute(part, axis, [(j, (j + shift) % count) for j in range(count)])  3.76 us
    ppermute x1, waiting for transfers between devices, halo_pieces(): high = lax.ppermute(head, axis, [(i + 1, i) for i in range(count - 1)])  3.7 us
    ppermute x1, starting transfers between devices, halo_pieces(): low = lax.ppermute(tail, axis, [(i, i + 1) for i in range(count - 1)])  3.2 us
  transfers between devices with their start and end apart: 7, of which 5 were waited for; matrix products, arithmetic and copies ran while one was open for 14% of the time, Pallas kernels for 0%

profile of v7, /device:TPU:13, one launch (start us, length us, event | category | flops | bytes accessed | tf_op | source)
XLA Modules:
  0.0 70.2 jit_solution(1265754557045532049)
XLA Ops:
  0.7 0.9 %slice_select_fusion = bf16[4,1,32,128]{3,2,1,0:T(8,128)(2,1)S(1)} fusion(bf16[4,16,32,128]{3,2,1,0:T(8,128)(2,1)} %param.4, pred[]{:T(512)S(6)} %eq.16), kind=kLoop, calls=%fused_computation.28 | loop fusion | flops 16384 | bytes 98305 | tf_op jit(solution)/shard_map/jit(_where)/select_n | solution.py:19
  1.6 1.2 %collective-permute-start = (bf16[4,1,32,128]{3,2,1,0:T(8,128)(2,1)S(1)}, bf16[4,1,32,128]{3,2,1,0:T(8,128)(2,1)S(1)}, u32[]{:S(2)}, u32[]{:S(2)}) collective-permute-start(bf16[4,1,32,128]{3,2,1,0:T(8,128)(2,1)S(1)} %slice_select_fusion), channel_id=1, source_target_pairs={{0,2},{2,0},{1,3},{3,1},{4,6},{6,4},{5,7},{7,5},{8,10},{10,8},{9,1... | collective-permute-start | bytes 98312 | tf_op jit(solution)/shard_map/ppermute | solution.py:19
  2.8 1.5 %fusion.21 = (bf16[4,16,32,64]{3,2,1,0:T(8,128)(2,1)S(1)}, bf16[4,16,32,64]{3,2,1,0:T(8,128)(2,1)S(1)}) fusion(bf16[4,16,32,128]{3,2,1,0:T(8,128)(2,1)} %param.4), kind=kLoop, calls=%fused_computation.44 | loop fusion | bytes 1048576 | tf_op jit(solution)/shard_map/slice | solution.py:31
  4.5 3.2 %collective-permute-start.1 = (bf16[1,18,32,128]{3,2,1,0:T(8,128)(2,1)S(1)}, bf16[1,18,32,128]{3,2,1,0:T(8,128)(2,1)S(1)}, u32[]{:S(2)}, u32[]{:S(2)}) collective-permute-start(bf16[1,18,32,128]{3,2,1,0:T(8,128)(2,1)S(1)} %get-tuple-element.15), channel_id=1, source_target_pairs={{0,4},{4,8},{8,12},{1,5},{5,9},{9,13},{2,6},{6,10},{10,14},{3,7},{... | collective-permute-start | bytes 442376 | tf_op jit(solution)/shard_map/ppermute | solution.py:23
  7.7 2.1 %collective-permute-start.2 = (bf16[1,18,32,128]{3,2,1,0:T(8,128)(2,1)S(1)}, bf16[1,18,32,128]{3,2,1,0:T(8,128)(2,1)S(1)}, u32[]{:S(2)}, u32[]{:S(2)}) collective-permute-start(bf16[1,18,32,128]{3,2,1,0:T(8,128)(2,1)S(1)} %get-tuple-element.16), channel_id=1, source_target_pairs={{4,0},{8,4},{12,8},{5,1},{9,5},{13,9},{6,2},{10,6},{14,10},{7,3},{... | collective-permute-start | bytes 442376 | tf_op jit(solution)/shard_map/ppermute | solution.py:24
  9.9 3.7 %collective-permute-done.2 = bf16[1,18,32,128]{3,2,1,0:T(8,128)(2,1)S(1)} collective-permute-done((bf16[1,18,32,128]{3,2,1,0:T(8,128)(2,1)S(1)}, bf16[1,18,32,128]{3,2,1,0:T(8,128)(2,1)S(1)}, u32[]{:S(2)}, u32[]{:S(2)}) %collective-permute-start.2) | collective-permute-done | bytes 147488 | tf_op jit(solution)/shard_map/ppermute | solution.py:24
  13.8 0.5 maximum_select_fusion
  14.3 0.8 %pad_slice_fusion.1 = (bf16[6,18,32,64]{3,2,1,0:T(8,128)(2,1)S(1)}, bf16[6,18,32,64]{3,2,1,0:T(8,128)(2,1)S(1)}) fusion(bf16[6,18,32,64]{3,2,1,0:T(8,128)(2,1)S(1)} %maximum_select_fusion), kind=kLoop, calls=%fused_computation.12 | loop fusion | bytes 1327104 | tf_op jit(solution)/shard_map/slice | solution.py:80
  15.1 0.9 %pad_maximum_fusion = bf16[6,18,32,192]{3,2,1,0:T(8,128)(2,1)S(1)} fusion(bf16[6,18,32,64]{3,2,1,0:T(8,128)(2,1)S(1)} %get-tuple-element.14, bf16[6,18,32,64]{3,2,1,0:T(8,128)(2,1)S(1)} %maximum_select_fusion, bf16[6,18,32,64]{3,2,1,0:T(8,128)(2,1)S(1)} %get-tuple-element.13), kind=kLoop, calls=%fused_computation.2 | loop fusion | flops 3981312 | bytes 2654208 | tf_op jit(solution)/shard_map/concatenate | solution.py:80
  16.0 0.2 copy-done.3
  16.1 0.5 fusion.34
  16.6 0.5 fusion.33
  17.1 0.5 fusion.32
  17.5 0.5 fusion.31
  18.0 0.5 fusion.30
  18.5 0.5 fusion.29
  18.9 0.5 fusion.28
  19.4 0.5 fusion.27
  19.9 0.5 fusion.26
  20.3 0.2 maximum_bitcast_fusion
  20.5 0.4 copy.72
  20.9 0.2 pad.5.clone
  21.1 1.2 %copy.48 = bf16[6,18,1,8,5,128]{5,3,4,1,0,2:T(8,128)(2,1)} copy(bf16[6,18,1,8,5,128]{5,1,4,3,0,2:T(8,128)(2,1)S(1)} %bitcast.142) | data formatting | bytes 2211840 | tf_op jit(solution)/shard_map/conv_general_dilated | solution.py:65
  22.3 1.9 %slice.103 = bf16[6,18,1,7,2,128]{5,3,4,1,0,2:T(8,128)(2,1)} slice(bf16[6,18,1,8,5,128]{5,3,4,1,0,2:T(8,128)(2,1)} %copy.48), slice={[0:6], [0:18], [0:1], [1:8], [0:2], [0:128]} | slice | bytes 774144 | tf_op jit(solution)/shard_map/conv_general_dilated | solution.py:65
  24.8 0.8 %copy.54 = f32[128,3,64]{2,0,1:T(8,128)} copy(f32[128,3,64]{0,2,1:T(8,128)S(1)} %bitcast.160) | data formatting | bytes 196608 | tf_op jit(solution)/shard_map/reshape | solution.py:88
  25.6 0.8 %copy.53 = f32[128,3,64]{2,0,1:T(8,128)} copy(f32[128,3,64]{0,2,1:T(8,128)S(1)} %bitcast.159) | data formatting | bytes 196608 | tf_op jit(solution)/shard_map/reshape | solution.py:88
  26.4 0.8 %copy.52 = f32[128,3,64]{2,0,1:T(8,128)} copy(f32[128,3,64]{0,2,1:T(8,128)S(1)} %bitcast.158) | data formatting | bytes 196608 | tf_op jit(solution)/shard_map/reshape | solution.py:88
  27.2 0.8 %copy.51 = f32[128,3,64]{2,0,1:T(8,128)} copy(f32[128,3,64]{0,2,1:T(8,128)S(1)} %bitcast.157) | data formatting | bytes 196608 | tf_op jit(solution)/shard_map/reshape | solution.py:88
  28.0 0.8 %copy.50 = f32[128,3,64]{2,0,1:T(8,128)} copy(f32[128,3,64]{0,2,1:T(8,128)S(1)} %bitcast.156) | data formatting | bytes 196608 | tf_op jit(solution)/shard_map/reshape | solution.py:88
  28.8 0.9 %constant_dynamic-update-slice_fusion.8 = f32[3456,64]{1,0:T(8,128)S(1)} fusion(f32[384,64]{1,0:T(8,128)} %bitcast.154), kind=kLoop, calls=%fused_computation.39 | loop fusion | bytes 294912
  29.8 0.9 %constant_dynamic-update-slice_fusion.7 = f32[3456,64]{1,0:T(8,128)S(1)} fusion(f32[3456,64]{1,0:T(8,128)S(1)} %constant_dynamic-update-slice_fusion.8, f32[384,64]{1,0:T(8,128)} %bitcast.153), kind=kLoop, calls=%fused_computation.38 | loop fusion | bytes 294912
  30.7 0.9 %constant_dynamic-update-slice_fusion.6 = f32[3456,64]{1,0:T(8,128)S(1)} fusion(f32[3456,64]{1,0:T(8,128)S(1)} %constant_dynamic-update-slice_fusion.7, f32[384,64]{1,0:T(8,128)} %bitcast.152), kind=kLoop, calls=%fused_computation.37 | loop fusion | bytes 294912
  31.7 0.9 %constant_dynamic-update-slice_fusion.5 = f32[3456,64]{1,0:T(8,128)S(1)} fusion(f32[3456,64]{1,0:T(8,128)S(1)} %constant_dynamic-update-slice_fusion.6, f32[384,64]{1,0:T(8,128)} %bitcast.151), kind=kLoop, calls=%fused_computation.36 | loop fusion | bytes 294912
  32.6 0.9 %constant_dynamic-update-slice_fusion.4 = f32[3456,64]{1,0:T(8,128)S(1)} fusion(f32[3456,64]{1,0:T(8,128)S(1)} %constant_dynamic-update-slice_fusion.5, f32[384,64]{1,0:T(8,128)} %bitcast.150), kind=kLoop, calls=%fused_computation.35 | loop fusion | bytes 294912
  33.7 1.1 %copy.59 = f32[4,1,432,64]{2,3,1,0:T(8,128)} copy(f32[4,1,432,64]{3,2,1,0:T(8,128)S(1)} %constant_dynamic-slice_fusion) | data formatting | bytes 884736 | tf_op jit(solution)/shard_map/jit(dynamic_index_in_dim)/dynamic_slice | solution.py:50
  34.9 1.1 %collective-permute-start.3 = (f32[4,432,64]{1,2,0:T(8,128)}, f32[4,432,64]{1,2,0:T(8,128)}, u32[]{:S(2)}, u32[]{:S(2)}) collective-permute-start(f32[4,432,64]{1,2,0:T(8,128)} %bitcast.155), channel_id=1, source_target_pairs={{0,2},{2,0},{1,3},{3,1},{4,6},{6,4},{5,7},{7,5},{8,10},{10,8},{9,1... | collective-permute-start | bytes 1327112 | tf_op jit(solution)/shard_map/ppermute | solution.py:51
  36.0 6.1 %fusion.11 = bf16[4,16,8,5,128]{4,2,3,1,0:T(8,128)(2,1)S(1)} fusion(bf16[3,3,3,128,128]{4,3,2,1,0:T(8,128)(2,1)S(1)} %bitcast.141, bf16[6,18,1,7,2,128]{5,3,4,1,0,2:T(8,128)(2,1)} %slice.103, bf16[6,18,1,8,5,128]{5,3,4,1,0,2:T(8,128)(2,1)} %copy.48, pred[8,5]{0,1:T(8,128)(4,1)S(1)} %copy-done.4), kind=kOutput, calls=%fused_computation.10 | convolution fusion | flops 2270224384 | bytes 3033128 | tf_op jit(solution)/shard_map/conv_general_dilated | solution.py:65
  42.1 0.9 %copy.49 = bf16[4,16,8,5,128]{4,1,3,2,0:T(8,128)(2,1)} copy(bf16[4,16,8,5,128]{4,2,3,1,0:T(8,128)(2,1)S(1)} %fusion.11) | data formatting | bytes 1310720 | tf_op jit(solution)/shard_map/convert_element_type | solution.py:70
  43.1 2.3 %collective-permute-done.3 = f32[4,432,64]{1,2,0:T(8,128)} collective-permute-done((f32[4,432,64]{1,2,0:T(8,128)}, f32[4,432,64]{1,2,0:T(8,128)}, u32[]{:S(2)}, u32[]{:S(2)}) %collective-permute-start.3) | collective-permute-done | bytes 442400 | tf_op jit(solution)/shard_map/ppermute | solution.py:51
  45.4 1.3 %copy.60 = f32[4,432,64]{2,1,0:T(8,128)S(1)} copy(f32[4,432,64]{1,2,0:T(8,128)} %collective-permute-done.3) | data formatting | bytes 884736 | tf_op jit(solution)/shard_map/ppermute | solution.py:51
  46.9 1.4 %collective-permute-start.4 = (f32[432,64]{1,0:T(8,128)S(1)}, f32[432,64]{1,0:T(8,128)S(1)}, u32[]{:S(2)}, u32[]{:S(2)}) collective-permute-start(f32[432,64]{1,0:T(8,128)S(1)} %get-tuple-element.10), channel_id=1, source_target_pairs={{0,4},{4,8},{8,12},{12,0},{1,5},{5,9},{9,13},{13,1},{2,6},{6,10},{... | collective-permute-start | bytes 331784 | tf_op jit(solution)/shard_map/ppermute | solution.py:51
  48.3 1.0 %collective-permute-start.5 = (f32[432,64]{1,0:T(8,128)S(1)}, f32[432,64]{1,0:T(8,128)S(1)}, u32[]{:S(2)}, u32[]{:S(2)}) collective-permute-start(f32[432,64]{1,0:T(8,128)S(1)} %get-tuple-element.11), channel_id=1, source_target_pairs={{0,8},{4,12},{8,0},{12,4},{1,9},{5,13},{9,1},{13,5},{2,10},{6,14},... | collective-permute-start | bytes 331784 | tf_op jit(solution)/shard_map/ppermute | solution.py:51
  49.2 0.3 collective-permute-start.6
  49.6 0.9 %copy.61 = bf16[4,16,32,128]{3,2,1,0:T(8,128)(2,1)} copy(bf16[4,16,32,128]{3,1,2,0:T(8,128)(2,1)S(1)} %slice_bitcast_fusion) | data formatting | bytes 1048576
  50.5 1.2 %collective-permute-done.4 = f32[432,64]{1,0:T(8,128)S(1)} collective-permute-done((f32[432,64]{1,0:T(8,128)S(1)}, f32[432,64]{1,0:T(8,128)S(1)}, u32[]{:S(2)}, u32[]{:S(2)}) %collective-permute-start.4) | collective-permute-done | bytes 110624 | tf_op jit(solution)/shard_map/ppermute | solution.py:51
  51.8 13.6 %collective-permute-done.5 = f32[432,64]{1,0:T(8,128)S(1)} collective-permute-done((f32[432,64]{1,0:T(8,128)S(1)}, f32[432,64]{1,0:T(8,128)S(1)}, u32[]{:S(2)}, u32[]{:S(2)}) %collective-permute-start.5) | collective-permute-done | bytes 110624 | tf_op jit(solution)/shard_map/ppermute | solution.py:51
  65.3 4.0 %collective-permute-done.6 = f32[432,64]{1,0:T(8,128)S(1)} collective-permute-done((f32[432,64]{1,0:T(8,128)S(1)}, f32[432,64]{1,0:T(8,128)S(1)}, u32[]{:S(2)}, u32[]{:S(2)}) %collective-permute-start.6) | collective-permute-done | bytes 110624 | tf_op jit(solution)/shard_map/ppermute | solution.py:51
  69.4 0.8 %copy.62 = f32[432,64]{0,1:T(8,128)} copy(f32[432,64]{1,0:T(8,128)S(1)} %fusion.17) | data formatting | bytes 221184
  (29 shorter events, 1.3 us)
Async XLA Ops:
  0.6 35.4 %copy-start = (bf16[27,128,128]{2,1,0:T(8,128)(2,1)S(1)}, bf16[27,128,128]{2,1,0:T(8,128)(2,1)}, u32[]{:S(2)}) copy-start(bf16[27,128,128]{2,1,0:T(8,128)(2,1)} %param.5) | copy-start | bytes 2654212
  0.6 3.8 %copy-start.1 = (bf16[4,16,32,128]{3,2,1,0:T(8,128)(2,1)S(1)}, bf16[4,16,32,128]{3,2,1,0:T(8,128)(2,1)}, u32[]{:S(2)}) copy-start(bf16[4,16,32,128]{3,2,1,0:T(8,128)(2,1)} %param.4) | copy-start | bytes 1572868
  1.6 2.8 %collective-permute-start = (bf16[4,1,32,128]{3,2,1,0:T(8,128)(2,1)S(1)}, bf16[4,1,32,128]{3,2,1,0:T(8,128)(2,1)S(1)}, u32[]{:S(2)}, u32[]{:S(2)}) collective-permute-start(bf16[4,1,32,128]{3,2,1,0:T(8,128)(2,1)S(1)} %slice_select_fusion), channel_id=1, source_target_pairs={{0,2},{2,0},{1,3},{3,1},{4,6},{6,4},{5,7},{7,5},{8,10},{10,8},{9,1... | collective-permute-start | bytes 98312 | tf_op jit(solution)/shard_map/ppermute | solution.py:19
  4.5 9.2 %collective-permute-start.1 = (bf16[1,18,32,128]{3,2,1,0:T(8,128)(2,1)S(1)}, bf16[1,18,32,128]{3,2,1,0:T(8,128)(2,1)S(1)}, u32[]{:S(2)}, u32[]{:S(2)}) collective-permute-start(bf16[1,18,32,128]{3,2,1,0:T(8,128)(2,1)S(1)} %get-tuple-element.15), channel_id=1, source_target_pairs={{0,4},{4,8},{8,12},{1,5},{5,9},{9,13},{2,6},{6,10},{10,14},{3,7},{... | collective-permute-start | bytes 442376 | tf_op jit(solution)/shard_map/ppermute | solution.py:23
  7.7 5.9 %collective-permute-start.2 = (bf16[1,18,32,128]{3,2,1,0:T(8,128)(2,1)S(1)}, bf16[1,18,32,128]{3,2,1,0:T(8,128)(2,1)S(1)}, u32[]{:S(2)}, u32[]{:S(2)}) collective-permute-start(bf16[1,18,32,128]{3,2,1,0:T(8,128)(2,1)S(1)} %get-tuple-element.16), channel_id=1, source_target_pairs={{4,0},{8,4},{12,8},{5,1},{9,5},{13,9},{6,2},{10,6},{14,10},{7,3},{... | collective-permute-start | bytes 442376 | tf_op jit(solution)/shard_map/ppermute | solution.py:24
  15.1 1.0 %copy-start.3 = (bf16[4,16,32,128]{3,2,1,0:T(8,128)(2,1)S(1)}, bf16[4,16,32,128]{3,2,1,0:T(8,128)(2,1)}, u32[]{:S(2)}) copy-start(bf16[4,16,32,128]{3,2,1,0:T(8,128)(2,1)} %param.3) | copy-start | bytes 1572868
  33.6 2.4 %copy-start.4 = (pred[8,5]{0,1:T(8,128)(4,1)S(1)}, pred[8,5]{0,1:T(8,128)(4,1)}, u32[]{:S(2)}) copy-start(pred[8,5]{0,1:T(8,128)(4,1)} %constant.75) | copy-start | bytes 124
  34.9 10.5 %collective-permute-start.3 = (f32[4,432,64]{1,2,0:T(8,128)}, f32[4,432,64]{1,2,0:T(8,128)}, u32[]{:S(2)}, u32[]{:S(2)}) collective-permute-start(f32[4,432,64]{1,2,0:T(8,128)} %bitcast.155), channel_id=1, source_target_pairs={{0,2},{2,0},{1,3},{3,1},{4,6},{6,4},{5,7},{7,5},{8,10},{10,8},{9,1... | collective-permute-start | bytes 1327112 | tf_op jit(solution)/shard_map/ppermute | solution.py:51
  46.8 2.8 %copy-start.2 = (bf16[4,16,8,5,128]{4,1,3,2,0:T(8,128)(2,1)S(1)}, bf16[4,16,8,5,128]{4,1,3,2,0:T(8,128)(2,1)}, u32[]{:S(2)}) copy-start(bf16[4,16,8,5,128]{4,1,3,2,0:T(8,128)(2,1)} %copy.49) | copy-start | bytes 1966084
  46.9 4.8 %collective-permute-start.4 = (f32[432,64]{1,0:T(8,128)S(1)}, f32[432,64]{1,0:T(8,128)S(1)}, u32[]{:S(2)}, u32[]{:S(2)}) collective-permute-start(f32[432,64]{1,0:T(8,128)S(1)} %get-tuple-element.10), channel_id=1, source_target_pairs={{0,4},{4,8},{8,12},{12,0},{1,5},{5,9},{9,13},{13,1},{2,6},{6,10},{... | collective-permute-start | bytes 331784 | tf_op jit(solution)/shard_map/ppermute | solution.py:51
  48.3 17.0 %collective-permute-start.5 = (f32[432,64]{1,0:T(8,128)S(1)}, f32[432,64]{1,0:T(8,128)S(1)}, u32[]{:S(2)}, u32[]{:S(2)}) collective-permute-start(f32[432,64]{1,0:T(8,128)S(1)} %get-tuple-element.11), channel_id=1, source_target_pairs={{0,8},{4,12},{8,0},{12,4},{1,9},{5,13},{9,1},{13,5},{2,10},{6,14},... | collective-permute-start | bytes 331784 | tf_op jit(solution)/shard_map/ppermute | solution.py:51
  49.2 20.1 %collective-permute-start.6 = (f32[432,64]{1,0:T(8,128)S(1)}, f32[432,64]{1,0:T(8,128)S(1)}, u32[]{:S(2)}, u32[]{:S(2)}) collective-permute-start(f32[432,64]{1,0:T(8,128)S(1)} %get-tuple-element.12), channel_id=1, source_target_pairs={{0,12},{4,0},{8,4},{12,8},{1,13},{5,1},{9,5},{13,9},{2,14},{6,2},{... | collective-permute-start | bytes 331784 | tf_op jit(solution)/shard_map/ppermute | solution.py:51

commit v8 on v4

--- a/solution.py
+++ b/solution.py
@@ -18,8 +18,11 @@
             low = jnp.where(me == 1, got, jnp.zeros_like(got))
             high = jnp.where(me == 0, got, jnp.zeros_like(got))
         else:
-            low = lax.ppermute(tail, axis, [(i, i + 1) for i in range(count - 1)])
-            high = lax.ppermute(head, axis, [(i + 1, i) for i in range(count - 1)])
+            me = lax.axis_index(axis)
+            low = lax.ppermute(tail, axis, [(i, (i + 1) % count) for i in range(count)])
+            high = lax.ppermute(head, axis, [((i + 1) % count, i) for i in range(count)])
+            low = jnp.where(me == 0, jnp.zeros_like(low), low)
+            high = jnp.where(me == count - 1, jnp.zeros_like(high), high)
         cells = jnp.concatenate([low, cells, high], axis=dim)
     return cells
 

time: 53 us -> 59.6 us (1.12)
  local copies, waits for them, and re-layouts: 7.39 us -> 14.4 us
  waiting for transfers between devices: 14.5 us -> 17.9 us
  starting transfers between devices: 15.5 us -> 13 us
  other arithmetic: 4.95 us -> 3.97 us
    unnamed x22, local copies, waits for them, and re-layouts: 2.13 us -> 7.34 us
    ppermute x4, waiting for transfers between devices: 6.97 us -> 10.8 us  [scatter_sum(): lax.ppermute(part, axis, [(j, (j + shift) % count) for j in range(count)])]
    ppermute x4, starting transfers between devices: 7.24 us -> 5.79 us  [scatter_sum(): lax.ppermute(part, axis, [(j, (j + shift) % count) for j in range(count)])]
    reshape x1, local copies, waits for them, and re-layouts: 1.37 us -> 2.57 us  [on_device(): weight_terms.reshape(nx, ny, weight_terms.shape[0] // (nx * ny), half)]
    concatenate x1, other arithmetic: 1.19 us -> 0.15 us  [with_halo(): cells = jnp.concatenate([low, cells, high], axis=dim)]
    ppermute x2, starting transfers between devices: 5.31 us -> 4.32 us  [the longest x1 2.16 us: with_halo(): low = lax.ppermute(tail, axis, [(i, (i + 1) % count) for i in range(count)])]
    concatenate x1, local copies, waits for them, and re-layouts: 0.01 us -> 0.65 us  [on_device(): weight_terms = jnp.concatenate(pieces, axis=0)]
  transfers between devices with their start and end apart: 7 -> 7, of which waited for: 6 -> 6; matrix products, arithmetic and copies ran while one was open for 13% -> 12% of each run, Pallas kernels for 0% -> 0%
where the time goes in v8:
time: 59.6 us; the launch traced here: 59.3 us
  waiting for transfers between devices  17.9 us (30%)
  local copies, waits for them, and re-layouts  14.4 us (24%)
  starting transfers between devices  13 us (22%)
  matrix products  9.09 us (15%)
  other arithmetic  3.97 us (7%)
  between operations  0.96 us (2%)
    ppermute x4, waiting for transfers between devices, scatter_sum(): lax.ppermute(part, axis, [(j, (j + shift) % count) for j in range(count)])  10.8 us
    unnamed x22, local copies, waits for them, and re-layouts  7.34 us
    ppermute x4, starting transfers between devices, scatter_sum(): lax.ppermute(part, axis, [(j, (j + shift) % count) for j in range(count)])  5.79 us
    conv_general_dilated x1, matrix products, on_device(): lax.conv_general_dilated(gh[None], kflip, (1, 1, 1), pad, dimension_numbe...  4.95 us
    ppermute x1, waiting for transfers between devices, with_halo(): low = lax.ppermute(tail, axis, [(i, (i + 1) % count) for i in range(count)])  4.2 us
    dot_general x9, matrix products, on_device(): lax.dot_general(x_act, window, (((0, 1, 2), (0, 1, 2)), ((), ())), prefer...  4.14 us
    ppermute x1, starting transfers between devices, with_halo(): got = lax.ppermute(jnp.where(me == 0, tail, head), axis, [(0, 1), (1, 0)])  2.94 us
    reshape x1, local copies, waits for them, and re-layouts, on_device(): weight_terms.reshape(nx, ny, weight_terms.shape[0] // (nx * ny), half)  2.57 us
  transfers between devices with their start and end apart: 7, of which 6 were waited for; matrix products, arithmetic and copies ran while one was open for 12% of the time, Pallas kernels for 0%

profile of v8, /device:TPU:0, one launch (start us, length us, event | category | flops | bytes accessed | tf_op | source)
XLA Modules:
  0.0 59.3 jit_solution(2816895765827281371)
XLA Ops:
  0.7 0.9 %slice_select_fusion = bf16[4,1,32,128]{3,2,1,0:T(8,128)(2,1)S(1)} fusion(bf16[4,16,32,128]{3,2,1,0:T(8,128)(2,1)} %param.4, pred[]{:T(512)S(6)} %eq.20), kind=kLoop, calls=%fused_computation.39 | loop fusion | flops 16384 | bytes 98305 | tf_op jit(solution)/shard_map/jit(_where)/select_n | solution.py:17
  1.6 2.9 %collective-permute-start = (bf16[4,1,32,128]{3,2,1,0:T(8,128)(2,1)S(1)}, bf16[4,1,32,128]{3,2,1,0:T(8,128)(2,1)S(1)}, u32[]{:S(2)}, u32[]{:S(2)}) collective-permute-start(bf16[4,1,32,128]{3,2,1,0:T(8,128)(2,1)S(1)} %slice_select_fusion), channel_id=1, source_target_pairs={{0,2},{2,0},{1,3},{3,1},{4,6},{6,4},{5,7},{7,5},{8,10},{10,8},{9,1... | collective-permute-start | bytes 98312 | tf_op jit(solution)/shard_map/ppermute | solution.py:17
  4.5 1.9 %collective-permute-done = bf16[4,1,32,128]{3,2,1,0:T(8,128)(2,1)S(1)} collective-permute-done((bf16[4,1,32,128]{3,2,1,0:T(8,128)(2,1)S(1)}, bf16[4,1,32,128]{3,2,1,0:T(8,128)(2,1)S(1)}, u32[]{:S(2)}, u32[]{:S(2)}) %collective-permute-start) | collective-permute-done | bytes 32800 | tf_op jit(solution)/shard_map/ppermute | solution.py:17
  6.4 1.0 %pad_maximum_fusion.4 = (bf16[1,18,32,128]{3,2,1,0:T(8,128)(2,1)S(1)}, bf16[1,18,32,128]{3,2,1,0:T(8,128)(2,1)S(1)}) fusion(bf16[4,1,32,128]{3,2,1,0:T(8,128)(2,1)S(1)} %get-tuple-element.15, bf16[4,16,32,128]{3,2,1,0:T(8,128)(2,1)} %param.4, bf16[4,1,32,128]{3,2,1,0:T(8,128)(2,1)S(1)} %get-tuple-element.14), kind=kLoop, calls=%fused_computation.20 | loop fusion | flops 294912 | bytes 884736 | tf_op jit(solution)/shard_map/slice | solution.py:11
  7.4 2.2 %collective-permute-start.1 = (bf16[1,18,32,128]{3,2,1,0:T(8,128)(2,1)S(1)}, bf16[1,18,32,128]{3,2,1,0:T(8,128)(2,1)S(1)}, u32[]{:S(2)}, u32[]{:S(2)}) collective-permute-start(bf16[1,18,32,128]{3,2,1,0:T(8,128)(2,1)S(1)} %get-tuple-element.8), channel_id=1, source_target_pairs={{0,4},{4,8},{8,12},{12,0},{1,5},{5,9},{9,13},{13,1},{2,6},{6,10},{... | collective-permute-start | bytes 442376 | tf_op jit(solution)/shard_map/ppermute | solution.py:22
  9.6 2.2 %collective-permute-start.2 = (bf16[1,18,32,128]{3,2,1,0:T(8,128)(2,1)S(1)}, bf16[1,18,32,128]{3,2,1,0:T(8,128)(2,1)S(1)}, u32[]{:S(2)}, u32[]{:S(2)}) collective-permute-start(bf16[1,18,32,128]{3,2,1,0:T(8,128)(2,1)S(1)} %get-tuple-element.9), channel_id=1, source_target_pairs={{4,0},{8,4},{12,8},{0,12},{5,1},{9,5},{13,9},{1,13},{6,2},{10,6},{... | collective-permute-start | bytes 442376 | tf_op jit(solution)/shard_map/ppermute | solution.py:23
  11.7 4.2 %collective-permute-done.1 = bf16[1,18,32,128]{3,2,1,0:T(8,128)(2,1)S(1)} collective-permute-done((bf16[1,18,32,128]{3,2,1,0:T(8,128)(2,1)S(1)}, bf16[1,18,32,128]{3,2,1,0:T(8,128)(2,1)S(1)}, u32[]{:S(2)}, u32[]{:S(2)}) %collective-permute-start.1) | collective-permute-done | bytes 147488 | tf_op jit(solution)/shard_map/ppermute | solution.py:22
  15.9 0.9 %collective-permute-done.2 = bf16[1,18,32,128]{3,2,1,0:T(8,128)(2,1)S(1)} collective-permute-done((bf16[1,18,32,128]{3,2,1,0:T(8,128)(2,1)S(1)}, bf16[1,18,32,128]{3,2,1,0:T(8,128)(2,1)S(1)}, u32[]{:S(2)}, u32[]{:S(2)}) %collective-permute-start.2) | collective-permute-done | bytes 147488 | tf_op jit(solution)/shard_map/ppermute | solution.py:23
  16.9 0.2 pad_maximum_fusion.1
  17.1 0.3 constant_dynamic-slice_fusion.6
  17.4 0.8 %pad_slice_fusion.1 = (bf16[6,18,32,64]{3,2,1,0:T(8,128)(2,1)S(1)}, bf16[6,18,32,64]{3,2,1,0:T(8,128)(2,1)S(1)}) fusion(bf16[6,18,32,64]{3,2,1,0:T(8,128)(2,1)S(1)} %constant_dynamic-slice_fusion.6), kind=kLoop, calls=%fused_computation.12 | loop fusion | bytes 1327104 | tf_op jit(solution)/shard_map/slice | solution.py:61
  18.2 0.9 %pad_maximum_fusion = bf16[6,18,32,192]{3,2,1,0:T(8,128)(2,1)S(1)} fusion(bf16[6,18,32,64]{3,2,1,0:T(8,128)(2,1)S(1)} %get-tuple-element.7, bf16[6,18,32,64]{3,2,1,0:T(8,128)(2,1)S(1)} %constant_dynamic-slice_fusion.6, bf16[6,18,32,64]{3,2,1,0:T(8,128)(2,1)S(1)} %get-tuple-element.6), kind=kLoop, calls=%fused_computation.2 | loop fusion | flops 3981312 | bytes 2654208 | tf_op jit(solution)/shard_map/concatenate | solution.py:61
  19.0 0.2 copy-done.2
  19.2 0.5 fusion.21
  19.7 0.5 fusion.22
  20.1 0.5 fusion.23
  20.6 0.5 fusion.24
  21.1 0.5 fusion.25
  21.5 0.5 fusion.26
  22.0 0.5 fusion.27
  22.5 0.5 fusion.28
  22.9 0.5 fusion.29
  23.6 0.7 %bitcast_dynamic-update-slice_fusion.8 = f32[3456,64]{0,1:T(8,128)} fusion(f32[8,8,3,128]{3,2,1,0:T(4,128)S(1)} %bitcast.185), kind=kLoop, calls=%fused_computation.38 | loop fusion | bytes 196608
  24.9 0.7 %bitcast_dynamic-update-slice_fusion.7 = f32[3456,64]{0,1:T(8,128)} fusion(f32[3456,64]{0,1:T(8,128)} %bitcast_dynamic-update-slice_fusion.8, f32[8,8,3,128]{3,2,1,0:T(4,128)S(1)} %bitcast.183), kind=kLoop, calls=%fused_computation.37 | loop fusion | bytes 196608
  25.6 0.6 %bitcast_dynamic-update-slice_fusion.6 = f32[3456,64]{0,1:T(8,128)} fusion(f32[3456,64]{0,1:T(8,128)} %bitcast_dynamic-update-slice_fusion.7, f32[8,8,3,128]{3,2,1,0:T(4,128)S(1)} %bitcast.184), kind=kLoop, calls=%fused_computation.36 | loop fusion | bytes 196608
  26.2 0.7 %bitcast_dynamic-update-slice_fusion.5 = f32[3456,64]{0,1:T(8,128)} fusion(f32[3456,64]{0,1:T(8,128)} %bitcast_dynamic-update-slice_fusion.6, f32[8,8,3,128]{3,2,1,0:T(4,128)S(1)} %bitcast.182), kind=kLoop, calls=%fused_computation.35 | loop fusion | bytes 196608
  26.9 0.7 %bitcast_dynamic-update-slice_fusion.4 = f32[3456,64]{0,1:T(8,128)} fusion(f32[3456,64]{0,1:T(8,128)} %bitcast_dynamic-update-slice_fusion.5, f32[8,8,3,128]{3,2,1,0:T(4,128)S(1)} %bitcast.181), kind=kLoop, calls=%fused_computation.34 | loop fusion | bytes 196608
  27.6 0.7 %bitcast_dynamic-update-slice_fusion.3 = f32[3456,64]{0,1:T(8,128)} fusion(f32[3456,64]{0,1:T(8,128)} %bitcast_dynamic-update-slice_fusion.4, f32[8,8,3,128]{3,2,1,0:T(4,128)S(1)} %bitcast.180), kind=kLoop, calls=%fused_computation.33 | loop fusion | bytes 196608
  28.2 0.7 %bitcast_dynamic-update-slice_fusion.2 = f32[3456,64]{0,1:T(8,128)} fusion(f32[3456,64]{0,1:T(8,128)} %bitcast_dynamic-update-slice_fusion.3, f32[8,8,3,128]{3,2,1,0:T(4,128)S(1)} %bitcast.179), kind=kLoop, calls=%fused_computation.32 | loop fusion | bytes 196608
  28.9 0.7 %bitcast_dynamic-update-slice_fusion.1 = f32[3456,64]{0,1:T(8,128)} fusion(f32[3456,64]{0,1:T(8,128)} %bitcast_dynamic-update-slice_fusion.2, f32[8,8,3,128]{3,2,1,0:T(4,128)S(1)} %bitcast.178), kind=kLoop, calls=%fused_computation.31 | loop fusion | bytes 196608
  29.5 0.6 %bitcast_dynamic-update-slice_fusion = f32[3456,64]{0,1:T(8,128)} fusion(f32[3456,64]{0,1:T(8,128)} %bitcast_dynamic-update-slice_fusion.1, f32[8,8,3,128]{3,2,1,0:T(4,128)S(1)} %bitcast.177), kind=kLoop, calls=%fused_computation.30 | loop fusion | bytes 196608 | tf_op jit(solution)/shard_map/concatenate | solution.py:70
  30.2 2.6 %reshape.84 = f32[4,2,432,64]{2,1,0,3:T(2,128)S(1)} reshape(f32[3456,64]{0,1:T(8,128)} %bitcast_dynamic-update-slice_fusion) | data formatting | bytes 1769472 | tf_op jit(solution)/shard_map/reshape | solution.py:73
  32.8 1.1 %constant_dynamic-slice_fusion.5 = (f32[4,1,432,64]{2,1,0,3:T(1,128)S(1)}, f32[4,1,432,64]{2,1,0,3:T(1,128)S(1)}) fusion(f32[4,2,432,64]{2,1,0,3:T(2,128)S(1)} %reshape.84, s32[]{:T(128)S(6)} %select_n.84, s32[]{:T(128)S(6)} %select_n.86), kind=kLoop, calls=%fused_computation.47 | loop fusion | bytes 1769480 | tf_op jit(solution)/shard_map/jit(dynamic_index_in_dim)/dynamic_slice | solution.py:37
  34.0 1.6 %collective-permute-start.3 = (f32[4,432,64]{1,0,2:T(4,128)S(1)}, f32[4,432,64]{1,0,2:T(4,128)S(1)}, u32[]{:S(2)}, u32[]{:S(2)}) collective-permute-start(f32[4,432,64]{1,0,2:T(4,128)S(1)} %bitcast.186), channel_id=1, source_target_pairs={{0,2},{2,0},{1,3},{3,1},{4,6},{6,4},{5,7},{7,5},{8,10},{10,8},{9,1... | collective-permute-start | bytes 1327112 | tf_op jit(solution)/shard_map/ppermute | solution.py:40
  35.6 0.4 copy.34
  35.9 0.2 pad.5.clone
  36.5 0.4 copy-done.3
  36.9 4.9 %fusion.11 = bf16[4,16,8,5,128]{4,2,3,1,0:T(8,128)(2,1)S(1)} fusion(bf16[3,3,3,128,128]{4,3,2,1,0:T(8,128)(2,1)S(1)} %bitcast.174, bf16[6,18,1,7,2,128]{5,3,4,1,0,2:T(8,128)(2,1)S(1)} %slice.63, bf16[6,18,1,8,5,128]{5,3,4,1,0,2:T(8,128)(2,1)S(1)} %copy.7, pred[8,5]{0,1:T(8,128)(4,1)S(1)} %copy-done.3), kind=kOutput, calls=%fused_computation.10 | convolution fusion | flops 2270224384 | bytes 3033128 | tf_op jit(solution)/shard_map/conv_general_dilated | solution.py:53
  41.9 4.5 %collective-permute-done.3 = f32[4,432,64]{1,0,2:T(4,128)S(1)} collective-permute-done((f32[4,432,64]{1,0,2:T(4,128)S(1)}, f32[4,432,64]{1,0,2:T(4,128)S(1)}, u32[]{:S(2)}, u32[]{:S(2)}) %collective-permute-start.3) | collective-permute-done | bytes 442400 | tf_op jit(solution)/shard_map/ppermute | solution.py:40
  46.4 0.2 bitcast_add_fusion
  46.6 0.5 constant_dynamic-slice_fusion.3
  47.1 1.7 %collective-permute-start.4 = (f32[432,64]{0,1:T(8,128)S(1)}, f32[432,64]{0,1:T(8,128)S(1)}, u32[]{:S(2)}, u32[]{:S(2)}) collective-permute-start(f32[432,64]{0,1:T(8,128)S(1)} %bitcast.187), channel_id=1, source_target_pairs={{0,4},{4,8},{8,12},{12,0},{1,5},{5,9},{9,13},{13,1},{2,6},{6,10},{... | collective-permute-start | bytes 331784 | tf_op jit(solution)/shard_map/ppermute | solution.py:40
  48.8 1.2 %collective-permute-start.5 = (f32[432,64]{0,1:T(8,128)S(1)}, f32[432,64]{0,1:T(8,128)S(1)}, u32[]{:S(2)}, u32[]{:S(2)}) collective-permute-start(f32[432,64]{0,1:T(8,128)S(1)} %bitcast.188), channel_id=1, source_target_pairs={{0,8},{4,12},{8,0},{12,4},{1,9},{5,13},{9,1},{13,5},{2,10},{6,14},... | collective-permute-start | bytes 331784 | tf_op jit(solution)/shard_map/ppermute | solution.py:40
  50.0 1.3 %collective-permute-start.6 = (f32[432,64]{0,1:T(8,128)S(1)}, f32[432,64]{0,1:T(8,128)S(1)}, u32[]{:S(2)}, u32[]{:S(2)}) collective-permute-start(f32[432,64]{0,1:T(8,128)S(1)} %bitcast.189), channel_id=1, source_target_pairs={{0,12},{4,0},{8,4},{12,8},{1,13},{5,1},{9,5},{13,9},{2,14},{6,2},{... | collective-permute-start | bytes 331784 | tf_op jit(solution)/shard_map/ppermute | solution.py:40
  51.4 0.9 %copy.18 = bf16[4,16,32,128]{3,2,1,0:T(8,128)(2,1)} copy(bf16[4,16,32,128]{3,1,2,0:T(8,128)(2,1)S(1)} %slice_bitcast_fusion) | data formatting | bytes 1048576
  52.3 2.7 %collective-permute-done.4 = f32[432,64]{0,1:T(8,128)S(1)} collective-permute-done((f32[432,64]{0,1:T(8,128)S(1)}, f32[432,64]{0,1:T(8,128)S(1)}, u32[]{:S(2)}, u32[]{:S(2)}) %collective-permute-start.4) | collective-permute-done | bytes 110624 | tf_op jit(solution)/shard_map/ppermute | solution.py:40
  55.0 3.7 %collective-permute-done.5 = f32[432,64]{0,1:T(8,128)S(1)} collective-permute-done((f32[432,64]{0,1:T(8,128)S(1)}, f32[432,64]{0,1:T(8,128)S(1)}, u32[]{:S(2)}, u32[]{:S(2)}) %collective-permute-start.5) | collective-permute-done | bytes 110624 | tf_op jit(solution)/shard_map/ppermute | solution.py:40
  58.6 0.7 %fusion.17 = f32[432,64]{0,1:T(8,128)} fusion(f32[432,64]{0,1:T(8,128)S(1)} %collective-permute-done.6, f32[432,64]{0,1:T(8,128)S(1)} %collective-permute-done.5, f32[432,64]{0,1:T(8,128)S(1)} %collective-permute-done.4, f32[1,432,64]{1,0,2:T(1,128)S(1)} %get-tuple-element.10), kind=kLoop, calls=%fused_computation.29 | loop fusion | flops 110592 | bytes 552960 | tf_op jit(solution)/shard_map/div | solution.py:76
  (28 shorter events, 1.4 us)
Async XLA Ops:
  0.6 35.9 %copy-start = (bf16[27,128,128]{2,1,0:T(8,128)(2,1)S(1)}, bf16[27,128,128]{2,1,0:T(8,128)(2,1)}, u32[]{:S(2)}) copy-start(bf16[27,128,128]{2,1,0:T(8,128)(2,1)} %param.5) | copy-start | bytes 2654212
  0.6 16.3 %copy-start.1 = (bf16[4,16,32,128]{3,2,1,0:T(8,128)(2,1)S(1)}, bf16[4,16,32,128]{3,2,1,0:T(8,128)(2,1)}, u32[]{:S(2)}) copy-start(bf16[4,16,32,128]{3,2,1,0:T(8,128)(2,1)} %param.4) | copy-start | bytes 1572868
  1.6 4.8 %collective-permute-start = (bf16[4,1,32,128]{3,2,1,0:T(8,128)(2,1)S(1)}, bf16[4,1,32,128]{3,2,1,0:T(8,128)(2,1)S(1)}, u32[]{:S(2)}, u32[]{:S(2)}) collective-permute-start(bf16[4,1,32,128]{3,2,1,0:T(8,128)(2,1)S(1)} %slice_select_fusion), channel_id=1, source_target_pairs={{0,2},{2,0},{1,3},{3,1},{4,6},{6,4},{5,7},{7,5},{8,10},{10,8},{9,1... | collective-permute-start | bytes 98312 | tf_op jit(solution)/shard_map/ppermute | solution.py:17
  7.4 8.5 %collective-permute-start.1 = (bf16[1,18,32,128]{3,2,1,0:T(8,128)(2,1)S(1)}, bf16[1,18,32,128]{3,2,1,0:T(8,128)(2,1)S(1)}, u32[]{:S(2)}, u32[]{:S(2)}) collective-permute-start(bf16[1,18,32,128]{3,2,1,0:T(8,128)(2,1)S(1)} %get-tuple-element.8), channel_id=1, source_target_pairs={{0,4},{4,8},{8,12},{12,0},{1,5},{5,9},{9,13},{13,1},{2,6},{6,10},{... | collective-permute-start | bytes 442376 | tf_op jit(solution)/shard_map/ppermute | solution.py:22
  9.6 7.3 %collective-permute-start.2 = (bf16[1,18,32,128]{3,2,1,0:T(8,128)(2,1)S(1)}, bf16[1,18,32,128]{3,2,1,0:T(8,128)(2,1)S(1)}, u32[]{:S(2)}, u32[]{:S(2)}) collective-permute-start(bf16[1,18,32,128]{3,2,1,0:T(8,128)(2,1)S(1)} %get-tuple-element.9), channel_id=1, source_target_pairs={{4,0},{8,4},{12,8},{0,12},{5,1},{9,5},{13,9},{1,13},{6,2},{10,6},{... | collective-permute-start | bytes 442376 | tf_op jit(solution)/shard_map/ppermute | solution.py:23
  18.2 1.0 %copy-start.2 = (bf16[4,16,32,128]{3,2,1,0:T(8,128)(2,1)S(1)}, bf16[4,16,32,128]{3,2,1,0:T(8,128)(2,1)}, u32[]{:S(2)}) copy-start(bf16[4,16,32,128]{3,2,1,0:T(8,128)(2,1)} %param.3) | copy-start | bytes 1572868
  34.0 12.4 %collective-permute-start.3 = (f32[4,432,64]{1,0,2:T(4,128)S(1)}, f32[4,432,64]{1,0,2:T(4,128)S(1)}, u32[]{:S(2)}, u32[]{:S(2)}) collective-permute-start(f32[4,432,64]{1,0,2:T(4,128)S(1)} %bitcast.186), channel_id=1, source_target_pairs={{0,2},{2,0},{1,3},{3,1},{4,6},{6,4},{5,7},{7,5},{8,10},{10,8},{9,1... | collective-permute-start | bytes 1327112 | tf_op jit(solution)/shard_map/ppermute | solution.py:40
  36.2 0.7 %copy-start.3 = (pred[8,5]{0,1:T(8,128)(4,1)S(1)}, pred[8,5]{0,1:T(8,128)(4,1)}, u32[]{:S(2)}) copy-start(pred[8,5]{0,1:T(8,128)(4,1)} %constant.80) | copy-start | bytes 124
  47.1 7.9 %collective-permute-start.4 = (f32[432,64]{0,1:T(8,128)S(1)}, f32[432,64]{0,1:T(8,128)S(1)}, u32[]{:S(2)}, u32[]{:S(2)}) collective-permute-start(f32[432,64]{0,1:T(8,128)S(1)} %bitcast.187), channel_id=1, source_target_pairs={{0,4},{4,8},{8,12},{12,0},{1,5},{5,9},{9,13},{13,1},{2,6},{6,10},{... | collective-permute-start | bytes 331784 | tf_op jit(solution)/shard_map/ppermute | solution.py:40
  48.8 9.8 %collective-permute-start.5 = (f32[432,64]{0,1:T(8,128)S(1)}, f32[432,64]{0,1:T(8,128)S(1)}, u32[]{:S(2)}, u32[]{:S(2)}) collective-permute-start(f32[432,64]{0,1:T(8,128)S(1)} %bitcast.188), channel_id=1, source_target_pairs={{0,8},{4,12},{8,0},{12,4},{1,9},{5,13},{9,1},{13,5},{2,10},{6,14},... | collective-permute-start | bytes 331784 | tf_op jit(solution)/shard_map/ppermute | solution.py:40
  50.0 8.6 %collective-permute-start.6 = (f32[432,64]{0,1:T(8,128)S(1)}, f32[432,64]{0,1:T(8,128)S(1)}, u32[]{:S(2)}, u32[]{:S(2)}) collective-permute-start(f32[432,64]{0,1:T(8,128)S(1)} %bitcast.189), channel_id=1, source_target_pairs={{0,12},{4,0},{8,4},{12,8},{1,13},{5,1},{9,5},{13,9},{2,14},{6,2},{... | collective-permute-start | bytes 331784 | tf_op jit(solution)/shard_map/ppermute | solution.py:40

commit v9 on v4

--- a/solution.py
+++ b/solution.py
@@ -38,6 +38,18 @@
     return total
 
 
+def take_rows(pieces, start, count):
+    step = pieces[0].shape[0]
+    out = []
+    row = start
+    while row < start + count:
+        at = row % step
+        take = min(start + count - row, step - at)
+        out.append(pieces[row // step][at : at + take])
+        row += take
+    return jnp.concatenate(out, axis=0) if len(out) > 1 else out[0]
+
+
 def on_device(x_act, grad_out, weight):
     size_x, size_y, depth, chans = x_act.shape
     ncores = lax.axis_size("col")
@@ -64,11 +76,23 @@
                 x_act, window, (((0, 1, 2), (0, 1, 2)), ((), ())), preferred_element_type=jnp.float32
             )
             pieces.append(jnp.transpose(term.reshape(chans, 3, half), (1, 0, 2)).reshape(3 * chans, half))
-    weight_terms = jnp.concatenate(pieces, axis=0)
     nx = lax.axis_size("gx")
     ny = lax.axis_size("gy")
-    blocks = weight_terms.reshape(nx, ny, weight_terms.shape[0] // (nx * ny), half)
-    owned = scatter_sum(scatter_sum(blocks, "gy", 1), "gx", 0)
+    owned_rows = 27 * chans // (nx * ny)
+    if ny == 2:
+        iy = lax.axis_index("gy")
+        side = [
+            jnp.stack([take_rows(pieces, (gx * 2 + y) * owned_rows, owned_rows) for gx in range(nx)])
+            for y in range(2)
+        ]
+        keep = jnp.where(iy == 0, side[0], side[1])
+        send = jnp.where(iy == 0, side[1], side[0])
+        partial = keep + lax.ppermute(send, "gy", [(0, 1), (1, 0)])
+    else:
+        weight_terms = jnp.concatenate(pieces, axis=0)
+        blocks = weight_terms.reshape(nx, ny, owned_rows, half)
+        partial = scatter_sum(blocks, "gy", 1)
+    owned = scatter_sum(partial, "gx", 0)
     total_cells = size_x * lax.axis_size("gx") * size_y * lax.axis_size("gy") * depth
     grad_weight = owned / jnp.sqrt(jnp.float32(total_cells))
     return (grad_in, grad_weight)

time: 53 us -> 51 us (0.962)
  local copies, waits for them, and re-layouts: 7.39 us -> 4.92 us
  other arithmetic: 4.95 us -> 5.48 us
    ppermute x0 -> x1, waiting for transfers between devices: none -> 3.25 us  [on_device(): partial = keep + lax.ppermute(send, 'gy', [(0, 1), (1, 0)])]
    ppermute x4 -> x3, waiting for transfers between devices: 6.97 us -> 4.08 us  [scatter_sum(): lax.ppermute(part, axis, [(j, (j + shift) % count) for j in range(count)])]
    ppermute x4 -> x3, starting transfers between devices: 7.24 us -> 5.56 us  [scatter_sum(): lax.ppermute(part, axis, [(j, (j + shift) % count) for j in range(count)])]
    ppermute x0 -> x1, starting transfers between devices: none -> 1.56 us  [on_device(): partial = keep + lax.ppermute(send, 'gy', [(0, 1), (1, 0)])]
    dynamic_slice x2 -> x0, local copies, waits for them, and re-layouts: 1.54 us -> none  [scatter_sum(): total = lax.dynamic_index_in_dim(blocks, me, dim, keepdims=False)]
    reshape x1 -> x0, local copies, waits for them, and re-layouts: 1.37 us -> none  [on_device(): weight_terms.reshape(nx, ny, weight_terms.shape[0] // (nx * ny), half)]
    slice x0 -> x11, local copies, waits for them, and re-layouts: none -> 0.56 us  [take_rows(): out.append(pieces[row // step][at:at + take])]
    unnamed x22 -> x19, local copies, waits for them, and re-layouts: 2.13 us -> 1.97 us
  transfers between devices with their start and end apart: 7 -> 7, of which waited for: 6 -> 6; matrix products, arithmetic and copies ran while one was open for 13% -> 14% of each run, Pallas kernels for 0% -> 0%
where the time goes in v9:
time: 51 us; the launch traced here: 50.7 us
  starting transfers between devices  15.4 us (30%)
  waiting for transfers between devices  14.9 us (29%)
  matrix products  8.9 us (17%)
  other arithmetic  5.48 us (11%)
  local copies, waits for them, and re-layouts  4.92 us (10%)
  between operations  1.1 us (2%)
    ppermute x3, starting transfers between devices, scatter_sum(): lax.ppermute(part, axis, [(j, (j + shift) % count) for j in range(count)])  5.56 us
    conv_general_dilated x1, matrix products, on_device(): lax.conv_general_dilated(gh[None], kflip, (1, 1, 1), pad, dimension_numbe...  4.75 us
    ppermute x1, waiting for transfers between devices, with_halo(): high = lax.ppermute(head, axis, [(i + 1, i) for i in range(count - 1)])  4.39 us
    dot_general x9, matrix products, on_device(): lax.dot_general(x_act, window, (((0, 1, 2), (0, 1, 2)), ((), ())), prefer...  4.15 us
    ppermute x3, waiting for transfers between devices, scatter_sum(): lax.ppermute(part, axis, [(j, (j + shift) % count) for j in range(count)])  4.08 us
    ppermute x1, starting transfers between devices, with_halo(): low = lax.ppermute(tail, axis, [(i, i + 1) for i in range(count - 1)])  4.02 us
    ppermute x1, waiting for transfers between devices, on_device(): partial = keep + lax.ppermute(send, 'gy', [(0, 1), (1, 0)])  3.25 us
    ppermute x1, starting transfers between devices, with_halo(): got = lax.ppermute(jnp.where(me == 0, tail, head), axis, [(0, 1), (1, 0)])  2.94 us
  transfers between devices with their start and end apart: 7, of which 6 were waited for; matrix products, arithmetic and copies ran while one was open for 14% of the time, Pallas kernels for 0%

profile of v9, /device:TPU:0, one launch (start us, length us, event | category | flops | bytes accessed | tf_op | source)
XLA Modules:
  0.0 50.7 jit_solution(17287834181444851953)
XLA Ops:
  0.7 0.9 %slice_select_fusion = bf16[4,1,32,128]{3,2,1,0:T(8,128)(2,1)S(1)} fusion(bf16[4,16,32,128]{3,2,1,0:T(8,128)(2,1)} %param.4, pred[]{:T(512)S(6)} %eq.14), kind=kLoop, calls=%fused_computation.47 | loop fusion | flops 16384 | bytes 98305 | tf_op jit(solution)/shard_map/jit(_where)/select_n | solution.py:17
  1.5 2.9 %collective-permute-start = (bf16[4,1,32,128]{3,2,1,0:T(8,128)(2,1)S(1)}, bf16[4,1,32,128]{3,2,1,0:T(8,128)(2,1)S(1)}, u32[]{:S(2)}, u32[]{:S(2)}) collective-permute-start(bf16[4,1,32,128]{3,2,1,0:T(8,128)(2,1)S(1)} %slice_select_fusion), channel_id=1, source_target_pairs={{0,2},{2,0},{1,3},{3,1},{4,6},{6,4},{5,7},{7,5},{8,10},{10,8},{9,1... | collective-permute-start | bytes 98312 | tf_op jit(solution)/shard_map/ppermute | solution.py:17
  4.5 1.9 %collective-permute-done = bf16[4,1,32,128]{3,2,1,0:T(8,128)(2,1)S(1)} collective-permute-done((bf16[4,1,32,128]{3,2,1,0:T(8,128)(2,1)S(1)}, bf16[4,1,32,128]{3,2,1,0:T(8,128)(2,1)S(1)}, u32[]{:S(2)}, u32[]{:S(2)}) %collective-permute-start) | collective-permute-done | bytes 32800 | tf_op jit(solution)/shard_map/ppermute | solution.py:17
  6.4 1.0 %pad_maximum_fusion.6 = (bf16[1,18,32,128]{3,2,1,0:T(8,128)(2,1)S(1)}, bf16[1,18,32,128]{3,2,1,0:T(8,128)(2,1)S(1)}) fusion(bf16[4,1,32,128]{3,2,1,0:T(8,128)(2,1)S(1)} %get-tuple-element.14, bf16[4,16,32,128]{3,2,1,0:T(8,128)(2,1)} %param.4, bf16[4,1,32,128]{3,2,1,0:T(8,128)(2,1)S(1)} %get-tuple-element.13), kind=kLoop, calls=%fused_computation.22 | loop fusion | flops 294912 | bytes 884736 | tf_op jit(solution)/shard_map/slice | solution.py:11
  7.4 4.0 %collective-permute-start.1 = (bf16[1,18,32,128]{3,2,1,0:T(8,128)(2,1)S(1)}, bf16[1,18,32,128]{3,2,1,0:T(8,128)(2,1)S(1)}, u32[]{:S(2)}, u32[]{:S(2)}) collective-permute-start(bf16[1,18,32,128]{3,2,1,0:T(8,128)(2,1)S(1)} %get-tuple-element.6), channel_id=1, source_target_pairs={{0,4},{4,8},{8,12},{1,5},{5,9},{9,13},{2,6},{6,10},{10,14},{3,7},{... | collective-permute-start | bytes 442376 | tf_op jit(solution)/shard_map/ppermute | solution.py:21
  11.4 1.3 %collective-permute-start.2 = (bf16[1,18,32,128]{3,2,1,0:T(8,128)(2,1)S(1)}, bf16[1,18,32,128]{3,2,1,0:T(8,128)(2,1)S(1)}, u32[]{:S(2)}, u32[]{:S(2)}) collective-permute-start(bf16[1,18,32,128]{3,2,1,0:T(8,128)(2,1)S(1)} %get-tuple-element.7), channel_id=1, source_target_pairs={{4,0},{8,4},{12,8},{5,1},{9,5},{13,9},{6,2},{10,6},{14,10},{7,3},{... | collective-permute-start | bytes 442376 | tf_op jit(solution)/shard_map/ppermute | solution.py:22
  12.7 1.3 %collective-permute-done.1 = bf16[1,18,32,128]{3,2,1,0:T(8,128)(2,1)S(1)} collective-permute-done((bf16[1,18,32,128]{3,2,1,0:T(8,128)(2,1)S(1)}, bf16[1,18,32,128]{3,2,1,0:T(8,128)(2,1)S(1)}, u32[]{:S(2)}, u32[]{:S(2)}) %collective-permute-start.1) | collective-permute-done | bytes 147488 | tf_op jit(solution)/shard_map/ppermute | solution.py:21
  14.1 4.4 %collective-permute-done.2 = bf16[1,18,32,128]{3,2,1,0:T(8,128)(2,1)S(1)} collective-permute-done((bf16[1,18,32,128]{3,2,1,0:T(8,128)(2,1)S(1)}, bf16[1,18,32,128]{3,2,1,0:T(8,128)(2,1)S(1)}, u32[]{:S(2)}, u32[]{:S(2)}) %collective-permute-start.2) | collective-permute-done | bytes 147488 | tf_op jit(solution)/shard_map/ppermute | solution.py:22
  18.4 1.2 %pad_maximum_fusion.1 = bf16[6,18,32,128]{3,2,1,0:T(8,128)(2,1)S(1)} fusion(bf16[1,18,32,128]{3,2,1,0:T(8,128)(2,1)S(1)} %collective-permute-done.2, bf16[4,1,32,128]{3,2,1,0:T(8,128)(2,1)S(1)} %get-tuple-element.14, bf16[4,16,32,128]{3,2,1,0:T(8,128)(2,1)} %param.4, bf16[4,1,32,128]{3,2,1,0:T(8,128)(2,1)S(1)} %get-tuple-element.13, ...), kind=kLoop, calls=%fused_computation.13 | loop fusion | flops 1769472 | bytes 1769472 | tf_op jit(solution)/shard_map/concatenate | solution.py:23
  19.6 0.3 constant_dynamic-slice_fusion
  19.9 0.8 %pad_slice_fusion.1 = (bf16[6,18,32,64]{3,2,1,0:T(8,128)(2,1)S(1)}, bf16[6,18,32,64]{3,2,1,0:T(8,128)(2,1)S(1)}) fusion(bf16[6,18,32,64]{3,2,1,0:T(8,128)(2,1)S(1)} %constant_dynamic-slice_fusion), kind=kLoop, calls=%fused_computation.12 | loop fusion | bytes 1327104 | tf_op jit(solution)/shard_map/slice | solution.py:70
  20.7 0.9 %pad_maximum_fusion = bf16[6,18,32,192]{3,2,1,0:T(8,128)(2,1)S(1)} fusion(bf16[6,18,32,64]{3,2,1,0:T(8,128)(2,1)S(1)} %get-tuple-element.5, bf16[6,18,32,64]{3,2,1,0:T(8,128)(2,1)S(1)} %constant_dynamic-slice_fusion, bf16[6,18,32,64]{3,2,1,0:T(8,128)(2,1)S(1)} %get-tuple-element.4), kind=kLoop, calls=%fused_computation.2 | loop fusion | flops 3981312 | bytes 2654208 | tf_op jit(solution)/shard_map/concatenate | solution.py:70
  21.6 0.2 copy-done.2
  21.8 0.5 fusion.25
  22.2 0.5 fusion.26
  22.7 0.5 fusion.24
  23.1 0.5 fusion.23
  23.7 0.1 slice.128
  23.8 0.5 fusion.29
  24.4 0.1 slice.122
  24.5 0.5 fusion.30
  24.9 0.5 fusion.27
  25.4 0.5 fusion.28
  26.3 0.5 fusion.31
  27.2 0.1 fusion.22
  27.5 0.1 maximum_bitcast_fusion
  27.6 0.1 maximum_bitcast_fusion.3
  27.7 0.1 maximum_bitcast_fusion.2
  27.8 0.1 maximum_bitcast_fusion.6
  27.9 0.1 fusion.15
  28.0 1.6 %collective-permute-start.3 = (f32[4,432,64]{1,2,0:T(8,128)S(1)}, f32[4,432,64]{1,2,0:T(8,128)S(1)}, u32[]{:S(2)}, u32[]{:S(2)}) collective-permute-start(f32[4,432,64]{1,2,0:T(8,128)S(1)} %fusion.15), channel_id=1, source_target_pairs={{0,2},{2,0},{1,3},{3,1},{4,6},{6,4},{5,7},{7,5},{8,10},{10,8},{9,1... | collective-permute-start | bytes 1327112 | tf_op jit(solution)/shard_map/ppermute | solution.py:90
  29.6 0.2 fusion.51
  29.7 0.4 copy.28
  30.1 0.2 pad.5.clone
  30.4 0.1 copy.7
  30.5 0.1 slice.119
  30.7 0.4 copy-done.3
  31.1 4.7 %fusion.11 = bf16[4,16,8,5,128]{4,2,3,1,0:T(8,128)(2,1)S(1)} fusion(bf16[3,3,3,128,128]{4,3,2,1,0:T(8,128)(2,1)S(1)} %bitcast.191, bf16[6,18,1,7,2,128]{5,3,4,1,0,2:T(8,128)(2,1)S(1)} %slice.119, bf16[6,18,1,8,5,128]{5,3,4,1,0,2:T(8,128)(2,1)S(1)} %copy.7, pred[8,5]{0,1:T(8,128)(4,1)S(1)} %copy-done.3), kind=kOutput, calls=%fused_computation.10 | convolution fusion | flops 2270224384 | bytes 3033128 | tf_op jit(solution)/shard_map/conv_general_dilated | solution.py:62
  35.8 0.1 copy.8
  35.9 3.3 %collective-permute-done.3 = f32[4,432,64]{1,2,0:T(8,128)S(1)} collective-permute-done((f32[4,432,64]{1,2,0:T(8,128)S(1)}, f32[4,432,64]{1,2,0:T(8,128)S(1)}, u32[]{:S(2)}, u32[]{:S(2)}) %collective-permute-start.3) | collective-permute-done | bytes 442400 | tf_op jit(solution)/shard_map/ppermute | solution.py:90
  39.2 0.2 select_add_fusion
  39.4 1.6 %collective-permute-start.4 = (f32[432,64]{0,1:T(8,128)S(1)}, f32[432,64]{0,1:T(8,128)S(1)}, u32[]{:S(2)}, u32[]{:S(2)}) collective-permute-start(f32[432,64]{0,1:T(8,128)S(1)} %get-tuple-element.8), channel_id=1, source_target_pairs={{0,4},{4,8},{8,12},{12,0},{1,5},{5,9},{9,13},{13,1},{2,6},{6,10},{... | collective-permute-start | bytes 331784 | tf_op jit(solution)/shard_map/ppermute | solution.py:37
  41.0 1.1 %collective-permute-start.5 = (f32[432,64]{0,1:T(8,128)S(1)}, f32[432,64]{0,1:T(8,128)S(1)}, u32[]{:S(2)}, u32[]{:S(2)}) collective-permute-start(f32[432,64]{0,1:T(8,128)S(1)} %get-tuple-element.10), channel_id=1, source_target_pairs={{0,8},{4,12},{8,0},{12,4},{1,9},{5,13},{9,1},{13,5},{2,10},{6,14},... | collective-permute-start | bytes 331784 | tf_op jit(solution)/shard_map/ppermute | solution.py:37
  42.1 2.8 %collective-permute-start.6 = (f32[432,64]{0,1:T(8,128)S(1)}, f32[432,64]{0,1:T(8,128)S(1)}, u32[]{:S(2)}, u32[]{:S(2)}) collective-permute-start(f32[432,64]{0,1:T(8,128)S(1)} %get-tuple-element.9), channel_id=1, source_target_pairs={{0,12},{4,0},{8,4},{12,8},{1,13},{5,1},{9,5},{13,9},{2,14},{6,2},{... | collective-permute-start | bytes 331784 | tf_op jit(solution)/shard_map/ppermute | solution.py:37
  45.0 0.9 %copy.18 = bf16[4,16,32,128]{3,2,1,0:T(8,128)(2,1)} copy(bf16[4,16,32,128]{3,1,2,0:T(8,128)(2,1)S(1)} %slice_bitcast_fusion) | data formatting | bytes 1048576
  45.9 0.5 collective-permute-done.4
  46.4 3.6 %collective-permute-done.5 = f32[432,64]{0,1:T(8,128)S(1)} collective-permute-done((f32[432,64]{0,1:T(8,128)S(1)}, f32[432,64]{0,1:T(8,128)S(1)}, u32[]{:S(2)}, u32[]{:S(2)}) %collective-permute-start.5) | collective-permute-done | bytes 110624 | tf_op jit(solution)/shard_map/ppermute | solution.py:37
  50.0 0.7 %fusion.18 = f32[432,64]{0,1:T(8,128)} fusion(f32[432,64]{0,1:T(8,128)S(1)} %collective-permute-done.6, f32[432,64]{0,1:T(8,128)S(1)} %collective-permute-done.5, f32[432,64]{0,1:T(8,128)S(1)} %collective-permute-done.4, f32[4,432,64]{1,2,0:T(8,128)S(1)} %select_add_fusion, s32[]{:T(128)S(6)} %select_n.70), kind=kLoop, calls=%fused_computation.34 | loop fusion | flops 110592 | bytes 552964 | tf_op jit(solution)/shard_map/div | solution.py:97
  (36 shorter events, 1.2 us)
Async XLA Ops:
  0.6 30.0 %copy-start = (bf16[27,128,128]{2,1,0:T(8,128)(2,1)S(1)}, bf16[27,128,128]{2,1,0:T(8,128)(2,1)}, u32[]{:S(2)}) copy-start(bf16[27,128,128]{2,1,0:T(8,128)(2,1)} %param.5) | copy-start | bytes 2654212
  1.5 4.8 %collective-permute-start = (bf16[4,1,32,128]{3,2,1,0:T(8,128)(2,1)S(1)}, bf16[4,1,32,128]{3,2,1,0:T(8,128)(2,1)S(1)}, u32[]{:S(2)}, u32[]{:S(2)}) collective-permute-start(bf16[4,1,32,128]{3,2,1,0:T(8,128)(2,1)S(1)} %slice_select_fusion), channel_id=1, source_target_pairs={{0,2},{2,0},{1,3},{3,1},{4,6},{6,4},{5,7},{7,5},{8,10},{10,8},{9,1... | collective-permute-start | bytes 98312 | tf_op jit(solution)/shard_map/ppermute | solution.py:17
  7.4 6.7 %collective-permute-start.1 = (bf16[1,18,32,128]{3,2,1,0:T(8,128)(2,1)S(1)}, bf16[1,18,32,128]{3,2,1,0:T(8,128)(2,1)S(1)}, u32[]{:S(2)}, u32[]{:S(2)}) collective-permute-start(bf16[1,18,32,128]{3,2,1,0:T(8,128)(2,1)S(1)} %get-tuple-element.6), channel_id=1, source_target_pairs={{0,4},{4,8},{8,12},{1,5},{5,9},{9,13},{2,6},{6,10},{10,14},{3,7},{... | collective-permute-start | bytes 442376 | tf_op jit(solution)/shard_map/ppermute | solution.py:21
  11.4 7.0 %collective-permute-start.2 = (bf16[1,18,32,128]{3,2,1,0:T(8,128)(2,1)S(1)}, bf16[1,18,32,128]{3,2,1,0:T(8,128)(2,1)S(1)}, u32[]{:S(2)}, u32[]{:S(2)}) collective-permute-start(bf16[1,18,32,128]{3,2,1,0:T(8,128)(2,1)S(1)} %get-tuple-element.7), channel_id=1, source_target_pairs={{4,0},{8,4},{12,8},{5,1},{9,5},{13,9},{6,2},{10,6},{14,10},{7,3},{... | collective-permute-start | bytes 442376 | tf_op jit(solution)/shard_map/ppermute | solution.py:22
  20.7 1.0 %copy-start.2 = (bf16[4,16,32,128]{3,2,1,0:T(8,128)(2,1)S(1)}, bf16[4,16,32,128]{3,2,1,0:T(8,128)(2,1)}, u32[]{:S(2)}) copy-start(bf16[4,16,32,128]{3,2,1,0:T(8,128)(2,1)} %param.3) | copy-start | bytes 1572868
  27.4 2.1 %copy-start.1 = (bf16[4,16,32,128]{3,2,1,0:T(8,128)(2,1)S(1)}, bf16[4,16,32,128]{3,2,1,0:T(8,128)(2,1)}, u32[]{:S(2)}) copy-start(bf16[4,16,32,128]{3,2,1,0:T(8,128)(2,1)} %param.4) | copy-start | bytes 1572868
  28.0 11.2 %collective-permute-start.3 = (f32[4,432,64]{1,2,0:T(8,128)S(1)}, f32[4,432,64]{1,2,0:T(8,128)S(1)}, u32[]{:S(2)}, u32[]{:S(2)}) collective-permute-start(f32[4,432,64]{1,2,0:T(8,128)S(1)} %fusion.15), channel_id=1, source_target_pairs={{0,2},{2,0},{1,3},{3,1},{4,6},{6,4},{5,7},{7,5},{8,10},{10,8},{9,1... | collective-permute-start | bytes 1327112 | tf_op jit(solution)/shard_map/ppermute | solution.py:90
  30.4 0.7 %copy-start.3 = (pred[8,5]{0,1:T(8,128)(4,1)S(1)}, pred[8,5]{0,1:T(8,128)(4,1)}, u32[]{:S(2)}) copy-start(pred[8,5]{0,1:T(8,128)(4,1)} %constant.66) | copy-start | bytes 124
  39.4 7.0 %collective-permute-start.4 = (f32[432,64]{0,1:T(8,128)S(1)}, f32[432,64]{0,1:T(8,128)S(1)}, u32[]{:S(2)}, u32[]{:S(2)}) collective-permute-start(f32[432,64]{0,1:T(8,128)S(1)} %get-tuple-element.8), channel_id=1, source_target_pairs={{0,4},{4,8},{8,12},{12,0},{1,5},{5,9},{9,13},{13,1},{2,6},{6,10},{... | collective-permute-start | bytes 331784 | tf_op jit(solution)/shard_map/ppermute | solution.py:37
  41.0 9.0 %collective-permute-start.5 = (f32[432,64]{0,1:T(8,128)S(1)}, f32[432,64]{0,1:T(8,128)S(1)}, u32[]{:S(2)}, u32[]{:S(2)}) collective-permute-start(f32[432,64]{0,1:T(8,128)S(1)} %get-tuple-element.10), channel_id=1, source_target_pairs={{0,8},{4,12},{8,0},{12,4},{1,9},{5,13},{9,1},{13,5},{2,10},{6,14},... | collective-permute-start | bytes 331784 | tf_op jit(solution)/shard_map/ppermute | solution.py:37
  42.1 7.9 %collective-permute-start.6 = (f32[432,64]{0,1:T(8,128)S(1)}, f32[432,64]{0,1:T(8,128)S(1)}, u32[]{:S(2)}, u32[]{:S(2)}) collective-permute-start(f32[432,64]{0,1:T(8,128)S(1)} %get-tuple-element.9), channel_id=1, source_target_pairs={{0,12},{4,0},{8,4},{12,8},{1,13},{5,1},{9,5},{13,9},{2,14},{6,2},{... | collective-permute-start | bytes 331784 | tf_op jit(solution)/shard_map/ppermute | solution.py:37

commit v10 on v9

--- a/solution.py
+++ b/solution.py
@@ -18,8 +18,11 @@
             low = jnp.where(me == 1, got, jnp.zeros_like(got))
             high = jnp.where(me == 0, got, jnp.zeros_like(got))
         else:
-            low = lax.ppermute(tail, axis, [(i, i + 1) for i in range(count - 1)])
-            high = lax.ppermute(head, axis, [(i + 1, i) for i in range(count - 1)])
+            me = lax.axis_index(axis)
+            low = lax.ppermute(tail, axis, [(i, (i + 1) % count) for i in range(count)])
+            high = lax.ppermute(head, axis, [((i + 1) % count, i) for i in range(count)])
+            low = jnp.where(me == 0, jnp.zeros_like(low), low)
+            high = jnp.where(me == count - 1, jnp.zeros_like(high), high)
         cells = jnp.concatenate([low, cells, high], axis=dim)
     return cells
 

time: 51 us -> 50.7 us (level)
  waiting for transfers between devices: 14.9 us -> 18.1 us
  starting transfers between devices: 15.4 us -> 13 us
  other arithmetic: 5.48 us -> 4.5 us
    ppermute x3, waiting for transfers between devices: 4.08 us -> 6.37 us  [scatter_sum(): lax.ppermute(part, axis, [(j, (j + shift) % count) for j in range(count)])]
    ppermute x1, waiting for transfers between devices: 3.25 us -> 4.69 us  [on_device(): partial = keep + lax.ppermute(send, 'gy', [(0, 1), (1, 0)])]
    ppermute x3, starting transfers between devices: 5.56 us -> 4.18 us  [scatter_sum(): lax.ppermute(part, axis, [(j, (j + shift) % count) for j in range(count)])]
    concatenate x1, other arithmetic: 1.19 us -> 0.15 us  [with_halo(): cells = jnp.concatenate([low, cells, high], axis=dim)]
    ppermute x2, starting transfers between devices: 5.31 us -> 4.3 us  [the longest x1 2.16 us: with_halo(): low = lax.ppermute(tail, axis, [(i, (i + 1) % count) for i in range(count)])]
    ppermute x2, waiting for transfers between devices: 5.69 us -> 5.16 us  [the longest x1 4.21 us: with_halo(): low = lax.ppermute(tail, axis, [(i, (i + 1) % count) for i in range(count)])]
  transfers between devices with their start and end apart: 7 -> 7, of which waited for: 6 -> 6; matrix products, arithmetic and copies ran while one was open for 14% -> 13% of each run, Pallas kernels for 0% -> 0%
where the time goes in v10:
time: 50.7 us; the launch traced here: 50.5 us
  waiting for transfers between devices  18.1 us (36%)
  starting transfers between devices  13 us (26%)
  matrix products  8.89 us (18%)
  local copies, waits for them, and re-layouts  4.92 us (10%)
  other arithmetic  4.5 us (9%)
  between operations  1.06 us (2%)
    ppermute x3, waiting for transfers between devices, scatter_sum(): lax.ppermute(part, axis, [(j, (j + shift) % count) for j in range(count)])  6.37 us
    conv_general_dilated x1, matrix products, on_device(): lax.conv_general_dilated(gh[None], kflip, (1, 1, 1), pad, dimension_numbe...  4.74 us
    ppermute x1, waiting for transfers between devices, on_device(): partial = keep + lax.ppermute(send, 'gy', [(0, 1), (1, 0)])  4.69 us
    ppermute x1, waiting for transfers between devices, with_halo(): low = lax.ppermute(tail, axis, [(i, (i + 1) % count) for i in range(count)])  4.21 us
    ppermute x3, starting transfers between devices, scatter_sum(): lax.ppermute(part, axis, [(j, (j + shift) % count) for j in range(count)])  4.18 us
    dot_general x9, matrix products, on_device(): lax.dot_general(x_act, window, (((0, 1, 2), (0, 1, 2)), ((), ())), prefer...  4.15 us
    ppermute x1, starting transfers between devices, with_halo(): got = lax.ppermute(jnp.where(me == 0, tail, head), axis, [(0, 1), (1, 0)])  2.94 us
    ppermute x1, starting transfers between devices, with_halo(): low = lax.ppermute(tail, axis, [(i, (i + 1) % count) for i in range(count)])  2.16 us
  transfers between devices with their start and end apart: 7, of which 6 were waited for; matrix products, arithmetic and copies ran while one was open for 13% of the time, Pallas kernels for 0%

profile of v10, /device:TPU:0, one launch (start us, length us, event | category | flops | bytes accessed | tf_op | source)
XLA Modules:
  0.0 50.5 jit_solution(13781729555900010069)
XLA Ops:
  0.7 0.9 %slice_select_fusion = bf16[4,1,32,128]{3,2,1,0:T(8,128)(2,1)S(1)} fusion(bf16[4,16,32,128]{3,2,1,0:T(8,128)(2,1)} %param.4, pred[]{:T(512)S(6)} %eq.21), kind=kLoop, calls=%fused_computation.49 | loop fusion | flops 16384 | bytes 98305 | tf_op jit(solution)/shard_map/jit(_where)/select_n | solution.py:17
  1.6 2.9 %collective-permute-start = (bf16[4,1,32,128]{3,2,1,0:T(8,128)(2,1)S(1)}, bf16[4,1,32,128]{3,2,1,0:T(8,128)(2,1)S(1)}, u32[]{:S(2)}, u32[]{:S(2)}) collective-permute-start(bf16[4,1,32,128]{3,2,1,0:T(8,128)(2,1)S(1)} %slice_select_fusion), channel_id=1, source_target_pairs={{0,2},{2,0},{1,3},{3,1},{4,6},{6,4},{5,7},{7,5},{8,10},{10,8},{9,1... | collective-permute-start | bytes 98312 | tf_op jit(solution)/shard_map/ppermute | solution.py:17
  4.5 1.9 %collective-permute-done = bf16[4,1,32,128]{3,2,1,0:T(8,128)(2,1)S(1)} collective-permute-done((bf16[4,1,32,128]{3,2,1,0:T(8,128)(2,1)S(1)}, bf16[4,1,32,128]{3,2,1,0:T(8,128)(2,1)S(1)}, u32[]{:S(2)}, u32[]{:S(2)}) %collective-permute-start) | collective-permute-done | bytes 32800 | tf_op jit(solution)/shard_map/ppermute | solution.py:17
  6.4 1.0 %pad_maximum_fusion.6 = (bf16[1,18,32,128]{3,2,1,0:T(8,128)(2,1)S(1)}, bf16[1,18,32,128]{3,2,1,0:T(8,128)(2,1)S(1)}) fusion(bf16[4,1,32,128]{3,2,1,0:T(8,128)(2,1)S(1)} %get-tuple-element.14, bf16[4,16,32,128]{3,2,1,0:T(8,128)(2,1)} %param.4, bf16[4,1,32,128]{3,2,1,0:T(8,128)(2,1)S(1)} %get-tuple-element.13), kind=kLoop, calls=%fused_computation.22 | loop fusion | flops 294912 | bytes 884736 | tf_op jit(solution)/shard_map/slice | solution.py:11
  7.4 2.2 %collective-permute-start.1 = (bf16[1,18,32,128]{3,2,1,0:T(8,128)(2,1)S(1)}, bf16[1,18,32,128]{3,2,1,0:T(8,128)(2,1)S(1)}, u32[]{:S(2)}, u32[]{:S(2)}) collective-permute-start(bf16[1,18,32,128]{3,2,1,0:T(8,128)(2,1)S(1)} %get-tuple-element.6), channel_id=1, source_target_pairs={{0,4},{4,8},{8,12},{12,0},{1,5},{5,9},{9,13},{13,1},{2,6},{6,10},{... | collective-permute-start | bytes 442376 | tf_op jit(solution)/shard_map/ppermute | solution.py:22
  9.6 2.1 %collective-permute-start.2 = (bf16[1,18,32,128]{3,2,1,0:T(8,128)(2,1)S(1)}, bf16[1,18,32,128]{3,2,1,0:T(8,128)(2,1)S(1)}, u32[]{:S(2)}, u32[]{:S(2)}) collective-permute-start(bf16[1,18,32,128]{3,2,1,0:T(8,128)(2,1)S(1)} %get-tuple-element.7), channel_id=1, source_target_pairs={{4,0},{8,4},{12,8},{0,12},{5,1},{9,5},{13,9},{1,13},{6,2},{10,6},{... | collective-permute-start | bytes 442376 | tf_op jit(solution)/shard_map/ppermute | solution.py:23
  11.7 4.2 %collective-permute-done.1 = bf16[1,18,32,128]{3,2,1,0:T(8,128)(2,1)S(1)} collective-permute-done((bf16[1,18,32,128]{3,2,1,0:T(8,128)(2,1)S(1)}, bf16[1,18,32,128]{3,2,1,0:T(8,128)(2,1)S(1)}, u32[]{:S(2)}, u32[]{:S(2)}) %collective-permute-start.1) | collective-permute-done | bytes 147488 | tf_op jit(solution)/shard_map/ppermute | solution.py:22
  15.9 0.9 %collective-permute-done.2 = bf16[1,18,32,128]{3,2,1,0:T(8,128)(2,1)S(1)} collective-permute-done((bf16[1,18,32,128]{3,2,1,0:T(8,128)(2,1)S(1)}, bf16[1,18,32,128]{3,2,1,0:T(8,128)(2,1)S(1)}, u32[]{:S(2)}, u32[]{:S(2)}) %collective-permute-start.2) | collective-permute-done | bytes 147488 | tf_op jit(solution)/shard_map/ppermute | solution.py:23
  16.9 0.2 pad_maximum_fusion.1
  17.1 0.3 constant_dynamic-slice_fusion
  17.4 0.8 %pad_slice_fusion.1 = (bf16[6,18,32,64]{3,2,1,0:T(8,128)(2,1)S(1)}, bf16[6,18,32,64]{3,2,1,0:T(8,128)(2,1)S(1)}) fusion(bf16[6,18,32,64]{3,2,1,0:T(8,128)(2,1)S(1)} %constant_dynamic-slice_fusion), kind=kLoop, calls=%fused_computation.12 | loop fusion | bytes 1327104 | tf_op jit(solution)/shard_map/slice | solution.py:73
  18.2 0.9 %pad_maximum_fusion = bf16[6,18,32,192]{3,2,1,0:T(8,128)(2,1)S(1)} fusion(bf16[6,18,32,64]{3,2,1,0:T(8,128)(2,1)S(1)} %get-tuple-element.5, bf16[6,18,32,64]{3,2,1,0:T(8,128)(2,1)S(1)} %constant_dynamic-slice_fusion, bf16[6,18,32,64]{3,2,1,0:T(8,128)(2,1)S(1)} %get-tuple-element.4), kind=kLoop, calls=%fused_computation.2 | loop fusion | flops 3981312 | bytes 2654208 | tf_op jit(solution)/shard_map/concatenate | solution.py:73
  19.0 0.2 copy-done.2
  19.2 0.5 fusion.25
  19.7 0.5 fusion.26
  20.1 0.5 fusion.24
  20.6 0.5 fusion.23
  21.2 0.1 slice.128
  21.3 0.5 fusion.29
  21.8 0.1 slice.122
  21.9 0.5 fusion.30
  22.4 0.5 fusion.27
  22.9 0.5 fusion.28
  23.7 0.5 fusion.31
  24.2 0.2 fusion.51
  24.8 0.1 fusion.22
  25.1 0.1 maximum_bitcast_fusion
  25.1 0.1 maximum_bitcast_fusion.3
  25.3 0.1 maximum_bitcast_fusion.2
  25.4 0.1 maximum_bitcast_fusion.6
  25.5 0.1 fusion.15
  25.6 1.6 %collective-permute-start.3 = (f32[4,432,64]{1,2,0:T(8,128)S(1)}, f32[4,432,64]{1,2,0:T(8,128)S(1)}, u32[]{:S(2)}, u32[]{:S(2)}) collective-permute-start(f32[4,432,64]{1,2,0:T(8,128)S(1)} %fusion.15), channel_id=1, source_target_pairs={{0,2},{2,0},{1,3},{3,1},{4,6},{6,4},{5,7},{7,5},{8,10},{10,8},{9,1... | collective-permute-start | bytes 1327112 | tf_op jit(solution)/shard_map/ppermute | solution.py:93
  27.2 0.4 copy.28
  27.6 0.2 pad.5.clone
  27.8 0.1 copy.7
  28.0 0.1 slice.119
  28.1 0.4 copy-done.3
  28.5 4.7 %fusion.11 = bf16[4,16,8,5,128]{4,2,3,1,0:T(8,128)(2,1)S(1)} fusion(bf16[3,3,3,128,128]{4,3,2,1,0:T(8,128)(2,1)S(1)} %bitcast.191, bf16[6,18,1,7,2,128]{5,3,4,1,0,2:T(8,128)(2,1)S(1)} %slice.119, bf16[6,18,1,8,5,128]{5,3,4,1,0,2:T(8,128)(2,1)S(1)} %copy.7, pred[8,5]{0,1:T(8,128)(4,1)S(1)} %copy-done.3), kind=kOutput, calls=%fused_computation.10 | convolution fusion | flops 2270224384 | bytes 3033128 | tf_op jit(solution)/shard_map/conv_general_dilated | solution.py:65
  33.2 0.1 copy.8
  33.3 4.7 %collective-permute-done.3 = f32[4,432,64]{1,2,0:T(8,128)S(1)} collective-permute-done((f32[4,432,64]{1,2,0:T(8,128)S(1)}, f32[4,432,64]{1,2,0:T(8,128)S(1)}, u32[]{:S(2)}, u32[]{:S(2)}) %collective-permute-start.3) | collective-permute-done | bytes 442400 | tf_op jit(solution)/shard_map/ppermute | solution.py:93
  38.0 0.2 select_add_fusion
  38.2 1.7 %collective-permute-start.4 = (f32[432,64]{0,1:T(8,128)S(1)}, f32[432,64]{0,1:T(8,128)S(1)}, u32[]{:S(2)}, u32[]{:S(2)}) collective-permute-start(f32[432,64]{0,1:T(8,128)S(1)} %get-tuple-element.8), channel_id=1, source_target_pairs={{0,4},{4,8},{8,12},{12,0},{1,5},{5,9},{9,13},{13,1},{2,6},{6,10},{... | collective-permute-start | bytes 331784 | tf_op jit(solution)/shard_map/ppermute | solution.py:40
  40.0 1.1 %collective-permute-start.5 = (f32[432,64]{0,1:T(8,128)S(1)}, f32[432,64]{0,1:T(8,128)S(1)}, u32[]{:S(2)}, u32[]{:S(2)}) collective-permute-start(f32[432,64]{0,1:T(8,128)S(1)} %get-tuple-element.10), channel_id=1, source_target_pairs={{0,8},{4,12},{8,0},{12,4},{1,9},{5,13},{9,1},{13,5},{2,10},{6,14},... | collective-permute-start | bytes 331784 | tf_op jit(solution)/shard_map/ppermute | solution.py:40
  41.1 1.4 %collective-permute-start.6 = (f32[432,64]{0,1:T(8,128)S(1)}, f32[432,64]{0,1:T(8,128)S(1)}, u32[]{:S(2)}, u32[]{:S(2)}) collective-permute-start(f32[432,64]{0,1:T(8,128)S(1)} %get-tuple-element.9), channel_id=1, source_target_pairs={{0,12},{4,0},{8,4},{12,8},{1,13},{5,1},{9,5},{13,9},{2,14},{6,2},{... | collective-permute-start | bytes 331784 | tf_op jit(solution)/shard_map/ppermute | solution.py:40
  42.5 0.9 %copy.18 = bf16[4,16,32,128]{3,2,1,0:T(8,128)(2,1)} copy(bf16[4,16,32,128]{3,1,2,0:T(8,128)(2,1)S(1)} %slice_bitcast_fusion) | data formatting | bytes 1048576
  43.4 2.8 %collective-permute-done.4 = f32[432,64]{0,1:T(8,128)S(1)} collective-permute-done((f32[432,64]{0,1:T(8,128)S(1)}, f32[432,64]{0,1:T(8,128)S(1)}, u32[]{:S(2)}, u32[]{:S(2)}) %collective-permute-start.4) | collective-permute-done | bytes 110624 | tf_op jit(solution)/shard_map/ppermute | solution.py:40
  46.1 3.6 %collective-permute-done.5 = f32[432,64]{0,1:T(8,128)S(1)} collective-permute-done((f32[432,64]{0,1:T(8,128)S(1)}, f32[432,64]{0,1:T(8,128)S(1)}, u32[]{:S(2)}, u32[]{:S(2)}) %collective-permute-start.5) | collective-permute-done | bytes 110624 | tf_op jit(solution)/shard_map/ppermute | solution.py:40
  49.8 0.7 %fusion.18 = f32[432,64]{0,1:T(8,128)} fusion(f32[432,64]{0,1:T(8,128)S(1)} %collective-permute-done.6, f32[432,64]{0,1:T(8,128)S(1)} %collective-permute-done.5, f32[432,64]{0,1:T(8,128)S(1)} %collective-permute-done.4, f32[4,432,64]{1,2,0:T(8,128)S(1)} %select_add_fusion, s32[]{:T(128)S(6)} %select_n.88), kind=kLoop, calls=%fused_computation.36 | loop fusion | flops 110592 | bytes 552964 | tf_op jit(solution)/shard_map/div | solution.py:100
  (38 shorter events, 1.2 us)
Async XLA Ops:
  0.6 27.5 %copy-start = (bf16[27,128,128]{2,1,0:T(8,128)(2,1)S(1)}, bf16[27,128,128]{2,1,0:T(8,128)(2,1)}, u32[]{:S(2)}) copy-start(bf16[27,128,128]{2,1,0:T(8,128)(2,1)} %param.5) | copy-start | bytes 2654212
  0.6 16.3 %copy-start.1 = (bf16[4,16,32,128]{3,2,1,0:T(8,128)(2,1)S(1)}, bf16[4,16,32,128]{3,2,1,0:T(8,128)(2,1)}, u32[]{:S(2)}) copy-start(bf16[4,16,32,128]{3,2,1,0:T(8,128)(2,1)} %param.4) | copy-start | bytes 1572868
  1.6 4.8 %collective-permute-start = (bf16[4,1,32,128]{3,2,1,0:T(8,128)(2,1)S(1)}, bf16[4,1,32,128]{3,2,1,0:T(8,128)(2,1)S(1)}, u32[]{:S(2)}, u32[]{:S(2)}) collective-permute-start(bf16[4,1,32,128]{3,2,1,0:T(8,128)(2,1)S(1)} %slice_select_fusion), channel_id=1, source_target_pairs={{0,2},{2,0},{1,3},{3,1},{4,6},{6,4},{5,7},{7,5},{8,10},{10,8},{9,1... | collective-permute-start | bytes 98312 | tf_op jit(solution)/shard_map/ppermute | solution.py:17
  7.4 8.5 %collective-permute-start.1 = (bf16[1,18,32,128]{3,2,1,0:T(8,128)(2,1)S(1)}, bf16[1,18,32,128]{3,2,1,0:T(8,128)(2,1)S(1)}, u32[]{:S(2)}, u32[]{:S(2)}) collective-permute-start(bf16[1,18,32,128]{3,2,1,0:T(8,128)(2,1)S(1)} %get-tuple-element.6), channel_id=1, source_target_pairs={{0,4},{4,8},{8,12},{12,0},{1,5},{5,9},{9,13},{13,1},{2,6},{6,10},{... | collective-permute-start | bytes 442376 | tf_op jit(solution)/shard_map/ppermute | solution.py:22
  9.6 7.3 %collective-permute-start.2 = (bf16[1,18,32,128]{3,2,1,0:T(8,128)(2,1)S(1)}, bf16[1,18,32,128]{3,2,1,0:T(8,128)(2,1)S(1)}, u32[]{:S(2)}, u32[]{:S(2)}) collective-permute-start(bf16[1,18,32,128]{3,2,1,0:T(8,128)(2,1)S(1)} %get-tuple-element.7), channel_id=1, source_target_pairs={{4,0},{8,4},{12,8},{0,12},{5,1},{9,5},{13,9},{1,13},{6,2},{10,6},{... | collective-permute-start | bytes 442376 | tf_op jit(solution)/shard_map/ppermute | solution.py:23
  18.2 1.0 %copy-start.2 = (bf16[4,16,32,128]{3,2,1,0:T(8,128)(2,1)S(1)}, bf16[4,16,32,128]{3,2,1,0:T(8,128)(2,1)}, u32[]{:S(2)}) copy-start(bf16[4,16,32,128]{3,2,1,0:T(8,128)(2,1)} %param.3) | copy-start | bytes 1572868
  25.6 12.4 %collective-permute-start.3 = (f32[4,432,64]{1,2,0:T(8,128)S(1)}, f32[4,432,64]{1,2,0:T(8,128)S(1)}, u32[]{:S(2)}, u32[]{:S(2)}) collective-permute-start(f32[4,432,64]{1,2,0:T(8,128)S(1)} %fusion.15), channel_id=1, source_target_pairs={{0,2},{2,0},{1,3},{3,1},{4,6},{6,4},{5,7},{7,5},{8,10},{10,8},{9,1... | collective-permute-start | bytes 1327112 | tf_op jit(solution)/shard_map/ppermute | solution.py:93
  27.8 0.7 %copy-start.3 = (pred[8,5]{0,1:T(8,128)(4,1)S(1)}, pred[8,5]{0,1:T(8,128)(4,1)}, u32[]{:S(2)}) copy-start(pred[8,5]{0,1:T(8,128)(4,1)} %constant.67) | copy-start | bytes 124
  38.2 7.9 %collective-permute-start.4 = (f32[432,64]{0,1:T(8,128)S(1)}, f32[432,64]{0,1:T(8,128)S(1)}, u32[]{:S(2)}, u32[]{:S(2)}) collective-permute-start(f32[432,64]{0,1:T(8,128)S(1)} %get-tuple-element.8), channel_id=1, source_target_pairs={{0,4},{4,8},{8,12},{12,0},{1,5},{5,9},{9,13},{13,1},{2,6},{6,10},{... | collective-permute-start | bytes 331784 | tf_op jit(solution)/shard_map/ppermute | solution.py:40
  40.0 9.8 %collective-permute-start.5 = (f32[432,64]{0,1:T(8,128)S(1)}, f32[432,64]{0,1:T(8,128)S(1)}, u32[]{:S(2)}, u32[]{:S(2)}) collective-permute-start(f32[432,64]{0,1:T(8,128)S(1)} %get-tuple-element.10), channel_id=1, source_target_pairs={{0,8},{4,12},{8,0},{12,4},{1,9},{5,13},{9,1},{13,5},{2,10},{6,14},... | collective-permute-start | bytes 331784 | tf_op jit(solution)/shard_map/ppermute | solution.py:40
  41.1 8.7 %collective-permute-start.6 = (f32[432,64]{0,1:T(8,128)S(1)}, f32[432,64]{0,1:T(8,128)S(1)}, u32[]{:S(2)}, u32[]{:S(2)}) collective-permute-start(f32[432,64]{0,1:T(8,128)S(1)} %get-tuple-element.9), channel_id=1, source_target_pairs={{0,12},{4,0},{8,4},{12,8},{1,13},{5,1},{9,5},{13,9},{2,14},{6,2},{... | collective-permute-start | bytes 331784 | tf_op jit(solution)/shard_map/ppermute | solution.py:40

commit v11 on v10

--- a/solution.py
+++ b/solution.py
@@ -88,14 +88,20 @@
             jnp.stack([take_rows(pieces, (gx * 2 + y) * owned_rows, owned_rows) for gx in range(nx)])
             for y in range(2)
         ]
-        keep = jnp.where(iy == 0, side[0], side[1])
-        send = jnp.where(iy == 0, side[1], side[0])
-        partial = keep + lax.ppermute(send, "gy", [(0, 1), (1, 0)])
+        split = owned_rows // 2 if owned_rows % 16 == 0 else owned_rows
+        parts = []
+        for lo, hi in ((0, split), (split, owned_rows)):
+            if lo == hi:
+                continue
+            keep = jnp.where(iy == 0, side[0][:, lo:hi], side[1][:, lo:hi])
+            send = jnp.where(iy == 0, side[1][:, lo:hi], side[0][:, lo:hi])
+            partial = keep + lax.ppermute(send, "gy", [(0, 1), (1, 0)])
+            parts.append(scatter_sum(partial, "gx", 0))
+        owned = jnp.concatenate(parts, axis=0) if len(parts) > 1 else parts[0]
     else:
         weight_terms = jnp.concatenate(pieces, axis=0)
         blocks = weight_terms.reshape(nx, ny, owned_rows, half)
-        partial = scatter_sum(blocks, "gy", 1)
-    owned = scatter_sum(partial, "gx", 0)
+        owned = scatter_sum(scatter_sum(blocks, "gy", 1), "gx", 0)
     total_cells = size_x * lax.axis_size("gx") * size_y * lax.axis_size("gy") * depth
     grad_weight = owned / jnp.sqrt(jnp.float32(total_cells))
     return (grad_in, grad_weight)

time: 50.7 us -> 50.5 us (level)
  waiting for transfers between devices: 18.1 us -> 13.2 us
  starting transfers between devices: 13 us -> 17 us
    ppermute x1 -> x2, waiting for transfers between devices: 4.69 us -> 0.75 us  [on_device(): partial = keep + lax.ppermute(send, 'gy', [(0, 1), (1, 0)])]
    ppermute x3 -> x6, starting transfers between devices: 4.18 us -> 7.58 us  [scatter_sum(): lax.ppermute(part, axis, [(j, (j + shift) % count) for j in range(count)])]
    ppermute x3 -> x6, waiting for transfers between devices: 6.37 us -> 5.41 us  [scatter_sum(): lax.ppermute(part, axis, [(j, (j + shift) % count) for j in range(count)])]
    ppermute x1 -> x2, starting transfers between devices: 1.56 us -> 2.15 us  [on_device(): partial = keep + lax.ppermute(send, 'gy', [(0, 1), (1, 0)])]
  transfers between devices with their start and end apart: 7 -> 11, of which waited for: 6 -> 6; matrix products, arithmetic and copies ran while one was open for 13% -> 14% of each run, Pallas kernels for 0% -> 0%
where the time goes in v11:
time: 50.5 us; the launch traced here: 50.3 us
  starting transfers between devices  17 us (34%)
  waiting for transfers between devices  13.2 us (26%)
  matrix products  9.1 us (18%)
  other arithmetic  4.95 us (10%)
  local copies, waits for them, and re-layouts  4.93 us (10%)
  between operations  1.11 us (2%)
    ppermute x6, starting transfers between devices, scatter_sum(): lax.ppermute(part, axis, [(j, (j + shift) % count) for j in range(count)])  7.58 us
    ppermute x6, waiting for transfers between devices, scatter_sum(): lax.ppermute(part, axis, [(j, (j + shift) % count) for j in range(count)])  5.41 us
    conv_general_dilated x1, matrix products, on_device(): lax.conv_general_dilated(gh[None], kflip, (1, 1, 1), pad, dimension_numbe...  4.96 us
    ppermute x1, waiting for transfers between devices, with_halo(): low = lax.ppermute(tail, axis, [(i, (i + 1) % count) for i in range(count)])  4.21 us
    dot_general x9, matrix products, on_device(): lax.dot_general(x_act, window, (((0, 1, 2), (0, 1, 2)), ((), ())), prefer...  4.14 us
    ppermute x1, starting transfers between devices, with_halo(): got = lax.ppermute(jnp.where(me == 0, tail, head), axis, [(0, 1), (1, 0)])  2.94 us
    ppermute x1, starting transfers between devices, with_halo(): low = lax.ppermute(tail, axis, [(i, (i + 1) % count) for i in range(count)])  2.16 us
    ppermute x2, starting transfers between devices, on_device(): partial = keep + lax.ppermute(send, 'gy', [(0, 1), (1, 0)])  2.15 us
  transfers between devices with their start and end apart: 11, of which 6 were waited for; matrix products, arithmetic and copies ran while one was open for 14% of the time, Pallas kernels for 0%

profile of v11, /device:TPU:0, one launch (start us, length us, event | category | flops | bytes accessed | tf_op | source)
XLA Modules:
  0.0 50.3 jit_solution(17374829293495079328)
XLA Ops:
  0.7 0.9 %slice_select_fusion.2 = bf16[4,1,32,128]{3,2,1,0:T(8,128)(2,1)S(1)} fusion(bf16[4,16,32,128]{3,2,1,0:T(8,128)(2,1)} %param.4, pred[]{:T(512)S(6)} %eq.26), kind=kLoop, calls=%fused_computation.57 | loop fusion | flops 16384 | bytes 98305 | tf_op jit(solution)/shard_map/jit(_where)/select_n | solution.py:17
  1.6 2.9 %collective-permute-start = (bf16[4,1,32,128]{3,2,1,0:T(8,128)(2,1)S(1)}, bf16[4,1,32,128]{3,2,1,0:T(8,128)(2,1)S(1)}, u32[]{:S(2)}, u32[]{:S(2)}) collective-permute-start(bf16[4,1,32,128]{3,2,1,0:T(8,128)(2,1)S(1)} %slice_select_fusion.2), channel_id=1, source_target_pairs={{0,2},{2,0},{1,3},{3,1},{4,6},{6,4},{5,7},{7,5},{8,10},{10,8},{9,1... | collective-permute-start | bytes 98312 | tf_op jit(solution)/shard_map/ppermute | solution.py:17
  4.5 1.9 %collective-permute-done = bf16[4,1,32,128]{3,2,1,0:T(8,128)(2,1)S(1)} collective-permute-done((bf16[4,1,32,128]{3,2,1,0:T(8,128)(2,1)S(1)}, bf16[4,1,32,128]{3,2,1,0:T(8,128)(2,1)S(1)}, u32[]{:S(2)}, u32[]{:S(2)}) %collective-permute-start) | collective-permute-done | bytes 32800 | tf_op jit(solution)/shard_map/ppermute | solution.py:17
  6.4 1.0 %pad_maximum_fusion.6 = (bf16[1,18,32,128]{3,2,1,0:T(8,128)(2,1)S(1)}, bf16[1,18,32,128]{3,2,1,0:T(8,128)(2,1)S(1)}) fusion(bf16[4,1,32,128]{3,2,1,0:T(8,128)(2,1)S(1)} %get-tuple-element.19, bf16[4,16,32,128]{3,2,1,0:T(8,128)(2,1)} %param.4, bf16[4,1,32,128]{3,2,1,0:T(8,128)(2,1)S(1)} %get-tuple-element.18), kind=kLoop, calls=%fused_computation.24 | loop fusion | flops 294912 | bytes 884736 | tf_op jit(solution)/shard_map/slice | solution.py:11
  7.4 2.2 %collective-permute-start.1 = (bf16[1,18,32,128]{3,2,1,0:T(8,128)(2,1)S(1)}, bf16[1,18,32,128]{3,2,1,0:T(8,128)(2,1)S(1)}, u32[]{:S(2)}, u32[]{:S(2)}) collective-permute-start(bf16[1,18,32,128]{3,2,1,0:T(8,128)(2,1)S(1)} %get-tuple-element.8), channel_id=1, source_target_pairs={{0,4},{4,8},{8,12},{12,0},{1,5},{5,9},{9,13},{13,1},{2,6},{6,10},{... | collective-permute-start | bytes 442376 | tf_op jit(solution)/shard_map/ppermute | solution.py:22
  9.6 2.1 %collective-permute-start.2 = (bf16[1,18,32,128]{3,2,1,0:T(8,128)(2,1)S(1)}, bf16[1,18,32,128]{3,2,1,0:T(8,128)(2,1)S(1)}, u32[]{:S(2)}, u32[]{:S(2)}) collective-permute-start(bf16[1,18,32,128]{3,2,1,0:T(8,128)(2,1)S(1)} %get-tuple-element.9), channel_id=1, source_target_pairs={{4,0},{8,4},{12,8},{0,12},{5,1},{9,5},{13,9},{1,13},{6,2},{10,6},{... | collective-permute-start | bytes 442376 | tf_op jit(solution)/shard_map/ppermute | solution.py:23
  11.7 4.2 %collective-permute-done.1 = bf16[1,18,32,128]{3,2,1,0:T(8,128)(2,1)S(1)} collective-permute-done((bf16[1,18,32,128]{3,2,1,0:T(8,128)(2,1)S(1)}, bf16[1,18,32,128]{3,2,1,0:T(8,128)(2,1)S(1)}, u32[]{:S(2)}, u32[]{:S(2)}) %collective-permute-start.1) | collective-permute-done | bytes 147488 | tf_op jit(solution)/shard_map/ppermute | solution.py:22
  15.9 0.9 %collective-permute-done.2 = bf16[1,18,32,128]{3,2,1,0:T(8,128)(2,1)S(1)} collective-permute-done((bf16[1,18,32,128]{3,2,1,0:T(8,128)(2,1)S(1)}, bf16[1,18,32,128]{3,2,1,0:T(8,128)(2,1)S(1)}, u32[]{:S(2)}, u32[]{:S(2)}) %collective-permute-start.2) | collective-permute-done | bytes 147488 | tf_op jit(solution)/shard_map/ppermute | solution.py:23
  16.9 0.2 pad_maximum_fusion.1
  17.1 0.3 constant_dynamic-slice_fusion
  17.4 0.8 %pad_slice_fusion.1 = (bf16[6,18,32,64]{3,2,1,0:T(8,128)(2,1)S(1)}, bf16[6,18,32,64]{3,2,1,0:T(8,128)(2,1)S(1)}) fusion(bf16[6,18,32,64]{3,2,1,0:T(8,128)(2,1)S(1)} %constant_dynamic-slice_fusion), kind=kLoop, calls=%fused_computation.12 | loop fusion | bytes 1327104 | tf_op jit(solution)/shard_map/slice | solution.py:73
  18.2 0.9 %pad_maximum_fusion = bf16[6,18,32,192]{3,2,1,0:T(8,128)(2,1)S(1)} fusion(bf16[6,18,32,64]{3,2,1,0:T(8,128)(2,1)S(1)} %get-tuple-element.7, bf16[6,18,32,64]{3,2,1,0:T(8,128)(2,1)S(1)} %constant_dynamic-slice_fusion, bf16[6,18,32,64]{3,2,1,0:T(8,128)(2,1)S(1)} %get-tuple-element.6), kind=kLoop, calls=%fused_computation.2 | loop fusion | flops 3981312 | bytes 2654208 | tf_op jit(solution)/shard_map/concatenate | solution.py:73
  19.0 0.2 copy-done.2
  19.2 0.5 fusion.25
  19.7 0.5 fusion.26
  20.1 0.5 fusion.24
  20.6 0.5 fusion.23
  21.1 0.5 fusion.29
  21.5 0.5 fusion.30
  22.0 0.5 fusion.27
  22.5 0.5 fusion.28
  23.7 0.5 fusion.31
  24.2 0.2 fusion.51
  25.0 0.1 maximum_bitcast_fusion.3
  25.1 0.1 maximum_bitcast_fusion.7
  25.3 0.1 maximum_bitcast_fusion.2
  25.5 0.1 maximum_bitcast_fusion.4
  25.7 1.6 %collective-permute-start.3 = (f32[4,216,64]{1,2,0:T(8,128)S(1)}, f32[4,216,64]{1,2,0:T(8,128)S(1)}, u32[]{:S(2)}, u32[]{:S(2)}) collective-permute-start(f32[4,216,64]{1,2,0:T(8,128)S(1)} %slice_select_fusion.1), channel_id=1, source_target_pairs={{0,2},{2,0},{1,3},{3,1},{4,6},{6,4},{5,7},{7,5},{8,10},{10,8},{9,1... | collective-permute-start | bytes 663560 | tf_op jit(solution)/shard_map/ppermute | solution.py:98
  27.3 0.4 copy.28
  27.7 0.2 pad.5.clone
  27.9 0.1 copy.7
  28.1 0.1 slice.139
  28.2 0.4 copy-done.3
  28.6 5.0 %fusion.11 = bf16[4,16,8,5,128]{4,2,3,1,0:T(8,128)(2,1)S(1)} fusion(bf16[3,3,3,128,128]{4,3,2,1,0:T(8,128)(2,1)S(1)} %bitcast.201, bf16[6,18,1,7,2,128]{5,3,4,1,0,2:T(8,128)(2,1)S(1)} %slice.139, bf16[6,18,1,8,5,128]{5,3,4,1,0,2:T(8,128)(2,1)S(1)} %copy.7, pred[8,5]{0,1:T(8,128)(4,1)S(1)} %copy-done.3), kind=kOutput, calls=%fused_computation.10 | convolution fusion | flops 2270224384 | bytes 3033128 | tf_op jit(solution)/shard_map/conv_general_dilated | solution.py:65
  33.6 0.1 copy.8
  33.7 0.2 select_add_fusion.1
  33.9 0.6 %collective-permute-start.7 = (f32[4,216,64]{1,2,0:T(8,128)S(1)}, f32[4,216,64]{1,2,0:T(8,128)S(1)}, u32[]{:S(2)}, u32[]{:S(2)}) collective-permute-start(f32[4,216,64]{1,2,0:T(8,128)S(1)} %get-tuple-element.5), channel_id=1, source_target_pairs={{0,2},{2,0},{1,3},{3,1},{4,6},{6,4},{5,7},{7,5},{8,10},{10,8},{9,1... | collective-permute-start | bytes 663560 | tf_op jit(solution)/shard_map/ppermute | solution.py:98
  34.5 0.9 %copy.18 = bf16[4,16,32,128]{3,2,1,0:T(8,128)(2,1)} copy(bf16[4,16,32,128]{3,1,2,0:T(8,128)(2,1)S(1)} %slice_bitcast_fusion) | data formatting | bytes 1048576
  35.5 1.4 %collective-permute-start.4 = (f32[216,64]{0,1:T(8,128)S(1)}, f32[216,64]{0,1:T(8,128)S(1)}, u32[]{:S(2)}, u32[]{:S(2)}) collective-permute-start(f32[216,64]{0,1:T(8,128)S(1)} %get-tuple-element.10), channel_id=1, source_target_pairs={{0,4},{4,8},{8,12},{12,0},{1,5},{5,9},{9,13},{13,1},{2,6},{6,10},{... | collective-permute-start | bytes 165896 | tf_op jit(solution)/shard_map/ppermute | solution.py:40
  36.9 2.0 %collective-permute-start.5 = (f32[216,64]{0,1:T(8,128)S(1)}, f32[216,64]{0,1:T(8,128)S(1)}, u32[]{:S(2)}, u32[]{:S(2)}) collective-permute-start(f32[216,64]{0,1:T(8,128)S(1)} %get-tuple-element.12), channel_id=1, source_target_pairs={{0,8},{4,12},{8,0},{12,4},{1,9},{5,13},{9,1},{13,5},{2,10},{6,14},... | collective-permute-start | bytes 165896 | tf_op jit(solution)/shard_map/ppermute | solution.py:40
  38.9 0.7 %collective-permute-start.6 = (f32[216,64]{0,1:T(8,128)S(1)}, f32[216,64]{0,1:T(8,128)S(1)}, u32[]{:S(2)}, u32[]{:S(2)}) collective-permute-start(f32[216,64]{0,1:T(8,128)S(1)} %get-tuple-element.11), channel_id=1, source_target_pairs={{0,12},{4,0},{8,4},{12,8},{1,13},{5,1},{9,5},{13,9},{2,14},{6,2},{... | collective-permute-start | bytes 165896 | tf_op jit(solution)/shard_map/ppermute | solution.py:40
  39.6 0.7 %collective-permute-done.7 = f32[4,216,64]{1,2,0:T(8,128)S(1)} collective-permute-done((f32[4,216,64]{1,2,0:T(8,128)S(1)}, f32[4,216,64]{1,2,0:T(8,128)S(1)}, u32[]{:S(2)}, u32[]{:S(2)}) %collective-permute-start.7) | collective-permute-done | bytes 221216 | tf_op jit(solution)/shard_map/ppermute | solution.py:98
  40.3 0.2 select_add_fusion
  40.6 2.8 %collective-permute-start.10 = (f32[216,64]{0,1:T(8,128)S(1)}, f32[216,64]{0,1:T(8,128)S(1)}, u32[]{:S(2)}, u32[]{:S(2)}) collective-permute-start(f32[216,64]{0,1:T(8,128)S(1)} %get-tuple-element.14), channel_id=1, source_target_pairs={{0,12},{4,0},{8,4},{12,8},{1,13},{5,1},{9,5},{13,9},{2,14},{6,2},{... | collective-permute-start | bytes 165896 | tf_op jit(solution)/shard_map/ppermute | solution.py:40
  43.4 0.6 %collective-permute-start.9 = (f32[216,64]{0,1:T(8,128)S(1)}, f32[216,64]{0,1:T(8,128)S(1)}, u32[]{:S(2)}, u32[]{:S(2)}) collective-permute-start(f32[216,64]{0,1:T(8,128)S(1)} %get-tuple-element.15), channel_id=1, source_target_pairs={{0,8},{4,12},{8,0},{12,4},{1,9},{5,13},{9,1},{13,5},{2,10},{6,14},... | collective-permute-start | bytes 165896 | tf_op jit(solution)/shard_map/ppermute | solution.py:40
  44.1 1.5 %collective-permute-done.10 = f32[216,64]{0,1:T(8,128)S(1)} collective-permute-done((f32[216,64]{0,1:T(8,128)S(1)}, f32[216,64]{0,1:T(8,128)S(1)}, u32[]{:S(2)}, u32[]{:S(2)}) %collective-permute-start.10) | collective-permute-done | bytes 55328 | tf_op jit(solution)/shard_map/ppermute | solution.py:40
  45.6 3.9 %collective-permute-done.8 = f32[216,64]{0,1:T(8,128)S(1)} collective-permute-done((f32[216,64]{0,1:T(8,128)S(1)}, f32[216,64]{0,1:T(8,128)S(1)}, u32[]{:S(2)}, u32[]{:S(2)}) %collective-permute-start.8) | collective-permute-done | bytes 55328 | tf_op jit(solution)/shard_map/ppermute | solution.py:40
  49.5 0.8 %maximum_multiply_fusion = f32[432,64]{0,1:T(8,128)} fusion(f32[216,64]{0,1:T(8,128)S(1)} %fusion.16, f32[216,64]{0,1:T(8,128)S(1)} %fusion.18), kind=kLoop, calls=%fused_computation.35 | loop fusion | flops 55296 | bytes 221184 | tf_op jit(solution)/shard_map/div | solution.py:106
  (53 shorter events, 1.7 us)
Async XLA Ops:
  0.6 27.6 %copy-start = (bf16[27,128,128]{2,1,0:T(8,128)(2,1)S(1)}, bf16[27,128,128]{2,1,0:T(8,128)(2,1)}, u32[]{:S(2)}) copy-start(bf16[27,128,128]{2,1,0:T(8,128)(2,1)} %param.5) | copy-start | bytes 2654212
  0.6 16.3 %copy-start.1 = (bf16[4,16,32,128]{3,2,1,0:T(8,128)(2,1)S(1)}, bf16[4,16,32,128]{3,2,1,0:T(8,128)(2,1)}, u32[]{:S(2)}) copy-start(bf16[4,16,32,128]{3,2,1,0:T(8,128)(2,1)} %param.4) | copy-start | bytes 1572868
  1.6 4.8 %collective-permute-start = (bf16[4,1,32,128]{3,2,1,0:T(8,128)(2,1)S(1)}, bf16[4,1,32,128]{3,2,1,0:T(8,128)(2,1)S(1)}, u32[]{:S(2)}, u32[]{:S(2)}) collective-permute-start(bf16[4,1,32,128]{3,2,1,0:T(8,128)(2,1)S(1)} %slice_select_fusion.2), channel_id=1, source_target_pairs={{0,2},{2,0},{1,3},{3,1},{4,6},{6,4},{5,7},{7,5},{8,10},{10,8},{9,1... | collective-permute-start | bytes 98312 | tf_op jit(solution)/shard_map/ppermute | solution.py:17
  7.4 8.5 %collective-permute-start.1 = (bf16[1,18,32,128]{3,2,1,0:T(8,128)(2,1)S(1)}, bf16[1,18,32,128]{3,2,1,0:T(8,128)(2,1)S(1)}, u32[]{:S(2)}, u32[]{:S(2)}) collective-permute-start(bf16[1,18,32,128]{3,2,1,0:T(8,128)(2,1)S(1)} %get-tuple-element.8), channel_id=1, source_target_pairs={{0,4},{4,8},{8,12},{12,0},{1,5},{5,9},{9,13},{13,1},{2,6},{6,10},{... | collective-permute-start | bytes 442376 | tf_op jit(solution)/shard_map/ppermute | solution.py:22
  9.6 7.3 %collective-permute-start.2 = (bf16[1,18,32,128]{3,2,1,0:T(8,128)(2,1)S(1)}, bf16[1,18,32,128]{3,2,1,0:T(8,128)(2,1)S(1)}, u32[]{:S(2)}, u32[]{:S(2)}) collective-permute-start(bf16[1,18,32,128]{3,2,1,0:T(8,128)(2,1)S(1)} %get-tuple-element.9), channel_id=1, source_target_pairs={{4,0},{8,4},{12,8},{0,12},{5,1},{9,5},{13,9},{1,13},{6,2},{10,6},{... | collective-permute-start | bytes 442376 | tf_op jit(solution)/shard_map/ppermute | solution.py:23
  18.2 1.0 %copy-start.2 = (bf16[4,16,32,128]{3,2,1,0:T(8,128)(2,1)S(1)}, bf16[4,16,32,128]{3,2,1,0:T(8,128)(2,1)}, u32[]{:S(2)}) copy-start(bf16[4,16,32,128]{3,2,1,0:T(8,128)(2,1)} %param.3) | copy-start | bytes 1572868
  25.7 8.0 %collective-permute-start.3 = (f32[4,216,64]{1,2,0:T(8,128)S(1)}, f32[4,216,64]{1,2,0:T(8,128)S(1)}, u32[]{:S(2)}, u32[]{:S(2)}) collective-permute-start(f32[4,216,64]{1,2,0:T(8,128)S(1)} %slice_select_fusion.1), channel_id=1, source_target_pairs={{0,2},{2,0},{1,3},{3,1},{4,6},{6,4},{5,7},{7,5},{8,10},{10,8},{9,1... | collective-permute-start | bytes 663560 | tf_op jit(solution)/shard_map/ppermute | solution.py:98
  27.9 0.7 %copy-start.3 = (pred[8,5]{0,1:T(8,128)(4,1)S(1)}, pred[8,5]{0,1:T(8,128)(4,1)}, u32[]{:S(2)}) copy-start(pred[8,5]{0,1:T(8,128)(4,1)} %constant.81) | copy-start | bytes 124
  33.9 6.4 %collective-permute-start.7 = (f32[4,216,64]{1,2,0:T(8,128)S(1)}, f32[4,216,64]{1,2,0:T(8,128)S(1)}, u32[]{:S(2)}, u32[]{:S(2)}) collective-permute-start(f32[4,216,64]{1,2,0:T(8,128)S(1)} %get-tuple-element.5), channel_id=1, source_target_pairs={{0,2},{2,0},{1,3},{3,1},{4,6},{6,4},{5,7},{7,5},{8,10},{10,8},{9,1... | collective-permute-start | bytes 663560 | tf_op jit(solution)/shard_map/ppermute | solution.py:98
  35.5 7.9 %collective-permute-start.4 = (f32[216,64]{0,1:T(8,128)S(1)}, f32[216,64]{0,1:T(8,128)S(1)}, u32[]{:S(2)}, u32[]{:S(2)}) collective-permute-start(f32[216,64]{0,1:T(8,128)S(1)} %get-tuple-element.10), channel_id=1, source_target_pairs={{0,4},{4,8},{8,12},{12,0},{1,5},{5,9},{9,13},{13,1},{2,6},{6,10},{... | collective-permute-start | bytes 165896 | tf_op jit(solution)/shard_map/ppermute | solution.py:40
  36.9 7.1 %collective-permute-start.5 = (f32[216,64]{0,1:T(8,128)S(1)}, f32[216,64]{0,1:T(8,128)S(1)}, u32[]{:S(2)}, u32[]{:S(2)}) collective-permute-start(f32[216,64]{0,1:T(8,128)S(1)} %get-tuple-element.12), channel_id=1, source_target_pairs={{0,8},{4,12},{8,0},{12,4},{1,9},{5,13},{9,1},{13,5},{2,10},{6,14},... | collective-permute-start | bytes 165896 | tf_op jit(solution)/shard_map/ppermute | solution.py:40
  38.9 5.2 %collective-permute-start.6 = (f32[216,64]{0,1:T(8,128)S(1)}, f32[216,64]{0,1:T(8,128)S(1)}, u32[]{:S(2)}, u32[]{:S(2)}) collective-permute-start(f32[216,64]{0,1:T(8,128)S(1)} %get-tuple-element.11), channel_id=1, source_target_pairs={{0,12},{4,0},{8,4},{12,8},{1,13},{5,1},{9,5},{13,9},{2,14},{6,2},{... | collective-permute-start | bytes 165896 | tf_op jit(solution)/shard_map/ppermute | solution.py:40
  40.6 5.0 %collective-permute-start.10 = (f32[216,64]{0,1:T(8,128)S(1)}, f32[216,64]{0,1:T(8,128)S(1)}, u32[]{:S(2)}, u32[]{:S(2)}) collective-permute-start(f32[216,64]{0,1:T(8,128)S(1)} %get-tuple-element.14), channel_id=1, source_target_pairs={{0,12},{4,0},{8,4},{12,8},{1,13},{5,1},{9,5},{13,9},{2,14},{6,2},{... | collective-permute-start | bytes 165896 | tf_op jit(solution)/shard_map/ppermute | solution.py:40
  43.4 6.1 %collective-permute-start.8 = (f32[216,64]{0,1:T(8,128)S(1)}, f32[216,64]{0,1:T(8,128)S(1)}, u32[]{:S(2)}, u32[]{:S(2)}) collective-permute-start(f32[216,64]{0,1:T(8,128)S(1)} %get-tuple-element.13), channel_id=1, source_target_pairs={{0,4},{4,8},{8,12},{12,0},{1,5},{5,9},{9,13},{13,1},{2,6},{6,10},{... | collective-permute-start | bytes 165896 | tf_op jit(solution)/shard_map/ppermute | solution.py:40
  43.4 6.1 %collective-permute-start.9 = (f32[216,64]{0,1:T(8,128)S(1)}, f32[216,64]{0,1:T(8,128)S(1)}, u32[]{:S(2)}, u32[]{:S(2)}) collective-permute-start(f32[216,64]{0,1:T(8,128)S(1)} %get-tuple-element.15), channel_id=1, source_target_pairs={{0,8},{4,12},{8,0},{12,4},{1,9},{5,13},{9,1},{13,5},{2,10},{6,14},... | collective-permute-start | bytes 165896 | tf_op jit(solution)/shard_map/ppermute | solution.py:40

commit v12 on v11

--- a/solution.py
+++ b/solution.py
@@ -62,12 +62,6 @@
     taps = weight.reshape(3, 3, 3, chans, weight.shape[2])
     kflip = jnp.transpose(taps[::-1, ::-1, ::-1], (0, 1, 2, 4, 3))
     pad = [(0, 0), (0, 0), (1, 1)]
-    inner = lax.conv_general_dilated(
-        gh[None], kflip, (1, 1, 1), pad,
-        dimension_numbers=("NDHWC", "DHWIO", "NDHWC"),
-        preferred_element_type=jnp.float32,
-    )[0]
-    grad_in = inner.astype(jnp.bfloat16)
     gshare = lax.dynamic_slice_in_dim(gh, offset, half, 3)
     gdeep = jnp.pad(gshare, ((0, 0), (0, 0), (1, 1), (0, 0)))
     stack = jnp.concatenate([lax.slice_in_dim(gdeep, 2 - c, 2 - c + depth, axis=2) for c in range(3)], axis=3)
@@ -82,6 +76,7 @@
     nx = lax.axis_size("gx")
     ny = lax.axis_size("gy")
     owned_rows = 27 * chans // (nx * ny)
+    gates = []
     if ny == 2:
         iy = lax.axis_index("gy")
         side = [
@@ -89,19 +84,28 @@
             for y in range(2)
         ]
         split = owned_rows // 2 if owned_rows % 16 == 0 else owned_rows
-        parts = []
+        partials = []
         for lo, hi in ((0, split), (split, owned_rows)):
             if lo == hi:
                 continue
             keep = jnp.where(iy == 0, side[0][:, lo:hi], side[1][:, lo:hi])
             send = jnp.where(iy == 0, side[1][:, lo:hi], side[0][:, lo:hi])
-            partial = keep + lax.ppermute(send, "gy", [(0, 1), (1, 0)])
-            parts.append(scatter_sum(partial, "gx", 0))
+            partials.append(keep + lax.ppermute(send, "gy", [(0, 1), (1, 0)]))
+        gates = partials
+        parts = [scatter_sum(partial, "gx", 0) for partial in partials]
         owned = jnp.concatenate(parts, axis=0) if len(parts) > 1 else parts[0]
     else:
         weight_terms = jnp.concatenate(pieces, axis=0)
         blocks = weight_terms.reshape(nx, ny, owned_rows, half)
         owned = scatter_sum(scatter_sum(blocks, "gy", 1), "gx", 0)
+    if gates:
+        gh = lax.optimization_barrier((gh, *gates))[0]
+    inner = lax.conv_general_dilated(
+        gh[None], kflip, (1, 1, 1), pad,
+        dimension_numbers=("NDHWC", "DHWIO", "NDHWC"),
+        preferred_element_type=jnp.float32,
+    )[0]
+    grad_in = inner.astype(jnp.bfloat16)
     total_cells = size_x * lax.axis_size("gx") * size_y * lax.axis_size("gy") * depth
     grad_weight = owned / jnp.sqrt(jnp.float32(total_cells))
     return (grad_in, grad_weight)

time: 50.5 us -> 58.2 us (1.15)
  waiting for transfers between devices: 13.2 us -> 17.5 us
  starting transfers between devices: 17 us -> 19.4 us
  local copies, waits for them, and re-layouts: 4.93 us -> 5.59 us
    ppermute x2, waiting for transfers between devices: 0.75 us -> 6.31 us  [on_device(): partials.append(keep + lax.ppermute(send, 'gy', [(0, 1), (1, 0)]))]
    ppermute x6, starting transfers between devices: 7.58 us -> 9.25 us  [scatter_sum(): lax.ppermute(part, axis, [(j, (j + shift) % count) for j in range(count)])]
    ppermute x6, waiting for transfers between devices: 5.41 us -> 4.12 us  [scatter_sum(): lax.ppermute(part, axis, [(j, (j + shift) % count) for j in range(count)])]
    ppermute x2, starting transfers between devices: 2.15 us -> 2.94 us  [on_device(): partials.append(keep + lax.ppermute(send, 'gy', [(0, 1), (1, 0)]))]
    squeeze x2, local copies, waits for them, and re-layouts: 0.04 us -> 0.7 us  [scatter_sum(): lax.dynamic_index_in_dim(blocks, (me + shift) % count, dim, keepdims=False)]
  transfers between devices with their start and end apart: 11 -> 11, of which waited for: 6 -> 7; matrix products, arithmetic and copies ran while one was open for 14% -> 12% of each run, Pallas kernels for 0% -> 0%
where the time goes in v12:
time: 58.2 us; the launch traced here: 58 us
  starting transfers between devices  19.4 us (33%)
  waiting for transfers between devices  17.5 us (30%)
  matrix products  8.89 us (15%)
  local copies, waits for them, and re-layouts  5.59 us (10%)
  other arithmetic  5.47 us (9%)
  between operations  1.1 us (2%)
    ppermute x6, starting transfers between devices, scatter_sum(): lax.ppermute(part, axis, [(j, (j + shift) % count) for j in range(count)])  9.25 us
    ppermute x2, waiting for transfers between devices, on_device(): partials.append(keep + lax.ppermute(send, 'gy', [(0, 1), (1, 0)]))  6.31 us
    conv_general_dilated x1, matrix products, on_device(): lax.conv_general_dilated(gh[None], kflip, (1, 1, 1), pad, dimension_numbe...  4.75 us
    ppermute x1, waiting for transfers between devices, with_halo(): low = lax.ppermute(tail, axis, [(i, (i + 1) % count) for i in range(count)])  4.25 us
    dot_general x9, matrix products, on_device(): lax.dot_general(x_act, window, (((0, 1, 2), (0, 1, 2)), ((), ())), prefer...  4.14 us
    ppermute x6, waiting for transfers between devices, scatter_sum(): lax.ppermute(part, axis, [(j, (j + shift) % count) for j in range(count)])  4.12 us
    ppermute x2, starting transfers between devices, on_device(): partials.append(keep + lax.ppermute(send, 'gy', [(0, 1), (1, 0)]))  2.94 us
    ppermute x1, starting transfers between devices, with_halo(): got = lax.ppermute(jnp.where(me == 0, tail, head), axis, [(0, 1), (1, 0)])  2.94 us
  transfers between devices with their start and end apart: 11, of which 7 were waited for; matrix products, arithmetic and copies ran while one was open for 12% of the time, Pallas kernels for 0%

profile of v12, /device:TPU:0, one launch (start us, length us, event | category | flops | bytes accessed | tf_op | source)
XLA Modules:
  0.0 58.0 jit_solution(699901495714141987)
XLA Ops:
  0.7 0.9 %slice_select_fusion.2 = bf16[4,1,32,128]{3,2,1,0:T(8,128)(2,1)S(1)} fusion(bf16[4,16,32,128]{3,2,1,0:T(8,128)(2,1)} %param.4, pred[]{:T(512)S(6)} %eq.26), kind=kLoop, calls=%fused_computation.57 | loop fusion | flops 16384 | bytes 98305 | tf_op jit(solution)/shard_map/jit(_where)/select_n | solution.py:17
  1.6 2.9 %collective-permute-start = (bf16[4,1,32,128]{3,2,1,0:T(8,128)(2,1)S(1)}, bf16[4,1,32,128]{3,2,1,0:T(8,128)(2,1)S(1)}, u32[]{:S(2)}, u32[]{:S(2)}) collective-permute-start(bf16[4,1,32,128]{3,2,1,0:T(8,128)(2,1)S(1)} %slice_select_fusion.2), channel_id=1, source_target_pairs={{0,2},{2,0},{1,3},{3,1},{4,6},{6,4},{5,7},{7,5},{8,10},{10,8},{9,1... | collective-permute-start | bytes 98312 | tf_op jit(solution)/shard_map/ppermute | solution.py:17
  4.5 1.9 %collective-permute-done = bf16[4,1,32,128]{3,2,1,0:T(8,128)(2,1)S(1)} collective-permute-done((bf16[4,1,32,128]{3,2,1,0:T(8,128)(2,1)S(1)}, bf16[4,1,32,128]{3,2,1,0:T(8,128)(2,1)S(1)}, u32[]{:S(2)}, u32[]{:S(2)}) %collective-permute-start) | collective-permute-done | bytes 32800 | tf_op jit(solution)/shard_map/ppermute | solution.py:17
  6.4 1.0 %pad_maximum_fusion.6 = (bf16[1,18,32,128]{3,2,1,0:T(8,128)(2,1)S(1)}, bf16[1,18,32,128]{3,2,1,0:T(8,128)(2,1)S(1)}) fusion(bf16[4,1,32,128]{3,2,1,0:T(8,128)(2,1)S(1)} %get-tuple-element.21, bf16[4,16,32,128]{3,2,1,0:T(8,128)(2,1)} %param.4, bf16[4,1,32,128]{3,2,1,0:T(8,128)(2,1)S(1)} %get-tuple-element.20), kind=kLoop, calls=%fused_computation.24 | loop fusion | flops 294912 | bytes 884736 | tf_op jit(solution)/shard_map/slice | solution.py:11
  7.4 2.2 %collective-permute-start.1 = (bf16[1,18,32,128]{3,2,1,0:T(8,128)(2,1)S(1)}, bf16[1,18,32,128]{3,2,1,0:T(8,128)(2,1)S(1)}, u32[]{:S(2)}, u32[]{:S(2)}) collective-permute-start(bf16[1,18,32,128]{3,2,1,0:T(8,128)(2,1)S(1)} %get-tuple-element.10), channel_id=1, source_target_pairs={{0,4},{4,8},{8,12},{12,0},{1,5},{5,9},{9,13},{13,1},{2,6},{6,10},{... | collective-permute-start | bytes 442376 | tf_op jit(solution)/shard_map/ppermute | solution.py:22
  9.6 2.1 %collective-permute-start.2 = (bf16[1,18,32,128]{3,2,1,0:T(8,128)(2,1)S(1)}, bf16[1,18,32,128]{3,2,1,0:T(8,128)(2,1)S(1)}, u32[]{:S(2)}, u32[]{:S(2)}) collective-permute-start(bf16[1,18,32,128]{3,2,1,0:T(8,128)(2,1)S(1)} %get-tuple-element.11), channel_id=1, source_target_pairs={{4,0},{8,4},{12,8},{0,12},{5,1},{9,5},{13,9},{1,13},{6,2},{10,6},{... | collective-permute-start | bytes 442376 | tf_op jit(solution)/shard_map/ppermute | solution.py:23
  11.7 4.3 %collective-permute-done.1 = bf16[1,18,32,128]{3,2,1,0:T(8,128)(2,1)S(1)} collective-permute-done((bf16[1,18,32,128]{3,2,1,0:T(8,128)(2,1)S(1)}, bf16[1,18,32,128]{3,2,1,0:T(8,128)(2,1)S(1)}, u32[]{:S(2)}, u32[]{:S(2)}) %collective-permute-start.1) | collective-permute-done | bytes 147488 | tf_op jit(solution)/shard_map/ppermute | solution.py:22
  15.9 0.9 %collective-permute-done.2 = bf16[1,18,32,128]{3,2,1,0:T(8,128)(2,1)S(1)} collective-permute-done((bf16[1,18,32,128]{3,2,1,0:T(8,128)(2,1)S(1)}, bf16[1,18,32,128]{3,2,1,0:T(8,128)(2,1)S(1)}, u32[]{:S(2)}, u32[]{:S(2)}) %collective-permute-start.2) | collective-permute-done | bytes 147488 | tf_op jit(solution)/shard_map/ppermute | solution.py:23
  16.9 0.2 pad_maximum_fusion.1
  17.1 0.3 constant_dynamic-slice_fusion
  17.4 0.8 %pad_slice_fusion.1 = (bf16[6,18,32,64]{3,2,1,0:T(8,128)(2,1)S(1)}, bf16[6,18,32,64]{3,2,1,0:T(8,128)(2,1)S(1)}) fusion(bf16[6,18,32,64]{3,2,1,0:T(8,128)(2,1)S(1)} %constant_dynamic-slice_fusion), kind=kLoop, calls=%fused_computation.12 | loop fusion | bytes 1327104 | tf_op jit(solution)/shard_map/slice | solution.py:67
  18.2 0.9 %pad_maximum_fusion = bf16[6,18,32,192]{3,2,1,0:T(8,128)(2,1)S(1)} fusion(bf16[6,18,32,64]{3,2,1,0:T(8,128)(2,1)S(1)} %get-tuple-element.9, bf16[6,18,32,64]{3,2,1,0:T(8,128)(2,1)S(1)} %constant_dynamic-slice_fusion, bf16[6,18,32,64]{3,2,1,0:T(8,128)(2,1)S(1)} %get-tuple-element.8), kind=kLoop, calls=%fused_computation.2 | loop fusion | flops 3981312 | bytes 2654208 | tf_op jit(solution)/shard_map/concatenate | solution.py:67
  19.0 0.2 copy-done.2
  19.2 0.5 fusion.25
  19.7 0.5 fusion.26
  20.1 0.5 fusion.24
  20.6 0.5 fusion.23
  21.1 0.5 fusion.29
  21.5 0.5 fusion.30
  22.0 0.5 fusion.27
  22.5 0.5 fusion.28
  23.7 0.5 fusion.31
  24.9 0.1 maximum_bitcast_fusion.3
  25.0 0.1 maximum_bitcast_fusion.7
  25.2 0.1 maximum_bitcast_fusion.2
  25.4 0.1 maximum_bitcast_fusion.4
  25.5 0.2 slice_select_fusion
  25.7 1.6 %collective-permute-start.4 = (f32[4,216,64]{1,2,0:T(8,128)S(1)}, f32[4,216,64]{1,2,0:T(8,128)S(1)}, u32[]{:S(2)}, u32[]{:S(2)}) collective-permute-start(f32[4,216,64]{1,2,0:T(8,128)S(1)} %slice_select_fusion), channel_id=1, source_target_pairs={{0,2},{2,0},{1,3},{3,1},{4,6},{6,4},{5,7},{7,5},{8,10},{10,8},{9,1... | collective-permute-start | bytes 663560 | tf_op jit(solution)/shard_map/ppermute | solution.py:93
  27.3 5.3 %collective-permute-done.4 = f32[4,216,64]{1,2,0:T(8,128)S(1)} collective-permute-done((f32[4,216,64]{1,2,0:T(8,128)S(1)}, f32[4,216,64]{1,2,0:T(8,128)S(1)}, u32[]{:S(2)}, u32[]{:S(2)}) %collective-permute-start.4) | collective-permute-done | bytes 221216 | tf_op jit(solution)/shard_map/ppermute | solution.py:93
  32.5 0.9 %select_add_fusion = (f32[4,216,64]{1,2,0:T(8,128)S(1)}, f32[4,216,64]{1,2,0:T(8,128)}) fusion(f32[4,216,64]{1,2,0:T(8,128)S(1)} %collective-permute-done.4, f32[4,432,64]{1,2,0:T(8,128)S(1)} %pad_maximum_fusion.3, f32[4,432,64]{1,2,0:T(8,128)S(1)} %pad_maximum_fusion.2, pred[]{:T(512)S(6)} %eq.26), kind=kLoop, calls=%fused_computation.18 | loop fusion | flops 165888 | bytes 1548289 | tf_op jit(solution)/shard_map/add | solution.py:93
  33.4 0.7 %dynamic-slice_bitcast_fusion.2 = (f32[216,64]{0,1:T(8,128)}, f32[216,64]{0,1:T(8,128)}, f32[216,64]{0,1:T(8,128)}) fusion(f32[4,216,64]{1,2,0:T(8,128)S(1)} %get-tuple-element.6, s32[]{:T(128)S(6)} %select_n.110, s32[]{:T(128)S(6)} %select_n.114, s32[]{:T(128)S(6)} %select_n.112), kind=kLoop, calls=%fused_computation.53 | loop fusion | bytes 331788 | tf_op jit(solution)/shard_map/jit(dynamic_index_in_dim)/squeeze | solution.py:39
  34.1 2.4 %collective-permute-start.10 = (f32[216,64]{0,1:T(8,128)}, f32[216,64]{0,1:T(8,128)S(1)}, u32[]{:S(2)}, u32[]{:S(2)}) collective-permute-start(f32[216,64]{0,1:T(8,128)} %get-tuple-element.16), channel_id=1, source_target_pairs={{0,12},{4,0},{8,4},{12,8},{1,13},{5,1},{9,5},{13,9},{2,14},{6,2},{... | collective-permute-start | bytes 165896 | tf_op jit(solution)/shard_map/ppermute | solution.py:40
  36.4 0.8 %collective-permute-start.9 = (f32[216,64]{0,1:T(8,128)}, f32[216,64]{0,1:T(8,128)S(1)}, u32[]{:S(2)}, u32[]{:S(2)}) collective-permute-start(f32[216,64]{0,1:T(8,128)} %get-tuple-element.17), channel_id=1, source_target_pairs={{0,8},{4,12},{8,0},{12,4},{1,9},{5,13},{9,1},{13,5},{2,10},{6,14},... | collective-permute-start | bytes 165896 | tf_op jit(solution)/shard_map/ppermute | solution.py:40
  37.2 1.4 %collective-permute-start.3 = (f32[4,216,64]{1,2,0:T(8,128)}, f32[4,216,64]{1,2,0:T(8,128)S(1)}, u32[]{:S(2)}, u32[]{:S(2)}) collective-permute-start(f32[4,216,64]{1,2,0:T(8,128)} %get-tuple-element.7), channel_id=1, source_target_pairs={{0,2},{2,0},{1,3},{3,1},{4,6},{6,4},{5,7},{7,5},{8,10},{10,8},{9,1... | collective-permute-start | bytes 663560 | tf_op jit(solution)/shard_map/ppermute | solution.py:93
  38.6 0.8 %collective-permute-done.10 = f32[216,64]{0,1:T(8,128)S(1)} collective-permute-done((f32[216,64]{0,1:T(8,128)}, f32[216,64]{0,1:T(8,128)S(1)}, u32[]{:S(2)}, u32[]{:S(2)}) %collective-permute-start.10) | collective-permute-done | bytes 55328 | tf_op jit(solution)/shard_map/ppermute | solution.py:40
  39.4 3.3 %collective-permute-done.8 = f32[216,64]{0,1:T(8,128)S(1)} collective-permute-done((f32[216,64]{0,1:T(8,128)}, f32[216,64]{0,1:T(8,128)S(1)}, u32[]{:S(2)}, u32[]{:S(2)}) %collective-permute-start.8) | collective-permute-done | bytes 55328 | tf_op jit(solution)/shard_map/ppermute | solution.py:40
  42.7 1.1 %collective-permute-done.3 = f32[4,216,64]{1,2,0:T(8,128)S(1)} collective-permute-done((f32[4,216,64]{1,2,0:T(8,128)}, f32[4,216,64]{1,2,0:T(8,128)S(1)}, u32[]{:S(2)}, u32[]{:S(2)}) %collective-permute-start.3) | collective-permute-done | bytes 221216 | tf_op jit(solution)/shard_map/ppermute | solution.py:93
  43.9 3.7 %collective-permute-start.5 = (f32[216,64]{0,1:T(8,128)S(1)}, f32[216,64]{0,1:T(8,128)S(1)}, u32[]{:S(2)}, u32[]{:S(2)}) collective-permute-start(f32[216,64]{0,1:T(8,128)S(1)} %get-tuple-element.12), channel_id=1, source_target_pairs={{0,4},{4,8},{8,12},{12,0},{1,5},{5,9},{9,13},{13,1},{2,6},{6,10},{... | collective-permute-start | bytes 165896 | tf_op jit(solution)/shard_map/ppermute | solution.py:40
  47.6 2.4 %collective-permute-start.7 = (f32[216,64]{0,1:T(8,128)S(1)}, f32[216,64]{0,1:T(8,128)S(1)}, u32[]{:S(2)}, u32[]{:S(2)}) collective-permute-start(f32[216,64]{0,1:T(8,128)S(1)} %get-tuple-element.13), channel_id=1, source_target_pairs={{0,12},{4,0},{8,4},{12,8},{1,13},{5,1},{9,5},{13,9},{2,14},{6,2},{... | collective-permute-start | bytes 165896 | tf_op jit(solution)/shard_map/ppermute | solution.py:40
  50.0 0.4 copy.30
  50.4 0.2 pad.5.clone
  50.7 0.1 copy.18
  50.8 0.1 slice.157
  50.9 0.4 copy-done.3
  51.3 4.7 %fusion.11 = bf16[4,16,8,5,128]{4,2,3,1,0:T(8,128)(2,1)S(1)} fusion(bf16[3,3,3,128,128]{4,3,2,1,0:T(8,128)(2,1)S(1)} %bitcast.200, bf16[6,18,1,7,2,128]{5,3,4,1,0,2:T(8,128)(2,1)S(1)} %slice.157, bf16[6,18,1,8,5,128]{5,3,4,1,0,2:T(8,128)(2,1)S(1)} %copy.18, pred[8,5]{0,1:T(8,128)(4,1)S(1)} %copy-done.3), kind=kOutput, calls=%fused_computation.10 | convolution fusion | flops 2270224384 | bytes 3033128 | tf_op jit(solution)/shard_map/conv_general_dilated | solution.py:103
  56.1 0.1 copy.19
  56.2 0.9 %copy.20 = bf16[4,16,32,128]{3,2,1,0:T(8,128)(2,1)} copy(bf16[4,16,32,128]{3,1,2,0:T(8,128)(2,1)S(1)} %slice_bitcast_fusion) | data formatting | bytes 1048576
  57.2 0.8 %maximum_multiply_fusion = f32[432,64]{0,1:T(8,128)} fusion(f32[216,64]{0,1:T(8,128)S(1)} %fusion.16, f32[216,64]{0,1:T(8,128)S(1)} %fusion.18), kind=kLoop, calls=%fused_computation.35 | loop fusion | flops 55296 | bytes 221184 | tf_op jit(solution)/shard_map/div | solution.py:110
  (52 shorter events, 1.7 us)
Async XLA Ops:
  0.6 50.3 %copy-start = (bf16[27,128,128]{2,1,0:T(8,128)(2,1)S(1)}, bf16[27,128,128]{2,1,0:T(8,128)(2,1)}, u32[]{:S(2)}) copy-start(bf16[27,128,128]{2,1,0:T(8,128)(2,1)} %param.5) | copy-start | bytes 2654212
  0.6 16.3 %copy-start.1 = (bf16[4,16,32,128]{3,2,1,0:T(8,128)(2,1)S(1)}, bf16[4,16,32,128]{3,2,1,0:T(8,128)(2,1)}, u32[]{:S(2)}) copy-start(bf16[4,16,32,128]{3,2,1,0:T(8,128)(2,1)} %param.4) | copy-start | bytes 1572868
  1.6 4.8 %collective-permute-start = (bf16[4,1,32,128]{3,2,1,0:T(8,128)(2,1)S(1)}, bf16[4,1,32,128]{3,2,1,0:T(8,128)(2,1)S(1)}, u32[]{:S(2)}, u32[]{:S(2)}) collective-permute-start(bf16[4,1,32,128]{3,2,1,0:T(8,128)(2,1)S(1)} %slice_select_fusion.2), channel_id=1, source_target_pairs={{0,2},{2,0},{1,3},{3,1},{4,6},{6,4},{5,7},{7,5},{8,10},{10,8},{9,1... | collective-permute-start | bytes 98312 | tf_op jit(solution)/shard_map/ppermute | solution.py:17
  7.4 8.5 %collective-permute-start.1 = (bf16[1,18,32,128]{3,2,1,0:T(8,128)(2,1)S(1)}, bf16[1,18,32,128]{3,2,1,0:T(8,128)(2,1)S(1)}, u32[]{:S(2)}, u32[]{:S(2)}) collective-permute-start(bf16[1,18,32,128]{3,2,1,0:T(8,128)(2,1)S(1)} %get-tuple-element.10), channel_id=1, source_target_pairs={{0,4},{4,8},{8,12},{12,0},{1,5},{5,9},{9,13},{13,1},{2,6},{6,10},{... | collective-permute-start | bytes 442376 | tf_op jit(solution)/shard_map/ppermute | solution.py:22
  9.6 7.3 %collective-permute-start.2 = (bf16[1,18,32,128]{3,2,1,0:T(8,128)(2,1)S(1)}, bf16[1,18,32,128]{3,2,1,0:T(8,128)(2,1)S(1)}, u32[]{:S(2)}, u32[]{:S(2)}) collective-permute-start(bf16[1,18,32,128]{3,2,1,0:T(8,128)(2,1)S(1)} %get-tuple-element.11), channel_id=1, source_target_pairs={{4,0},{8,4},{12,8},{0,12},{5,1},{9,5},{13,9},{1,13},{6,2},{10,6},{... | collective-permute-start | bytes 442376 | tf_op jit(solution)/shard_map/ppermute | solution.py:23
  18.2 1.0 %copy-start.2 = (bf16[4,16,32,128]{3,2,1,0:T(8,128)(2,1)S(1)}, bf16[4,16,32,128]{3,2,1,0:T(8,128)(2,1)}, u32[]{:S(2)}) copy-start(bf16[4,16,32,128]{3,2,1,0:T(8,128)(2,1)} %param.3) | copy-start | bytes 1572868
  25.7 6.8 %collective-permute-start.4 = (f32[4,216,64]{1,2,0:T(8,128)S(1)}, f32[4,216,64]{1,2,0:T(8,128)S(1)}, u32[]{:S(2)}, u32[]{:S(2)}) collective-permute-start(f32[4,216,64]{1,2,0:T(8,128)S(1)} %slice_select_fusion), channel_id=1, source_target_pairs={{0,2},{2,0},{1,3},{3,1},{4,6},{6,4},{5,7},{7,5},{8,10},{10,8},{9,1... | collective-permute-start | bytes 663560 | tf_op jit(solution)/shard_map/ppermute | solution.py:93
  34.1 5.4 %collective-permute-start.10 = (f32[216,64]{0,1:T(8,128)}, f32[216,64]{0,1:T(8,128)S(1)}, u32[]{:S(2)}, u32[]{:S(2)}) collective-permute-start(f32[216,64]{0,1:T(8,128)} %get-tuple-element.16), channel_id=1, source_target_pairs={{0,12},{4,0},{8,4},{12,8},{1,13},{5,1},{9,5},{13,9},{2,14},{6,2},{... | collective-permute-start | bytes 165896 | tf_op jit(solution)/shard_map/ppermute | solution.py:40
  36.4 6.3 %collective-permute-start.8 = (f32[216,64]{0,1:T(8,128)}, f32[216,64]{0,1:T(8,128)S(1)}, u32[]{:S(2)}, u32[]{:S(2)}) collective-permute-start(f32[216,64]{0,1:T(8,128)} %get-tuple-element.15), channel_id=1, source_target_pairs={{0,4},{4,8},{8,12},{12,0},{1,5},{5,9},{9,13},{13,1},{2,6},{6,10},{... | collective-permute-start | bytes 165896 | tf_op jit(solution)/shard_map/ppermute | solution.py:40
  36.4 6.3 %collective-permute-start.9 = (f32[216,64]{0,1:T(8,128)}, f32[216,64]{0,1:T(8,128)S(1)}, u32[]{:S(2)}, u32[]{:S(2)}) collective-permute-start(f32[216,64]{0,1:T(8,128)} %get-tuple-element.17), channel_id=1, source_target_pairs={{0,8},{4,12},{8,0},{12,4},{1,9},{5,13},{9,1},{13,5},{2,10},{6,14},... | collective-permute-start | bytes 165896 | tf_op jit(solution)/shard_map/ppermute | solution.py:40
  37.2 6.6 %collective-permute-start.3 = (f32[4,216,64]{1,2,0:T(8,128)}, f32[4,216,64]{1,2,0:T(8,128)S(1)}, u32[]{:S(2)}, u32[]{:S(2)}) collective-permute-start(f32[4,216,64]{1,2,0:T(8,128)} %get-tuple-element.7), channel_id=1, source_target_pairs={{0,2},{2,0},{1,3},{3,1},{4,6},{6,4},{5,7},{7,5},{8,10},{10,8},{9,1... | collective-permute-start | bytes 663560 | tf_op jit(solution)/shard_map/ppermute | solution.py:93
  43.9 13.3 %collective-permute-start.5 = (f32[216,64]{0,1:T(8,128)S(1)}, f32[216,64]{0,1:T(8,128)S(1)}, u32[]{:S(2)}, u32[]{:S(2)}) collective-permute-start(f32[216,64]{0,1:T(8,128)S(1)} %get-tuple-element.12), channel_id=1, source_target_pairs={{0,4},{4,8},{8,12},{12,0},{1,5},{5,9},{9,13},{13,1},{2,6},{6,10},{... | collective-permute-start | bytes 165896 | tf_op jit(solution)/shard_map/ppermute | solution.py:40
  47.6 9.6 %collective-permute-start.6 = (f32[216,64]{0,1:T(8,128)S(1)}, f32[216,64]{0,1:T(8,128)S(1)}, u32[]{:S(2)}, u32[]{:S(2)}) collective-permute-start(f32[216,64]{0,1:T(8,128)S(1)} %get-tuple-element.14), channel_id=1, source_target_pairs={{0,8},{4,12},{8,0},{12,4},{1,9},{5,13},{9,1},{13,5},{2,10},{6,14},... | collective-permute-start | bytes 165896 | tf_op jit(solution)/shard_map/ppermute | solution.py:40
  47.6 9.6 %collective-permute-start.7 = (f32[216,64]{0,1:T(8,128)S(1)}, f32[216,64]{0,1:T(8,128)S(1)}, u32[]{:S(2)}, u32[]{:S(2)}) collective-permute-start(f32[216,64]{0,1:T(8,128)S(1)} %get-tuple-element.13), channel_id=1, source_target_pairs={{0,12},{4,0},{8,4},{12,8},{1,13},{5,1},{9,5},{13,9},{2,14},{6,2},{... | collective-permute-start | bytes 165896 | tf_op jit(solution)/shard_map/ppermute | solution.py:40
  50.6 0.7 %copy-start.3 = (pred[8,5]{0,1:T(8,128)(4,1)S(1)}, pred[8,5]{0,1:T(8,128)(4,1)}, u32[]{:S(2)}) copy-start(pred[8,5]{0,1:T(8,128)(4,1)} %constant.81) | copy-start | bytes 124

commit v13 on v11

--- a/solution.py
+++ b/solution.py
@@ -58,7 +58,8 @@
     ncores = lax.axis_size("col")
     half = weight.shape[2] // ncores
     offset = lax.axis_index("col") * half
-    gh = with_halo(grad_out, (("gy", 1), ("gx", 0)), 1)
+    widened = with_halo(grad_out, (("gy", 1),), 1)
+    gh = with_halo(widened, (("gx", 0),), 1)
     taps = weight.reshape(3, 3, 3, chans, weight.shape[2])
     kflip = jnp.transpose(taps[::-1, ::-1, ::-1], (0, 1, 2, 4, 3))
     pad = [(0, 0), (0, 0), (1, 1)]
@@ -68,16 +69,28 @@
         preferred_element_type=jnp.float32,
     )[0]
     grad_in = inner.astype(jnp.bfloat16)
+
+    def depth_stack(cells):
+        deep = jnp.pad(cells, ((0, 0), (0, 0), (1, 1), (0, 0)))
+        return jnp.concatenate([lax.slice_in_dim(deep, 2 - c, 2 - c + depth, axis=2) for c in range(3)], axis=3)
+
+    def contract(xs, ws):
+        return lax.dot_general(xs, ws, (((0, 1, 2), (0, 1, 2)), ((), ())), preferred_element_type=jnp.float32)
+
+    local = depth_stack(lax.dynamic_slice_in_dim(widened, offset, half, 3))
     gshare = lax.dynamic_slice_in_dim(gh, offset, half, 3)
-    gdeep = jnp.pad(gshare, ((0, 0), (0, 0), (1, 1), (0, 0)))
-    stack = jnp.concatenate([lax.slice_in_dim(gdeep, 2 - c, 2 - c + depth, axis=2) for c in range(3)], axis=3)
+    below = depth_stack(gshare[:1])
+    above = depth_stack(gshare[size_x + 1 :])
     pieces = []
     for a in range(3):
         for b in range(3):
-            window = stack[2 - a : 2 - a + size_x, 2 - b : 2 - b + size_y]
-            term = lax.dot_general(
-                x_act, window, (((0, 1, 2), (0, 1, 2)), ((), ())), preferred_element_type=jnp.float32
-            )
+            cols = slice(2 - b, 2 - b + size_y)
+            if a == 1:
+                term = contract(x_act, local[:, cols])
+            elif a == 0:
+                term = contract(x_act[: size_x - 1], local[1:, cols]) + contract(x_act[size_x - 1 :], above[:, cols])
+            else:
+                term = contract(x_act[1:], local[: size_x - 1, cols]) + contract(x_act[:1], below[:, cols])
             pieces.append(jnp.transpose(term.reshape(chans, 3, half), (1, 0, 2)).reshape(3 * chans, half))
     nx = lax.axis_size("gx")
     ny = lax.axis_size("gy")

time: 50.5 us -> 53.2 us (1.053)
  waiting for transfers between devices: 13.2 us -> 14.6 us
  matrix products: 9.1 us -> 9.96 us
    ppermute x1, waiting for transfers between devices: 0.95 us -> 3.24 us  [with_halo(): lax.ppermute(head, axis, [((i + 1) % count, i) for i in range(count)])]
    ppermute x1, starting transfers between devices: 2.16 us -> 0.01 us  [with_halo(): low = lax.ppermute(tail, axis, [(i, (i + 1) % count) for i in range(count)])]
    ppermute x1, starting transfers between devices: 2.14 us -> 4.18 us  [with_halo(): lax.ppermute(head, axis, [((i + 1) % count, i) for i in range(count)])]
    concatenate x1 -> x2, other arithmetic: 0.15 us -> 1.27 us  [with_halo(): cells = jnp.concatenate([low, cells, high], axis=dim)]
    dot_general x9 -> x15, matrix products: 4.14 us -> 5.21 us  [contract(): lax.dot_general(xs, ws, (((0, 1, 2), (0, 1, 2)), ((), ())), preferred_ele...]
    slice x1 -> x0, other arithmetic: 1.01 us -> none  [with_halo(): lax.slice_in_dim(cells, cells.shape[dim] - width, cells.shape[dim], axis=...]
    ppermute x2, starting transfers between devices: 2.15 us -> 3.13 us  [on_device(): partial = keep + lax.ppermute(send, 'gy', [(0, 1), (1, 0)])]
    ppermute x1, waiting for transfers between devices: 4.21 us -> 3.39 us  [with_halo(): low = lax.ppermute(tail, axis, [(i, (i + 1) % count) for i in range(count)])]
  transfers between devices with their start and end apart: 11 -> 11, of which waited for: 6 -> 8; matrix products, arithmetic and copies ran while one was open for 14% -> 12% of each run, Pallas kernels for 0% -> 0%
where the time goes in v13:
time: 53.2 us; the launch traced here: 53 us
  starting transfers between devices  17.3 us (33%)
  waiting for transfers between devices  14.6 us (27%)
  matrix products  9.96 us (19%)
  other arithmetic  5.16 us (10%)
  local copies, waits for them, and re-layouts  4.74 us (9%)
  between operations  1.2 us (2%)
    ppermute x6, starting transfers between devices, scatter_sum(): lax.ppermute(part, axis, [(j, (j + shift) % count) for j in range(count)])  7.08 us
    ppermute x6, waiting for transfers between devices, scatter_sum(): lax.ppermute(part, axis, [(j, (j + shift) % count) for j in range(count)])  5.88 us
    dot_general x15, matrix products, contract(): lax.dot_general(xs, ws, (((0, 1, 2), (0, 1, 2)), ((), ())), preferred_ele...  5.21 us
    conv_general_dilated x1, matrix products, on_device(): lax.conv_general_dilated(gh[None], kflip, (1, 1, 1), pad, dimension_numbe...  4.75 us
    ppermute x1, starting transfers between devices, with_halo(): lax.ppermute(head, axis, [((i + 1) % count, i) for i in range(count)])  4.18 us
    ppermute x1, waiting for transfers between devices, with_halo(): low = lax.ppermute(tail, axis, [(i, (i + 1) % count) for i in range(count)])  3.39 us
    ppermute x1, waiting for transfers between devices, with_halo(): lax.ppermute(head, axis, [((i + 1) % count, i) for i in range(count)])  3.24 us
    ppermute x2, starting transfers between devices, on_device(): partial = keep + lax.ppermute(send, 'gy', [(0, 1), (1, 0)])  3.13 us
  transfers between devices with their start and end apart: 11, of which 8 were waited for; matrix products, arithmetic and copies ran while one was open for 12% of the time, Pallas kernels for 0%

profile of v13, /device:TPU:0, one launch (start us, length us, event | category | flops | bytes accessed | tf_op | source)
XLA Modules:
  0.0 53.0 jit_solution(16343540102499765731)
XLA Ops:
  0.7 0.9 %slice_select_fusion.2 = bf16[4,1,32,128]{3,2,1,0:T(8,128)(2,1)S(1)} fusion(bf16[4,16,32,128]{3,2,1,0:T(8,128)(2,1)} %param.4, pred[]{:T(512)S(6)} %eq.26), kind=kLoop, calls=%fused_computation.103 | loop fusion | flops 16384 | bytes 98305 | tf_op jit(solution)/shard_map/jit(_where)/select_n | solution.py:17
  1.5 2.9 %collective-permute-start = (bf16[4,1,32,128]{3,2,1,0:T(8,128)(2,1)S(1)}, bf16[4,1,32,128]{3,2,1,0:T(8,128)(2,1)S(1)}, u32[]{:S(2)}, u32[]{:S(2)}) collective-permute-start(bf16[4,1,32,128]{3,2,1,0:T(8,128)(2,1)S(1)} %slice_select_fusion.2), channel_id=1, source_target_pairs={{0,2},{2,0},{1,3},{3,1},{4,6},{6,4},{5,7},{7,5},{8,10},{10,8},{9,1... | collective-permute-start | bytes 98312 | tf_op jit(solution)/shard_map/ppermute | solution.py:17
  4.5 1.9 %collective-permute-done = bf16[4,1,32,128]{3,2,1,0:T(8,128)(2,1)S(1)} collective-permute-done((bf16[4,1,32,128]{3,2,1,0:T(8,128)(2,1)S(1)}, bf16[4,1,32,128]{3,2,1,0:T(8,128)(2,1)S(1)}, u32[]{:S(2)}, u32[]{:S(2)}) %collective-permute-start) | collective-permute-done | bytes 32800 | tf_op jit(solution)/shard_map/ppermute | solution.py:17
  6.4 1.1 %pad_maximum_fusion.2 = bf16[4,18,32,128]{3,2,1,0:T(8,128)(2,1)S(1)} fusion(bf16[4,1,32,128]{3,2,1,0:T(8,128)(2,1)S(1)} %get-tuple-element.25, bf16[4,16,32,128]{3,2,1,0:T(8,128)(2,1)} %param.4, bf16[4,1,32,128]{3,2,1,0:T(8,128)(2,1)S(1)} %get-tuple-element.24), kind=kLoop, calls=%fused_computation.33 | loop fusion | flops 589824 | bytes 1179648 | tf_op jit(solution)/shard_map/concatenate | solution.py:26
  7.5 0.2 constant_dynamic-slice_fusion.2
  7.7 0.5 pad_slice_fusion.1
  8.2 0.6 %pad_maximum_fusion = bf16[4,18,32,192]{3,2,1,0:T(8,128)(2,1)S(1)} fusion(bf16[4,18,32,64]{3,2,1,0:T(8,128)(2,1)S(1)} %get-tuple-element.9, bf16[4,18,32,64]{3,2,1,0:T(8,128)(2,1)S(1)} %constant_dynamic-slice_fusion.2, bf16[4,18,32,64]{3,2,1,0:T(8,128)(2,1)S(1)} %get-tuple-element.8), kind=kLoop, calls=%fused_computation.10 | loop fusion | flops 2654208 | bytes 1769472 | tf_op jit(solution)/shard_map/concatenate | solution.py:75
  8.9 0.4 copy-done.2
  9.3 0.4 convolution_bitcast_fusion
  9.7 0.4 convolution_bitcast_fusion.1
  10.1 0.4 convolution_bitcast_fusion.2
  10.5 0.5 fusion.50
  11.1 0.5 fusion.49
  11.6 0.5 fusion.48
  12.1 0.4 convolution_bitcast_fusion.3
  12.5 0.4 convolution_bitcast_fusion.4
  13.1 0.4 convolution_bitcast_fusion.5
  13.5 4.2 %collective-permute-start.2 = (bf16[1,18,32,128]{3,2,1,0:T(8,128)(2,1)S(1)}, bf16[1,18,32,128]{3,2,1,0:T(8,128)(2,1)S(1)}, u32[]{:S(2)}, u32[]{:S(2)}) collective-permute-start(bf16[1,18,32,128]{3,2,1,0:T(8,128)(2,1)S(1)} %get-tuple-element.11), channel_id=1, source_target_pairs={{4,0},{8,4},{12,8},{0,12},{5,1},{9,5},{13,9},{1,13},{6,2},{10,6},{... | collective-permute-start | bytes 442376 | tf_op jit(solution)/shard_map/ppermute | solution.py:23
  18.0 3.2 %collective-permute-done.2 = bf16[1,18,32,128]{3,2,1,0:T(8,128)(2,1)S(1)} collective-permute-done((bf16[1,18,32,128]{3,2,1,0:T(8,128)(2,1)S(1)}, bf16[1,18,32,128]{3,2,1,0:T(8,128)(2,1)S(1)}, u32[]{:S(2)}, u32[]{:S(2)}) %collective-permute-start.2) | collective-permute-done | bytes 147488 | tf_op jit(solution)/shard_map/ppermute | solution.py:23
  21.2 3.4 %collective-permute-done.1 = bf16[1,18,32,128]{3,2,1,0:T(8,128)(2,1)S(1)} collective-permute-done((bf16[1,18,32,128]{3,2,1,0:T(8,128)(2,1)S(1)}, bf16[1,18,32,128]{3,2,1,0:T(8,128)(2,1)S(1)}, u32[]{:S(2)}, u32[]{:S(2)}) %collective-permute-start.1) | collective-permute-done | bytes 147488 | tf_op jit(solution)/shard_map/ppermute | solution.py:22
  24.9 0.2 constant_dynamic-slice_fusion
  25.3 0.3 pad_maximum_fusion.5
  25.6 0.2 fusion.16
  26.0 0.2 fusion.15
  26.5 0.4 copy.28
  26.9 0.2 pad.14.clone
  27.4 0.2 fusion.19
  27.7 0.2 fusion.18
  28.2 0.2 fusion.17
  28.6 0.2 fusion.14
  29.6 1.6 %collective-permute-start.3 = (f32[4,216,64]{1,2,0:T(8,128)S(1)}, f32[4,216,64]{1,2,0:T(8,128)S(1)}, u32[]{:S(2)}, u32[]{:S(2)}) collective-permute-start(f32[4,216,64]{1,2,0:T(8,128)S(1)} %slice_select_fusion.1), channel_id=1, source_target_pairs={{0,2},{2,0},{1,3},{3,1},{4,6},{6,4},{5,7},{7,5},{8,10},{10,8},{9,1... | collective-permute-start | bytes 663560 | tf_op jit(solution)/shard_map/ppermute | solution.py:111
  31.1 4.7 %fusion.11 = bf16[4,16,8,5,128]{4,2,3,1,0:T(8,128)(2,1)S(1)} fusion(bf16[3,3,3,128,128]{4,3,2,1,0:T(8,128)(2,1)S(1)} %bitcast.251, bf16[6,18,1,7,2,128]{5,3,4,1,0,2:T(8,128)(2,1)S(1)} %slice.215, bf16[6,18,1,8,5,128]{5,3,4,1,0,2:T(8,128)(2,1)S(1)} %copy.7, pred[8,5]{0,1:T(8,128)(4,1)S(1)} %copy-done.3), kind=kOutput, calls=%fused_computation.9 | convolution fusion | flops 2270224384 | bytes 3033128 | tf_op jit(solution)/shard_map/conv_general_dilated | solution.py:66
  36.0 0.2 select_add_fusion.1
  36.2 1.6 %collective-permute-start.7 = (f32[4,216,64]{1,2,0:T(8,128)S(1)}, f32[4,216,64]{1,2,0:T(8,128)S(1)}, u32[]{:S(2)}, u32[]{:S(2)}) collective-permute-start(f32[4,216,64]{1,2,0:T(8,128)S(1)} %get-tuple-element.5), channel_id=1, source_target_pairs={{0,2},{2,0},{1,3},{3,1},{4,6},{6,4},{5,7},{7,5},{8,10},{10,8},{9,1... | collective-permute-start | bytes 663560 | tf_op jit(solution)/shard_map/ppermute | solution.py:111
  37.9 0.9 %copy.18 = bf16[4,16,32,128]{3,2,1,0:T(8,128)(2,1)} copy(bf16[4,16,32,128]{3,1,2,0:T(8,128)(2,1)S(1)} %slice_bitcast_fusion) | data formatting | bytes 1048576
  38.8 2.1 %collective-permute-start.6 = (f32[216,64]{0,1:T(8,128)S(1)}, f32[216,64]{0,1:T(8,128)S(1)}, u32[]{:S(2)}, u32[]{:S(2)}) collective-permute-start(f32[216,64]{0,1:T(8,128)S(1)} %get-tuple-element.13), channel_id=1, source_target_pairs={{0,12},{4,0},{8,4},{12,8},{1,13},{5,1},{9,5},{13,9},{2,14},{6,2},{... | collective-permute-start | bytes 165896 | tf_op jit(solution)/shard_map/ppermute | solution.py:40
  40.9 0.6 %collective-permute-start.5 = (f32[216,64]{0,1:T(8,128)S(1)}, f32[216,64]{0,1:T(8,128)S(1)}, u32[]{:S(2)}, u32[]{:S(2)}) collective-permute-start(f32[216,64]{0,1:T(8,128)S(1)} %get-tuple-element.14), channel_id=1, source_target_pairs={{0,8},{4,12},{8,0},{12,4},{1,9},{5,13},{9,1},{13,5},{2,10},{6,14},... | collective-permute-start | bytes 165896 | tf_op jit(solution)/shard_map/ppermute | solution.py:40
  41.5 1.0 %collective-permute-start.4 = (f32[216,64]{0,1:T(8,128)S(1)}, f32[216,64]{0,1:T(8,128)S(1)}, u32[]{:S(2)}, u32[]{:S(2)}) collective-permute-start(f32[216,64]{0,1:T(8,128)S(1)} %get-tuple-element.12), channel_id=1, source_target_pairs={{0,4},{4,8},{8,12},{12,0},{1,5},{5,9},{9,13},{13,1},{2,6},{6,10},{... | collective-permute-start | bytes 165896 | tf_op jit(solution)/shard_map/ppermute | solution.py:40
  42.5 0.2 collective-permute-done.7
  42.7 0.2 select_add_fusion
  42.9 2.7 %collective-permute-start.10 = (f32[216,64]{0,1:T(8,128)S(1)}, f32[216,64]{0,1:T(8,128)S(1)}, u32[]{:S(2)}, u32[]{:S(2)}) collective-permute-start(f32[216,64]{0,1:T(8,128)S(1)} %get-tuple-element.16), channel_id=1, source_target_pairs={{0,12},{4,0},{8,4},{12,8},{1,13},{5,1},{9,5},{13,9},{2,14},{6,2},{... | collective-permute-start | bytes 165896 | tf_op jit(solution)/shard_map/ppermute | solution.py:40
  45.7 0.5 collective-permute-start.9
  46.2 0.2 collective-permute-start.8
  46.3 1.8 %collective-permute-done.5 = f32[216,64]{0,1:T(8,128)S(1)} collective-permute-done((f32[216,64]{0,1:T(8,128)S(1)}, f32[216,64]{0,1:T(8,128)S(1)}, u32[]{:S(2)}, u32[]{:S(2)}) %collective-permute-start.5) | collective-permute-done | bytes 55328 | tf_op jit(solution)/shard_map/ppermute | solution.py:40
  48.1 0.6 %collective-permute-done.10 = f32[216,64]{0,1:T(8,128)S(1)} collective-permute-done((f32[216,64]{0,1:T(8,128)S(1)}, f32[216,64]{0,1:T(8,128)S(1)}, u32[]{:S(2)}, u32[]{:S(2)}) %collective-permute-start.10) | collective-permute-done | bytes 55328 | tf_op jit(solution)/shard_map/ppermute | solution.py:40
  48.7 2.1 %collective-permute-done.9 = f32[216,64]{0,1:T(8,128)S(1)} collective-permute-done((f32[216,64]{0,1:T(8,128)S(1)}, f32[216,64]{0,1:T(8,128)S(1)}, u32[]{:S(2)}, u32[]{:S(2)}) %collective-permute-start.9) | collective-permute-done | bytes 55328 | tf_op jit(solution)/shard_map/ppermute | solution.py:40
  50.8 1.4 %collective-permute-done.8 = f32[216,64]{0,1:T(8,128)S(1)} collective-permute-done((f32[216,64]{0,1:T(8,128)S(1)}, f32[216,64]{0,1:T(8,128)S(1)}, u32[]{:S(2)}, u32[]{:S(2)}) %collective-permute-start.8) | collective-permute-done | bytes 55328 | tf_op jit(solution)/shard_map/ppermute | solution.py:40
  52.2 0.8 %maximum_multiply_fusion = f32[432,64]{0,1:T(8,128)} fusion(f32[216,64]{0,1:T(8,128)S(1)} %fusion.40, f32[216,64]{0,1:T(8,128)S(1)} %fusion.42), kind=kLoop, calls=%fused_computation.69 | loop fusion | flops 55296 | bytes 221184 | tf_op jit(solution)/shard_map/div | solution.py:119
  (66 shorter events, 3.0 us)
Async XLA Ops:
  0.6 30.5 %copy-start = (bf16[27,128,128]{2,1,0:T(8,128)(2,1)S(1)}, bf16[27,128,128]{2,1,0:T(8,128)(2,1)}, u32[]{:S(2)}) copy-start(bf16[27,128,128]{2,1,0:T(8,128)(2,1)} %param.5) | copy-start | bytes 2654212
  1.5 4.8 %collective-permute-start = (bf16[4,1,32,128]{3,2,1,0:T(8,128)(2,1)S(1)}, bf16[4,1,32,128]{3,2,1,0:T(8,128)(2,1)S(1)}, u32[]{:S(2)}, u32[]{:S(2)}) collective-permute-start(bf16[4,1,32,128]{3,2,1,0:T(8,128)(2,1)S(1)} %slice_select_fusion.2), channel_id=1, source_target_pairs={{0,2},{2,0},{1,3},{3,1},{4,6},{6,4},{5,7},{7,5},{8,10},{10,8},{9,1... | collective-permute-start | bytes 98312 | tf_op jit(solution)/shard_map/ppermute | solution.py:17
  8.2 1.0 %copy-start.2 = (bf16[4,16,32,128]{3,2,1,0:T(8,128)(2,1)S(1)}, bf16[4,16,32,128]{3,2,1,0:T(8,128)(2,1)}, u32[]{:S(2)}) copy-start(bf16[4,16,32,128]{3,2,1,0:T(8,128)(2,1)} %param.3) | copy-start | bytes 1572868
  13.5 11.2 %copy-start.1 = (bf16[4,16,32,128]{3,2,1,0:T(8,128)(2,1)S(1)}, bf16[4,16,32,128]{3,2,1,0:T(8,128)(2,1)}, u32[]{:S(2)}) copy-start(bf16[4,16,32,128]{3,2,1,0:T(8,128)(2,1)} %param.4) | copy-start | bytes 1572868
  13.5 7.7 %collective-permute-start.2 = (bf16[1,18,32,128]{3,2,1,0:T(8,128)(2,1)S(1)}, bf16[1,18,32,128]{3,2,1,0:T(8,128)(2,1)S(1)}, u32[]{:S(2)}, u32[]{:S(2)}) collective-permute-start(bf16[1,18,32,128]{3,2,1,0:T(8,128)(2,1)S(1)} %get-tuple-element.11), channel_id=1, source_target_pairs={{4,0},{8,4},{12,8},{0,12},{5,1},{9,5},{13,9},{1,13},{6,2},{10,6},{... | collective-permute-start | bytes 442376 | tf_op jit(solution)/shard_map/ppermute | solution.py:23
  17.7 6.9 %collective-permute-start.1 = (bf16[1,18,32,128]{3,2,1,0:T(8,128)(2,1)S(1)}, bf16[1,18,32,128]{3,2,1,0:T(8,128)(2,1)S(1)}, u32[]{:S(2)}, u32[]{:S(2)}) collective-permute-start(bf16[1,18,32,128]{3,2,1,0:T(8,128)(2,1)S(1)} %get-tuple-element.10), channel_id=1, source_target_pairs={{0,4},{4,8},{8,12},{12,0},{1,5},{5,9},{9,13},{13,1},{2,6},{6,10},{... | collective-permute-start | bytes 442376 | tf_op jit(solution)/shard_map/ppermute | solution.py:22
  29.5 1.7 %copy-start.3 = (pred[8,5]{0,1:T(8,128)(4,1)S(1)}, pred[8,5]{0,1:T(8,128)(4,1)}, u32[]{:S(2)}) copy-start(pred[8,5]{0,1:T(8,128)(4,1)} %constant.85) | copy-start | bytes 124
  29.6 6.4 %collective-permute-start.3 = (f32[4,216,64]{1,2,0:T(8,128)S(1)}, f32[4,216,64]{1,2,0:T(8,128)S(1)}, u32[]{:S(2)}, u32[]{:S(2)}) collective-permute-start(f32[4,216,64]{1,2,0:T(8,128)S(1)} %slice_select_fusion.1), channel_id=1, source_target_pairs={{0,2},{2,0},{1,3},{3,1},{4,6},{6,4},{5,7},{7,5},{8,10},{10,8},{9,1... | collective-permute-start | bytes 663560 | tf_op jit(solution)/shard_map/ppermute | solution.py:111
  36.2 6.4 %collective-permute-start.7 = (f32[4,216,64]{1,2,0:T(8,128)S(1)}, f32[4,216,64]{1,2,0:T(8,128)S(1)}, u32[]{:S(2)}, u32[]{:S(2)}) collective-permute-start(f32[4,216,64]{1,2,0:T(8,128)S(1)} %get-tuple-element.5), channel_id=1, source_target_pairs={{0,2},{2,0},{1,3},{3,1},{4,6},{6,4},{5,7},{7,5},{8,10},{10,8},{9,1... | collective-permute-start | bytes 663560 | tf_op jit(solution)/shard_map/ppermute | solution.py:111
  38.8 7.3 %collective-permute-start.6 = (f32[216,64]{0,1:T(8,128)S(1)}, f32[216,64]{0,1:T(8,128)S(1)}, u32[]{:S(2)}, u32[]{:S(2)}) collective-permute-start(f32[216,64]{0,1:T(8,128)S(1)} %get-tuple-element.13), channel_id=1, source_target_pairs={{0,12},{4,0},{8,4},{12,8},{1,13},{5,1},{9,5},{13,9},{2,14},{6,2},{... | collective-permute-start | bytes 165896 | tf_op jit(solution)/shard_map/ppermute | solution.py:40
  40.9 7.2 %collective-permute-start.5 = (f32[216,64]{0,1:T(8,128)S(1)}, f32[216,64]{0,1:T(8,128)S(1)}, u32[]{:S(2)}, u32[]{:S(2)}) collective-permute-start(f32[216,64]{0,1:T(8,128)S(1)} %get-tuple-element.14), channel_id=1, source_target_pairs={{0,8},{4,12},{8,0},{12,4},{1,9},{5,13},{9,1},{13,5},{2,10},{6,14},... | collective-permute-start | bytes 165896 | tf_op jit(solution)/shard_map/ppermute | solution.py:40
  41.5 6.6 %collective-permute-start.4 = (f32[216,64]{0,1:T(8,128)S(1)}, f32[216,64]{0,1:T(8,128)S(1)}, u32[]{:S(2)}, u32[]{:S(2)}) collective-permute-start(f32[216,64]{0,1:T(8,128)S(1)} %get-tuple-element.12), channel_id=1, source_target_pairs={{0,4},{4,8},{8,12},{12,0},{1,5},{5,9},{9,13},{13,1},{2,6},{6,10},{... | collective-permute-start | bytes 165896 | tf_op jit(solution)/shard_map/ppermute | solution.py:40
  42.9 5.8 %collective-permute-start.10 = (f32[216,64]{0,1:T(8,128)S(1)}, f32[216,64]{0,1:T(8,128)S(1)}, u32[]{:S(2)}, u32[]{:S(2)}) collective-permute-start(f32[216,64]{0,1:T(8,128)S(1)} %get-tuple-element.16), channel_id=1, source_target_pairs={{0,12},{4,0},{8,4},{12,8},{1,13},{5,1},{9,5},{13,9},{2,14},{6,2},{... | collective-permute-start | bytes 165896 | tf_op jit(solution)/shard_map/ppermute | solution.py:40
  45.7 5.2 %collective-permute-start.9 = (f32[216,64]{0,1:T(8,128)S(1)}, f32[216,64]{0,1:T(8,128)S(1)}, u32[]{:S(2)}, u32[]{:S(2)}) collective-permute-start(f32[216,64]{0,1:T(8,128)S(1)} %get-tuple-element.17), channel_id=1, source_target_pairs={{0,8},{4,12},{8,0},{12,4},{1,9},{5,13},{9,1},{13,5},{2,10},{6,14},... | collective-permute-start | bytes 165896 | tf_op jit(solution)/shard_map/ppermute | solution.py:40
  46.2 6.1 %collective-permute-start.8 = (f32[216,64]{0,1:T(8,128)S(1)}, f32[216,64]{0,1:T(8,128)S(1)}, u32[]{:S(2)}, u32[]{:S(2)}) collective-permute-start(f32[216,64]{0,1:T(8,128)S(1)} %get-tuple-element.15), channel_id=1, source_target_pairs={{0,4},{4,8},{8,12},{12,0},{1,5},{5,9},{9,13},{13,1},{2,6},{6,10},{... | collective-permute-start | bytes 165896 | tf_op jit(solution)/shard_map/ppermute | solution.py:40

commit v14 on v11

--- a/solution.py
+++ b/solution.py
@@ -62,12 +62,6 @@
     taps = weight.reshape(3, 3, 3, chans, weight.shape[2])
     kflip = jnp.transpose(taps[::-1, ::-1, ::-1], (0, 1, 2, 4, 3))
     pad = [(0, 0), (0, 0), (1, 1)]
-    inner = lax.conv_general_dilated(
-        gh[None], kflip, (1, 1, 1), pad,
-        dimension_numbers=("NDHWC", "DHWIO", "NDHWC"),
-        preferred_element_type=jnp.float32,
-    )[0]
-    grad_in = inner.astype(jnp.bfloat16)
     gshare = lax.dynamic_slice_in_dim(gh, offset, half, 3)
     gdeep = jnp.pad(gshare, ((0, 0), (0, 0), (1, 1), (0, 0)))
     stack = jnp.concatenate([lax.slice_in_dim(gdeep, 2 - c, 2 - c + depth, axis=2) for c in range(3)], axis=3)
@@ -82,6 +76,7 @@
     nx = lax.axis_size("gx")
     ny = lax.axis_size("gy")
     owned_rows = 27 * chans // (nx * ny)
+    gates = []
     if ny == 2:
         iy = lax.axis_index("gy")
         side = [
@@ -96,12 +91,27 @@
             keep = jnp.where(iy == 0, side[0][:, lo:hi], side[1][:, lo:hi])
             send = jnp.where(iy == 0, side[1][:, lo:hi], side[0][:, lo:hi])
             partial = keep + lax.ppermute(send, "gy", [(0, 1), (1, 0)])
+            gates.append(partial)
             parts.append(scatter_sum(partial, "gx", 0))
         owned = jnp.concatenate(parts, axis=0) if len(parts) > 1 else parts[0]
     else:
         weight_terms = jnp.concatenate(pieces, axis=0)
         blocks = weight_terms.reshape(nx, ny, owned_rows, half)
         owned = scatter_sum(scatter_sum(blocks, "gy", 1), "gx", 0)
+    rows = size_x // 2 if size_x % 2 == 0 else size_x
+    halves = []
+    for lo in range(0, size_x, rows):
+        source = gh
+        if lo > 0 and gates:
+            source = lax.optimization_barrier((gh, gates[0]))[0]
+        halves.append(
+            lax.conv_general_dilated(
+                source[None, lo : lo + rows + 2], kflip, (1, 1, 1), pad,
+                dimension_numbers=("NDHWC", "DHWIO", "NDHWC"),
+                preferred_element_type=jnp.float32,
+            )[0].astype(jnp.bfloat16)
+        )
+    grad_in = jnp.concatenate(halves, axis=0) if len(halves) > 1 else halves[0]
     total_cells = size_x * lax.axis_size("gx") * size_y * lax.axis_size("gy") * depth
     grad_weight = owned / jnp.sqrt(jnp.float32(total_cells))
     return (grad_in, grad_weight)

time: 50.5 us -> 54.3 us (1.075)
  starting transfers between devices: 17 us -> 19.7 us
  local copies, waits for them, and re-layouts: 4.93 us -> 5.7 us
    ppermute x2, waiting for transfers between devices: 0.75 us -> 2.77 us  [on_device(): partial = keep + lax.ppermute(send, 'gy', [(0, 1), (1, 0)])]
    ppermute x6, starting transfers between devices: 7.58 us -> 9.34 us  [scatter_sum(): lax.ppermute(part, axis, [(j, (j + shift) % count) for j in range(count)])]
    ppermute x6, waiting for transfers between devices: 5.41 us -> 3.68 us  [scatter_sum(): lax.ppermute(part, axis, [(j, (j + shift) % count) for j in range(count)])]
    ppermute x2, starting transfers between devices: 2.15 us -> 3.11 us  [on_device(): partial = keep + lax.ppermute(send, 'gy', [(0, 1), (1, 0)])]
    unnamed x19 -> x20, local copies, waits for them, and re-layouts: 1.97 us -> 2.32 us
    conv_general_dilated x1 -> x2, matrix products: 4.96 us -> 4.92 us  [on_device(): lax.conv_general_dilated(source[None, lo:lo + rows + 2], kflip, (1, 1, 1)...]
  transfers between devices with their start and end apart: 11 -> 11, of which waited for: 6 -> 7; matrix products, arithmetic and copies ran while one was open for 14% -> 15% of each run, Pallas kernels for 0% -> 0%
where the time goes in v14:
time: 54.3 us; the launch traced here: 54.1 us
  starting transfers between devices  19.7 us (36%)
  waiting for transfers between devices  13.5 us (25%)
  matrix products  9.06 us (17%)
  local copies, waits for them, and re-layouts  5.7 us (10%)
  other arithmetic  4.93 us (9%)
  between operations  1.18 us (2%)
    ppermute x6, starting transfers between devices, scatter_sum(): lax.ppermute(part, axis, [(j, (j + shift) % count) for j in range(count)])  9.34 us
    conv_general_dilated x2, matrix products, on_device(): lax.conv_general_dilated(source[None, lo:lo + rows + 2], kflip, (1, 1, 1)...  4.92 us
    ppermute x1, waiting for transfers between devices, with_halo(): low = lax.ppermute(tail, axis, [(i, (i + 1) % count) for i in range(count)])  4.21 us
    dot_general x9, matrix products, on_device(): lax.dot_general(x_act, window, (((0, 1, 2), (0, 1, 2)), ((), ())), prefer...  4.14 us
    ppermute x6, waiting for transfers between devices, scatter_sum(): lax.ppermute(part, axis, [(j, (j + shift) % count) for j in range(count)])  3.68 us
    ppermute x2, starting transfers between devices, on_device(): partial = keep + lax.ppermute(send, 'gy', [(0, 1), (1, 0)])  3.11 us
    ppermute x1, starting transfers between devices, with_halo(): got = lax.ppermute(jnp.where(me == 0, tail, head), axis, [(0, 1), (1, 0)])  2.94 us
    ppermute x2, waiting for transfers between devices, on_device(): partial = keep + lax.ppermute(send, 'gy', [(0, 1), (1, 0)])  2.77 us
  transfers between devices with their start and end apart: 11, of which 7 were waited for; matrix products, arithmetic and copies ran while one was open for 15% of the time, Pallas kernels for 0%

profile of v14, /device:TPU:0, one launch (start us, length us, event | category | flops | bytes accessed | tf_op | source)
XLA Modules:
  0.0 54.1 jit_solution(9538026230274250766)
XLA Ops:
  0.7 0.9 %slice_select_fusion.2 = bf16[4,1,32,128]{3,2,1,0:T(8,128)(2,1)S(1)} fusion(bf16[4,16,32,128]{3,2,1,0:T(8,128)(2,1)} %param.4, pred[]{:T(512)S(6)} %eq.26), kind=kLoop, calls=%fused_computation.72 | loop fusion | flops 16384 | bytes 98305 | tf_op jit(solution)/shard_map/jit(_where)/select_n | solution.py:17
  1.6 2.9 %collective-permute-start = (bf16[4,1,32,128]{3,2,1,0:T(8,128)(2,1)S(1)}, bf16[4,1,32,128]{3,2,1,0:T(8,128)(2,1)S(1)}, u32[]{:S(2)}, u32[]{:S(2)}) collective-permute-start(bf16[4,1,32,128]{3,2,1,0:T(8,128)(2,1)S(1)} %slice_select_fusion.2), channel_id=1, source_target_pairs={{0,2},{2,0},{1,3},{3,1},{4,6},{6,4},{5,7},{7,5},{8,10},{10,8},{9,1... | collective-permute-start | bytes 98312 | tf_op jit(solution)/shard_map/ppermute | solution.py:17
  4.5 1.9 %collective-permute-done = bf16[4,1,32,128]{3,2,1,0:T(8,128)(2,1)S(1)} collective-permute-done((bf16[4,1,32,128]{3,2,1,0:T(8,128)(2,1)S(1)}, bf16[4,1,32,128]{3,2,1,0:T(8,128)(2,1)S(1)}, u32[]{:S(2)}, u32[]{:S(2)}) %collective-permute-start) | collective-permute-done | bytes 32800 | tf_op jit(solution)/shard_map/ppermute | solution.py:17
  6.4 1.0 %pad_maximum_fusion.10 = (bf16[1,18,32,128]{3,2,1,0:T(8,128)(2,1)S(1)}, bf16[1,18,32,128]{3,2,1,0:T(8,128)(2,1)S(1)}) fusion(bf16[4,1,32,128]{3,2,1,0:T(8,128)(2,1)S(1)} %get-tuple-element.21, bf16[4,16,32,128]{3,2,1,0:T(8,128)(2,1)} %param.4, bf16[4,1,32,128]{3,2,1,0:T(8,128)(2,1)S(1)} %get-tuple-element.20), kind=kLoop, calls=%fused_computation.39 | loop fusion | flops 294912 | bytes 884736 | tf_op jit(solution)/shard_map/slice | solution.py:11
  7.4 2.2 %collective-permute-start.1 = (bf16[1,18,32,128]{3,2,1,0:T(8,128)(2,1)S(1)}, bf16[1,18,32,128]{3,2,1,0:T(8,128)(2,1)S(1)}, u32[]{:S(2)}, u32[]{:S(2)}) collective-permute-start(bf16[1,18,32,128]{3,2,1,0:T(8,128)(2,1)S(1)} %get-tuple-element.10), channel_id=1, source_target_pairs={{0,4},{4,8},{8,12},{12,0},{1,5},{5,9},{9,13},{13,1},{2,6},{6,10},{... | collective-permute-start | bytes 442376 | tf_op jit(solution)/shard_map/ppermute | solution.py:22
  9.6 2.1 %collective-permute-start.2 = (bf16[1,18,32,128]{3,2,1,0:T(8,128)(2,1)S(1)}, bf16[1,18,32,128]{3,2,1,0:T(8,128)(2,1)S(1)}, u32[]{:S(2)}, u32[]{:S(2)}) collective-permute-start(bf16[1,18,32,128]{3,2,1,0:T(8,128)(2,1)S(1)} %get-tuple-element.11), channel_id=1, source_target_pairs={{4,0},{8,4},{12,8},{0,12},{5,1},{9,5},{13,9},{1,13},{6,2},{10,6},{... | collective-permute-start | bytes 442376 | tf_op jit(solution)/shard_map/ppermute | solution.py:23
  11.7 4.2 %collective-permute-done.1 = bf16[1,18,32,128]{3,2,1,0:T(8,128)(2,1)S(1)} collective-permute-done((bf16[1,18,32,128]{3,2,1,0:T(8,128)(2,1)S(1)}, bf16[1,18,32,128]{3,2,1,0:T(8,128)(2,1)S(1)}, u32[]{:S(2)}, u32[]{:S(2)}) %collective-permute-start.1) | collective-permute-done | bytes 147488 | tf_op jit(solution)/shard_map/ppermute | solution.py:22
  15.9 0.9 %collective-permute-done.2 = bf16[1,18,32,128]{3,2,1,0:T(8,128)(2,1)S(1)} collective-permute-done((bf16[1,18,32,128]{3,2,1,0:T(8,128)(2,1)S(1)}, bf16[1,18,32,128]{3,2,1,0:T(8,128)(2,1)S(1)}, u32[]{:S(2)}, u32[]{:S(2)}) %collective-permute-start.2) | collective-permute-done | bytes 147488 | tf_op jit(solution)/shard_map/ppermute | solution.py:23
  16.9 0.2 pad_maximum_fusion.1
  17.1 0.3 constant_dynamic-slice_fusion
  17.4 0.8 %pad_slice_fusion.1 = (bf16[6,18,32,64]{3,2,1,0:T(8,128)(2,1)S(1)}, bf16[6,18,32,64]{3,2,1,0:T(8,128)(2,1)S(1)}) fusion(bf16[6,18,32,64]{3,2,1,0:T(8,128)(2,1)S(1)} %constant_dynamic-slice_fusion), kind=kLoop, calls=%fused_computation.9 | loop fusion | bytes 1327104 | tf_op jit(solution)/shard_map/slice | solution.py:67
  18.2 0.9 %pad_maximum_fusion = bf16[6,18,32,192]{3,2,1,0:T(8,128)(2,1)S(1)} fusion(bf16[6,18,32,64]{3,2,1,0:T(8,128)(2,1)S(1)} %get-tuple-element.9, bf16[6,18,32,64]{3,2,1,0:T(8,128)(2,1)S(1)} %constant_dynamic-slice_fusion, bf16[6,18,32,64]{3,2,1,0:T(8,128)(2,1)S(1)} %get-tuple-element.8), kind=kLoop, calls=%fused_computation.3 | loop fusion | flops 3981312 | bytes 2654208 | tf_op jit(solution)/shard_map/concatenate | solution.py:67
  19.0 0.2 copy-done.2
  19.2 0.5 fusion.32
  19.7 0.5 fusion.33
  20.1 0.5 fusion.31
  20.6 0.5 fusion.30
  21.1 0.5 fusion.36
  21.5 0.5 fusion.37
  22.0 0.5 fusion.34
  22.5 0.5 fusion.35
  23.7 0.5 fusion.38
  25.1 0.1 maximum_bitcast_fusion.7
  25.3 0.1 maximum_bitcast_fusion.2
  25.4 0.1 maximum_bitcast_fusion.4
  25.6 0.2 slice_select_fusion
  25.8 1.6 %collective-permute-start.7 = (f32[4,216,64]{1,2,0:T(8,128)S(1)}, f32[4,216,64]{1,2,0:T(8,128)S(1)}, u32[]{:S(2)}, u32[]{:S(2)}) collective-permute-start(f32[4,216,64]{1,2,0:T(8,128)S(1)} %slice_select_fusion), channel_id=1, source_target_pairs={{0,2},{2,0},{1,3},{3,1},{4,6},{6,4},{5,7},{7,5},{8,10},{10,8},{9,1... | collective-permute-start | bytes 663560 | tf_op jit(solution)/shard_map/ppermute | solution.py:93
  27.4 0.5 copy.34
  27.8 0.3 pad.5.clone
  28.1 0.1 copy.9
  28.3 0.2 copy-done.3
  28.5 2.5 %fusion.2 = bf16[2,16,8,5,128]{4,2,3,1,0:T(8,128)(2,1)S(1)} fusion(bf16[3,3,3,128,128]{4,3,2,1,0:T(8,128)(2,1)S(1)} %bitcast.207, bf16[4,18,1,7,2,128]{5,3,4,1,0,2:T(8,128)(2,1)S(1)} %slice.150, bf16[4,18,1,8,5,128]{5,3,4,1,0,2:T(8,128)(2,1)S(1)} %copy.9, pred[8,5]{0,1:T(8,128)(4,1)S(1)} %copy-done.3), kind=kOutput, calls=%fused_computation.6 | convolution fusion | flops 1135886336 | bytes 2207784 | tf_op jit(solution)/shard_map/conv_general_dilated | solution.py:108
  31.0 1.6 %collective-permute-done.7 = f32[4,216,64]{1,2,0:T(8,128)S(1)} collective-permute-done((f32[4,216,64]{1,2,0:T(8,128)S(1)}, f32[4,216,64]{1,2,0:T(8,128)S(1)}, u32[]{:S(2)}, u32[]{:S(2)}) %collective-permute-start.7) | collective-permute-done | bytes 221216 | tf_op jit(solution)/shard_map/ppermute | solution.py:93
  32.6 0.2 select_add_fusion
  32.9 2.5 %collective-permute-start.10 = (f32[216,64]{0,1:T(8,128)S(1)}, f32[216,64]{0,1:T(8,128)S(1)}, u32[]{:S(2)}, u32[]{:S(2)}) collective-permute-start(f32[216,64]{0,1:T(8,128)S(1)} %get-tuple-element.16), channel_id=1, source_target_pairs={{0,12},{4,0},{8,4},{12,8},{1,13},{5,1},{9,5},{13,9},{2,14},{6,2},{... | collective-permute-start | bytes 165896 | tf_op jit(solution)/shard_map/ppermute | solution.py:40
  35.3 0.8 %collective-permute-start.9 = (f32[216,64]{0,1:T(8,128)S(1)}, f32[216,64]{0,1:T(8,128)S(1)}, u32[]{:S(2)}, u32[]{:S(2)}) collective-permute-start(f32[216,64]{0,1:T(8,128)S(1)} %get-tuple-element.17), channel_id=1, source_target_pairs={{0,8},{4,12},{8,0},{12,4},{1,9},{5,13},{9,1},{13,5},{2,10},{6,14},... | collective-permute-start | bytes 165896 | tf_op jit(solution)/shard_map/ppermute | solution.py:40
  36.1 1.6 %collective-permute-start.3 = (f32[4,216,64]{1,2,0:T(8,128)S(1)}, f32[4,216,64]{1,2,0:T(8,128)S(1)}, u32[]{:S(2)}, u32[]{:S(2)}) collective-permute-start(f32[4,216,64]{1,2,0:T(8,128)S(1)} %get-tuple-element.7), channel_id=1, source_target_pairs={{0,2},{2,0},{1,3},{3,1},{4,6},{6,4},{5,7},{7,5},{8,10},{10,8},{9,1... | collective-permute-start | bytes 663560 | tf_op jit(solution)/shard_map/ppermute | solution.py:93
  37.7 0.5 collective-permute-done.10
  38.2 3.1 %collective-permute-done.8 = f32[216,64]{0,1:T(8,128)S(1)} collective-permute-done((f32[216,64]{0,1:T(8,128)S(1)}, f32[216,64]{0,1:T(8,128)S(1)}, u32[]{:S(2)}, u32[]{:S(2)}) %collective-permute-start.8) | collective-permute-done | bytes 55328 | tf_op jit(solution)/shard_map/ppermute | solution.py:40
  41.4 1.2 %collective-permute-done.3 = f32[4,216,64]{1,2,0:T(8,128)S(1)} collective-permute-done((f32[4,216,64]{1,2,0:T(8,128)S(1)}, f32[4,216,64]{1,2,0:T(8,128)S(1)}, u32[]{:S(2)}, u32[]{:S(2)}) %collective-permute-start.3) | collective-permute-done | bytes 221216 | tf_op jit(solution)/shard_map/ppermute | solution.py:93
  42.7 3.6 %collective-permute-start.4 = (f32[216,64]{0,1:T(8,128)S(1)}, f32[216,64]{0,1:T(8,128)S(1)}, u32[]{:S(2)}, u32[]{:S(2)}) collective-permute-start(f32[216,64]{0,1:T(8,128)S(1)} %get-tuple-element.12), channel_id=1, source_target_pairs={{0,4},{4,8},{8,12},{12,0},{1,5},{5,9},{9,13},{13,1},{2,6},{6,10},{... | collective-permute-start | bytes 165896 | tf_op jit(solution)/shard_map/ppermute | solution.py:40
  46.3 2.4 %collective-permute-start.6 = (f32[216,64]{0,1:T(8,128)S(1)}, f32[216,64]{0,1:T(8,128)S(1)}, u32[]{:S(2)}, u32[]{:S(2)}) collective-permute-start(f32[216,64]{0,1:T(8,128)S(1)} %get-tuple-element.13), channel_id=1, source_target_pairs={{0,12},{4,0},{8,4},{12,8},{1,13},{5,1},{9,5},{13,9},{2,14},{6,2},{... | collective-permute-start | bytes 165896 | tf_op jit(solution)/shard_map/ppermute | solution.py:40
  48.8 0.5 copy.35
  49.3 0.3 pad.7.clone
  49.6 0.1 copy.22
  49.7 2.5 %fusion.3 = bf16[2,16,8,5,128]{4,2,3,1,0:T(8,128)(2,1)S(1)} fusion(bf16[3,3,3,128,128]{4,3,2,1,0:T(8,128)(2,1)S(1)} %bitcast.208, bf16[4,18,1,7,2,128]{5,3,4,1,0,2:T(8,128)(2,1)S(1)} %slice.168, bf16[4,18,1,8,5,128]{5,3,4,1,0,2:T(8,128)(2,1)S(1)} %copy.22, pred[8,5]{0,1:T(8,128)(4,1)S(1)} %copy-done.3), kind=kOutput, calls=%fused_computation.7 | convolution fusion | flops 1135886336 | bytes 2207784 | tf_op jit(solution)/shard_map/conv_general_dilated | solution.py:108
  52.4 0.9 %copy.24 = bf16[4,16,32,128]{3,2,1,0:T(8,128)(2,1)} copy(bf16[4,16,32,128]{3,1,2,0:T(8,128)(2,1)S(1)} %pad_maximum_fusion.7) | data formatting | bytes 1048576
  53.3 0.8 %maximum_multiply_fusion = f32[432,64]{0,1:T(8,128)} fusion(f32[216,64]{0,1:T(8,128)S(1)} %fusion.20, f32[216,64]{0,1:T(8,128)S(1)} %fusion.22), kind=kLoop, calls=%fused_computation.50 | loop fusion | flops 55296 | bytes 221184 | tf_op jit(solution)/shard_map/div | solution.py:116
  (62 shorter events, 2.3 us)
Async XLA Ops:
  0.6 27.7 %copy-start = (bf16[27,128,128]{2,1,0:T(8,128)(2,1)S(1)}, bf16[27,128,128]{2,1,0:T(8,128)(2,1)}, u32[]{:S(2)}) copy-start(bf16[27,128,128]{2,1,0:T(8,128)(2,1)} %param.5) | copy-start | bytes 2654212
  0.6 16.3 %copy-start.1 = (bf16[4,16,32,128]{3,2,1,0:T(8,128)(2,1)S(1)}, bf16[4,16,32,128]{3,2,1,0:T(8,128)(2,1)}, u32[]{:S(2)}) copy-start(bf16[4,16,32,128]{3,2,1,0:T(8,128)(2,1)} %param.4) | copy-start | bytes 1572868
  1.6 4.8 %collective-permute-start = (bf16[4,1,32,128]{3,2,1,0:T(8,128)(2,1)S(1)}, bf16[4,1,32,128]{3,2,1,0:T(8,128)(2,1)S(1)}, u32[]{:S(2)}, u32[]{:S(2)}) collective-permute-start(bf16[4,1,32,128]{3,2,1,0:T(8,128)(2,1)S(1)} %slice_select_fusion.2), channel_id=1, source_target_pairs={{0,2},{2,0},{1,3},{3,1},{4,6},{6,4},{5,7},{7,5},{8,10},{10,8},{9,1... | collective-permute-start | bytes 98312 | tf_op jit(solution)/shard_map/ppermute | solution.py:17
  7.4 8.5 %collective-permute-start.1 = (bf16[1,18,32,128]{3,2,1,0:T(8,128)(2,1)S(1)}, bf16[1,18,32,128]{3,2,1,0:T(8,128)(2,1)S(1)}, u32[]{:S(2)}, u32[]{:S(2)}) collective-permute-start(bf16[1,18,32,128]{3,2,1,0:T(8,128)(2,1)S(1)} %get-tuple-element.10), channel_id=1, source_target_pairs={{0,4},{4,8},{8,12},{12,0},{1,5},{5,9},{9,13},{13,1},{2,6},{6,10},{... | collective-permute-start | bytes 442376 | tf_op jit(solution)/shard_map/ppermute | solution.py:22
  9.6 7.3 %collective-permute-start.2 = (bf16[1,18,32,128]{3,2,1,0:T(8,128)(2,1)S(1)}, bf16[1,18,32,128]{3,2,1,0:T(8,128)(2,1)S(1)}, u32[]{:S(2)}, u32[]{:S(2)}) collective-permute-start(bf16[1,18,32,128]{3,2,1,0:T(8,128)(2,1)S(1)} %get-tuple-element.11), channel_id=1, source_target_pairs={{4,0},{8,4},{12,8},{0,12},{5,1},{9,5},{13,9},{1,13},{6,2},{10,6},{... | collective-permute-start | bytes 442376 | tf_op jit(solution)/shard_map/ppermute | solution.py:23
  18.2 1.0 %copy-start.2 = (bf16[4,16,32,128]{3,2,1,0:T(8,128)(2,1)S(1)}, bf16[4,16,32,128]{3,2,1,0:T(8,128)(2,1)}, u32[]{:S(2)}) copy-start(bf16[4,16,32,128]{3,2,1,0:T(8,128)(2,1)} %param.3) | copy-start | bytes 1572868
  25.8 6.8 %collective-permute-start.7 = (f32[4,216,64]{1,2,0:T(8,128)S(1)}, f32[4,216,64]{1,2,0:T(8,128)S(1)}, u32[]{:S(2)}, u32[]{:S(2)}) collective-permute-start(f32[4,216,64]{1,2,0:T(8,128)S(1)} %slice_select_fusion), channel_id=1, source_target_pairs={{0,2},{2,0},{1,3},{3,1},{4,6},{6,4},{5,7},{7,5},{8,10},{10,8},{9,1... | collective-permute-start | bytes 663560 | tf_op jit(solution)/shard_map/ppermute | solution.py:93
  27.8 0.7 %copy-start.3 = (pred[8,5]{0,1:T(8,128)(4,1)S(1)}, pred[8,5]{0,1:T(8,128)(4,1)}, u32[]{:S(2)}) copy-start(pred[8,5]{0,1:T(8,128)(4,1)} %constant.85) | copy-start | bytes 124
  32.9 5.4 %collective-permute-start.10 = (f32[216,64]{0,1:T(8,128)S(1)}, f32[216,64]{0,1:T(8,128)S(1)}, u32[]{:S(2)}, u32[]{:S(2)}) collective-permute-start(f32[216,64]{0,1:T(8,128)S(1)} %get-tuple-element.16), channel_id=1, source_target_pairs={{0,12},{4,0},{8,4},{12,8},{1,13},{5,1},{9,5},{13,9},{2,14},{6,2},{... | collective-permute-start | bytes 165896 | tf_op jit(solution)/shard_map/ppermute | solution.py:40
  35.3 6.1 %collective-permute-start.8 = (f32[216,64]{0,1:T(8,128)S(1)}, f32[216,64]{0,1:T(8,128)S(1)}, u32[]{:S(2)}, u32[]{:S(2)}) collective-permute-start(f32[216,64]{0,1:T(8,128)S(1)} %get-tuple-element.15), channel_id=1, source_target_pairs={{0,4},{4,8},{8,12},{12,0},{1,5},{5,9},{9,13},{13,1},{2,6},{6,10},{... | collective-permute-start | bytes 165896 | tf_op jit(solution)/shard_map/ppermute | solution.py:40
  35.3 6.1 %collective-permute-start.9 = (f32[216,64]{0,1:T(8,128)S(1)}, f32[216,64]{0,1:T(8,128)S(1)}, u32[]{:S(2)}, u32[]{:S(2)}) collective-permute-start(f32[216,64]{0,1:T(8,128)S(1)} %get-tuple-element.17), channel_id=1, source_target_pairs={{0,8},{4,12},{8,0},{12,4},{1,9},{5,13},{9,1},{13,5},{2,10},{6,14},... | collective-permute-start | bytes 165896 | tf_op jit(solution)/shard_map/ppermute | solution.py:40
  36.1 6.4 %collective-permute-start.3 = (f32[4,216,64]{1,2,0:T(8,128)S(1)}, f32[4,216,64]{1,2,0:T(8,128)S(1)}, u32[]{:S(2)}, u32[]{:S(2)}) collective-permute-start(f32[4,216,64]{1,2,0:T(8,128)S(1)} %get-tuple-element.7), channel_id=1, source_target_pairs={{0,2},{2,0},{1,3},{3,1},{4,6},{6,4},{5,7},{7,5},{8,10},{10,8},{9,1... | collective-permute-start | bytes 663560 | tf_op jit(solution)/shard_map/ppermute | solution.py:93
  42.7 10.6 %collective-permute-start.4 = (f32[216,64]{0,1:T(8,128)S(1)}, f32[216,64]{0,1:T(8,128)S(1)}, u32[]{:S(2)}, u32[]{:S(2)}) collective-permute-start(f32[216,64]{0,1:T(8,128)S(1)} %get-tuple-element.12), channel_id=1, source_target_pairs={{0,4},{4,8},{8,12},{12,0},{1,5},{5,9},{9,13},{13,1},{2,6},{6,10},{... | collective-permute-start | bytes 165896 | tf_op jit(solution)/shard_map/ppermute | solution.py:40
  46.3 7.0 %collective-permute-start.5 = (f32[216,64]{0,1:T(8,128)S(1)}, f32[216,64]{0,1:T(8,128)S(1)}, u32[]{:S(2)}, u32[]{:S(2)}) collective-permute-start(f32[216,64]{0,1:T(8,128)S(1)} %get-tuple-element.14), channel_id=1, source_target_pairs={{0,8},{4,12},{8,0},{12,4},{1,9},{5,13},{9,1},{13,5},{2,10},{6,14},... | collective-permute-start | bytes 165896 | tf_op jit(solution)/shard_map/ppermute | solution.py:40
  46.3 7.0 %collective-permute-start.6 = (f32[216,64]{0,1:T(8,128)S(1)}, f32[216,64]{0,1:T(8,128)S(1)}, u32[]{:S(2)}, u32[]{:S(2)}) collective-permute-start(f32[216,64]{0,1:T(8,128)S(1)} %get-tuple-element.13), channel_id=1, source_target_pairs={{0,12},{4,0},{8,4},{12,8},{1,13},{5,1},{9,5},{13,9},{2,14},{6,2},{... | collective-permute-start | bytes 165896 | tf_op jit(solution)/shard_map/ppermute | solution.py:40

commit v15 on v11

--- a/solution.py
+++ b/solution.py
@@ -88,7 +88,7 @@
             jnp.stack([take_rows(pieces, (gx * 2 + y) * owned_rows, owned_rows) for gx in range(nx)])
             for y in range(2)
         ]
-        split = owned_rows // 2 if owned_rows % 16 == 0 else owned_rows
+        split = (owned_rows * 3 // 4) // 8 * 8 if owned_rows % 8 == 0 else owned_rows
         parts = []
         for lo, hi in ((0, split), (split, owned_rows)):
             if lo == hi:

time: 50.5 us -> 53.1 us (1.051)
  starting transfers between devices: 17 us -> 18.5 us
  waiting for transfers between devices: 13.2 us -> 14.5 us
    ppermute x2, waiting for transfers between devices: 0.75 us -> 2.97 us  [on_device(): partial = keep + lax.ppermute(send, 'gy', [(0, 1), (1, 0)])]
    ppermute x6, starting transfers between devices: 7.58 us -> 9.14 us  [scatter_sum(): lax.ppermute(part, axis, [(j, (j + shift) % count) for j in range(count)])]
    ppermute x6, waiting for transfers between devices: 5.41 us -> 4.52 us  [scatter_sum(): lax.ppermute(part, axis, [(j, (j + shift) % count) for j in range(count)])]
  transfers between devices with their start and end apart: 11 -> 11, of which waited for: 6 -> 6; matrix products, arithmetic and copies ran while one was open for 14% -> 13% of each run, Pallas kernels for 0% -> 0%
where the time goes in v15:
time: 53.1 us; the launch traced here: 52.9 us
  starting transfers between devices  18.5 us (35%)
  waiting for transfers between devices  14.5 us (27%)
  matrix products  9.11 us (17%)
  local copies, waits for them, and re-layouts  4.93 us (9%)
  other arithmetic  4.74 us (9%)
  between operations  1.11 us (2%)
    ppermute x6, starting transfers between devices, scatter_sum(): lax.ppermute(part, axis, [(j, (j + shift) % count) for j in range(count)])  9.14 us
    conv_general_dilated x1, matrix products, on_device(): lax.conv_general_dilated(gh[None], kflip, (1, 1, 1), pad, dimension_numbe...  4.96 us
    ppermute x6, waiting for transfers between devices, scatter_sum(): lax.ppermute(part, axis, [(j, (j + shift) % count) for j in range(count)])  4.52 us
    ppermute x1, waiting for transfers between devices, with_halo(): low = lax.ppermute(tail, axis, [(i, (i + 1) % count) for i in range(count)])  4.21 us
    dot_general x9, matrix products, on_device(): lax.dot_general(x_act, window, (((0, 1, 2), (0, 1, 2)), ((), ())), prefer...  4.15 us
    ppermute x2, waiting for transfers between devices, on_device(): partial = keep + lax.ppermute(send, 'gy', [(0, 1), (1, 0)])  2.97 us
    ppermute x1, starting transfers between devices, with_halo(): got = lax.ppermute(jnp.where(me == 0, tail, head), axis, [(0, 1), (1, 0)])  2.94 us
    ppermute x1, starting transfers between devices, with_halo(): low = lax.ppermute(tail, axis, [(i, (i + 1) % count) for i in range(count)])  2.16 us
  transfers between devices with their start and end apart: 11, of which 6 were waited for; matrix products, arithmetic and copies ran while one was open for 13% of the time, Pallas kernels for 0%

profile of v15, /device:TPU:0, one launch (start us, length us, event | category | flops | bytes accessed | tf_op | source)
XLA Modules:
  0.0 52.9 jit_solution(14119680866552443482)
XLA Ops:
  0.7 0.9 %slice_select_fusion.1 = bf16[4,1,32,128]{3,2,1,0:T(8,128)(2,1)S(1)} fusion(bf16[4,16,32,128]{3,2,1,0:T(8,128)(2,1)} %param.4, pred[]{:T(512)S(6)} %eq.26), kind=kLoop, calls=%fused_computation.59 | loop fusion | flops 16384 | bytes 98305 | tf_op jit(solution)/shard_map/jit(_where)/select_n | solution.py:17
  1.6 2.9 %collective-permute-start = (bf16[4,1,32,128]{3,2,1,0:T(8,128)(2,1)S(1)}, bf16[4,1,32,128]{3,2,1,0:T(8,128)(2,1)S(1)}, u32[]{:S(2)}, u32[]{:S(2)}) collective-permute-start(bf16[4,1,32,128]{3,2,1,0:T(8,128)(2,1)S(1)} %slice_select_fusion.1), channel_id=1, source_target_pairs={{0,2},{2,0},{1,3},{3,1},{4,6},{6,4},{5,7},{7,5},{8,10},{10,8},{9,1... | collective-permute-start | bytes 98312 | tf_op jit(solution)/shard_map/ppermute | solution.py:17
  4.5 1.9 %collective-permute-done = bf16[4,1,32,128]{3,2,1,0:T(8,128)(2,1)S(1)} collective-permute-done((bf16[4,1,32,128]{3,2,1,0:T(8,128)(2,1)S(1)}, bf16[4,1,32,128]{3,2,1,0:T(8,128)(2,1)S(1)}, u32[]{:S(2)}, u32[]{:S(2)}) %collective-permute-start) | collective-permute-done | bytes 32800 | tf_op jit(solution)/shard_map/ppermute | solution.py:17
  6.4 1.0 %pad_maximum_fusion.6 = (bf16[1,18,32,128]{3,2,1,0:T(8,128)(2,1)S(1)}, bf16[1,18,32,128]{3,2,1,0:T(8,128)(2,1)S(1)}) fusion(bf16[4,1,32,128]{3,2,1,0:T(8,128)(2,1)S(1)} %get-tuple-element.20, bf16[4,16,32,128]{3,2,1,0:T(8,128)(2,1)} %param.4, bf16[4,1,32,128]{3,2,1,0:T(8,128)(2,1)S(1)} %get-tuple-element.19), kind=kLoop, calls=%fused_computation.22 | loop fusion | flops 294912 | bytes 884736 | tf_op jit(solution)/shard_map/slice | solution.py:11
  7.4 2.2 %collective-permute-start.1 = (bf16[1,18,32,128]{3,2,1,0:T(8,128)(2,1)S(1)}, bf16[1,18,32,128]{3,2,1,0:T(8,128)(2,1)S(1)}, u32[]{:S(2)}, u32[]{:S(2)}) collective-permute-start(bf16[1,18,32,128]{3,2,1,0:T(8,128)(2,1)S(1)} %get-tuple-element.9), channel_id=1, source_target_pairs={{0,4},{4,8},{8,12},{12,0},{1,5},{5,9},{9,13},{13,1},{2,6},{6,10},{... | collective-permute-start | bytes 442376 | tf_op jit(solution)/shard_map/ppermute | solution.py:22
  9.6 2.1 %collective-permute-start.2 = (bf16[1,18,32,128]{3,2,1,0:T(8,128)(2,1)S(1)}, bf16[1,18,32,128]{3,2,1,0:T(8,128)(2,1)S(1)}, u32[]{:S(2)}, u32[]{:S(2)}) collective-permute-start(bf16[1,18,32,128]{3,2,1,0:T(8,128)(2,1)S(1)} %get-tuple-element.10), channel_id=1, source_target_pairs={{4,0},{8,4},{12,8},{0,12},{5,1},{9,5},{13,9},{1,13},{6,2},{10,6},{... | collective-permute-start | bytes 442376 | tf_op jit(solution)/shard_map/ppermute | solution.py:23
  11.7 4.2 %collective-permute-done.1 = bf16[1,18,32,128]{3,2,1,0:T(8,128)(2,1)S(1)} collective-permute-done((bf16[1,18,32,128]{3,2,1,0:T(8,128)(2,1)S(1)}, bf16[1,18,32,128]{3,2,1,0:T(8,128)(2,1)S(1)}, u32[]{:S(2)}, u32[]{:S(2)}) %collective-permute-start.1) | collective-permute-done | bytes 147488 | tf_op jit(solution)/shard_map/ppermute | solution.py:22
  15.9 0.9 %collective-permute-done.2 = bf16[1,18,32,128]{3,2,1,0:T(8,128)(2,1)S(1)} collective-permute-done((bf16[1,18,32,128]{3,2,1,0:T(8,128)(2,1)S(1)}, bf16[1,18,32,128]{3,2,1,0:T(8,128)(2,1)S(1)}, u32[]{:S(2)}, u32[]{:S(2)}) %collective-permute-start.2) | collective-permute-done | bytes 147488 | tf_op jit(solution)/shard_map/ppermute | solution.py:23
  16.9 0.2 pad_maximum_fusion.1
  17.1 0.3 constant_dynamic-slice_fusion
  17.4 0.8 %pad_slice_fusion.1 = (bf16[6,18,32,64]{3,2,1,0:T(8,128)(2,1)S(1)}, bf16[6,18,32,64]{3,2,1,0:T(8,128)(2,1)S(1)}) fusion(bf16[6,18,32,64]{3,2,1,0:T(8,128)(2,1)S(1)} %constant_dynamic-slice_fusion), kind=kLoop, calls=%fused_computation.12 | loop fusion | bytes 1327104 | tf_op jit(solution)/shard_map/slice | solution.py:73
  18.2 0.9 %pad_maximum_fusion = bf16[6,18,32,192]{3,2,1,0:T(8,128)(2,1)S(1)} fusion(bf16[6,18,32,64]{3,2,1,0:T(8,128)(2,1)S(1)} %get-tuple-element.8, bf16[6,18,32,64]{3,2,1,0:T(8,128)(2,1)S(1)} %constant_dynamic-slice_fusion, bf16[6,18,32,64]{3,2,1,0:T(8,128)(2,1)S(1)} %get-tuple-element.7), kind=kLoop, calls=%fused_computation.2 | loop fusion | flops 3981312 | bytes 2654208 | tf_op jit(solution)/shard_map/concatenate | solution.py:73
  19.0 0.2 copy-done.2
  19.2 0.5 fusion.25
  19.7 0.5 fusion.26
  20.1 0.5 fusion.24
  20.6 0.5 fusion.23
  21.1 0.5 fusion.27
  21.5 0.5 fusion.28
  22.3 0.1 slice.149
  22.4 0.5 fusion.29
  23.1 0.5 fusion.30
  23.7 0.5 fusion.31
  24.9 0.1 maximum_bitcast_fusion
  25.0 0.1 maximum_bitcast_fusion.2
  25.1 0.1 maximum_bitcast_fusion.3
  25.3 0.1 maximum_bitcast_fusion.6
  25.4 0.1 broadcast_select_fusion.2
  25.6 0.2 fusion.51
  25.8 1.6 %collective-permute-start.3 = (f32[4,320,64]{1,2,0:T(8,128)S(1)}, f32[4,320,64]{1,2,0:T(8,128)S(1)}, u32[]{:S(2)}, u32[]{:S(2)}) collective-permute-start(f32[4,320,64]{1,2,0:T(8,128)S(1)} %slice_select_fusion), channel_id=1, source_target_pairs={{0,2},{2,0},{1,3},{3,1},{4,6},{6,4},{5,7},{7,5},{8,10},{10,8},{9,1... | collective-permute-start | bytes 983048 | tf_op jit(solution)/shard_map/ppermute | solution.py:98
  27.4 0.5 %collective-permute-start.7 = (f32[4,112,64]{1,2,0:T(8,128)S(1)}, f32[4,112,64]{1,2,0:T(8,128)S(1)}, u32[]{:S(2)}, u32[]{:S(2)}) collective-permute-start(f32[4,112,64]{1,2,0:T(8,128)S(1)} %get-tuple-element.4), channel_id=1, source_target_pairs={{0,2},{2,0},{1,3},{3,1},{4,6},{6,4},{5,7},{7,5},{8,10},{10,8},{9,1... | collective-permute-start | bytes 344072 | tf_op jit(solution)/shard_map/ppermute | solution.py:98
  27.9 0.4 copy.28
  28.3 0.2 pad.5.clone
  28.6 0.1 copy.7
  28.7 0.1 slice.139
  28.8 0.4 copy-done.3
  29.2 5.0 %fusion.11 = bf16[4,16,8,5,128]{4,2,3,1,0:T(8,128)(2,1)S(1)} fusion(bf16[3,3,3,128,128]{4,3,2,1,0:T(8,128)(2,1)S(1)} %bitcast.201, bf16[6,18,1,7,2,128]{5,3,4,1,0,2:T(8,128)(2,1)S(1)} %slice.139, bf16[6,18,1,8,5,128]{5,3,4,1,0,2:T(8,128)(2,1)S(1)} %copy.7, pred[8,5]{0,1:T(8,128)(4,1)S(1)} %copy-done.3), kind=kOutput, calls=%fused_computation.10 | convolution fusion | flops 2270224384 | bytes 3033128 | tf_op jit(solution)/shard_map/conv_general_dilated | solution.py:65
  34.2 0.1 copy.8
  34.3 0.9 %copy.18 = bf16[4,16,32,128]{3,2,1,0:T(8,128)(2,1)} copy(bf16[4,16,32,128]{3,1,2,0:T(8,128)(2,1)S(1)} %slice_bitcast_fusion) | data formatting | bytes 1048576
  35.3 3.0 %collective-permute-done.7 = f32[4,112,64]{1,2,0:T(8,128)S(1)} collective-permute-done((f32[4,112,64]{1,2,0:T(8,128)S(1)}, f32[4,112,64]{1,2,0:T(8,128)S(1)}, u32[]{:S(2)}, u32[]{:S(2)}) %collective-permute-start.7) | collective-permute-done | bytes 114720 | tf_op jit(solution)/shard_map/ppermute | solution.py:98
  38.3 2.3 %collective-permute-start.10 = (f32[112,64]{0,1:T(8,128)S(1)}, f32[112,64]{0,1:T(8,128)S(1)}, u32[]{:S(2)}, u32[]{:S(2)}) collective-permute-start(f32[112,64]{0,1:T(8,128)S(1)} %get-tuple-element.15), channel_id=1, source_target_pairs={{0,12},{4,0},{8,4},{12,8},{1,13},{5,1},{9,5},{13,9},{2,14},{6,2},{... | collective-permute-start | bytes 86024 | tf_op jit(solution)/shard_map/ppermute | solution.py:40
  40.6 0.9 %collective-permute-start.9 = (f32[112,64]{0,1:T(8,128)S(1)}, f32[112,64]{0,1:T(8,128)S(1)}, u32[]{:S(2)}, u32[]{:S(2)}) collective-permute-start(f32[112,64]{0,1:T(8,128)S(1)} %get-tuple-element.16), channel_id=1, source_target_pairs={{0,8},{4,12},{8,0},{12,4},{1,9},{5,13},{9,1},{13,5},{2,10},{6,14},... | collective-permute-start | bytes 86024 | tf_op jit(solution)/shard_map/ppermute | solution.py:40
  41.5 0.1 select_add_fusion
  41.7 3.5 %collective-permute-start.4 = (f32[320,64]{0,1:T(8,128)S(1)}, f32[320,64]{0,1:T(8,128)S(1)}, u32[]{:S(2)}, u32[]{:S(2)}) collective-permute-start(f32[320,64]{0,1:T(8,128)S(1)} %get-tuple-element.11), channel_id=1, source_target_pairs={{0,4},{4,8},{8,12},{12,0},{1,5},{5,9},{9,13},{13,1},{2,6},{6,10},{... | collective-permute-start | bytes 245768 | tf_op jit(solution)/shard_map/ppermute | solution.py:40
  45.2 2.4 %collective-permute-start.6 = (f32[320,64]{0,1:T(8,128)S(1)}, f32[320,64]{0,1:T(8,128)S(1)}, u32[]{:S(2)}, u32[]{:S(2)}) collective-permute-start(f32[320,64]{0,1:T(8,128)S(1)} %get-tuple-element.12), channel_id=1, source_target_pairs={{0,12},{4,0},{8,4},{12,8},{1,13},{5,1},{9,5},{13,9},{2,14},{6,2},{... | collective-permute-start | bytes 245768 | tf_op jit(solution)/shard_map/ppermute | solution.py:40
  47.6 1.0 %collective-permute-done.4 = f32[320,64]{0,1:T(8,128)S(1)} collective-permute-done((f32[320,64]{0,1:T(8,128)S(1)}, f32[320,64]{0,1:T(8,128)S(1)}, u32[]{:S(2)}, u32[]{:S(2)}) %collective-permute-start.4) | collective-permute-done | bytes 81952 | tf_op jit(solution)/shard_map/ppermute | solution.py:40
  48.6 3.5 %collective-permute-done.5 = f32[320,64]{0,1:T(8,128)S(1)} collective-permute-done((f32[320,64]{0,1:T(8,128)S(1)}, f32[320,64]{0,1:T(8,128)S(1)}, u32[]{:S(2)}, u32[]{:S(2)}) %collective-permute-start.5) | collective-permute-done | bytes 81952 | tf_op jit(solution)/shard_map/ppermute | solution.py:40
  52.2 0.7 %maximum_multiply_fusion = f32[432,64]{0,1:T(8,128)} fusion(f32[112,64]{0,1:T(8,128)S(1)} %fusion.18, f32[320,64]{0,1:T(8,128)S(1)} %fusion.16), kind=kLoop, calls=%fused_computation.35 | loop fusion | flops 55296 | bytes 221184 | tf_op jit(solution)/shard_map/div | solution.py:106
  (53 shorter events, 1.6 us)
Async XLA Ops:
  0.6 28.2 %copy-start = (bf16[27,128,128]{2,1,0:T(8,128)(2,1)S(1)}, bf16[27,128,128]{2,1,0:T(8,128)(2,1)}, u32[]{:S(2)}) copy-start(bf16[27,128,128]{2,1,0:T(8,128)(2,1)} %param.5) | copy-start | bytes 2654212
  0.6 16.3 %copy-start.1 = (bf16[4,16,32,128]{3,2,1,0:T(8,128)(2,1)S(1)}, bf16[4,16,32,128]{3,2,1,0:T(8,128)(2,1)}, u32[]{:S(2)}) copy-start(bf16[4,16,32,128]{3,2,1,0:T(8,128)(2,1)} %param.4) | copy-start | bytes 1572868
  1.6 4.8 %collective-permute-start = (bf16[4,1,32,128]{3,2,1,0:T(8,128)(2,1)S(1)}, bf16[4,1,32,128]{3,2,1,0:T(8,128)(2,1)S(1)}, u32[]{:S(2)}, u32[]{:S(2)}) collective-permute-start(bf16[4,1,32,128]{3,2,1,0:T(8,128)(2,1)S(1)} %slice_select_fusion.1), channel_id=1, source_target_pairs={{0,2},{2,0},{1,3},{3,1},{4,6},{6,4},{5,7},{7,5},{8,10},{10,8},{9,1... | collective-permute-start | bytes 98312 | tf_op jit(solution)/shard_map/ppermute | solution.py:17
  7.4 8.5 %collective-permute-start.1 = (bf16[1,18,32,128]{3,2,1,0:T(8,128)(2,1)S(1)}, bf16[1,18,32,128]{3,2,1,0:T(8,128)(2,1)S(1)}, u32[]{:S(2)}, u32[]{:S(2)}) collective-permute-start(bf16[1,18,32,128]{3,2,1,0:T(8,128)(2,1)S(1)} %get-tuple-element.9), channel_id=1, source_target_pairs={{0,4},{4,8},{8,12},{12,0},{1,5},{5,9},{9,13},{13,1},{2,6},{6,10},{... | collective-permute-start | bytes 442376 | tf_op jit(solution)/shard_map/ppermute | solution.py:22
  9.6 7.3 %collective-permute-start.2 = (bf16[1,18,32,128]{3,2,1,0:T(8,128)(2,1)S(1)}, bf16[1,18,32,128]{3,2,1,0:T(8,128)(2,1)S(1)}, u32[]{:S(2)}, u32[]{:S(2)}) collective-permute-start(bf16[1,18,32,128]{3,2,1,0:T(8,128)(2,1)S(1)} %get-tuple-element.10), channel_id=1, source_target_pairs={{4,0},{8,4},{12,8},{0,12},{5,1},{9,5},{13,9},{1,13},{6,2},{10,6},{... | collective-permute-start | bytes 442376 | tf_op jit(solution)/shard_map/ppermute | solution.py:23
  18.2 1.0 %copy-start.2 = (bf16[4,16,32,128]{3,2,1,0:T(8,128)(2,1)S(1)}, bf16[4,16,32,128]{3,2,1,0:T(8,128)(2,1)}, u32[]{:S(2)}) copy-start(bf16[4,16,32,128]{3,2,1,0:T(8,128)(2,1)} %param.3) | copy-start | bytes 1572868
  25.8 15.7 %collective-permute-start.3 = (f32[4,320,64]{1,2,0:T(8,128)S(1)}, f32[4,320,64]{1,2,0:T(8,128)S(1)}, u32[]{:S(2)}, u32[]{:S(2)}) collective-permute-start(f32[4,320,64]{1,2,0:T(8,128)S(1)} %slice_select_fusion), channel_id=1, source_target_pairs={{0,2},{2,0},{1,3},{3,1},{4,6},{6,4},{5,7},{7,5},{8,10},{10,8},{9,1... | collective-permute-start | bytes 983048 | tf_op jit(solution)/shard_map/ppermute | solution.py:98
  27.4 10.9 %collective-permute-start.7 = (f32[4,112,64]{1,2,0:T(8,128)S(1)}, f32[4,112,64]{1,2,0:T(8,128)S(1)}, u32[]{:S(2)}, u32[]{:S(2)}) collective-permute-start(f32[4,112,64]{1,2,0:T(8,128)S(1)} %get-tuple-element.4), channel_id=1, source_target_pairs={{0,2},{2,0},{1,3},{3,1},{4,6},{6,4},{5,7},{7,5},{8,10},{10,8},{9,1... | collective-permute-start | bytes 344072 | tf_op jit(solution)/shard_map/ppermute | solution.py:98
  28.5 0.7 %copy-start.3 = (pred[8,5]{0,1:T(8,128)(4,1)S(1)}, pred[8,5]{0,1:T(8,128)(4,1)}, u32[]{:S(2)}) copy-start(pred[8,5]{0,1:T(8,128)(4,1)} %constant.83) | copy-start | bytes 124
  38.3 6.9 %collective-permute-start.10 = (f32[112,64]{0,1:T(8,128)S(1)}, f32[112,64]{0,1:T(8,128)S(1)}, u32[]{:S(2)}, u32[]{:S(2)}) collective-permute-start(f32[112,64]{0,1:T(8,128)S(1)} %get-tuple-element.15), channel_id=1, source_target_pairs={{0,12},{4,0},{8,4},{12,8},{1,13},{5,1},{9,5},{13,9},{2,14},{6,2},{... | collective-permute-start | bytes 86024 | tf_op jit(solution)/shard_map/ppermute | solution.py:40
  40.6 7.0 %collective-permute-start.8 = (f32[112,64]{0,1:T(8,128)S(1)}, f32[112,64]{0,1:T(8,128)S(1)}, u32[]{:S(2)}, u32[]{:S(2)}) collective-permute-start(f32[112,64]{0,1:T(8,128)S(1)} %get-tuple-element.14), channel_id=1, source_target_pairs={{0,4},{4,8},{8,12},{12,0},{1,5},{5,9},{9,13},{13,1},{2,6},{6,10},{... | collective-permute-start | bytes 86024 | tf_op jit(solution)/shard_map/ppermute | solution.py:40
  40.6 7.0 %collective-permute-start.9 = (f32[112,64]{0,1:T(8,128)S(1)}, f32[112,64]{0,1:T(8,128)S(1)}, u32[]{:S(2)}, u32[]{:S(2)}) collective-permute-start(f32[112,64]{0,1:T(8,128)S(1)} %get-tuple-element.16), channel_id=1, source_target_pairs={{0,8},{4,12},{8,0},{12,4},{1,9},{5,13},{9,1},{13,5},{2,10},{6,14},... | collective-permute-start | bytes 86024 | tf_op jit(solution)/shard_map/ppermute | solution.py:40
  41.7 7.0 %collective-permute-start.4 = (f32[320,64]{0,1:T(8,128)S(1)}, f32[320,64]{0,1:T(8,128)S(1)}, u32[]{:S(2)}, u32[]{:S(2)}) collective-permute-start(f32[320,64]{0,1:T(8,128)S(1)} %get-tuple-element.11), channel_id=1, source_target_pairs={{0,4},{4,8},{8,12},{12,0},{1,5},{5,9},{9,13},{13,1},{2,6},{6,10},{... | collective-permute-start | bytes 245768 | tf_op jit(solution)/shard_map/ppermute | solution.py:40
  45.1 7.0 %collective-permute-start.5 = (f32[320,64]{0,1:T(8,128)S(1)}, f32[320,64]{0,1:T(8,128)S(1)}, u32[]{:S(2)}, u32[]{:S(2)}) collective-permute-start(f32[320,64]{0,1:T(8,128)S(1)} %get-tuple-element.13), channel_id=1, source_target_pairs={{0,8},{4,12},{8,0},{12,4},{1,9},{5,13},{9,1},{13,5},{2,10},{6,14},... | collective-permute-start | bytes 245768 | tf_op jit(solution)/shard_map/ppermute | solution.py:40
  45.2 6.9 %collective-permute-start.6 = (f32[320,64]{0,1:T(8,128)S(1)}, f32[320,64]{0,1:T(8,128)S(1)}, u32[]{:S(2)}, u32[]{:S(2)}) collective-permute-start(f32[320,64]{0,1:T(8,128)S(1)} %get-tuple-element.12), channel_id=1, source_target_pairs={{0,12},{4,0},{8,4},{12,8},{1,13},{5,1},{9,5},{13,9},{2,14},{6,2},{... | collective-permute-start | bytes 245768 | tf_op jit(solution)/shard_map/ppermute | solution.py:40

commit v16 on v11

--- a/solution.py
+++ b/solution.py
@@ -62,12 +62,23 @@
     taps = weight.reshape(3, 3, 3, chans, weight.shape[2])
     kflip = jnp.transpose(taps[::-1, ::-1, ::-1], (0, 1, 2, 4, 3))
     pad = [(0, 0), (0, 0), (1, 1)]
-    inner = lax.conv_general_dilated(
-        gh[None], kflip, (1, 1, 1), pad,
-        dimension_numbers=("NDHWC", "DHWIO", "NDHWC"),
-        preferred_element_type=jnp.float32,
-    )[0]
-    grad_in = inner.astype(jnp.bfloat16)
+    def conv_rows(source):
+        return lax.conv_general_dilated(
+            source[None], kflip, (1, 1, 1), pad,
+            dimension_numbers=("NDHWC", "DHWIO", "NDHWC"),
+            preferred_element_type=jnp.float32,
+        )[0].astype(jnp.bfloat16)
+
+    if ncores == 2 and size_x % 2 == 0:
+        core = lax.axis_index("col")
+        rows = size_x // 2
+        mine = conv_rows(lax.dynamic_slice_in_dim(gh, core * rows, rows + 2, axis=0))
+        other = lax.ppermute(mine, "col", [(0, 1), (1, 0)])
+        grad_in = jnp.where(
+            core == 0, jnp.concatenate([mine, other], axis=0), jnp.concatenate([other, mine], axis=0)
+        )
+    else:
+        grad_in = conv_rows(gh)
     gshare = lax.dynamic_slice_in_dim(gh, offset, half, 3)
     gdeep = jnp.pad(gshare, ((0, 0), (0, 0), (1, 1), (0, 0)))
     stack = jnp.concatenate([lax.slice_in_dim(gdeep, 2 - c, 2 - c + depth, axis=2) for c in range(3)], axis=3)

time: 50.5 us -> 54.7 us (1.083)
  waiting for transfers between devices: 13.2 us -> 19.9 us
  matrix products: 9.1 us -> 6.6 us
    ppermute x2, waiting for transfers between devices: 0.75 us -> 5.24 us  [on_device(): partial = keep + lax.ppermute(send, 'gy', [(0, 1), (1, 0)])]
    ppermute x1, waiting for transfers between devices: 0.95 us -> 3.53 us  [with_halo(): lax.ppermute(head, axis, [((i + 1) % count, i) for i in range(count)])]
    conv_general_dilated x1, matrix products: 4.96 us -> 2.46 us  [conv_rows(): lax.conv_general_dilated(source[None], kflip, (1, 1, 1), pad, dimension_n...]
    ppermute x1, starting transfers between devices: 2.16 us -> 0.01 us  [with_halo(): low = lax.ppermute(tail, axis, [(i, (i + 1) % count) for i in range(count)])]
    ppermute x1, starting transfers between devices: 2.14 us -> 4.19 us  [with_halo(): lax.ppermute(head, axis, [((i + 1) % count, i) for i in range(count)])]
    ppermute x2, starting transfers between devices: 2.15 us -> 3.12 us  [on_device(): partial = keep + lax.ppermute(send, 'gy', [(0, 1), (1, 0)])]
    ppermute x1, waiting for transfers between devices: 4.21 us -> 3.39 us  [with_halo(): low = lax.ppermute(tail, axis, [(i, (i + 1) % count) for i in range(count)])]
    ppermute x6, starting transfers between devices: 7.58 us -> 6.97 us  [scatter_sum(): lax.ppermute(part, axis, [(j, (j + shift) % count) for j in range(count)])]
  transfers between devices with their start and end apart: 11 -> 12, of which waited for: 6 -> 9; matrix products, arithmetic and copies ran while one was open for 14% -> 3% of each run, Pallas kernels for 0% -> 0%
where the time goes in v16:
time: 54.7 us; the launch traced here: 54.5 us
  waiting for transfers between devices  19.9 us (36%)
  starting transfers between devices  17.3 us (32%)
  matrix products  6.6 us (12%)
  other arithmetic  4.86 us (9%)
  local copies, waits for them, and re-layouts  4.73 us (9%)
  between operations  1.12 us (2%)
    ppermute x6, starting transfers between devices, scatter_sum(): lax.ppermute(part, axis, [(j, (j + shift) % count) for j in range(count)])  6.97 us
    ppermute x6, waiting for transfers between devices, scatter_sum(): lax.ppermute(part, axis, [(j, (j + shift) % count) for j in range(count)])  5.84 us
    ppermute x2, waiting for transfers between devices, on_device(): partial = keep + lax.ppermute(send, 'gy', [(0, 1), (1, 0)])  5.24 us
    ppermute x1, starting transfers between devices, with_halo(): lax.ppermute(head, axis, [((i + 1) % count, i) for i in range(count)])  4.19 us
    dot_general x9, matrix products, on_device(): lax.dot_general(x_act, window, (((0, 1, 2), (0, 1, 2)), ((), ())), prefer...  4.14 us
    ppermute x1, waiting for transfers between devices, with_halo(): lax.ppermute(head, axis, [((i + 1) % count, i) for i in range(count)])  3.53 us
    ppermute x1, waiting for transfers between devices, with_halo(): low = lax.ppermute(tail, axis, [(i, (i + 1) % count) for i in range(count)])  3.39 us
    ppermute x2, starting transfers between devices, on_device(): partial = keep + lax.ppermute(send, 'gy', [(0, 1), (1, 0)])  3.12 us
  transfers between devices with their start and end apart: 12, of which 9 were waited for; matrix products, arithmetic and copies ran while one was open for 3% of the time, Pallas kernels for 0%

profile of v16, /device:TPU:0, one launch (start us, length us, event | category | flops | bytes accessed | tf_op | source)
XLA Modules:
  0.0 54.5 jit_solution(5631329557658768071)
XLA Ops:
  0.7 0.9 %slice_select_fusion.2 = bf16[4,1,32,128]{3,2,1,0:T(8,128)(2,1)S(1)} fusion(bf16[4,16,32,128]{3,2,1,0:T(8,128)(2,1)} %param.4, pred[]{:T(512)S(6)} %eq.30), kind=kLoop, calls=%fused_computation.58 | loop fusion | flops 16384 | bytes 98305 | tf_op jit(solution)/shard_map/jit(_where)/select_n | solution.py:17
  1.6 2.9 %collective-permute-start = (bf16[4,1,32,128]{3,2,1,0:T(8,128)(2,1)S(1)}, bf16[4,1,32,128]{3,2,1,0:T(8,128)(2,1)S(1)}, u32[]{:S(2)}, u32[]{:S(2)}) collective-permute-start(bf16[4,1,32,128]{3,2,1,0:T(8,128)(2,1)S(1)} %slice_select_fusion.2), channel_id=1, source_target_pairs={{0,2},{2,0},{1,3},{3,1},{4,6},{6,4},{5,7},{7,5},{8,10},{10,8},{9,1... | collective-permute-start | bytes 98312 | tf_op jit(solution)/shard_map/ppermute | solution.py:17
  4.5 1.9 %collective-permute-done = bf16[4,1,32,128]{3,2,1,0:T(8,128)(2,1)S(1)} collective-permute-done((bf16[4,1,32,128]{3,2,1,0:T(8,128)(2,1)S(1)}, bf16[4,1,32,128]{3,2,1,0:T(8,128)(2,1)S(1)}, u32[]{:S(2)}, u32[]{:S(2)}) %collective-permute-start) | collective-permute-done | bytes 32800 | tf_op jit(solution)/shard_map/ppermute | solution.py:17
  6.4 1.0 %pad_maximum_fusion.6 = (bf16[1,18,32,128]{3,2,1,0:T(8,128)(2,1)S(1)}, bf16[1,18,32,128]{3,2,1,0:T(8,128)(2,1)S(1)}) fusion(bf16[4,1,32,128]{3,2,1,0:T(8,128)(2,1)S(1)} %get-tuple-element.21, bf16[4,16,32,128]{3,2,1,0:T(8,128)(2,1)} %param.4, bf16[4,1,32,128]{3,2,1,0:T(8,128)(2,1)S(1)} %get-tuple-element.20), kind=kLoop, calls=%fused_computation.25 | loop fusion | flops 294912 | bytes 884736 | tf_op jit(solution)/shard_map/slice | solution.py:11
  7.4 4.2 %collective-permute-start.2 = (bf16[1,18,32,128]{3,2,1,0:T(8,128)(2,1)S(1)}, bf16[1,18,32,128]{3,2,1,0:T(8,128)(2,1)S(1)}, u32[]{:S(2)}, u32[]{:S(2)}) collective-permute-start(bf16[1,18,32,128]{3,2,1,0:T(8,128)(2,1)S(1)} %get-tuple-element.11), channel_id=1, source_target_pairs={{4,0},{8,4},{12,8},{0,12},{5,1},{9,5},{13,9},{1,13},{6,2},{10,6},{... | collective-permute-start | bytes 442376 | tf_op jit(solution)/shard_map/ppermute | solution.py:23
  11.6 3.5 %collective-permute-done.2 = bf16[1,18,32,128]{3,2,1,0:T(8,128)(2,1)S(1)} collective-permute-done((bf16[1,18,32,128]{3,2,1,0:T(8,128)(2,1)S(1)}, bf16[1,18,32,128]{3,2,1,0:T(8,128)(2,1)S(1)}, u32[]{:S(2)}, u32[]{:S(2)}) %collective-permute-start.2) | collective-permute-done | bytes 147488 | tf_op jit(solution)/shard_map/ppermute | solution.py:23
  15.2 3.4 %collective-permute-done.1 = bf16[1,18,32,128]{3,2,1,0:T(8,128)(2,1)S(1)} collective-permute-done((bf16[1,18,32,128]{3,2,1,0:T(8,128)(2,1)S(1)}, bf16[1,18,32,128]{3,2,1,0:T(8,128)(2,1)S(1)}, u32[]{:S(2)}, u32[]{:S(2)}) %collective-permute-start.1) | collective-permute-done | bytes 147488 | tf_op jit(solution)/shard_map/ppermute | solution.py:22
  18.6 0.2 pad_maximum_fusion.1
  18.7 0.3 constant_dynamic-slice_fusion
  19.0 0.8 %pad_slice_fusion.1 = (bf16[6,18,32,64]{3,2,1,0:T(8,128)(2,1)S(1)}, bf16[6,18,32,64]{3,2,1,0:T(8,128)(2,1)S(1)}) fusion(bf16[6,18,32,64]{3,2,1,0:T(8,128)(2,1)S(1)} %constant_dynamic-slice_fusion), kind=kLoop, calls=%fused_computation.6 | loop fusion | bytes 1327104 | tf_op jit(solution)/shard_map/slice | solution.py:84
  19.8 0.9 %pad_maximum_fusion = bf16[6,18,32,192]{3,2,1,0:T(8,128)(2,1)S(1)} fusion(bf16[6,18,32,64]{3,2,1,0:T(8,128)(2,1)S(1)} %get-tuple-element.9, bf16[6,18,32,64]{3,2,1,0:T(8,128)(2,1)S(1)} %constant_dynamic-slice_fusion, bf16[6,18,32,64]{3,2,1,0:T(8,128)(2,1)S(1)} %get-tuple-element.8), kind=kLoop, calls=%fused_computation.2 | loop fusion | flops 3981312 | bytes 2654208 | tf_op jit(solution)/shard_map/concatenate | solution.py:84
  20.7 0.2 copy-done.2
  20.8 0.5 fusion.25
  21.3 0.5 fusion.24
  21.8 0.5 fusion.19
  22.2 0.5 fusion.18
  22.7 0.5 fusion.23
  23.2 0.5 fusion.22
  23.8 0.5 fusion.21
  24.3 0.5 fusion.20
  25.0 0.5 fusion.17
  25.9 0.5 copy.41
  26.4 0.3 pad.5.clone
  26.6 0.1 copy.20
  26.8 0.2 copy-done.3
  27.0 2.5 %fusion.1 = bf16[2,16,8,5,128]{4,2,3,1,0:T(8,128)(2,1)S(1)} fusion(bf16[3,3,3,128,128]{4,3,2,1,0:T(8,128)(2,1)S(1)} %bitcast.197, bf16[4,18,1,7,2,128]{5,3,4,1,0,2:T(8,128)(2,1)S(1)} %slice.139, bf16[4,18,1,8,5,128]{5,3,4,1,0,2:T(8,128)(2,1)S(1)} %copy.20, pred[8,5]{0,1:T(8,128)(4,1)S(1)} %copy-done.3), kind=kOutput, calls=%fused_computation.4 | convolution fusion | flops 1135886336 | bytes 2207784 | tf_op jit(solution)/shard_map/conv_general_dilated | solution.py:66
  30.3 0.1 maximum_bitcast_fusion.7
  30.4 0.1 maximum_bitcast_fusion.3
  30.5 0.1 maximum_bitcast_fusion.4
  30.6 0.1 maximum_bitcast_fusion.2
  30.9 1.6 %collective-permute-start.4 = (f32[4,216,64]{1,2,0:T(8,128)S(1)}, f32[4,216,64]{1,2,0:T(8,128)S(1)}, u32[]{:S(2)}, u32[]{:S(2)}) collective-permute-start(f32[4,216,64]{1,2,0:T(8,128)S(1)} %slice_select_fusion.1), channel_id=1, source_target_pairs={{0,2},{2,0},{1,3},{3,1},{4,6},{6,4},{5,7},{7,5},{8,10},{10,8},{9,1... | collective-permute-start | bytes 663560 | tf_op jit(solution)/shard_map/ppermute | solution.py:109
  32.6 5.0 %collective-permute-done.4 = f32[4,216,64]{1,2,0:T(8,128)S(1)} collective-permute-done((f32[4,216,64]{1,2,0:T(8,128)S(1)}, f32[4,216,64]{1,2,0:T(8,128)S(1)}, u32[]{:S(2)}, u32[]{:S(2)}) %collective-permute-start.4) | collective-permute-done | bytes 221216 | tf_op jit(solution)/shard_map/ppermute | solution.py:109
  37.6 0.2 select_add_fusion.1
  37.8 1.6 %collective-permute-start.8 = (f32[4,216,64]{1,2,0:T(8,128)S(1)}, f32[4,216,64]{1,2,0:T(8,128)S(1)}, u32[]{:S(2)}, u32[]{:S(2)}) collective-permute-start(f32[4,216,64]{1,2,0:T(8,128)S(1)} %get-tuple-element.7), channel_id=1, source_target_pairs={{0,2},{2,0},{1,3},{3,1},{4,6},{6,4},{5,7},{7,5},{8,10},{10,8},{9,1... | collective-permute-start | bytes 663560 | tf_op jit(solution)/shard_map/ppermute | solution.py:109
  39.3 2.0 %collective-permute-start.7 = (f32[216,64]{0,1:T(8,128)S(1)}, f32[216,64]{0,1:T(8,128)S(1)}, u32[]{:S(2)}, u32[]{:S(2)}) collective-permute-start(f32[216,64]{0,1:T(8,128)S(1)} %get-tuple-element.13), channel_id=1, source_target_pairs={{0,12},{4,0},{8,4},{12,8},{1,13},{5,1},{9,5},{13,9},{2,14},{6,2},{... | collective-permute-start | bytes 165896 | tf_op jit(solution)/shard_map/ppermute | solution.py:40
  41.4 0.7 %collective-permute-start.6 = (f32[216,64]{0,1:T(8,128)S(1)}, f32[216,64]{0,1:T(8,128)S(1)}, u32[]{:S(2)}, u32[]{:S(2)}) collective-permute-start(f32[216,64]{0,1:T(8,128)S(1)} %get-tuple-element.14), channel_id=1, source_target_pairs={{0,8},{4,12},{8,0},{12,4},{1,9},{5,13},{9,1},{13,5},{2,10},{6,14},... | collective-permute-start | bytes 165896 | tf_op jit(solution)/shard_map/ppermute | solution.py:40
  42.1 0.8 %collective-permute-start.5 = (f32[216,64]{0,1:T(8,128)S(1)}, f32[216,64]{0,1:T(8,128)S(1)}, u32[]{:S(2)}, u32[]{:S(2)}) collective-permute-start(f32[216,64]{0,1:T(8,128)S(1)} %get-tuple-element.12), channel_id=1, source_target_pairs={{0,4},{4,8},{8,12},{12,0},{1,5},{5,9},{9,13},{13,1},{2,6},{6,10},{... | collective-permute-start | bytes 165896 | tf_op jit(solution)/shard_map/ppermute | solution.py:40
  43.0 0.9 %copy.31 = bf16[4,16,32,128]{3,2,1,0:T(8,128)(2,1)} copy(bf16[4,16,32,128]{3,1,2,0:T(8,128)(2,1)S(1)} %maximum_select_fusion) | data formatting | bytes 1048576
  43.9 0.3 collective-permute-done.8
  44.2 0.2 select_add_fusion
  44.4 2.8 %collective-permute-start.11 = (f32[216,64]{0,1:T(8,128)S(1)}, f32[216,64]{0,1:T(8,128)S(1)}, u32[]{:S(2)}, u32[]{:S(2)}) collective-permute-start(f32[216,64]{0,1:T(8,128)S(1)} %get-tuple-element.16), channel_id=1, source_target_pairs={{0,12},{4,0},{8,4},{12,8},{1,13},{5,1},{9,5},{13,9},{2,14},{6,2},{... | collective-permute-start | bytes 165896 | tf_op jit(solution)/shard_map/ppermute | solution.py:40
  47.2 0.4 collective-permute-start.10
  47.7 0.2 collective-permute-start.9
  47.9 1.3 %collective-permute-done.6 = f32[216,64]{0,1:T(8,128)S(1)} collective-permute-done((f32[216,64]{0,1:T(8,128)S(1)}, f32[216,64]{0,1:T(8,128)S(1)}, u32[]{:S(2)}, u32[]{:S(2)}) %collective-permute-start.6) | collective-permute-done | bytes 55328 | tf_op jit(solution)/shard_map/ppermute | solution.py:40
  49.2 0.6 %collective-permute-done.11 = f32[216,64]{0,1:T(8,128)S(1)} collective-permute-done((f32[216,64]{0,1:T(8,128)S(1)}, f32[216,64]{0,1:T(8,128)S(1)}, u32[]{:S(2)}, u32[]{:S(2)}) %collective-permute-start.11) | collective-permute-done | bytes 55328 | tf_op jit(solution)/shard_map/ppermute | solution.py:40
  49.8 2.6 %collective-permute-done.10 = f32[216,64]{0,1:T(8,128)S(1)} collective-permute-done((f32[216,64]{0,1:T(8,128)S(1)}, f32[216,64]{0,1:T(8,128)S(1)}, u32[]{:S(2)}, u32[]{:S(2)}) %collective-permute-start.10) | collective-permute-done | bytes 55328 | tf_op jit(solution)/shard_map/ppermute | solution.py:40
  52.4 1.3 %collective-permute-done.9 = f32[216,64]{0,1:T(8,128)S(1)} collective-permute-done((f32[216,64]{0,1:T(8,128)S(1)}, f32[216,64]{0,1:T(8,128)S(1)}, u32[]{:S(2)}, u32[]{:S(2)}) %collective-permute-start.9) | collective-permute-done | bytes 55328 | tf_op jit(solution)/shard_map/ppermute | solution.py:40
  53.7 0.8 %maximum_multiply_fusion = f32[432,64]{0,1:T(8,128)} fusion(f32[216,64]{0,1:T(8,128)S(1)} %fusion.10, f32[216,64]{0,1:T(8,128)S(1)} %fusion.12), kind=kLoop, calls=%fused_computation.36 | loop fusion | flops 55296 | bytes 221184 | tf_op jit(solution)/shard_map/div | solution.py:117
  (56 shorter events, 2.0 us)
Async XLA Ops:
  0.6 26.2 %copy-start = (bf16[27,128,128]{2,1,0:T(8,128)(2,1)S(1)}, bf16[27,128,128]{2,1,0:T(8,128)(2,1)}, u32[]{:S(2)}) copy-start(bf16[27,128,128]{2,1,0:T(8,128)(2,1)} %param.5) | copy-start | bytes 2654212
  0.6 17.9 %copy-start.1 = (bf16[4,16,32,128]{3,2,1,0:T(8,128)(2,1)S(1)}, bf16[4,16,32,128]{3,2,1,0:T(8,128)(2,1)}, u32[]{:S(2)}) copy-start(bf16[4,16,32,128]{3,2,1,0:T(8,128)(2,1)} %param.4) | copy-start | bytes 1572868
  1.6 4.8 %collective-permute-start = (bf16[4,1,32,128]{3,2,1,0:T(8,128)(2,1)S(1)}, bf16[4,1,32,128]{3,2,1,0:T(8,128)(2,1)S(1)}, u32[]{:S(2)}, u32[]{:S(2)}) collective-permute-start(bf16[4,1,32,128]{3,2,1,0:T(8,128)(2,1)S(1)} %slice_select_fusion.2), channel_id=1, source_target_pairs={{0,2},{2,0},{1,3},{3,1},{4,6},{6,4},{5,7},{7,5},{8,10},{10,8},{9,1... | collective-permute-start | bytes 98312 | tf_op jit(solution)/shard_map/ppermute | solution.py:17
  7.4 7.7 %collective-permute-start.2 = (bf16[1,18,32,128]{3,2,1,0:T(8,128)(2,1)S(1)}, bf16[1,18,32,128]{3,2,1,0:T(8,128)(2,1)S(1)}, u32[]{:S(2)}, u32[]{:S(2)}) collective-permute-start(bf16[1,18,32,128]{3,2,1,0:T(8,128)(2,1)S(1)} %get-tuple-element.11), channel_id=1, source_target_pairs={{4,0},{8,4},{12,8},{0,12},{5,1},{9,5},{13,9},{1,13},{6,2},{10,6},{... | collective-permute-start | bytes 442376 | tf_op jit(solution)/shard_map/ppermute | solution.py:23
  11.6 6.9 %collective-permute-start.1 = (bf16[1,18,32,128]{3,2,1,0:T(8,128)(2,1)S(1)}, bf16[1,18,32,128]{3,2,1,0:T(8,128)(2,1)S(1)}, u32[]{:S(2)}, u32[]{:S(2)}) collective-permute-start(bf16[1,18,32,128]{3,2,1,0:T(8,128)(2,1)S(1)} %get-tuple-element.10), channel_id=1, source_target_pairs={{0,4},{4,8},{8,12},{12,0},{1,5},{5,9},{9,13},{13,1},{2,6},{6,10},{... | collective-permute-start | bytes 442376 | tf_op jit(solution)/shard_map/ppermute | solution.py:22
  19.8 1.0 %copy-start.2 = (bf16[4,16,32,128]{3,2,1,0:T(8,128)(2,1)S(1)}, bf16[4,16,32,128]{3,2,1,0:T(8,128)(2,1)}, u32[]{:S(2)}) copy-start(bf16[4,16,32,128]{3,2,1,0:T(8,128)(2,1)} %param.3) | copy-start | bytes 1572868
  26.3 0.7 %copy-start.3 = (pred[8,5]{0,1:T(8,128)(4,1)S(1)}, pred[8,5]{0,1:T(8,128)(4,1)}, u32[]{:S(2)}) copy-start(pred[8,5]{0,1:T(8,128)(4,1)} %constant.83) | copy-start | bytes 124
  30.9 6.6 %collective-permute-start.4 = (f32[4,216,64]{1,2,0:T(8,128)S(1)}, f32[4,216,64]{1,2,0:T(8,128)S(1)}, u32[]{:S(2)}, u32[]{:S(2)}) collective-permute-start(f32[4,216,64]{1,2,0:T(8,128)S(1)} %slice_select_fusion.1), channel_id=1, source_target_pairs={{0,2},{2,0},{1,3},{3,1},{4,6},{6,4},{5,7},{7,5},{8,10},{10,8},{9,1... | collective-permute-start | bytes 663560 | tf_op jit(solution)/shard_map/ppermute | solution.py:109
  32.5 10.4 %collective-permute-start.3 = (bf16[2,16,32,128]{3,1,2,0:T(8,128)(2,1)S(1)}, bf16[2,16,32,128]{3,1,2,0:T(8,128)(2,1)S(1)}, u32[]{:S(2)}, u32[]{:S(2)}) collective-permute-start(bf16[2,16,32,128]{3,1,2,0:T(8,128)(2,1)S(1)} %slice_bitcast_fusion), channel_id=1, source_target_pairs={{0,1},{1,0},{2,3},{3,2},{4,5},{5,4},{6,7},{7,6},{8,9},{9,8},{10,11... | collective-permute-start | bytes 786440 | tf_op jit(solution)/shard_map/ppermute | solution.py:76
  37.8 6.4 %collective-permute-start.8 = (f32[4,216,64]{1,2,0:T(8,128)S(1)}, f32[4,216,64]{1,2,0:T(8,128)S(1)}, u32[]{:S(2)}, u32[]{:S(2)}) collective-permute-start(f32[4,216,64]{1,2,0:T(8,128)S(1)} %get-tuple-element.7), channel_id=1, source_target_pairs={{0,2},{2,0},{1,3},{3,1},{4,6},{6,4},{5,7},{7,5},{8,10},{10,8},{9,1... | collective-permute-start | bytes 663560 | tf_op jit(solution)/shard_map/ppermute | solution.py:109
  39.3 8.3 %collective-permute-start.7 = (f32[216,64]{0,1:T(8,128)S(1)}, f32[216,64]{0,1:T(8,128)S(1)}, u32[]{:S(2)}, u32[]{:S(2)}) collective-permute-start(f32[216,64]{0,1:T(8,128)S(1)} %get-tuple-element.13), channel_id=1, source_target_pairs={{0,12},{4,0},{8,4},{12,8},{1,13},{5,1},{9,5},{13,9},{2,14},{6,2},{... | collective-permute-start | bytes 165896 | tf_op jit(solution)/shard_map/ppermute | solution.py:40
  41.4 7.8 %collective-permute-start.6 = (f32[216,64]{0,1:T(8,128)S(1)}, f32[216,64]{0,1:T(8,128)S(1)}, u32[]{:S(2)}, u32[]{:S(2)}) collective-permute-start(f32[216,64]{0,1:T(8,128)S(1)} %get-tuple-element.14), channel_id=1, source_target_pairs={{0,8},{4,12},{8,0},{12,4},{1,9},{5,13},{9,1},{13,5},{2,10},{6,14},... | collective-permute-start | bytes 165896 | tf_op jit(solution)/shard_map/ppermute | solution.py:40
  42.1 7.1 %collective-permute-start.5 = (f32[216,64]{0,1:T(8,128)S(1)}, f32[216,64]{0,1:T(8,128)S(1)}, u32[]{:S(2)}, u32[]{:S(2)}) collective-permute-start(f32[216,64]{0,1:T(8,128)S(1)} %get-tuple-element.12), channel_id=1, source_target_pairs={{0,4},{4,8},{8,12},{12,0},{1,5},{5,9},{9,13},{13,1},{2,6},{6,10},{... | collective-permute-start | bytes 165896 | tf_op jit(solution)/shard_map/ppermute | solution.py:40
  44.4 5.3 %collective-permute-start.11 = (f32[216,64]{0,1:T(8,128)S(1)}, f32[216,64]{0,1:T(8,128)S(1)}, u32[]{:S(2)}, u32[]{:S(2)}) collective-permute-start(f32[216,64]{0,1:T(8,128)S(1)} %get-tuple-element.16), channel_id=1, source_target_pairs={{0,12},{4,0},{8,4},{12,8},{1,13},{5,1},{9,5},{13,9},{2,14},{6,2},{... | collective-permute-start | bytes 165896 | tf_op jit(solution)/shard_map/ppermute | solution.py:40
  47.2 5.2 %collective-permute-start.10 = (f32[216,64]{0,1:T(8,128)S(1)}, f32[216,64]{0,1:T(8,128)S(1)}, u32[]{:S(2)}, u32[]{:S(2)}) collective-permute-start(f32[216,64]{0,1:T(8,128)S(1)} %get-tuple-element.17), channel_id=1, source_target_pairs={{0,8},{4,12},{8,0},{12,4},{1,9},{5,13},{9,1},{13,5},{2,10},{6,14},... | collective-permute-start | bytes 165896 | tf_op jit(solution)/shard_map/ppermute | solution.py:40
  47.7 6.1 %collective-permute-start.9 = (f32[216,64]{0,1:T(8,128)S(1)}, f32[216,64]{0,1:T(8,128)S(1)}, u32[]{:S(2)}, u32[]{:S(2)}) collective-permute-start(f32[216,64]{0,1:T(8,128)S(1)} %get-tuple-element.15), channel_id=1, source_target_pairs={{0,4},{4,8},{8,12},{12,0},{1,5},{5,9},{9,13},{13,1},{2,6},{6,10},{... | collective-permute-start | bytes 165896 | tf_op jit(solution)/shard_map/ppermute | solution.py:40

commit v17 on v11

--- a/solution.py
+++ b/solution.py
@@ -58,7 +58,7 @@
     ncores = lax.axis_size("col")
     half = weight.shape[2] // ncores
     offset = lax.axis_index("col") * half
-    gh = with_halo(grad_out, (("gy", 1), ("gx", 0)), 1)
+    gh = with_halo(grad_out, (("gx", 0), ("gy", 1)), 1)
     taps = weight.reshape(3, 3, 3, chans, weight.shape[2])
     kflip = jnp.transpose(taps[::-1, ::-1, ::-1], (0, 1, 2, 4, 3))
     pad = [(0, 0), (0, 0), (1, 1)]

time: 50.5 us -> 52 us (1.030)
  waiting for transfers between devices: 13.2 us -> 15.2 us
  local copies, waits for them, and re-layouts: 4.93 us -> 6.02 us
  other arithmetic: 4.95 us -> 3.88 us
  starting transfers between devices: 17 us -> 16.4 us
    ppermute x1, starting transfers between devices: 2.14 us -> 5.1 us  [with_halo(): lax.ppermute(head, axis, [((i + 1) % count, i) for i in range(count)])]
    ppermute x1, waiting for transfers between devices: 0.95 us -> 3.9 us  [with_halo(): lax.ppermute(head, axis, [((i + 1) % count, i) for i in range(count)])]
    ppermute x1, starting transfers between devices: 2.16 us -> 0.01 us  [with_halo(): low = lax.ppermute(tail, axis, [(i, (i + 1) % count) for i in range(count)])]
    ppermute x1, starting transfers between devices: 2.94 us -> 1.56 us  [with_halo(): got = lax.ppermute(jnp.where(me == 0, tail, head), axis, [(0, 1), (1, 0)])]
    ppermute x1, waiting for transfers between devices: 4.21 us -> 2.84 us  [with_halo(): low = lax.ppermute(tail, axis, [(i, (i + 1) % count) for i in range(count)])]
    slice x0 -> x1, local copies, waits for them, and re-layouts: none -> 1.09 us  [with_halo(): lax.slice_in_dim(cells, cells.shape[dim] - width, cells.shape[dim], axis=...]
    slice x1 -> x0, other arithmetic: 1.01 us -> none  [with_halo(): lax.slice_in_dim(cells, cells.shape[dim] - width, cells.shape[dim], axis=...]
    ppermute x1, waiting for transfers between devices: 1.89 us -> 2.6 us  [with_halo(): got = lax.ppermute(jnp.where(me == 0, tail, head), axis, [(0, 1), (1, 0)])]
  transfers between devices with their start and end apart: 11 -> 11, of which waited for: 6 -> 8; matrix products, arithmetic and copies ran while one was open for 14% -> 14% of each run, Pallas kernels for 0% -> 0%
where the time goes in v17:
time: 52 us; the launch traced here: 51.7 us
  starting transfers between devices  16.4 us (32%)
  waiting for transfers between devices  15.2 us (29%)
  matrix products  9.1 us (18%)
  local copies, waits for them, and re-layouts  6.02 us (12%)
  other arithmetic  3.88 us (7%)
  between operations  1.1 us (2%)
    ppermute x6, starting transfers between devices, scatter_sum(): lax.ppermute(part, axis, [(j, (j + shift) % count) for j in range(count)])  7.61 us
    ppermute x6, waiting for transfers between devices, scatter_sum(): lax.ppermute(part, axis, [(j, (j + shift) % count) for j in range(count)])  5.51 us
    ppermute x1, starting transfers between devices, with_halo(): lax.ppermute(head, axis, [((i + 1) % count, i) for i in range(count)])  5.1 us
    conv_general_dilated x1, matrix products, on_device(): lax.conv_general_dilated(gh[None], kflip, (1, 1, 1), pad, dimension_numbe...  4.96 us
    dot_general x9, matrix products, on_device(): lax.dot_general(x_act, window, (((0, 1, 2), (0, 1, 2)), ((), ())), prefer...  4.14 us
    ppermute x1, waiting for transfers between devices, with_halo(): lax.ppermute(head, axis, [((i + 1) % count, i) for i in range(count)])  3.9 us
    ppermute x1, waiting for transfers between devices, with_halo(): low = lax.ppermute(tail, axis, [(i, (i + 1) % count) for i in range(count)])  2.84 us
    ppermute x1, waiting for transfers between devices, with_halo(): got = lax.ppermute(jnp.where(me == 0, tail, head), axis, [(0, 1), (1, 0)])  2.6 us
  transfers between devices with their start and end apart: 11, of which 8 were waited for; matrix products, arithmetic and copies ran while one was open for 14% of the time, Pallas kernels for 0%

profile of v17, /device:TPU:0, one launch (start us, length us, event | category | flops | bytes accessed | tf_op | source)
XLA Modules:
  0.0 51.7 jit_solution(1273699158739125647)
XLA Ops:
  0.7 1.1 %fusion.23 = (bf16[1,16,32,128]{3,2,1,0:T(8,128)(2,1)S(1)}, bf16[1,16,32,128]{3,2,1,0:T(8,128)(2,1)S(1)}) fusion(bf16[4,16,32,128]{3,2,1,0:T(8,128)(2,1)} %param.4), kind=kLoop, calls=%fused_computation.63 | loop fusion | bytes 524288 | tf_op jit(solution)/shard_map/slice | solution.py:11
  1.8 5.1 %collective-permute-start.1 = (bf16[1,16,32,128]{3,2,1,0:T(8,128)(2,1)S(1)}, bf16[1,16,32,128]{3,2,1,0:T(8,128)(2,1)S(1)}, u32[]{:S(2)}, u32[]{:S(2)}) collective-permute-start(bf16[1,16,32,128]{3,2,1,0:T(8,128)(2,1)S(1)} %get-tuple-element.9), channel_id=1, source_target_pairs={{4,0},{8,4},{12,8},{0,12},{5,1},{9,5},{13,9},{1,13},{6,2},{10,6},{... | collective-permute-start | bytes 393224 | tf_op jit(solution)/shard_map/ppermute | solution.py:23
  6.9 3.9 %collective-permute-done.1 = bf16[1,16,32,128]{3,2,1,0:T(8,128)(2,1)S(1)} collective-permute-done((bf16[1,16,32,128]{3,2,1,0:T(8,128)(2,1)S(1)}, bf16[1,16,32,128]{3,2,1,0:T(8,128)(2,1)S(1)}, u32[]{:S(2)}, u32[]{:S(2)}) %collective-permute-start.1) | collective-permute-done | bytes 131104 | tf_op jit(solution)/shard_map/ppermute | solution.py:23
  10.8 2.8 %collective-permute-done = bf16[1,16,32,128]{3,2,1,0:T(8,128)(2,1)S(1)} collective-permute-done((bf16[1,16,32,128]{3,2,1,0:T(8,128)(2,1)S(1)}, bf16[1,16,32,128]{3,2,1,0:T(8,128)(2,1)S(1)}, u32[]{:S(2)}, u32[]{:S(2)}) %collective-permute-start) | collective-permute-done | bytes 131104 | tf_op jit(solution)/shard_map/ppermute | solution.py:22
  13.6 0.8 %fusion.19 = bf16[6,1,32,128]{3,2,1,0:T(8,128)(2,1)S(1)} fusion(bf16[1,16,32,128]{3,2,1,0:T(8,128)(2,1)S(1)} %broadcast_select_fusion, bf16[4,16,32,128]{3,2,1,0:T(8,128)(2,1)} %param.4, bf16[1,16,32,128]{3,2,1,0:T(8,128)(2,1)S(1)} %broadcast_select_fusion.1, pred[]{:T(512)S(6)} %eq.25), kind=kLoop, calls=%fused_computation.55 | loop fusion | flops 122880 | bytes 835585 | tf_op jit(solution)/shard_map/jit(_where)/select_n | solution.py:17
  14.4 1.6 %collective-permute-start.2 = (bf16[6,1,32,128]{3,2,1,0:T(8,128)(2,1)S(1)}, bf16[6,1,32,128]{3,2,1,0:T(8,128)(2,1)S(1)}, u32[]{:S(2)}, u32[]{:S(2)}) collective-permute-start(bf16[6,1,32,128]{3,2,1,0:T(8,128)(2,1)S(1)} %fusion.19), channel_id=1, source_target_pairs={{0,2},{2,0},{1,3},{3,1},{4,6},{6,4},{5,7},{7,5},{8,10},{10,8},{9,1... | collective-permute-start | bytes 147464 | tf_op jit(solution)/shard_map/ppermute | solution.py:17
  16.0 2.6 %collective-permute-done.2 = bf16[6,1,32,128]{3,2,1,0:T(8,128)(2,1)S(1)} collective-permute-done((bf16[6,1,32,128]{3,2,1,0:T(8,128)(2,1)S(1)}, bf16[6,1,32,128]{3,2,1,0:T(8,128)(2,1)S(1)}, u32[]{:S(2)}, u32[]{:S(2)}) %collective-permute-start.2) | collective-permute-done | bytes 49184 | tf_op jit(solution)/shard_map/ppermute | solution.py:17
  18.6 0.2 pad_maximum_fusion.1
  18.8 0.3 constant_dynamic-slice_fusion
  19.1 0.8 %pad_slice_fusion.1 = (bf16[6,18,32,64]{3,2,1,0:T(8,128)(2,1)S(1)}, bf16[6,18,32,64]{3,2,1,0:T(8,128)(2,1)S(1)}) fusion(bf16[6,18,32,64]{3,2,1,0:T(8,128)(2,1)S(1)} %constant_dynamic-slice_fusion), kind=kLoop, calls=%fused_computation.12 | loop fusion | bytes 1327104 | tf_op jit(solution)/shard_map/slice | solution.py:73
  19.9 0.9 %pad_maximum_fusion = bf16[6,18,32,192]{3,2,1,0:T(8,128)(2,1)S(1)} fusion(bf16[6,18,32,64]{3,2,1,0:T(8,128)(2,1)S(1)} %get-tuple-element.7, bf16[6,18,32,64]{3,2,1,0:T(8,128)(2,1)S(1)} %constant_dynamic-slice_fusion, bf16[6,18,32,64]{3,2,1,0:T(8,128)(2,1)S(1)} %get-tuple-element.6), kind=kLoop, calls=%fused_computation.2 | loop fusion | flops 3981312 | bytes 2654208 | tf_op jit(solution)/shard_map/concatenate | solution.py:73
  20.7 0.2 copy-done.2
  20.9 0.5 fusion.27
  21.4 0.5 fusion.28
  21.8 0.5 fusion.26
  22.3 0.5 fusion.25
  22.8 0.5 fusion.31
  23.2 0.5 fusion.32
  23.7 0.5 fusion.29
  24.2 0.5 fusion.30
  25.4 0.5 fusion.33
  25.9 0.2 fusion.53
  26.9 0.1 maximum_bitcast_fusion.7
  27.1 0.1 maximum_bitcast_fusion.2
  27.2 0.1 maximum_bitcast_fusion.4
  27.5 1.6 %collective-permute-start.3 = (f32[4,216,64]{1,2,0:T(8,128)S(1)}, f32[4,216,64]{1,2,0:T(8,128)S(1)}, u32[]{:S(2)}, u32[]{:S(2)}) collective-permute-start(f32[4,216,64]{1,2,0:T(8,128)S(1)} %slice_select_fusion.1), channel_id=1, source_target_pairs={{0,2},{2,0},{1,3},{3,1},{4,6},{6,4},{5,7},{7,5},{8,10},{10,8},{9,1... | collective-permute-start | bytes 663560 | tf_op jit(solution)/shard_map/ppermute | solution.py:98
  29.0 0.4 copy.28
  29.4 0.2 pad.5.clone
  29.7 0.1 copy.7
  29.8 0.1 slice.139
  30.0 0.4 copy-done.3
  30.3 5.0 %fusion.11 = bf16[4,16,8,5,128]{4,2,3,1,0:T(8,128)(2,1)S(1)} fusion(bf16[3,3,3,128,128]{4,3,2,1,0:T(8,128)(2,1)S(1)} %bitcast.201, bf16[6,18,1,7,2,128]{5,3,4,1,0,2:T(8,128)(2,1)S(1)} %slice.139, bf16[6,18,1,8,5,128]{5,3,4,1,0,2:T(8,128)(2,1)S(1)} %copy.7, pred[8,5]{0,1:T(8,128)(4,1)S(1)} %copy-done.3), kind=kOutput, calls=%fused_computation.10 | convolution fusion | flops 2270224384 | bytes 3033128 | tf_op jit(solution)/shard_map/conv_general_dilated | solution.py:65
  35.4 0.2 select_add_fusion.1
  35.6 0.6 %collective-permute-start.7 = (f32[4,216,64]{1,2,0:T(8,128)S(1)}, f32[4,216,64]{1,2,0:T(8,128)S(1)}, u32[]{:S(2)}, u32[]{:S(2)}) collective-permute-start(f32[4,216,64]{1,2,0:T(8,128)S(1)} %get-tuple-element.5), channel_id=1, source_target_pairs={{0,2},{2,0},{1,3},{3,1},{4,6},{6,4},{5,7},{7,5},{8,10},{10,8},{9,1... | collective-permute-start | bytes 663560 | tf_op jit(solution)/shard_map/ppermute | solution.py:98
  36.3 0.9 %copy.18 = bf16[4,16,32,128]{3,2,1,0:T(8,128)(2,1)} copy(bf16[4,16,32,128]{3,1,2,0:T(8,128)(2,1)S(1)} %slice_bitcast_fusion) | data formatting | bytes 1048576
  37.2 1.4 %collective-permute-start.4 = (f32[216,64]{0,1:T(8,128)S(1)}, f32[216,64]{0,1:T(8,128)S(1)}, u32[]{:S(2)}, u32[]{:S(2)}) collective-permute-start(f32[216,64]{0,1:T(8,128)S(1)} %get-tuple-element.10), channel_id=1, source_target_pairs={{0,4},{4,8},{8,12},{12,0},{1,5},{5,9},{9,13},{13,1},{2,6},{6,10},{... | collective-permute-start | bytes 165896 | tf_op jit(solution)/shard_map/ppermute | solution.py:40
  38.6 0.7 %collective-permute-start.5 = (f32[216,64]{0,1:T(8,128)S(1)}, f32[216,64]{0,1:T(8,128)S(1)}, u32[]{:S(2)}, u32[]{:S(2)}) collective-permute-start(f32[216,64]{0,1:T(8,128)S(1)} %get-tuple-element.12), channel_id=1, source_target_pairs={{0,8},{4,12},{8,0},{12,4},{1,9},{5,13},{9,1},{13,5},{2,10},{6,14},... | collective-permute-start | bytes 165896 | tf_op jit(solution)/shard_map/ppermute | solution.py:40
  39.3 2.4 %collective-permute-start.6 = (f32[216,64]{0,1:T(8,128)S(1)}, f32[216,64]{0,1:T(8,128)S(1)}, u32[]{:S(2)}, u32[]{:S(2)}) collective-permute-start(f32[216,64]{0,1:T(8,128)S(1)} %get-tuple-element.11), channel_id=1, source_target_pairs={{0,12},{4,0},{8,4},{12,8},{1,13},{5,1},{9,5},{13,9},{2,14},{6,2},{... | collective-permute-start | bytes 165896 | tf_op jit(solution)/shard_map/ppermute | solution.py:40
  41.7 0.4 collective-permute-done.7
  42.1 0.2 select_add_fusion
  42.3 1.5 %collective-permute-start.10 = (f32[216,64]{0,1:T(8,128)S(1)}, f32[216,64]{0,1:T(8,128)S(1)}, u32[]{:S(2)}, u32[]{:S(2)}) collective-permute-start(f32[216,64]{0,1:T(8,128)S(1)} %get-tuple-element.14), channel_id=1, source_target_pairs={{0,12},{4,0},{8,4},{12,8},{1,13},{5,1},{9,5},{13,9},{2,14},{6,2},{... | collective-permute-start | bytes 165896 | tf_op jit(solution)/shard_map/ppermute | solution.py:40
  43.8 0.6 %collective-permute-start.8 = (f32[216,64]{0,1:T(8,128)S(1)}, f32[216,64]{0,1:T(8,128)S(1)}, u32[]{:S(2)}, u32[]{:S(2)}) collective-permute-start(f32[216,64]{0,1:T(8,128)S(1)} %get-tuple-element.13), channel_id=1, source_target_pairs={{0,4},{4,8},{8,12},{12,0},{1,5},{5,9},{9,13},{13,1},{2,6},{6,10},{... | collective-permute-start | bytes 165896 | tf_op jit(solution)/shard_map/ppermute | solution.py:40
  44.4 1.0 %collective-permute-start.9 = (f32[216,64]{0,1:T(8,128)S(1)}, f32[216,64]{0,1:T(8,128)S(1)}, u32[]{:S(2)}, u32[]{:S(2)}) collective-permute-start(f32[216,64]{0,1:T(8,128)S(1)} %get-tuple-element.15), channel_id=1, source_target_pairs={{0,8},{4,12},{8,0},{12,4},{1,9},{5,13},{9,1},{13,5},{2,10},{6,14},... | collective-permute-start | bytes 165896 | tf_op jit(solution)/shard_map/ppermute | solution.py:40
  45.4 1.6 %collective-permute-done.5 = f32[216,64]{0,1:T(8,128)S(1)} collective-permute-done((f32[216,64]{0,1:T(8,128)S(1)}, f32[216,64]{0,1:T(8,128)S(1)}, u32[]{:S(2)}, u32[]{:S(2)}) %collective-permute-start.5) | collective-permute-done | bytes 55328 | tf_op jit(solution)/shard_map/ppermute | solution.py:40
  47.0 0.5 collective-permute-done.10
  47.5 2.5 %collective-permute-done.8 = f32[216,64]{0,1:T(8,128)S(1)} collective-permute-done((f32[216,64]{0,1:T(8,128)S(1)}, f32[216,64]{0,1:T(8,128)S(1)}, u32[]{:S(2)}, u32[]{:S(2)}) %collective-permute-start.8) | collective-permute-done | bytes 55328 | tf_op jit(solution)/shard_map/ppermute | solution.py:40
  50.0 1.0 %collective-permute-done.9 = f32[216,64]{0,1:T(8,128)S(1)} collective-permute-done((f32[216,64]{0,1:T(8,128)S(1)}, f32[216,64]{0,1:T(8,128)S(1)}, u32[]{:S(2)}, u32[]{:S(2)}) %collective-permute-start.9) | collective-permute-done | bytes 55328 | tf_op jit(solution)/shard_map/ppermute | solution.py:40
  51.0 0.8 %maximum_multiply_fusion = f32[432,64]{0,1:T(8,128)} fusion(f32[216,64]{0,1:T(8,128)S(1)} %fusion.16, f32[216,64]{0,1:T(8,128)S(1)} %fusion.18), kind=kLoop, calls=%fused_computation.30 | loop fusion | flops 55296 | bytes 221184 | tf_op jit(solution)/shard_map/div | solution.py:106
  (53 shorter events, 1.9 us)
Async XLA Ops:
  0.6 29.3 %copy-start = (bf16[27,128,128]{2,1,0:T(8,128)(2,1)S(1)}, bf16[27,128,128]{2,1,0:T(8,128)(2,1)}, u32[]{:S(2)}) copy-start(bf16[27,128,128]{2,1,0:T(8,128)(2,1)} %param.5) | copy-start | bytes 2654212
  0.6 18.0 %copy-start.1 = (bf16[4,16,32,128]{3,2,1,0:T(8,128)(2,1)S(1)}, bf16[4,16,32,128]{3,2,1,0:T(8,128)(2,1)}, u32[]{:S(2)}) copy-start(bf16[4,16,32,128]{3,2,1,0:T(8,128)(2,1)} %param.4) | copy-start | bytes 1572868
  1.8 9.0 %collective-permute-start.1 = (bf16[1,16,32,128]{3,2,1,0:T(8,128)(2,1)S(1)}, bf16[1,16,32,128]{3,2,1,0:T(8,128)(2,1)S(1)}, u32[]{:S(2)}, u32[]{:S(2)}) collective-permute-start(bf16[1,16,32,128]{3,2,1,0:T(8,128)(2,1)S(1)} %get-tuple-element.9), channel_id=1, source_target_pairs={{4,0},{8,4},{12,8},{0,12},{5,1},{9,5},{13,9},{1,13},{6,2},{10,6},{... | collective-permute-start | bytes 393224 | tf_op jit(solution)/shard_map/ppermute | solution.py:23
  6.9 6.8 %collective-permute-start = (bf16[1,16,32,128]{3,2,1,0:T(8,128)(2,1)S(1)}, bf16[1,16,32,128]{3,2,1,0:T(8,128)(2,1)S(1)}, u32[]{:S(2)}, u32[]{:S(2)}) collective-permute-start(bf16[1,16,32,128]{3,2,1,0:T(8,128)(2,1)S(1)} %get-tuple-element.8), channel_id=1, source_target_pairs={{0,4},{4,8},{8,12},{12,0},{1,5},{5,9},{9,13},{13,1},{2,6},{6,10},{... | collective-permute-start | bytes 393224 | tf_op jit(solution)/shard_map/ppermute | solution.py:22
  14.4 4.2 %collective-permute-start.2 = (bf16[6,1,32,128]{3,2,1,0:T(8,128)(2,1)S(1)}, bf16[6,1,32,128]{3,2,1,0:T(8,128)(2,1)S(1)}, u32[]{:S(2)}, u32[]{:S(2)}) collective-permute-start(bf16[6,1,32,128]{3,2,1,0:T(8,128)(2,1)S(1)} %fusion.19), channel_id=1, source_target_pairs={{0,2},{2,0},{1,3},{3,1},{4,6},{6,4},{5,7},{7,5},{8,10},{10,8},{9,1... | collective-permute-start | bytes 147464 | tf_op jit(solution)/shard_map/ppermute | solution.py:17
  19.9 1.0 %copy-start.2 = (bf16[4,16,32,128]{3,2,1,0:T(8,128)(2,1)S(1)}, bf16[4,16,32,128]{3,2,1,0:T(8,128)(2,1)}, u32[]{:S(2)}) copy-start(bf16[4,16,32,128]{3,2,1,0:T(8,128)(2,1)} %param.3) | copy-start | bytes 1572868
  27.5 8.0 %collective-permute-start.3 = (f32[4,216,64]{1,2,0:T(8,128)S(1)}, f32[4,216,64]{1,2,0:T(8,128)S(1)}, u32[]{:S(2)}, u32[]{:S(2)}) collective-permute-start(f32[4,216,64]{1,2,0:T(8,128)S(1)} %slice_select_fusion.1), channel_id=1, source_target_pairs={{0,2},{2,0},{1,3},{3,1},{4,6},{6,4},{5,7},{7,5},{8,10},{10,8},{9,1... | collective-permute-start | bytes 663560 | tf_op jit(solution)/shard_map/ppermute | solution.py:98
  29.7 0.7 %copy-start.3 = (pred[8,5]{0,1:T(8,128)(4,1)S(1)}, pred[8,5]{0,1:T(8,128)(4,1)}, u32[]{:S(2)}) copy-start(pred[8,5]{0,1:T(8,128)(4,1)} %constant.81) | copy-start | bytes 124
  35.6 6.4 %collective-permute-start.7 = (f32[4,216,64]{1,2,0:T(8,128)S(1)}, f32[4,216,64]{1,2,0:T(8,128)S(1)}, u32[]{:S(2)}, u32[]{:S(2)}) collective-permute-start(f32[4,216,64]{1,2,0:T(8,128)S(1)} %get-tuple-element.5), channel_id=1, source_target_pairs={{0,2},{2,0},{1,3},{3,1},{4,6},{6,4},{5,7},{7,5},{8,10},{10,8},{9,1... | collective-permute-start | bytes 663560 | tf_op jit(solution)/shard_map/ppermute | solution.py:98
  37.2 7.2 %collective-permute-start.4 = (f32[216,64]{0,1:T(8,128)S(1)}, f32[216,64]{0,1:T(8,128)S(1)}, u32[]{:S(2)}, u32[]{:S(2)}) collective-permute-start(f32[216,64]{0,1:T(8,128)S(1)} %get-tuple-element.10), channel_id=1, source_target_pairs={{0,4},{4,8},{8,12},{12,0},{1,5},{5,9},{9,13},{13,1},{2,6},{6,10},{... | collective-permute-start | bytes 165896 | tf_op jit(solution)/shard_map/ppermute | solution.py:40
  38.6 8.4 %collective-permute-start.5 = (f32[216,64]{0,1:T(8,128)S(1)}, f32[216,64]{0,1:T(8,128)S(1)}, u32[]{:S(2)}, u32[]{:S(2)}) collective-permute-start(f32[216,64]{0,1:T(8,128)S(1)} %get-tuple-element.12), channel_id=1, source_target_pairs={{0,8},{4,12},{8,0},{12,4},{1,9},{5,13},{9,1},{13,5},{2,10},{6,14},... | collective-permute-start | bytes 165896 | tf_op jit(solution)/shard_map/ppermute | solution.py:40
  39.3 7.7 %collective-permute-start.6 = (f32[216,64]{0,1:T(8,128)S(1)}, f32[216,64]{0,1:T(8,128)S(1)}, u32[]{:S(2)}, u32[]{:S(2)}) collective-permute-start(f32[216,64]{0,1:T(8,128)S(1)} %get-tuple-element.11), channel_id=1, source_target_pairs={{0,12},{4,0},{8,4},{12,8},{1,13},{5,1},{9,5},{13,9},{2,14},{6,2},{... | collective-permute-start | bytes 165896 | tf_op jit(solution)/shard_map/ppermute | solution.py:40
  42.3 5.2 %collective-permute-start.10 = (f32[216,64]{0,1:T(8,128)S(1)}, f32[216,64]{0,1:T(8,128)S(1)}, u32[]{:S(2)}, u32[]{:S(2)}) collective-permute-start(f32[216,64]{0,1:T(8,128)S(1)} %get-tuple-element.14), channel_id=1, source_target_pairs={{0,12},{4,0},{8,4},{12,8},{1,13},{5,1},{9,5},{13,9},{2,14},{6,2},{... | collective-permute-start | bytes 165896 | tf_op jit(solution)/shard_map/ppermute | solution.py:40
  43.8 6.2 %collective-permute-start.8 = (f32[216,64]{0,1:T(8,128)S(1)}, f32[216,64]{0,1:T(8,128)S(1)}, u32[]{:S(2)}, u32[]{:S(2)}) collective-permute-start(f32[216,64]{0,1:T(8,128)S(1)} %get-tuple-element.13), channel_id=1, source_target_pairs={{0,4},{4,8},{8,12},{12,0},{1,5},{5,9},{9,13},{13,1},{2,6},{6,10},{... | collective-permute-start | bytes 165896 | tf_op jit(solution)/shard_map/ppermute | solution.py:40
  44.4 6.6 %collective-permute-start.9 = (f32[216,64]{0,1:T(8,128)S(1)}, f32[216,64]{0,1:T(8,128)S(1)}, u32[]{:S(2)}, u32[]{:S(2)}) collective-permute-start(f32[216,64]{0,1:T(8,128)S(1)} %get-tuple-element.15), channel_id=1, source_target_pairs={{0,8},{4,12},{8,0},{12,4},{1,9},{5,13},{9,1},{13,5},{2,10},{6,14},... | collective-permute-start | bytes 165896 | tf_op jit(solution)/shard_map/ppermute | solution.py:40

commit v18 on v11

--- a/solution.py
+++ b/solution.py
@@ -35,7 +35,7 @@
         return lax.psum_scatter(blocks, axis, scatter_dimension=dim, tiled=False)
     me = lax.axis_index(axis)
     total = lax.dynamic_index_in_dim(blocks, me, dim, keepdims=False)
-    for shift in range(1, count):
+    for shift in sorted(range(1, count), key=lambda s: -min(s, count - s)):
         part = lax.dynamic_index_in_dim(blocks, (me + shift) % count, dim, keepdims=False)
         total = total + lax.ppermute(part, axis, [(j, (j + shift) % count) for j in range(count)])
     return total

time: 50.5 us -> 50.8 us (level)
  starting transfers between devices: 17 us -> 17.7 us
    ppermute x6, starting transfers between devices: 7.58 us -> 8.33 us  [scatter_sum(): lax.ppermute(part, axis, [(j, (j + shift) % count) for j in range(count)])]
    ppermute x2, waiting for transfers between devices: 0.75 us -> 0.01 us  [on_device(): partial = keep + lax.ppermute(send, 'gy', [(0, 1), (1, 0)])]
where the time goes in v18:
time: 50.8 us; the launch traced here: 50.6 us
  starting transfers between devices  17.7 us (35%)
  waiting for transfers between devices  12.8 us (25%)
  matrix products  9.1 us (18%)
  other arithmetic  4.95 us (10%)
  local copies, waits for them, and re-layouts  4.93 us (10%)
  between operations  1.11 us (2%)
    ppermute x6, starting transfers between devices, scatter_sum(): lax.ppermute(part, axis, [(j, (j + shift) % count) for j in range(count)])  8.33 us
    ppermute x6, waiting for transfers between devices, scatter_sum(): lax.ppermute(part, axis, [(j, (j + shift) % count) for j in range(count)])  5.74 us
    conv_general_dilated x1, matrix products, on_device(): lax.conv_general_dilated(gh[None], kflip, (1, 1, 1), pad, dimension_numbe...  4.96 us
    ppermute x1, waiting for transfers between devices, with_halo(): low = lax.ppermute(tail, axis, [(i, (i + 1) % count) for i in range(count)])  4.21 us
    dot_general x9, matrix products, on_device(): lax.dot_general(x_act, window, (((0, 1, 2), (0, 1, 2)), ((), ())), prefer...  4.14 us
    ppermute x1, starting transfers between devices, with_halo(): got = lax.ppermute(jnp.where(me == 0, tail, head), axis, [(0, 1), (1, 0)])  2.94 us
    ppermute x1, starting transfers between devices, with_halo(): low = lax.ppermute(tail, axis, [(i, (i + 1) % count) for i in range(count)])  2.16 us
    ppermute x2, starting transfers between devices, on_device(): partial = keep + lax.ppermute(send, 'gy', [(0, 1), (1, 0)])  2.15 us
  transfers between devices with their start and end apart: 11, of which 6 were waited for; matrix products, arithmetic and copies ran while one was open for 14% of the time, Pallas kernels for 0%

profile of v18, /device:TPU:0, one launch (start us, length us, event | category | flops | bytes accessed | tf_op | source)
XLA Modules:
  0.0 50.6 jit_solution(10929300312011490299)
XLA Ops:
  0.7 0.9 %slice_select_fusion.2 = bf16[4,1,32,128]{3,2,1,0:T(8,128)(2,1)S(1)} fusion(bf16[4,16,32,128]{3,2,1,0:T(8,128)(2,1)} %param.4, pred[]{:T(512)S(6)} %eq.26), kind=kLoop, calls=%fused_computation.57 | loop fusion | flops 16384 | bytes 98305 | tf_op jit(solution)/shard_map/jit(_where)/select_n | solution.py:17
  1.6 2.9 %collective-permute-start = (bf16[4,1,32,128]{3,2,1,0:T(8,128)(2,1)S(1)}, bf16[4,1,32,128]{3,2,1,0:T(8,128)(2,1)S(1)}, u32[]{:S(2)}, u32[]{:S(2)}) collective-permute-start(bf16[4,1,32,128]{3,2,1,0:T(8,128)(2,1)S(1)} %slice_select_fusion.2), channel_id=1, source_target_pairs={{0,2},{2,0},{1,3},{3,1},{4,6},{6,4},{5,7},{7,5},{8,10},{10,8},{9,1... | collective-permute-start | bytes 98312 | tf_op jit(solution)/shard_map/ppermute | solution.py:17
  4.5 1.9 %collective-permute-done = bf16[4,1,32,128]{3,2,1,0:T(8,128)(2,1)S(1)} collective-permute-done((bf16[4,1,32,128]{3,2,1,0:T(8,128)(2,1)S(1)}, bf16[4,1,32,128]{3,2,1,0:T(8,128)(2,1)S(1)}, u32[]{:S(2)}, u32[]{:S(2)}) %collective-permute-start) | collective-permute-done | bytes 32800 | tf_op jit(solution)/shard_map/ppermute | solution.py:17
  6.4 1.0 %pad_maximum_fusion.6 = (bf16[1,18,32,128]{3,2,1,0:T(8,128)(2,1)S(1)}, bf16[1,18,32,128]{3,2,1,0:T(8,128)(2,1)S(1)}) fusion(bf16[4,1,32,128]{3,2,1,0:T(8,128)(2,1)S(1)} %get-tuple-element.19, bf16[4,16,32,128]{3,2,1,0:T(8,128)(2,1)} %param.4, bf16[4,1,32,128]{3,2,1,0:T(8,128)(2,1)S(1)} %get-tuple-element.18), kind=kLoop, calls=%fused_computation.24 | loop fusion | flops 294912 | bytes 884736 | tf_op jit(solution)/shard_map/slice | solution.py:11
  7.4 2.2 %collective-permute-start.1 = (bf16[1,18,32,128]{3,2,1,0:T(8,128)(2,1)S(1)}, bf16[1,18,32,128]{3,2,1,0:T(8,128)(2,1)S(1)}, u32[]{:S(2)}, u32[]{:S(2)}) collective-permute-start(bf16[1,18,32,128]{3,2,1,0:T(8,128)(2,1)S(1)} %get-tuple-element.8), channel_id=1, source_target_pairs={{0,4},{4,8},{8,12},{12,0},{1,5},{5,9},{9,13},{13,1},{2,6},{6,10},{... | collective-permute-start | bytes 442376 | tf_op jit(solution)/shard_map/ppermute | solution.py:22
  9.6 2.1 %collective-permute-start.2 = (bf16[1,18,32,128]{3,2,1,0:T(8,128)(2,1)S(1)}, bf16[1,18,32,128]{3,2,1,0:T(8,128)(2,1)S(1)}, u32[]{:S(2)}, u32[]{:S(2)}) collective-permute-start(bf16[1,18,32,128]{3,2,1,0:T(8,128)(2,1)S(1)} %get-tuple-element.9), channel_id=1, source_target_pairs={{4,0},{8,4},{12,8},{0,12},{5,1},{9,5},{13,9},{1,13},{6,2},{10,6},{... | collective-permute-start | bytes 442376 | tf_op jit(solution)/shard_map/ppermute | solution.py:23
  11.7 4.2 %collective-permute-done.1 = bf16[1,18,32,128]{3,2,1,0:T(8,128)(2,1)S(1)} collective-permute-done((bf16[1,18,32,128]{3,2,1,0:T(8,128)(2,1)S(1)}, bf16[1,18,32,128]{3,2,1,0:T(8,128)(2,1)S(1)}, u32[]{:S(2)}, u32[]{:S(2)}) %collective-permute-start.1) | collective-permute-done | bytes 147488 | tf_op jit(solution)/shard_map/ppermute | solution.py:22
  15.9 0.9 %collective-permute-done.2 = bf16[1,18,32,128]{3,2,1,0:T(8,128)(2,1)S(1)} collective-permute-done((bf16[1,18,32,128]{3,2,1,0:T(8,128)(2,1)S(1)}, bf16[1,18,32,128]{3,2,1,0:T(8,128)(2,1)S(1)}, u32[]{:S(2)}, u32[]{:S(2)}) %collective-permute-start.2) | collective-permute-done | bytes 147488 | tf_op jit(solution)/shard_map/ppermute | solution.py:23
  16.9 0.2 pad_maximum_fusion.1
  17.1 0.3 constant_dynamic-slice_fusion
  17.4 0.8 %pad_slice_fusion.1 = (bf16[6,18,32,64]{3,2,1,0:T(8,128)(2,1)S(1)}, bf16[6,18,32,64]{3,2,1,0:T(8,128)(2,1)S(1)}) fusion(bf16[6,18,32,64]{3,2,1,0:T(8,128)(2,1)S(1)} %constant_dynamic-slice_fusion), kind=kLoop, calls=%fused_computation.12 | loop fusion | bytes 1327104 | tf_op jit(solution)/shard_map/slice | solution.py:73
  18.2 0.9 %pad_maximum_fusion = bf16[6,18,32,192]{3,2,1,0:T(8,128)(2,1)S(1)} fusion(bf16[6,18,32,64]{3,2,1,0:T(8,128)(2,1)S(1)} %get-tuple-element.7, bf16[6,18,32,64]{3,2,1,0:T(8,128)(2,1)S(1)} %constant_dynamic-slice_fusion, bf16[6,18,32,64]{3,2,1,0:T(8,128)(2,1)S(1)} %get-tuple-element.6), kind=kLoop, calls=%fused_computation.2 | loop fusion | flops 3981312 | bytes 2654208 | tf_op jit(solution)/shard_map/concatenate | solution.py:73
  19.0 0.2 copy-done.2
  19.2 0.5 fusion.25
  19.7 0.5 fusion.26
  20.1 0.5 fusion.24
  20.6 0.5 fusion.23
  21.1 0.5 fusion.29
  21.5 0.5 fusion.30
  22.0 0.5 fusion.27
  22.5 0.5 fusion.28
  23.7 0.5 fusion.31
  24.2 0.2 fusion.51
  25.1 0.1 maximum_bitcast_fusion.7
  25.3 0.1 maximum_bitcast_fusion.2
  25.5 0.1 maximum_bitcast_fusion.4
  25.7 1.6 %collective-permute-start.3 = (f32[4,216,64]{1,2,0:T(8,128)S(1)}, f32[4,216,64]{1,2,0:T(8,128)S(1)}, u32[]{:S(2)}, u32[]{:S(2)}) collective-permute-start(f32[4,216,64]{1,2,0:T(8,128)S(1)} %slice_select_fusion.1), channel_id=1, source_target_pairs={{0,2},{2,0},{1,3},{3,1},{4,6},{6,4},{5,7},{7,5},{8,10},{10,8},{9,1... | collective-permute-start | bytes 663560 | tf_op jit(solution)/shard_map/ppermute | solution.py:98
  27.3 0.4 copy.28
  27.7 0.2 pad.5.clone
  27.9 0.1 copy.7
  28.1 0.1 slice.139
  28.2 0.4 copy-done.3
  28.6 5.0 %fusion.11 = bf16[4,16,8,5,128]{4,2,3,1,0:T(8,128)(2,1)S(1)} fusion(bf16[3,3,3,128,128]{4,3,2,1,0:T(8,128)(2,1)S(1)} %bitcast.201, bf16[6,18,1,7,2,128]{5,3,4,1,0,2:T(8,128)(2,1)S(1)} %slice.139, bf16[6,18,1,8,5,128]{5,3,4,1,0,2:T(8,128)(2,1)S(1)} %copy.7, pred[8,5]{0,1:T(8,128)(4,1)S(1)} %copy-done.3), kind=kOutput, calls=%fused_computation.10 | convolution fusion | flops 2270224384 | bytes 3033128 | tf_op jit(solution)/shard_map/conv_general_dilated | solution.py:65
  33.6 0.1 copy.8
  33.7 0.2 select_add_fusion.1
  33.9 0.6 %collective-permute-start.7 = (f32[4,216,64]{1,2,0:T(8,128)S(1)}, f32[4,216,64]{1,2,0:T(8,128)S(1)}, u32[]{:S(2)}, u32[]{:S(2)}) collective-permute-start(f32[4,216,64]{1,2,0:T(8,128)S(1)} %get-tuple-element.5), channel_id=1, source_target_pairs={{0,2},{2,0},{1,3},{3,1},{4,6},{6,4},{5,7},{7,5},{8,10},{10,8},{9,1... | collective-permute-start | bytes 663560 | tf_op jit(solution)/shard_map/ppermute | solution.py:98
  34.5 0.9 %copy.18 = bf16[4,16,32,128]{3,2,1,0:T(8,128)(2,1)} copy(bf16[4,16,32,128]{3,1,2,0:T(8,128)(2,1)S(1)} %slice_bitcast_fusion) | data formatting | bytes 1048576
  35.5 1.2 %collective-permute-start.4 = (f32[216,64]{0,1:T(8,128)S(1)}, f32[216,64]{0,1:T(8,128)S(1)}, u32[]{:S(2)}, u32[]{:S(2)}) collective-permute-start(f32[216,64]{0,1:T(8,128)S(1)} %get-tuple-element.10), channel_id=1, source_target_pairs={{0,8},{4,12},{8,0},{12,4},{1,9},{5,13},{9,1},{13,5},{2,10},{6,14},... | collective-permute-start | bytes 165896 | tf_op jit(solution)/shard_map/ppermute | solution.py:40
  36.7 2.2 %collective-permute-start.5 = (f32[216,64]{0,1:T(8,128)S(1)}, f32[216,64]{0,1:T(8,128)S(1)}, u32[]{:S(2)}, u32[]{:S(2)}) collective-permute-start(f32[216,64]{0,1:T(8,128)S(1)} %get-tuple-element.12), channel_id=1, source_target_pairs={{0,4},{4,8},{8,12},{12,0},{1,5},{5,9},{9,13},{13,1},{2,6},{6,10},{... | collective-permute-start | bytes 165896 | tf_op jit(solution)/shard_map/ppermute | solution.py:40
  38.9 1.6 %collective-permute-start.6 = (f32[216,64]{0,1:T(8,128)S(1)}, f32[216,64]{0,1:T(8,128)S(1)}, u32[]{:S(2)}, u32[]{:S(2)}) collective-permute-start(f32[216,64]{0,1:T(8,128)S(1)} %get-tuple-element.11), channel_id=1, source_target_pairs={{0,12},{4,0},{8,4},{12,8},{1,13},{5,1},{9,5},{13,9},{2,14},{6,2},{... | collective-permute-start | bytes 165896 | tf_op jit(solution)/shard_map/ppermute | solution.py:40
  40.5 0.2 select_add_fusion
  40.8 2.7 %collective-permute-start.10 = (f32[216,64]{0,1:T(8,128)S(1)}, f32[216,64]{0,1:T(8,128)S(1)}, u32[]{:S(2)}, u32[]{:S(2)}) collective-permute-start(f32[216,64]{0,1:T(8,128)S(1)} %get-tuple-element.14), channel_id=1, source_target_pairs={{0,12},{4,0},{8,4},{12,8},{1,13},{5,1},{9,5},{13,9},{2,14},{6,2},{... | collective-permute-start | bytes 165896 | tf_op jit(solution)/shard_map/ppermute | solution.py:40
  43.4 0.3 collective-permute-start.8
  43.8 0.3 collective-permute-start.9
  44.1 1.7 %collective-permute-done.10 = f32[216,64]{0,1:T(8,128)S(1)} collective-permute-done((f32[216,64]{0,1:T(8,128)S(1)}, f32[216,64]{0,1:T(8,128)S(1)}, u32[]{:S(2)}, u32[]{:S(2)}) %collective-permute-start.10) | collective-permute-done | bytes 55328 | tf_op jit(solution)/shard_map/ppermute | solution.py:40
  45.8 2.8 %collective-permute-done.8 = f32[216,64]{0,1:T(8,128)S(1)} collective-permute-done((f32[216,64]{0,1:T(8,128)S(1)}, f32[216,64]{0,1:T(8,128)S(1)}, u32[]{:S(2)}, u32[]{:S(2)}) %collective-permute-start.8) | collective-permute-done | bytes 55328 | tf_op jit(solution)/shard_map/ppermute | solution.py:40
  48.6 1.2 %collective-permute-done.9 = f32[216,64]{0,1:T(8,128)S(1)} collective-permute-done((f32[216,64]{0,1:T(8,128)S(1)}, f32[216,64]{0,1:T(8,128)S(1)}, u32[]{:S(2)}, u32[]{:S(2)}) %collective-permute-start.9) | collective-permute-done | bytes 55328 | tf_op jit(solution)/shard_map/ppermute | solution.py:40
  49.8 0.8 %maximum_multiply_fusion = f32[432,64]{0,1:T(8,128)} fusion(f32[216,64]{0,1:T(8,128)S(1)} %fusion.16, f32[216,64]{0,1:T(8,128)S(1)} %fusion.18), kind=kLoop, calls=%fused_computation.35 | loop fusion | flops 55296 | bytes 221184 | tf_op jit(solution)/shard_map/div | solution.py:106
  (53 shorter events, 1.8 us)
Async XLA Ops:
  0.6 27.6 %copy-start = (bf16[27,128,128]{2,1,0:T(8,128)(2,1)S(1)}, bf16[27,128,128]{2,1,0:T(8,128)(2,1)}, u32[]{:S(2)}) copy-start(bf16[27,128,128]{2,1,0:T(8,128)(2,1)} %param.5) | copy-start | bytes 2654212
  0.6 16.3 %copy-start.1 = (bf16[4,16,32,128]{3,2,1,0:T(8,128)(2,1)S(1)}, bf16[4,16,32,128]{3,2,1,0:T(8,128)(2,1)}, u32[]{:S(2)}) copy-start(bf16[4,16,32,128]{3,2,1,0:T(8,128)(2,1)} %param.4) | copy-start | bytes 1572868
  1.6 4.8 %collective-permute-start = (bf16[4,1,32,128]{3,2,1,0:T(8,128)(2,1)S(1)}, bf16[4,1,32,128]{3,2,1,0:T(8,128)(2,1)S(1)}, u32[]{:S(2)}, u32[]{:S(2)}) collective-permute-start(bf16[4,1,32,128]{3,2,1,0:T(8,128)(2,1)S(1)} %slice_select_fusion.2), channel_id=1, source_target_pairs={{0,2},{2,0},{1,3},{3,1},{4,6},{6,4},{5,7},{7,5},{8,10},{10,8},{9,1... | collective-permute-start | bytes 98312 | tf_op jit(solution)/shard_map/ppermute | solution.py:17
  7.4 8.5 %collective-permute-start.1 = (bf16[1,18,32,128]{3,2,1,0:T(8,128)(2,1)S(1)}, bf16[1,18,32,128]{3,2,1,0:T(8,128)(2,1)S(1)}, u32[]{:S(2)}, u32[]{:S(2)}) collective-permute-start(bf16[1,18,32,128]{3,2,1,0:T(8,128)(2,1)S(1)} %get-tuple-element.8), channel_id=1, source_target_pairs={{0,4},{4,8},{8,12},{12,0},{1,5},{5,9},{9,13},{13,1},{2,6},{6,10},{... | collective-permute-start | bytes 442376 | tf_op jit(solution)/shard_map/ppermute | solution.py:22
  9.6 7.3 %collective-permute-start.2 = (bf16[1,18,32,128]{3,2,1,0:T(8,128)(2,1)S(1)}, bf16[1,18,32,128]{3,2,1,0:T(8,128)(2,1)S(1)}, u32[]{:S(2)}, u32[]{:S(2)}) collective-permute-start(bf16[1,18,32,128]{3,2,1,0:T(8,128)(2,1)S(1)} %get-tuple-element.9), channel_id=1, source_target_pairs={{4,0},{8,4},{12,8},{0,12},{5,1},{9,5},{13,9},{1,13},{6,2},{10,6},{... | collective-permute-start | bytes 442376 | tf_op jit(solution)/shard_map/ppermute | solution.py:23
  18.2 1.0 %copy-start.2 = (bf16[4,16,32,128]{3,2,1,0:T(8,128)(2,1)S(1)}, bf16[4,16,32,128]{3,2,1,0:T(8,128)(2,1)}, u32[]{:S(2)}) copy-start(bf16[4,16,32,128]{3,2,1,0:T(8,128)(2,1)} %param.3) | copy-start | bytes 1572868
  25.7 8.0 %collective-permute-start.3 = (f32[4,216,64]{1,2,0:T(8,128)S(1)}, f32[4,216,64]{1,2,0:T(8,128)S(1)}, u32[]{:S(2)}, u32[]{:S(2)}) collective-permute-start(f32[4,216,64]{1,2,0:T(8,128)S(1)} %slice_select_fusion.1), channel_id=1, source_target_pairs={{0,2},{2,0},{1,3},{3,1},{4,6},{6,4},{5,7},{7,5},{8,10},{10,8},{9,1... | collective-permute-start | bytes 663560 | tf_op jit(solution)/shard_map/ppermute | solution.py:98
  27.9 0.7 %copy-start.3 = (pred[8,5]{0,1:T(8,128)(4,1)S(1)}, pred[8,5]{0,1:T(8,128)(4,1)}, u32[]{:S(2)}) copy-start(pred[8,5]{0,1:T(8,128)(4,1)} %constant.81) | copy-start | bytes 124
  33.9 6.6 %collective-permute-start.7 = (f32[4,216,64]{1,2,0:T(8,128)S(1)}, f32[4,216,64]{1,2,0:T(8,128)S(1)}, u32[]{:S(2)}, u32[]{:S(2)}) collective-permute-start(f32[4,216,64]{1,2,0:T(8,128)S(1)} %get-tuple-element.5), channel_id=1, source_target_pairs={{0,2},{2,0},{1,3},{3,1},{4,6},{6,4},{5,7},{7,5},{8,10},{10,8},{9,1... | collective-permute-start | bytes 663560 | tf_op jit(solution)/shard_map/ppermute | solution.py:98
  35.5 8.3 %collective-permute-start.4 = (f32[216,64]{0,1:T(8,128)S(1)}, f32[216,64]{0,1:T(8,128)S(1)}, u32[]{:S(2)}, u32[]{:S(2)}) collective-permute-start(f32[216,64]{0,1:T(8,128)S(1)} %get-tuple-element.10), channel_id=1, source_target_pairs={{0,8},{4,12},{8,0},{12,4},{1,9},{5,13},{9,1},{13,5},{2,10},{6,14},... | collective-permute-start | bytes 165896 | tf_op jit(solution)/shard_map/ppermute | solution.py:40
  36.7 7.4 %collective-permute-start.5 = (f32[216,64]{0,1:T(8,128)S(1)}, f32[216,64]{0,1:T(8,128)S(1)}, u32[]{:S(2)}, u32[]{:S(2)}) collective-permute-start(f32[216,64]{0,1:T(8,128)S(1)} %get-tuple-element.12), channel_id=1, source_target_pairs={{0,4},{4,8},{8,12},{12,0},{1,5},{5,9},{9,13},{13,1},{2,6},{6,10},{... | collective-permute-start | bytes 165896 | tf_op jit(solution)/shard_map/ppermute | solution.py:40
  38.9 5.2 %collective-permute-start.6 = (f32[216,64]{0,1:T(8,128)S(1)}, f32[216,64]{0,1:T(8,128)S(1)}, u32[]{:S(2)}, u32[]{:S(2)}) collective-permute-start(f32[216,64]{0,1:T(8,128)S(1)} %get-tuple-element.11), channel_id=1, source_target_pairs={{0,12},{4,0},{8,4},{12,8},{1,13},{5,1},{9,5},{13,9},{2,14},{6,2},{... | collective-permute-start | bytes 165896 | tf_op jit(solution)/shard_map/ppermute | solution.py:40
  40.8 5.0 %collective-permute-start.10 = (f32[216,64]{0,1:T(8,128)S(1)}, f32[216,64]{0,1:T(8,128)S(1)}, u32[]{:S(2)}, u32[]{:S(2)}) collective-permute-start(f32[216,64]{0,1:T(8,128)S(1)} %get-tuple-element.14), channel_id=1, source_target_pairs={{0,12},{4,0},{8,4},{12,8},{1,13},{5,1},{9,5},{13,9},{2,14},{6,2},{... | collective-permute-start | bytes 165896 | tf_op jit(solution)/shard_map/ppermute | solution.py:40
  43.4 5.2 %collective-permute-start.8 = (f32[216,64]{0,1:T(8,128)S(1)}, f32[216,64]{0,1:T(8,128)S(1)}, u32[]{:S(2)}, u32[]{:S(2)}) collective-permute-start(f32[216,64]{0,1:T(8,128)S(1)} %get-tuple-element.13), channel_id=1, source_target_pairs={{0,8},{4,12},{8,0},{12,4},{1,9},{5,13},{9,1},{13,5},{2,10},{6,14},... | collective-permute-start | bytes 165896 | tf_op jit(solution)/shard_map/ppermute | solution.py:40
  43.8 6.1 %collective-permute-start.9 = (f32[216,64]{0,1:T(8,128)S(1)}, f32[216,64]{0,1:T(8,128)S(1)}, u32[]{:S(2)}, u32[]{:S(2)}) collective-permute-start(f32[216,64]{0,1:T(8,128)S(1)} %get-tuple-element.15), channel_id=1, source_target_pairs={{0,4},{4,8},{8,12},{12,0},{1,5},{5,9},{9,13},{13,1},{2,6},{6,10},{... | collective-permute-start | bytes 165896 | tf_op jit(solution)/shard_map/ppermute | solution.py:40

commit v19 on v17

--- a/solution.py
+++ b/solution.py
@@ -4,7 +4,8 @@
 from jax.sharding import PartitionSpec as P
 
 
-def with_halo(cells, sides, width):
+def halo_parts(cells, sides, width):
+    got = []
     for axis, dim in sides:
         count = lax.axis_size(axis)
         head = lax.slice_in_dim(cells, 0, width, axis=dim)
@@ -14,16 +15,26 @@
             high = jnp.zeros_like(head)
         elif count == 2:
             me = lax.axis_index(axis)
-            got = lax.ppermute(jnp.where(me == 0, tail, head), axis, [(0, 1), (1, 0)])
-            low = jnp.where(me == 1, got, jnp.zeros_like(got))
-            high = jnp.where(me == 0, got, jnp.zeros_like(got))
+            recv = lax.ppermute(jnp.where(me == 0, tail, head), axis, [(0, 1), (1, 0)])
+            low = jnp.where(me == 1, recv, jnp.zeros_like(recv))
+            high = jnp.where(me == 0, recv, jnp.zeros_like(recv))
         else:
             me = lax.axis_index(axis)
             low = lax.ppermute(tail, axis, [(i, (i + 1) % count) for i in range(count)])
             high = lax.ppermute(head, axis, [((i + 1) % count, i) for i in range(count)])
             low = jnp.where(me == 0, jnp.zeros_like(low), low)
             high = jnp.where(me == count - 1, jnp.zeros_like(high), high)
+        got.append((dim, low, high))
         cells = jnp.concatenate([low, cells, high], axis=dim)
+    return got
+
+
+def assemble(cells, got, lo, hi):
+    cells = lax.slice_in_dim(cells, lo, hi, axis=3)
+    for dim, low, high in got:
+        cells = jnp.concatenate(
+            [lax.slice_in_dim(low, lo, hi, axis=3), cells, lax.slice_in_dim(high, lo, hi, axis=3)], axis=dim
+        )
     return cells
 
 
@@ -58,7 +69,8 @@
     ncores = lax.axis_size("col")
     half = weight.shape[2] // ncores
     offset = lax.axis_index("col") * half
-    gh = with_halo(grad_out, (("gx", 0), ("gy", 1)), 1)
+    got = halo_parts(grad_out, (("gy", 1), ("gx", 0)), 1)
+    gh = assemble(grad_out, got, 0, chans)
     taps = weight.reshape(3, 3, 3, chans, weight.shape[2])
     kflip = jnp.transpose(taps[::-1, ::-1, ::-1], (0, 1, 2, 4, 3))
     pad = [(0, 0), (0, 0), (1, 1)]
@@ -68,7 +80,12 @@
         preferred_element_type=jnp.float32,
     )[0]
     grad_in = inner.astype(jnp.bfloat16)
-    gshare = lax.dynamic_slice_in_dim(gh, offset, half, 3)
+    if ncores == 1:
+        gshare = assemble(grad_out, got, 0, half)
+    else:
+        gshare = jnp.where(
+            lax.axis_index("col") == 0, assemble(grad_out, got, 0, half), assemble(grad_out, got, half, 2 * half)
+        )
     gdeep = jnp.pad(gshare, ((0, 0), (0, 0), (1, 1), (0, 0)))
     stack = jnp.concatenate([lax.slice_in_dim(gdeep, 2 - c, 2 - c + depth, axis=2) for c in range(3)], axis=3)
     pieces = []

time: 52 us -> 49.9 us (0.960)
  waiting for transfers between devices: 15.2 us -> 11.4 us
  starting transfers between devices: 16.4 us -> 17 us
  other arithmetic: 3.88 us -> 4.48 us
    ppermute x3, waiting for transfers between devices: 9.34 us -> 5.35 us  [the longest x1 4.23 us: halo_parts(): low = lax.ppermute(tail, axis, [(i, (i + 1) % count) for i in range(count)])]
    slice x1 -> x4, local copies, waits for them, and re-layouts: 1.09 us -> 1.86 us  [the longest x1 1.55 us: assemble(): cells = lax.slice_in_dim(cells, lo, hi, axis=3)]
    select_n x4 -> x5, other arithmetic: 0.84 us -> 1.45 us  [the longest x1 0.89 us: halo_parts(): recv = lax.ppermute(jnp.where(me == 0, tail, head), axis, [(0, 1), (1, 0)])]
    ppermute x3, starting transfers between devices: 6.66 us -> 7.19 us  [the longest x1 2.94 us: halo_parts(): recv = lax.ppermute(jnp.where(me == 0, tail, head), axis, [(0, 1), (1, 0)])]
  transfers between devices with their start and end apart: 11 -> 11, of which waited for: 8 -> 6; matrix products, arithmetic and copies ran while one was open for 14% -> 18% of each run, Pallas kernels for 0% -> 0%
where the time goes in v19:
time: 49.9 us; the launch traced here: 49.7 us
  starting transfers between devices  17 us (34%)
  waiting for transfers between devices  11.4 us (23%)
  matrix products  9.11 us (18%)
  local copies, waits for them, and re-layouts  6.47 us (13%)
  other arithmetic  4.48 us (9%)
  between operations  1.21 us (2%)
    ppermute x6, starting transfers between devices, scatter_sum(): lax.ppermute(part, axis, [(j, (j + shift) % count) for j in range(count)])  7.65 us
    ppermute x6, waiting for transfers between devices, scatter_sum(): lax.ppermute(part, axis, [(j, (j + shift) % count) for j in range(count)])  5.41 us
    conv_general_dilated x1, matrix products, on_device(): lax.conv_general_dilated(gh[None], kflip, (1, 1, 1), pad, dimension_numbe...  4.96 us
    ppermute x1, waiting for transfers between devices, halo_parts(): low = lax.ppermute(tail, axis, [(i, (i + 1) % count) for i in range(count)])  4.23 us
    dot_general x9, matrix products, on_device(): lax.dot_general(x_act, window, (((0, 1, 2), (0, 1, 2)), ((), ())), prefer...  4.15 us
    ppermute x1, starting transfers between devices, halo_parts(): recv = lax.ppermute(jnp.where(me == 0, tail, head), axis, [(0, 1), (1, 0)])  2.94 us
    ppermute x1, starting transfers between devices, halo_parts(): low = lax.ppermute(tail, axis, [(i, (i + 1) % count) for i in range(count)])  2.16 us
    ppermute x2, starting transfers between devices, on_device(): partial = keep + lax.ppermute(send, 'gy', [(0, 1), (1, 0)])  2.15 us
  transfers between devices with their start and end apart: 11, of which 6 were waited for; matrix products, arithmetic and copies ran while one was open for 18% of the time, Pallas kernels for 0%

profile of v19, /device:TPU:0, one launch (start us, length us, event | category | flops | bytes accessed | tf_op | source)
XLA Modules:
  0.0 49.7 jit_solution(587772630884628949)
XLA Ops:
  0.7 0.9 %slice_select_fusion.2 = bf16[4,1,32,128]{3,2,1,0:T(8,128)(2,1)S(1)} fusion(bf16[4,16,32,128]{3,2,1,0:T(8,128)(2,1)} %param.4, pred[]{:T(512)S(6)} %eq.29), kind=kLoop, calls=%fused_computation.58 | loop fusion | flops 16384 | bytes 98305 | tf_op jit(solution)/shard_map/jit(_where)/select_n | solution.py:18
  1.6 2.9 %collective-permute-start = (bf16[4,1,32,128]{3,2,1,0:T(8,128)(2,1)S(1)}, bf16[4,1,32,128]{3,2,1,0:T(8,128)(2,1)S(1)}, u32[]{:S(2)}, u32[]{:S(2)}) collective-permute-start(bf16[4,1,32,128]{3,2,1,0:T(8,128)(2,1)S(1)} %slice_select_fusion.2), channel_id=1, source_target_pairs={{0,2},{2,0},{1,3},{3,1},{4,6},{6,4},{5,7},{7,5},{8,10},{10,8},{9,1... | collective-permute-start | bytes 98312 | tf_op jit(solution)/shard_map/ppermute | solution.py:18
  4.5 1.5 %fusion.22 = (bf16[4,16,32,64]{3,2,1,0:T(8,128)(2,1)S(1)}, bf16[4,16,32,64]{3,2,1,0:T(8,128)(2,1)S(1)}) fusion(bf16[4,16,32,128]{3,2,1,0:T(8,128)(2,1)} %param.4), kind=kLoop, calls=%fused_computation.64 | loop fusion | bytes 1048576 | tf_op jit(solution)/shard_map/slice | solution.py:33
  6.1 0.3 collective-permute-done
  6.5 2.2 %collective-permute-start.1 = (bf16[1,18,32,128]{3,2,1,0:T(8,128)(2,1)S(1)}, bf16[1,18,32,128]{3,2,1,0:T(8,128)(2,1)S(1)}, u32[]{:S(2)}, u32[]{:S(2)}) collective-permute-start(bf16[1,18,32,128]{3,2,1,0:T(8,128)(2,1)S(1)} %get-tuple-element.8), channel_id=1, source_target_pairs={{0,4},{4,8},{8,12},{12,0},{1,5},{5,9},{9,13},{13,1},{2,6},{6,10},{... | collective-permute-start | bytes 442376 | tf_op jit(solution)/shard_map/ppermute | solution.py:23
  8.6 2.1 %collective-permute-start.2 = (bf16[1,18,32,128]{3,2,1,0:T(8,128)(2,1)S(1)}, bf16[1,18,32,128]{3,2,1,0:T(8,128)(2,1)S(1)}, u32[]{:S(2)}, u32[]{:S(2)}) collective-permute-start(bf16[1,18,32,128]{3,2,1,0:T(8,128)(2,1)S(1)} %get-tuple-element.9), channel_id=1, source_target_pairs={{4,0},{8,4},{12,8},{0,12},{5,1},{9,5},{13,9},{1,13},{6,2},{10,6},{... | collective-permute-start | bytes 442376 | tf_op jit(solution)/shard_map/ppermute | solution.py:24
  10.8 4.2 %collective-permute-done.1 = bf16[1,18,32,128]{3,2,1,0:T(8,128)(2,1)S(1)} collective-permute-done((bf16[1,18,32,128]{3,2,1,0:T(8,128)(2,1)S(1)}, bf16[1,18,32,128]{3,2,1,0:T(8,128)(2,1)S(1)}, u32[]{:S(2)}, u32[]{:S(2)}) %collective-permute-start.1) | collective-permute-done | bytes 147488 | tf_op jit(solution)/shard_map/ppermute | solution.py:23
  15.1 0.1 fusion.23
  15.2 0.8 %collective-permute-done.2 = bf16[1,18,32,128]{3,2,1,0:T(8,128)(2,1)S(1)} collective-permute-done((bf16[1,18,32,128]{3,2,1,0:T(8,128)(2,1)S(1)}, bf16[1,18,32,128]{3,2,1,0:T(8,128)(2,1)S(1)}, u32[]{:S(2)}, u32[]{:S(2)}) %collective-permute-start.2) | collective-permute-done | bytes 147488 | tf_op jit(solution)/shard_map/ppermute | solution.py:24
  16.0 0.1 fusion.24
  16.1 0.5 %maximum_select_fusion = bf16[6,18,32,64]{3,2,1,0:T(8,128)(2,1)S(1)} fusion(bf16[1,18,32,64]{3,2,1,0:T(8,128)(2,1)S(1)} %get-tuple-element.21, bf16[4,1,32,64]{3,2,1,0:T(8,128)(2,1)S(1)} %get-tuple-element.30, bf16[4,16,32,64]{3,2,1,0:T(8,128)(2,1)S(1)} %get-tuple-element.11, bf16[4,1,32,64]{3,2,1,0:T(8,128)(2,1)S(1)} %get-tuple-element.25, ...), kind=kLoop, calls=%fused_computation.14 | loop fusion | flops 1990656 | bytes 1327105 | tf_op jit(solution)/shard_map/jit(_where)/select_n | solution.py:86
  16.7 0.8 %pad_slice_fusion.1 = (bf16[6,18,32,64]{3,2,1,0:T(8,128)(2,1)S(1)}, bf16[6,18,32,64]{3,2,1,0:T(8,128)(2,1)S(1)}) fusion(bf16[6,18,32,64]{3,2,1,0:T(8,128)(2,1)S(1)} %maximum_select_fusion), kind=kLoop, calls=%fused_computation.12 | loop fusion | bytes 1327104 | tf_op jit(solution)/shard_map/slice | solution.py:90
  17.4 0.9 %pad_maximum_fusion = bf16[6,18,32,192]{3,2,1,0:T(8,128)(2,1)S(1)} fusion(bf16[6,18,32,64]{3,2,1,0:T(8,128)(2,1)S(1)} %get-tuple-element.7, bf16[6,18,32,64]{3,2,1,0:T(8,128)(2,1)S(1)} %maximum_select_fusion, bf16[6,18,32,64]{3,2,1,0:T(8,128)(2,1)S(1)} %get-tuple-element.6), kind=kLoop, calls=%fused_computation.2 | loop fusion | flops 3981312 | bytes 2654208 | tf_op jit(solution)/shard_map/concatenate | solution.py:90
  18.3 0.2 copy-done.2
  18.5 0.5 fusion.29
  18.9 0.5 fusion.28
  19.4 0.5 fusion.30
  19.9 0.5 fusion.31
  20.3 0.5 fusion.32
  20.8 0.5 fusion.33
  21.3 0.5 fusion.34
  21.7 0.5 fusion.35
  23.0 0.5 fusion.36
  23.5 0.2 maximum_bitcast_fusion
  24.5 0.1 maximum_bitcast_fusion.4
  24.8 0.1 maximum_bitcast_fusion.7
  24.9 0.1 maximum_bitcast_fusion.8
  25.2 1.5 %collective-permute-start.3 = (f32[4,216,64]{1,2,0:T(8,128)S(1)}, f32[4,216,64]{1,2,0:T(8,128)S(1)}, u32[]{:S(2)}, u32[]{:S(2)}) collective-permute-start(f32[4,216,64]{1,2,0:T(8,128)S(1)} %slice_select_fusion.1), channel_id=1, source_target_pairs={{0,2},{2,0},{1,3},{3,1},{4,6},{6,4},{5,7},{7,5},{8,10},{10,8},{9,1... | collective-permute-start | bytes 663560 | tf_op jit(solution)/shard_map/ppermute | solution.py:115
  26.6 0.4 copy.28
  27.0 0.2 pad.5.clone
  27.3 0.1 copy.7
  27.4 0.1 slice.179
  27.6 0.4 copy-done.3
  28.0 5.0 %fusion.11 = bf16[4,16,8,5,128]{4,2,3,1,0:T(8,128)(2,1)S(1)} fusion(bf16[3,3,3,128,128]{4,3,2,1,0:T(8,128)(2,1)S(1)} %bitcast.201, bf16[6,18,1,7,2,128]{5,3,4,1,0,2:T(8,128)(2,1)S(1)} %slice.179, bf16[6,18,1,8,5,128]{5,3,4,1,0,2:T(8,128)(2,1)S(1)} %copy.7, pred[8,5]{0,1:T(8,128)(4,1)S(1)} %copy-done.3), kind=kOutput, calls=%fused_computation.10 | convolution fusion | flops 2270224384 | bytes 3033128 | tf_op jit(solution)/shard_map/conv_general_dilated | solution.py:77
  32.9 0.1 copy.8
  33.0 0.2 select_add_fusion.1
  33.3 0.7 %collective-permute-start.7 = (f32[4,216,64]{1,2,0:T(8,128)S(1)}, f32[4,216,64]{1,2,0:T(8,128)S(1)}, u32[]{:S(2)}, u32[]{:S(2)}) collective-permute-start(f32[4,216,64]{1,2,0:T(8,128)S(1)} %get-tuple-element.5), channel_id=1, source_target_pairs={{0,2},{2,0},{1,3},{3,1},{4,6},{6,4},{5,7},{7,5},{8,10},{10,8},{9,1... | collective-permute-start | bytes 663560 | tf_op jit(solution)/shard_map/ppermute | solution.py:115
  34.0 0.9 %copy.18 = bf16[4,16,32,128]{3,2,1,0:T(8,128)(2,1)} copy(bf16[4,16,32,128]{3,1,2,0:T(8,128)(2,1)S(1)} %slice_bitcast_fusion) | data formatting | bytes 1048576
  34.9 1.4 %collective-permute-start.4 = (f32[216,64]{0,1:T(8,128)S(1)}, f32[216,64]{0,1:T(8,128)S(1)}, u32[]{:S(2)}, u32[]{:S(2)}) collective-permute-start(f32[216,64]{0,1:T(8,128)S(1)} %get-tuple-element.12), channel_id=1, source_target_pairs={{0,4},{4,8},{8,12},{12,0},{1,5},{5,9},{9,13},{13,1},{2,6},{6,10},{... | collective-permute-start | bytes 165896 | tf_op jit(solution)/shard_map/ppermute | solution.py:51
  36.3 2.1 %collective-permute-start.5 = (f32[216,64]{0,1:T(8,128)S(1)}, f32[216,64]{0,1:T(8,128)S(1)}, u32[]{:S(2)}, u32[]{:S(2)}) collective-permute-start(f32[216,64]{0,1:T(8,128)S(1)} %get-tuple-element.14), channel_id=1, source_target_pairs={{0,8},{4,12},{8,0},{12,4},{1,9},{5,13},{9,1},{13,5},{2,10},{6,14},... | collective-permute-start | bytes 165896 | tf_op jit(solution)/shard_map/ppermute | solution.py:51
  38.4 0.6 %collective-permute-start.6 = (f32[216,64]{0,1:T(8,128)S(1)}, f32[216,64]{0,1:T(8,128)S(1)}, u32[]{:S(2)}, u32[]{:S(2)}) collective-permute-start(f32[216,64]{0,1:T(8,128)S(1)} %get-tuple-element.13), channel_id=1, source_target_pairs={{0,12},{4,0},{8,4},{12,8},{1,13},{5,1},{9,5},{13,9},{2,14},{6,2},{... | collective-permute-start | bytes 165896 | tf_op jit(solution)/shard_map/ppermute | solution.py:51
  39.0 0.7 %collective-permute-done.7 = f32[4,216,64]{1,2,0:T(8,128)S(1)} collective-permute-done((f32[4,216,64]{1,2,0:T(8,128)S(1)}, f32[4,216,64]{1,2,0:T(8,128)S(1)}, u32[]{:S(2)}, u32[]{:S(2)}) %collective-permute-start.7) | collective-permute-done | bytes 221216 | tf_op jit(solution)/shard_map/ppermute | solution.py:115
  39.7 0.2 select_add_fusion
  39.9 2.9 %collective-permute-start.10 = (f32[216,64]{0,1:T(8,128)S(1)}, f32[216,64]{0,1:T(8,128)S(1)}, u32[]{:S(2)}, u32[]{:S(2)}) collective-permute-start(f32[216,64]{0,1:T(8,128)S(1)} %get-tuple-element.16), channel_id=1, source_target_pairs={{0,12},{4,0},{8,4},{12,8},{1,13},{5,1},{9,5},{13,9},{2,14},{6,2},{... | collective-permute-start | bytes 165896 | tf_op jit(solution)/shard_map/ppermute | solution.py:51
  42.9 0.6 %collective-permute-start.9 = (f32[216,64]{0,1:T(8,128)S(1)}, f32[216,64]{0,1:T(8,128)S(1)}, u32[]{:S(2)}, u32[]{:S(2)}) collective-permute-start(f32[216,64]{0,1:T(8,128)S(1)} %get-tuple-element.17), channel_id=1, source_target_pairs={{0,8},{4,12},{8,0},{12,4},{1,9},{5,13},{9,1},{13,5},{2,10},{6,14},... | collective-permute-start | bytes 165896 | tf_op jit(solution)/shard_map/ppermute | solution.py:51
  43.5 1.3 %collective-permute-done.10 = f32[216,64]{0,1:T(8,128)S(1)} collective-permute-done((f32[216,64]{0,1:T(8,128)S(1)}, f32[216,64]{0,1:T(8,128)S(1)}, u32[]{:S(2)}, u32[]{:S(2)}) %collective-permute-start.10) | collective-permute-done | bytes 55328 | tf_op jit(solution)/shard_map/ppermute | solution.py:51
  44.8 4.1 %collective-permute-done.8 = f32[216,64]{0,1:T(8,128)S(1)} collective-permute-done((f32[216,64]{0,1:T(8,128)S(1)}, f32[216,64]{0,1:T(8,128)S(1)}, u32[]{:S(2)}, u32[]{:S(2)}) %collective-permute-start.8) | collective-permute-done | bytes 55328 | tf_op jit(solution)/shard_map/ppermute | solution.py:51
  48.9 0.8 %maximum_multiply_fusion = f32[432,64]{0,1:T(8,128)} fusion(f32[216,64]{0,1:T(8,128)S(1)} %fusion.16, f32[216,64]{0,1:T(8,128)S(1)} %fusion.18), kind=kLoop, calls=%fused_computation.36 | loop fusion | flops 55296 | bytes 221184 | tf_op jit(solution)/shard_map/div | solution.py:123
  (59 shorter events, 2.1 us)
Async XLA Ops:
  0.6 26.9 %copy-start = (bf16[27,128,128]{2,1,0:T(8,128)(2,1)S(1)}, bf16[27,128,128]{2,1,0:T(8,128)(2,1)}, u32[]{:S(2)}) copy-start(bf16[27,128,128]{2,1,0:T(8,128)(2,1)} %param.5) | copy-start | bytes 2654212
  0.6 5.8 %copy-start.1 = (bf16[4,16,32,128]{3,2,1,0:T(8,128)(2,1)S(1)}, bf16[4,16,32,128]{3,2,1,0:T(8,128)(2,1)}, u32[]{:S(2)}) copy-start(bf16[4,16,32,128]{3,2,1,0:T(8,128)(2,1)} %param.4) | copy-start | bytes 1572868
  1.6 4.8 %collective-permute-start = (bf16[4,1,32,128]{3,2,1,0:T(8,128)(2,1)S(1)}, bf16[4,1,32,128]{3,2,1,0:T(8,128)(2,1)S(1)}, u32[]{:S(2)}, u32[]{:S(2)}) collective-permute-start(bf16[4,1,32,128]{3,2,1,0:T(8,128)(2,1)S(1)} %slice_select_fusion.2), channel_id=1, source_target_pairs={{0,2},{2,0},{1,3},{3,1},{4,6},{6,4},{5,7},{7,5},{8,10},{10,8},{9,1... | collective-permute-start | bytes 98312 | tf_op jit(solution)/shard_map/ppermute | solution.py:18
  6.5 8.6 %collective-permute-start.1 = (bf16[1,18,32,128]{3,2,1,0:T(8,128)(2,1)S(1)}, bf16[1,18,32,128]{3,2,1,0:T(8,128)(2,1)S(1)}, u32[]{:S(2)}, u32[]{:S(2)}) collective-permute-start(bf16[1,18,32,128]{3,2,1,0:T(8,128)(2,1)S(1)} %get-tuple-element.8), channel_id=1, source_target_pairs={{0,4},{4,8},{8,12},{12,0},{1,5},{5,9},{9,13},{13,1},{2,6},{6,10},{... | collective-permute-start | bytes 442376 | tf_op jit(solution)/shard_map/ppermute | solution.py:23
  8.6 7.4 %collective-permute-start.2 = (bf16[1,18,32,128]{3,2,1,0:T(8,128)(2,1)S(1)}, bf16[1,18,32,128]{3,2,1,0:T(8,128)(2,1)S(1)}, u32[]{:S(2)}, u32[]{:S(2)}) collective-permute-start(bf16[1,18,32,128]{3,2,1,0:T(8,128)(2,1)S(1)} %get-tuple-element.9), channel_id=1, source_target_pairs={{4,0},{8,4},{12,8},{0,12},{5,1},{9,5},{13,9},{1,13},{6,2},{10,6},{... | collective-permute-start | bytes 442376 | tf_op jit(solution)/shard_map/ppermute | solution.py:24
  17.4 1.0 %copy-start.2 = (bf16[4,16,32,128]{3,2,1,0:T(8,128)(2,1)S(1)}, bf16[4,16,32,128]{3,2,1,0:T(8,128)(2,1)}, u32[]{:S(2)}) copy-start(bf16[4,16,32,128]{3,2,1,0:T(8,128)(2,1)} %param.3) | copy-start | bytes 1572868
  25.2 7.9 %collective-permute-start.3 = (f32[4,216,64]{1,2,0:T(8,128)S(1)}, f32[4,216,64]{1,2,0:T(8,128)S(1)}, u32[]{:S(2)}, u32[]{:S(2)}) collective-permute-start(f32[4,216,64]{1,2,0:T(8,128)S(1)} %slice_select_fusion.1), channel_id=1, source_target_pairs={{0,2},{2,0},{1,3},{3,1},{4,6},{6,4},{5,7},{7,5},{8,10},{10,8},{9,1... | collective-permute-start | bytes 663560 | tf_op jit(solution)/shard_map/ppermute | solution.py:115
  27.3 0.7 %copy-start.3 = (pred[8,5]{0,1:T(8,128)(4,1)S(1)}, pred[8,5]{0,1:T(8,128)(4,1)}, u32[]{:S(2)}) copy-start(pred[8,5]{0,1:T(8,128)(4,1)} %constant.77) | copy-start | bytes 124
  33.3 6.4 %collective-permute-start.7 = (f32[4,216,64]{1,2,0:T(8,128)S(1)}, f32[4,216,64]{1,2,0:T(8,128)S(1)}, u32[]{:S(2)}, u32[]{:S(2)}) collective-permute-start(f32[4,216,64]{1,2,0:T(8,128)S(1)} %get-tuple-element.5), channel_id=1, source_target_pairs={{0,2},{2,0},{1,3},{3,1},{4,6},{6,4},{5,7},{7,5},{8,10},{10,8},{9,1... | collective-permute-start | bytes 663560 | tf_op jit(solution)/shard_map/ppermute | solution.py:115
  34.9 7.9 %collective-permute-start.4 = (f32[216,64]{0,1:T(8,128)S(1)}, f32[216,64]{0,1:T(8,128)S(1)}, u32[]{:S(2)}, u32[]{:S(2)}) collective-permute-start(f32[216,64]{0,1:T(8,128)S(1)} %get-tuple-element.12), channel_id=1, source_target_pairs={{0,4},{4,8},{8,12},{12,0},{1,5},{5,9},{9,13},{13,1},{2,6},{6,10},{... | collective-permute-start | bytes 165896 | tf_op jit(solution)/shard_map/ppermute | solution.py:51
  36.3 7.2 %collective-permute-start.5 = (f32[216,64]{0,1:T(8,128)S(1)}, f32[216,64]{0,1:T(8,128)S(1)}, u32[]{:S(2)}, u32[]{:S(2)}) collective-permute-start(f32[216,64]{0,1:T(8,128)S(1)} %get-tuple-element.14), channel_id=1, source_target_pairs={{0,8},{4,12},{8,0},{12,4},{1,9},{5,13},{9,1},{13,5},{2,10},{6,14},... | collective-permute-start | bytes 165896 | tf_op jit(solution)/shard_map/ppermute | solution.py:51
  38.4 5.1 %collective-permute-start.6 = (f32[216,64]{0,1:T(8,128)S(1)}, f32[216,64]{0,1:T(8,128)S(1)}, u32[]{:S(2)}, u32[]{:S(2)}) collective-permute-start(f32[216,64]{0,1:T(8,128)S(1)} %get-tuple-element.13), channel_id=1, source_target_pairs={{0,12},{4,0},{8,4},{12,8},{1,13},{5,1},{9,5},{13,9},{2,14},{6,2},{... | collective-permute-start | bytes 165896 | tf_op jit(solution)/shard_map/ppermute | solution.py:51
  39.9 4.9 %collective-permute-start.10 = (f32[216,64]{0,1:T(8,128)S(1)}, f32[216,64]{0,1:T(8,128)S(1)}, u32[]{:S(2)}, u32[]{:S(2)}) collective-permute-start(f32[216,64]{0,1:T(8,128)S(1)} %get-tuple-element.16), channel_id=1, source_target_pairs={{0,12},{4,0},{8,4},{12,8},{1,13},{5,1},{9,5},{13,9},{2,14},{6,2},{... | collective-permute-start | bytes 165896 | tf_op jit(solution)/shard_map/ppermute | solution.py:51
  42.8 6.1 %collective-permute-start.8 = (f32[216,64]{0,1:T(8,128)S(1)}, f32[216,64]{0,1:T(8,128)S(1)}, u32[]{:S(2)}, u32[]{:S(2)}) collective-permute-start(f32[216,64]{0,1:T(8,128)S(1)} %get-tuple-element.15), channel_id=1, source_target_pairs={{0,4},{4,8},{8,12},{12,0},{1,5},{5,9},{9,13},{13,1},{2,6},{6,10},{... | collective-permute-start | bytes 165896 | tf_op jit(solution)/shard_map/ppermute | solution.py:51
  42.9 6.1 %collective-permute-start.9 = (f32[216,64]{0,1:T(8,128)S(1)}, f32[216,64]{0,1:T(8,128)S(1)}, u32[]{:S(2)}, u32[]{:S(2)}) collective-permute-start(f32[216,64]{0,1:T(8,128)S(1)} %get-tuple-element.17), channel_id=1, source_target_pairs={{0,8},{4,12},{8,0},{12,4},{1,9},{5,13},{9,1},{13,5},{2,10},{6,14},... | collective-permute-start | bytes 165896 | tf_op jit(solution)/shard_map/ppermute | solution.py:51

commit v20 on v19

--- a/solution.py
+++ b/solution.py
@@ -15,7 +15,8 @@
             high = jnp.zeros_like(head)
         elif count == 2:
             me = lax.axis_index(axis)
-            recv = lax.ppermute(jnp.where(me == 0, tail, head), axis, [(0, 1), (1, 0)])
+            edge = lax.dynamic_slice_in_dim(cells, (1 - me) * (cells.shape[dim] - width), width, axis=dim)
+            recv = lax.ppermute(edge, axis, [(0, 1), (1, 0)])
             low = jnp.where(me == 1, recv, jnp.zeros_like(recv))
             high = jnp.where(me == 0, recv, jnp.zeros_like(recv))
         else:

time: 49.9 us -> 49.9 us (level)
  other arithmetic: 4.48 us -> 3.59 us
  local copies, waits for them, and re-layouts: 6.47 us -> 7.34 us
    select_n x1 -> x0, other arithmetic: 0.89 us -> none  [halo_parts(): recv = lax.ppermute(jnp.where(me == 0, tail, head), axis, [(0, 1), (1, 0)])]
    dynamic_slice x0 -> x1, local copies, waits for them, and re-layouts: none -> 0.87 us  [halo_parts(): lax.dynamic_slice_in_dim(cells, (1 - me) * (cells.shape[dim] - width), wi...]
where the time goes in v20:
time: 49.9 us; the launch traced here: 49.7 us
  starting transfers between devices  17 us (34%)
  waiting for transfers between devices  11.4 us (23%)
  matrix products  9.1 us (18%)
  local copies, waits for them, and re-layouts  7.34 us (15%)
  other arithmetic  3.59 us (7%)
  between operations  1.21 us (2%)
    ppermute x6, starting transfers between devices, scatter_sum(): lax.ppermute(part, axis, [(j, (j + shift) % count) for j in range(count)])  7.62 us
    ppermute x6, waiting for transfers between devices, scatter_sum(): lax.ppermute(part, axis, [(j, (j + shift) % count) for j in range(count)])  5.41 us
    conv_general_dilated x1, matrix products, on_device(): lax.conv_general_dilated(gh[None], kflip, (1, 1, 1), pad, dimension_numbe...  4.95 us
    ppermute x1, waiting for transfers between devices, halo_parts(): low = lax.ppermute(tail, axis, [(i, (i + 1) % count) for i in range(count)])  4.24 us
    dot_general x9, matrix products, on_device(): lax.dot_general(x_act, window, (((0, 1, 2), (0, 1, 2)), ((), ())), prefer...  4.15 us
    ppermute x1, starting transfers between devices, halo_parts(): recv = lax.ppermute(edge, axis, [(0, 1), (1, 0)])  2.94 us
    ppermute x2, starting transfers between devices, on_device(): partial = keep + lax.ppermute(send, 'gy', [(0, 1), (1, 0)])  2.17 us
    ppermute x1, starting transfers between devices, halo_parts(): low = lax.ppermute(tail, axis, [(i, (i + 1) % count) for i in range(count)])  2.16 us
  transfers between devices with their start and end apart: 11, of which 6 were waited for; matrix products, arithmetic and copies ran while one was open for 18% of the time, Pallas kernels for 0%

profile of v20, /device:TPU:0, one launch (start us, length us, event | category | flops | bytes accessed | tf_op | source)
XLA Modules:
  0.0 49.7 jit_solution(17480441066851999571)
XLA Ops:
  0.7 0.9 %constant_dynamic-slice_fusion = bf16[4,1,32,128]{3,2,1,0:T(8,128)(2,1)S(1)} fusion(bf16[4,16,32,128]{3,2,1,0:T(8,128)(2,1)} %param.4, s32[]{:T(128)S(6)} %select_n.99), kind=kLoop, calls=%fused_computation.60 | loop fusion | bytes 65540 | tf_op jit(solution)/shard_map/dynamic_slice | solution.py:18
  1.5 2.9 %collective-permute-start = (bf16[4,1,32,128]{3,2,1,0:T(8,128)(2,1)S(1)}, bf16[4,1,32,128]{3,2,1,0:T(8,128)(2,1)S(1)}, u32[]{:S(2)}, u32[]{:S(2)}) collective-permute-start(bf16[4,1,32,128]{3,2,1,0:T(8,128)(2,1)S(1)} %constant_dynamic-slice_fusion), channel_id=1, source_target_pairs={{0,2},{2,0},{1,3},{3,1},{4,6},{6,4},{5,7},{7,5},{8,10},{10,8},{9,1... | collective-permute-start | bytes 98312 | tf_op jit(solution)/shard_map/ppermute | solution.py:19
  4.5 1.5 %fusion.22 = (bf16[4,16,32,64]{3,2,1,0:T(8,128)(2,1)S(1)}, bf16[4,16,32,64]{3,2,1,0:T(8,128)(2,1)S(1)}) fusion(bf16[4,16,32,128]{3,2,1,0:T(8,128)(2,1)} %param.4), kind=kLoop, calls=%fused_computation.64 | loop fusion | bytes 1048576 | tf_op jit(solution)/shard_map/slice | solution.py:34
  6.1 0.3 collective-permute-done
  6.4 2.2 %collective-permute-start.1 = (bf16[1,18,32,128]{3,2,1,0:T(8,128)(2,1)S(1)}, bf16[1,18,32,128]{3,2,1,0:T(8,128)(2,1)S(1)}, u32[]{:S(2)}, u32[]{:S(2)}) collective-permute-start(bf16[1,18,32,128]{3,2,1,0:T(8,128)(2,1)S(1)} %get-tuple-element.8), channel_id=1, source_target_pairs={{0,4},{4,8},{8,12},{12,0},{1,5},{5,9},{9,13},{13,1},{2,6},{6,10},{... | collective-permute-start | bytes 442376 | tf_op jit(solution)/shard_map/ppermute | solution.py:24
  8.6 2.1 %collective-permute-start.2 = (bf16[1,18,32,128]{3,2,1,0:T(8,128)(2,1)S(1)}, bf16[1,18,32,128]{3,2,1,0:T(8,128)(2,1)S(1)}, u32[]{:S(2)}, u32[]{:S(2)}) collective-permute-start(bf16[1,18,32,128]{3,2,1,0:T(8,128)(2,1)S(1)} %get-tuple-element.9), channel_id=1, source_target_pairs={{4,0},{8,4},{12,8},{0,12},{5,1},{9,5},{13,9},{1,13},{6,2},{10,6},{... | collective-permute-start | bytes 442376 | tf_op jit(solution)/shard_map/ppermute | solution.py:25
  10.8 4.2 %collective-permute-done.1 = bf16[1,18,32,128]{3,2,1,0:T(8,128)(2,1)S(1)} collective-permute-done((bf16[1,18,32,128]{3,2,1,0:T(8,128)(2,1)S(1)}, bf16[1,18,32,128]{3,2,1,0:T(8,128)(2,1)S(1)}, u32[]{:S(2)}, u32[]{:S(2)}) %collective-permute-start.1) | collective-permute-done | bytes 147488 | tf_op jit(solution)/shard_map/ppermute | solution.py:24
  15.0 0.1 fusion.23
  15.2 0.8 %collective-permute-done.2 = bf16[1,18,32,128]{3,2,1,0:T(8,128)(2,1)S(1)} collective-permute-done((bf16[1,18,32,128]{3,2,1,0:T(8,128)(2,1)S(1)}, bf16[1,18,32,128]{3,2,1,0:T(8,128)(2,1)S(1)}, u32[]{:S(2)}, u32[]{:S(2)}) %collective-permute-start.2) | collective-permute-done | bytes 147488 | tf_op jit(solution)/shard_map/ppermute | solution.py:25
  16.0 0.1 fusion.24
  16.1 0.5 %maximum_select_fusion = bf16[6,18,32,64]{3,2,1,0:T(8,128)(2,1)S(1)} fusion(bf16[1,18,32,64]{3,2,1,0:T(8,128)(2,1)S(1)} %get-tuple-element.21, bf16[4,1,32,64]{3,2,1,0:T(8,128)(2,1)S(1)} %get-tuple-element.30, bf16[4,16,32,64]{3,2,1,0:T(8,128)(2,1)S(1)} %get-tuple-element.11, bf16[4,1,32,64]{3,2,1,0:T(8,128)(2,1)S(1)} %get-tuple-element.25, ...), kind=kLoop, calls=%fused_computation.14 | loop fusion | flops 1990656 | bytes 1327105 | tf_op jit(solution)/shard_map/jit(_where)/select_n | solution.py:87
  16.7 0.8 %pad_slice_fusion.1 = (bf16[6,18,32,64]{3,2,1,0:T(8,128)(2,1)S(1)}, bf16[6,18,32,64]{3,2,1,0:T(8,128)(2,1)S(1)}) fusion(bf16[6,18,32,64]{3,2,1,0:T(8,128)(2,1)S(1)} %maximum_select_fusion), kind=kLoop, calls=%fused_computation.12 | loop fusion | bytes 1327104 | tf_op jit(solution)/shard_map/slice | solution.py:91
  17.4 0.9 %pad_maximum_fusion = bf16[6,18,32,192]{3,2,1,0:T(8,128)(2,1)S(1)} fusion(bf16[6,18,32,64]{3,2,1,0:T(8,128)(2,1)S(1)} %get-tuple-element.7, bf16[6,18,32,64]{3,2,1,0:T(8,128)(2,1)S(1)} %maximum_select_fusion, bf16[6,18,32,64]{3,2,1,0:T(8,128)(2,1)S(1)} %get-tuple-element.6), kind=kLoop, calls=%fused_computation.2 | loop fusion | flops 3981312 | bytes 2654208 | tf_op jit(solution)/shard_map/concatenate | solution.py:91
  18.3 0.2 copy-done.2
  18.5 0.5 fusion.29
  18.9 0.5 fusion.28
  19.4 0.5 fusion.30
  19.9 0.5 fusion.31
  20.3 0.5 fusion.32
  20.8 0.5 fusion.33
  21.3 0.5 fusion.34
  21.7 0.5 fusion.35
  23.0 0.5 fusion.36
  23.4 0.2 maximum_bitcast_fusion
  24.5 0.1 maximum_bitcast_fusion.4
  24.8 0.1 maximum_bitcast_fusion.7
  24.9 0.1 maximum_bitcast_fusion.8
  25.1 1.5 %collective-permute-start.3 = (f32[4,216,64]{1,2,0:T(8,128)S(1)}, f32[4,216,64]{1,2,0:T(8,128)S(1)}, u32[]{:S(2)}, u32[]{:S(2)}) collective-permute-start(f32[4,216,64]{1,2,0:T(8,128)S(1)} %slice_select_fusion.1), channel_id=1, source_target_pairs={{0,2},{2,0},{1,3},{3,1},{4,6},{6,4},{5,7},{7,5},{8,10},{10,8},{9,1... | collective-permute-start | bytes 663560 | tf_op jit(solution)/shard_map/ppermute | solution.py:116
  26.6 0.4 copy.28
  27.0 0.2 pad.5.clone
  27.3 0.1 copy.7
  27.4 0.1 slice.171
  27.6 0.4 copy-done.3
  27.9 5.0 %fusion.11 = bf16[4,16,8,5,128]{4,2,3,1,0:T(8,128)(2,1)S(1)} fusion(bf16[3,3,3,128,128]{4,3,2,1,0:T(8,128)(2,1)S(1)} %bitcast.201, bf16[6,18,1,7,2,128]{5,3,4,1,0,2:T(8,128)(2,1)S(1)} %slice.171, bf16[6,18,1,8,5,128]{5,3,4,1,0,2:T(8,128)(2,1)S(1)} %copy.7, pred[8,5]{0,1:T(8,128)(4,1)S(1)} %copy-done.3), kind=kOutput, calls=%fused_computation.10 | convolution fusion | flops 2270224384 | bytes 3033128 | tf_op jit(solution)/shard_map/conv_general_dilated | solution.py:78
  32.9 0.1 copy.8
  33.0 0.2 select_add_fusion.1
  33.2 0.7 %collective-permute-start.7 = (f32[4,216,64]{1,2,0:T(8,128)S(1)}, f32[4,216,64]{1,2,0:T(8,128)S(1)}, u32[]{:S(2)}, u32[]{:S(2)}) collective-permute-start(f32[4,216,64]{1,2,0:T(8,128)S(1)} %get-tuple-element.5), channel_id=1, source_target_pairs={{0,2},{2,0},{1,3},{3,1},{4,6},{6,4},{5,7},{7,5},{8,10},{10,8},{9,1... | collective-permute-start | bytes 663560 | tf_op jit(solution)/shard_map/ppermute | solution.py:116
  34.0 0.9 %copy.18 = bf16[4,16,32,128]{3,2,1,0:T(8,128)(2,1)} copy(bf16[4,16,32,128]{3,1,2,0:T(8,128)(2,1)S(1)} %slice_bitcast_fusion) | data formatting | bytes 1048576
  34.9 1.4 %collective-permute-start.4 = (f32[216,64]{0,1:T(8,128)S(1)}, f32[216,64]{0,1:T(8,128)S(1)}, u32[]{:S(2)}, u32[]{:S(2)}) collective-permute-start(f32[216,64]{0,1:T(8,128)S(1)} %get-tuple-element.12), channel_id=1, source_target_pairs={{0,4},{4,8},{8,12},{12,0},{1,5},{5,9},{9,13},{13,1},{2,6},{6,10},{... | collective-permute-start | bytes 165896 | tf_op jit(solution)/shard_map/ppermute | solution.py:52
  36.3 2.1 %collective-permute-start.5 = (f32[216,64]{0,1:T(8,128)S(1)}, f32[216,64]{0,1:T(8,128)S(1)}, u32[]{:S(2)}, u32[]{:S(2)}) collective-permute-start(f32[216,64]{0,1:T(8,128)S(1)} %get-tuple-element.14), channel_id=1, source_target_pairs={{0,8},{4,12},{8,0},{12,4},{1,9},{5,13},{9,1},{13,5},{2,10},{6,14},... | collective-permute-start | bytes 165896 | tf_op jit(solution)/shard_map/ppermute | solution.py:52
  38.4 0.6 %collective-permute-start.6 = (f32[216,64]{0,1:T(8,128)S(1)}, f32[216,64]{0,1:T(8,128)S(1)}, u32[]{:S(2)}, u32[]{:S(2)}) collective-permute-start(f32[216,64]{0,1:T(8,128)S(1)} %get-tuple-element.13), channel_id=1, source_target_pairs={{0,12},{4,0},{8,4},{12,8},{1,13},{5,1},{9,5},{13,9},{2,14},{6,2},{... | collective-permute-start | bytes 165896 | tf_op jit(solution)/shard_map/ppermute | solution.py:52
  39.0 0.7 %collective-permute-done.7 = f32[4,216,64]{1,2,0:T(8,128)S(1)} collective-permute-done((f32[4,216,64]{1,2,0:T(8,128)S(1)}, f32[4,216,64]{1,2,0:T(8,128)S(1)}, u32[]{:S(2)}, u32[]{:S(2)}) %collective-permute-start.7) | collective-permute-done | bytes 221216 | tf_op jit(solution)/shard_map/ppermute | solution.py:116
  39.7 0.2 select_add_fusion
  39.9 2.9 %collective-permute-start.10 = (f32[216,64]{0,1:T(8,128)S(1)}, f32[216,64]{0,1:T(8,128)S(1)}, u32[]{:S(2)}, u32[]{:S(2)}) collective-permute-start(f32[216,64]{0,1:T(8,128)S(1)} %get-tuple-element.16), channel_id=1, source_target_pairs={{0,12},{4,0},{8,4},{12,8},{1,13},{5,1},{9,5},{13,9},{2,14},{6,2},{... | collective-permute-start | bytes 165896 | tf_op jit(solution)/shard_map/ppermute | solution.py:52
  42.8 0.6 %collective-permute-start.9 = (f32[216,64]{0,1:T(8,128)S(1)}, f32[216,64]{0,1:T(8,128)S(1)}, u32[]{:S(2)}, u32[]{:S(2)}) collective-permute-start(f32[216,64]{0,1:T(8,128)S(1)} %get-tuple-element.17), channel_id=1, source_target_pairs={{0,8},{4,12},{8,0},{12,4},{1,9},{5,13},{9,1},{13,5},{2,10},{6,14},... | collective-permute-start | bytes 165896 | tf_op jit(solution)/shard_map/ppermute | solution.py:52
  43.5 1.3 %collective-permute-done.10 = f32[216,64]{0,1:T(8,128)S(1)} collective-permute-done((f32[216,64]{0,1:T(8,128)S(1)}, f32[216,64]{0,1:T(8,128)S(1)}, u32[]{:S(2)}, u32[]{:S(2)}) %collective-permute-start.10) | collective-permute-done | bytes 55328 | tf_op jit(solution)/shard_map/ppermute | solution.py:52
  44.8 4.1 %collective-permute-done.8 = f32[216,64]{0,1:T(8,128)S(1)} collective-permute-done((f32[216,64]{0,1:T(8,128)S(1)}, f32[216,64]{0,1:T(8,128)S(1)}, u32[]{:S(2)}, u32[]{:S(2)}) %collective-permute-start.8) | collective-permute-done | bytes 55328 | tf_op jit(solution)/shard_map/ppermute | solution.py:52
  48.9 0.8 %maximum_multiply_fusion = f32[432,64]{0,1:T(8,128)} fusion(f32[216,64]{0,1:T(8,128)S(1)} %fusion.16, f32[216,64]{0,1:T(8,128)S(1)} %fusion.18), kind=kLoop, calls=%fused_computation.36 | loop fusion | flops 55296 | bytes 221184 | tf_op jit(solution)/shard_map/div | solution.py:124
  (59 shorter events, 2.1 us)
Async XLA Ops:
  0.6 26.9 %copy-start = (bf16[27,128,128]{2,1,0:T(8,128)(2,1)S(1)}, bf16[27,128,128]{2,1,0:T(8,128)(2,1)}, u32[]{:S(2)}) copy-start(bf16[27,128,128]{2,1,0:T(8,128)(2,1)} %param.5) | copy-start | bytes 2654212
  0.6 5.7 %copy-start.1 = (bf16[4,16,32,128]{3,2,1,0:T(8,128)(2,1)S(1)}, bf16[4,16,32,128]{3,2,1,0:T(8,128)(2,1)}, u32[]{:S(2)}) copy-start(bf16[4,16,32,128]{3,2,1,0:T(8,128)(2,1)} %param.4) | copy-start | bytes 1572868
  1.5 4.8 %collective-permute-start = (bf16[4,1,32,128]{3,2,1,0:T(8,128)(2,1)S(1)}, bf16[4,1,32,128]{3,2,1,0:T(8,128)(2,1)S(1)}, u32[]{:S(2)}, u32[]{:S(2)}) collective-permute-start(bf16[4,1,32,128]{3,2,1,0:T(8,128)(2,1)S(1)} %constant_dynamic-slice_fusion), channel_id=1, source_target_pairs={{0,2},{2,0},{1,3},{3,1},{4,6},{6,4},{5,7},{7,5},{8,10},{10,8},{9,1... | collective-permute-start | bytes 98312 | tf_op jit(solution)/shard_map/ppermute | solution.py:19
  6.4 8.6 %collective-permute-start.1 = (bf16[1,18,32,128]{3,2,1,0:T(8,128)(2,1)S(1)}, bf16[1,18,32,128]{3,2,1,0:T(8,128)(2,1)S(1)}, u32[]{:S(2)}, u32[]{:S(2)}) collective-permute-start(bf16[1,18,32,128]{3,2,1,0:T(8,128)(2,1)S(1)} %get-tuple-element.8), channel_id=1, source_target_pairs={{0,4},{4,8},{8,12},{12,0},{1,5},{5,9},{9,13},{13,1},{2,6},{6,10},{... | collective-permute-start | bytes 442376 | tf_op jit(solution)/shard_map/ppermute | solution.py:24
  8.6 7.4 %collective-permute-start.2 = (bf16[1,18,32,128]{3,2,1,0:T(8,128)(2,1)S(1)}, bf16[1,18,32,128]{3,2,1,0:T(8,128)(2,1)S(1)}, u32[]{:S(2)}, u32[]{:S(2)}) collective-permute-start(bf16[1,18,32,128]{3,2,1,0:T(8,128)(2,1)S(1)} %get-tuple-element.9), channel_id=1, source_target_pairs={{4,0},{8,4},{12,8},{0,12},{5,1},{9,5},{13,9},{1,13},{6,2},{10,6},{... | collective-permute-start | bytes 442376 | tf_op jit(solution)/shard_map/ppermute | solution.py:25
  17.4 1.0 %copy-start.2 = (bf16[4,16,32,128]{3,2,1,0:T(8,128)(2,1)S(1)}, bf16[4,16,32,128]{3,2,1,0:T(8,128)(2,1)}, u32[]{:S(2)}) copy-start(bf16[4,16,32,128]{3,2,1,0:T(8,128)(2,1)} %param.3) | copy-start | bytes 1572868
  25.1 7.9 %collective-permute-start.3 = (f32[4,216,64]{1,2,0:T(8,128)S(1)}, f32[4,216,64]{1,2,0:T(8,128)S(1)}, u32[]{:S(2)}, u32[]{:S(2)}) collective-permute-start(f32[4,216,64]{1,2,0:T(8,128)S(1)} %slice_select_fusion.1), channel_id=1, source_target_pairs={{0,2},{2,0},{1,3},{3,1},{4,6},{6,4},{5,7},{7,5},{8,10},{10,8},{9,1... | collective-permute-start | bytes 663560 | tf_op jit(solution)/shard_map/ppermute | solution.py:116
  27.3 0.7 %copy-start.3 = (pred[8,5]{0,1:T(8,128)(4,1)S(1)}, pred[8,5]{0,1:T(8,128)(4,1)}, u32[]{:S(2)}) copy-start(pred[8,5]{0,1:T(8,128)(4,1)} %constant.81) | copy-start | bytes 124
  33.2 6.4 %collective-permute-start.7 = (f32[4,216,64]{1,2,0:T(8,128)S(1)}, f32[4,216,64]{1,2,0:T(8,128)S(1)}, u32[]{:S(2)}, u32[]{:S(2)}) collective-permute-start(f32[4,216,64]{1,2,0:T(8,128)S(1)} %get-tuple-element.5), channel_id=1, source_target_pairs={{0,2},{2,0},{1,3},{3,1},{4,6},{6,4},{5,7},{7,5},{8,10},{10,8},{9,1... | collective-permute-start | bytes 663560 | tf_op jit(solution)/shard_map/ppermute | solution.py:116
  34.9 7.9 %collective-permute-start.4 = (f32[216,64]{0,1:T(8,128)S(1)}, f32[216,64]{0,1:T(8,128)S(1)}, u32[]{:S(2)}, u32[]{:S(2)}) collective-permute-start(f32[216,64]{0,1:T(8,128)S(1)} %get-tuple-element.12), channel_id=1, source_target_pairs={{0,4},{4,8},{8,12},{12,0},{1,5},{5,9},{9,13},{13,1},{2,6},{6,10},{... | collective-permute-start | bytes 165896 | tf_op jit(solution)/shard_map/ppermute | solution.py:52
  36.3 7.2 %collective-permute-start.5 = (f32[216,64]{0,1:T(8,128)S(1)}, f32[216,64]{0,1:T(8,128)S(1)}, u32[]{:S(2)}, u32[]{:S(2)}) collective-permute-start(f32[216,64]{0,1:T(8,128)S(1)} %get-tuple-element.14), channel_id=1, source_target_pairs={{0,8},{4,12},{8,0},{12,4},{1,9},{5,13},{9,1},{13,5},{2,10},{6,14},... | collective-permute-start | bytes 165896 | tf_op jit(solution)/shard_map/ppermute | solution.py:52
  38.4 5.1 %collective-permute-start.6 = (f32[216,64]{0,1:T(8,128)S(1)}, f32[216,64]{0,1:T(8,128)S(1)}, u32[]{:S(2)}, u32[]{:S(2)}) collective-permute-start(f32[216,64]{0,1:T(8,128)S(1)} %get-tuple-element.13), channel_id=1, source_target_pairs={{0,12},{4,0},{8,4},{12,8},{1,13},{5,1},{9,5},{13,9},{2,14},{6,2},{... | collective-permute-start | bytes 165896 | tf_op jit(solution)/shard_map/ppermute | solution.py:52
  39.9 4.9 %collective-permute-start.10 = (f32[216,64]{0,1:T(8,128)S(1)}, f32[216,64]{0,1:T(8,128)S(1)}, u32[]{:S(2)}, u32[]{:S(2)}) collective-permute-start(f32[216,64]{0,1:T(8,128)S(1)} %get-tuple-element.16), channel_id=1, source_target_pairs={{0,12},{4,0},{8,4},{12,8},{1,13},{5,1},{9,5},{13,9},{2,14},{6,2},{... | collective-permute-start | bytes 165896 | tf_op jit(solution)/shard_map/ppermute | solution.py:52
  42.8 6.1 %collective-permute-start.8 = (f32[216,64]{0,1:T(8,128)S(1)}, f32[216,64]{0,1:T(8,128)S(1)}, u32[]{:S(2)}, u32[]{:S(2)}) collective-permute-start(f32[216,64]{0,1:T(8,128)S(1)} %get-tuple-element.15), channel_id=1, source_target_pairs={{0,4},{4,8},{8,12},{12,0},{1,5},{5,9},{9,13},{13,1},{2,6},{6,10},{... | collective-permute-start | bytes 165896 | tf_op jit(solution)/shard_map/ppermute | solution.py:52
  42.8 6.1 %collective-permute-start.9 = (f32[216,64]{0,1:T(8,128)S(1)}, f32[216,64]{0,1:T(8,128)S(1)}, u32[]{:S(2)}, u32[]{:S(2)}) collective-permute-start(f32[216,64]{0,1:T(8,128)S(1)} %get-tuple-element.17), channel_id=1, source_target_pairs={{0,8},{4,12},{8,0},{12,4},{1,9},{5,13},{9,1},{13,5},{2,10},{6,14},... | collective-permute-start | bytes 165896 | tf_op jit(solution)/shard_map/ppermute | solution.py:52

commit v21 on v19

--- a/solution.py
+++ b/solution.py
@@ -113,7 +113,9 @@
             keep = jnp.where(iy == 0, side[0][:, lo:hi], side[1][:, lo:hi])
             send = jnp.where(iy == 0, side[1][:, lo:hi], side[0][:, lo:hi])
             partial = keep + lax.ppermute(send, "gy", [(0, 1), (1, 0)])
+            last = partial
             parts.append(scatter_sum(partial, "gx", 0))
+        grad_in = lax.optimization_barrier((grad_in, last))[0]
         owned = jnp.concatenate(parts, axis=0) if len(parts) > 1 else parts[0]
     else:
         weight_terms = jnp.concatenate(pieces, axis=0)

time: 49.9 us -> 49.9 us (level)
    ppermute x6, waiting for transfers between devices: 5.41 us -> 4.48 us  [scatter_sum(): lax.ppermute(part, axis, [(j, (j + shift) % count) for j in range(count)])]
    ppermute x2, waiting for transfers between devices: 0.67 us -> 1.59 us  [on_device(): partial = keep + lax.ppermute(send, 'gy', [(0, 1), (1, 0)])]
where the time goes in v21:
time: 49.9 us; the launch traced here: 49.7 us
  starting transfers between devices  17 us (34%)
  waiting for transfers between devices  11.4 us (23%)
  matrix products  9.11 us (18%)
  local copies, waits for them, and re-layouts  6.48 us (13%)
  other arithmetic  4.48 us (9%)
  between operations  1.21 us (2%)
    ppermute x6, starting transfers between devices, scatter_sum(): lax.ppermute(part, axis, [(j, (j + shift) % count) for j in range(count)])  7.65 us
    conv_general_dilated x1, matrix products, on_device(): lax.conv_general_dilated(gh[None], kflip, (1, 1, 1), pad, dimension_numbe...  4.96 us
    ppermute x6, waiting for transfers between devices, scatter_sum(): lax.ppermute(part, axis, [(j, (j + shift) % count) for j in range(count)])  4.48 us
    ppermute x1, waiting for transfers between devices, halo_parts(): low = lax.ppermute(tail, axis, [(i, (i + 1) % count) for i in range(count)])  4.23 us
    dot_general x9, matrix products, on_device(): lax.dot_general(x_act, window, (((0, 1, 2), (0, 1, 2)), ((), ())), prefer...  4.15 us
    ppermute x1, starting transfers between devices, halo_parts(): recv = lax.ppermute(jnp.where(me == 0, tail, head), axis, [(0, 1), (1, 0)])  2.94 us
    ppermute x1, starting transfers between devices, halo_parts(): low = lax.ppermute(tail, axis, [(i, (i + 1) % count) for i in range(count)])  2.16 us
    ppermute x2, starting transfers between devices, on_device(): partial = keep + lax.ppermute(send, 'gy', [(0, 1), (1, 0)])  2.15 us
  transfers between devices with their start and end apart: 11, of which 6 were waited for; matrix products, arithmetic and copies ran while one was open for 18% of the time, Pallas kernels for 0%

profile of v21, /device:TPU:0, one launch (start us, length us, event | category | flops | bytes accessed | tf_op | source)
XLA Modules:
  0.0 49.7 jit_solution(5546233201719026958)
XLA Ops:
  0.7 0.9 %slice_select_fusion.2 = bf16[4,1,32,128]{3,2,1,0:T(8,128)(2,1)S(1)} fusion(bf16[4,16,32,128]{3,2,1,0:T(8,128)(2,1)} %param.4, pred[]{:T(512)S(6)} %eq.29), kind=kLoop, calls=%fused_computation.58 | loop fusion | flops 16384 | bytes 98305 | tf_op jit(solution)/shard_map/jit(_where)/select_n | solution.py:18
  1.6 2.9 %collective-permute-start = (bf16[4,1,32,128]{3,2,1,0:T(8,128)(2,1)S(1)}, bf16[4,1,32,128]{3,2,1,0:T(8,128)(2,1)S(1)}, u32[]{:S(2)}, u32[]{:S(2)}) collective-permute-start(bf16[4,1,32,128]{3,2,1,0:T(8,128)(2,1)S(1)} %slice_select_fusion.2), channel_id=1, source_target_pairs={{0,2},{2,0},{1,3},{3,1},{4,6},{6,4},{5,7},{7,5},{8,10},{10,8},{9,1... | collective-permute-start | bytes 98312 | tf_op jit(solution)/shard_map/ppermute | solution.py:18
  4.5 1.5 %fusion.22 = (bf16[4,16,32,64]{3,2,1,0:T(8,128)(2,1)S(1)}, bf16[4,16,32,64]{3,2,1,0:T(8,128)(2,1)S(1)}) fusion(bf16[4,16,32,128]{3,2,1,0:T(8,128)(2,1)} %param.4), kind=kLoop, calls=%fused_computation.64 | loop fusion | bytes 1048576 | tf_op jit(solution)/shard_map/slice | solution.py:33
  6.1 0.3 collective-permute-done
  6.5 2.2 %collective-permute-start.1 = (bf16[1,18,32,128]{3,2,1,0:T(8,128)(2,1)S(1)}, bf16[1,18,32,128]{3,2,1,0:T(8,128)(2,1)S(1)}, u32[]{:S(2)}, u32[]{:S(2)}) collective-permute-start(bf16[1,18,32,128]{3,2,1,0:T(8,128)(2,1)S(1)} %get-tuple-element.10), channel_id=1, source_target_pairs={{0,4},{4,8},{8,12},{12,0},{1,5},{5,9},{9,13},{13,1},{2,6},{6,10},{... | collective-permute-start | bytes 442376 | tf_op jit(solution)/shard_map/ppermute | solution.py:23
  8.6 2.1 %collective-permute-start.2 = (bf16[1,18,32,128]{3,2,1,0:T(8,128)(2,1)S(1)}, bf16[1,18,32,128]{3,2,1,0:T(8,128)(2,1)S(1)}, u32[]{:S(2)}, u32[]{:S(2)}) collective-permute-start(bf16[1,18,32,128]{3,2,1,0:T(8,128)(2,1)S(1)} %get-tuple-element.11), channel_id=1, source_target_pairs={{4,0},{8,4},{12,8},{0,12},{5,1},{9,5},{13,9},{1,13},{6,2},{10,6},{... | collective-permute-start | bytes 442376 | tf_op jit(solution)/shard_map/ppermute | solution.py:24
  10.8 4.2 %collective-permute-done.1 = bf16[1,18,32,128]{3,2,1,0:T(8,128)(2,1)S(1)} collective-permute-done((bf16[1,18,32,128]{3,2,1,0:T(8,128)(2,1)S(1)}, bf16[1,18,32,128]{3,2,1,0:T(8,128)(2,1)S(1)}, u32[]{:S(2)}, u32[]{:S(2)}) %collective-permute-start.1) | collective-permute-done | bytes 147488 | tf_op jit(solution)/shard_map/ppermute | solution.py:23
  15.1 0.1 fusion.23
  15.2 0.8 %collective-permute-done.2 = bf16[1,18,32,128]{3,2,1,0:T(8,128)(2,1)S(1)} collective-permute-done((bf16[1,18,32,128]{3,2,1,0:T(8,128)(2,1)S(1)}, bf16[1,18,32,128]{3,2,1,0:T(8,128)(2,1)S(1)}, u32[]{:S(2)}, u32[]{:S(2)}) %collective-permute-start.2) | collective-permute-done | bytes 147488 | tf_op jit(solution)/shard_map/ppermute | solution.py:24
  16.0 0.1 fusion.24
  16.1 0.5 %maximum_select_fusion = bf16[6,18,32,64]{3,2,1,0:T(8,128)(2,1)S(1)} fusion(bf16[1,18,32,64]{3,2,1,0:T(8,128)(2,1)S(1)} %get-tuple-element.23, bf16[4,1,32,64]{3,2,1,0:T(8,128)(2,1)S(1)} %get-tuple-element.32, bf16[4,16,32,64]{3,2,1,0:T(8,128)(2,1)S(1)} %get-tuple-element.13, bf16[4,1,32,64]{3,2,1,0:T(8,128)(2,1)S(1)} %get-tuple-element.27, ...), kind=kLoop, calls=%fused_computation.14 | loop fusion | flops 1990656 | bytes 1327105 | tf_op jit(solution)/shard_map/jit(_where)/select_n | solution.py:86
  16.7 0.8 %pad_slice_fusion.1 = (bf16[6,18,32,64]{3,2,1,0:T(8,128)(2,1)S(1)}, bf16[6,18,32,64]{3,2,1,0:T(8,128)(2,1)S(1)}) fusion(bf16[6,18,32,64]{3,2,1,0:T(8,128)(2,1)S(1)} %maximum_select_fusion), kind=kLoop, calls=%fused_computation.12 | loop fusion | bytes 1327104 | tf_op jit(solution)/shard_map/slice | solution.py:90
  17.4 0.9 %pad_maximum_fusion = bf16[6,18,32,192]{3,2,1,0:T(8,128)(2,1)S(1)} fusion(bf16[6,18,32,64]{3,2,1,0:T(8,128)(2,1)S(1)} %get-tuple-element.9, bf16[6,18,32,64]{3,2,1,0:T(8,128)(2,1)S(1)} %maximum_select_fusion, bf16[6,18,32,64]{3,2,1,0:T(8,128)(2,1)S(1)} %get-tuple-element.8), kind=kLoop, calls=%fused_computation.2 | loop fusion | flops 3981312 | bytes 2654208 | tf_op jit(solution)/shard_map/concatenate | solution.py:90
  18.3 0.2 copy-done.2
  18.5 0.5 fusion.29
  18.9 0.5 fusion.28
  19.4 0.5 fusion.30
  19.9 0.5 fusion.31
  20.3 0.5 fusion.32
  20.8 0.5 fusion.33
  21.3 0.5 fusion.34
  21.7 0.5 fusion.35
  23.0 0.5 fusion.36
  23.5 0.2 maximum_bitcast_fusion
  24.5 0.1 maximum_bitcast_fusion.4
  24.8 0.1 maximum_bitcast_fusion.7
  24.9 0.1 maximum_bitcast_fusion.8
  25.2 1.5 %collective-permute-start.4 = (f32[4,216,64]{1,2,0:T(8,128)S(1)}, f32[4,216,64]{1,2,0:T(8,128)S(1)}, u32[]{:S(2)}, u32[]{:S(2)}) collective-permute-start(f32[4,216,64]{1,2,0:T(8,128)S(1)} %slice_select_fusion), channel_id=1, source_target_pairs={{0,2},{2,0},{1,3},{3,1},{4,6},{6,4},{5,7},{7,5},{8,10},{10,8},{9,1... | collective-permute-start | bytes 663560 | tf_op jit(solution)/shard_map/ppermute | solution.py:115
  26.6 0.4 copy.28
  27.0 0.2 pad.5.clone
  27.3 0.1 copy.7
  27.4 0.1 slice.179
  27.6 0.4 copy-done.3
  28.0 5.0 %fusion.11 = bf16[4,16,8,5,128]{4,2,3,1,0:T(8,128)(2,1)S(1)} fusion(bf16[3,3,3,128,128]{4,3,2,1,0:T(8,128)(2,1)S(1)} %bitcast.201, bf16[6,18,1,7,2,128]{5,3,4,1,0,2:T(8,128)(2,1)S(1)} %slice.179, bf16[6,18,1,8,5,128]{5,3,4,1,0,2:T(8,128)(2,1)S(1)} %copy.7, pred[8,5]{0,1:T(8,128)(4,1)S(1)} %copy-done.3), kind=kOutput, calls=%fused_computation.10 | convolution fusion | flops 2270224384 | bytes 3033128 | tf_op jit(solution)/shard_map/conv_general_dilated | solution.py:77
  32.9 0.1 copy.8
  33.0 0.2 select_add_fusion
  33.3 0.7 %collective-permute-start.3 = (f32[4,216,64]{1,2,0:T(8,128)S(1)}, f32[4,216,64]{1,2,0:T(8,128)S(1)}, u32[]{:S(2)}, u32[]{:S(2)}) collective-permute-start(f32[4,216,64]{1,2,0:T(8,128)S(1)} %get-tuple-element.7), channel_id=1, source_target_pairs={{0,2},{2,0},{1,3},{3,1},{4,6},{6,4},{5,7},{7,5},{8,10},{10,8},{9,1... | collective-permute-start | bytes 663560 | tf_op jit(solution)/shard_map/ppermute | solution.py:115
  34.0 1.4 %collective-permute-start.5 = (f32[216,64]{0,1:T(8,128)S(1)}, f32[216,64]{0,1:T(8,128)S(1)}, u32[]{:S(2)}, u32[]{:S(2)}) collective-permute-start(f32[216,64]{0,1:T(8,128)S(1)} %get-tuple-element.14), channel_id=1, source_target_pairs={{0,4},{4,8},{8,12},{12,0},{1,5},{5,9},{9,13},{13,1},{2,6},{6,10},{... | collective-permute-start | bytes 165896 | tf_op jit(solution)/shard_map/ppermute | solution.py:51
  35.4 2.1 %collective-permute-start.6 = (f32[216,64]{0,1:T(8,128)S(1)}, f32[216,64]{0,1:T(8,128)S(1)}, u32[]{:S(2)}, u32[]{:S(2)}) collective-permute-start(f32[216,64]{0,1:T(8,128)S(1)} %get-tuple-element.16), channel_id=1, source_target_pairs={{0,8},{4,12},{8,0},{12,4},{1,9},{5,13},{9,1},{13,5},{2,10},{6,14},... | collective-permute-start | bytes 165896 | tf_op jit(solution)/shard_map/ppermute | solution.py:51
  37.5 0.6 %collective-permute-start.7 = (f32[216,64]{0,1:T(8,128)S(1)}, f32[216,64]{0,1:T(8,128)S(1)}, u32[]{:S(2)}, u32[]{:S(2)}) collective-permute-start(f32[216,64]{0,1:T(8,128)S(1)} %get-tuple-element.15), channel_id=1, source_target_pairs={{0,12},{4,0},{8,4},{12,8},{1,13},{5,1},{9,5},{13,9},{2,14},{6,2},{... | collective-permute-start | bytes 165896 | tf_op jit(solution)/shard_map/ppermute | solution.py:51
  38.1 1.6 %collective-permute-done.3 = f32[4,216,64]{1,2,0:T(8,128)S(1)} collective-permute-done((f32[4,216,64]{1,2,0:T(8,128)S(1)}, f32[4,216,64]{1,2,0:T(8,128)S(1)}, u32[]{:S(2)}, u32[]{:S(2)}) %collective-permute-start.3) | collective-permute-done | bytes 221216 | tf_op jit(solution)/shard_map/ppermute | solution.py:115
  39.7 0.2 select_add_fusion.1
  39.9 2.9 %collective-permute-start.10 = (f32[216,64]{0,1:T(8,128)S(1)}, f32[216,64]{0,1:T(8,128)S(1)}, u32[]{:S(2)}, u32[]{:S(2)}) collective-permute-start(f32[216,64]{0,1:T(8,128)S(1)} %get-tuple-element.18), channel_id=1, source_target_pairs={{0,12},{4,0},{8,4},{12,8},{1,13},{5,1},{9,5},{13,9},{2,14},{6,2},{... | collective-permute-start | bytes 165896 | tf_op jit(solution)/shard_map/ppermute | solution.py:51
  42.9 0.6 %collective-permute-start.9 = (f32[216,64]{0,1:T(8,128)S(1)}, f32[216,64]{0,1:T(8,128)S(1)}, u32[]{:S(2)}, u32[]{:S(2)}) collective-permute-start(f32[216,64]{0,1:T(8,128)S(1)} %get-tuple-element.19), channel_id=1, source_target_pairs={{0,8},{4,12},{8,0},{12,4},{1,9},{5,13},{9,1},{13,5},{2,10},{6,14},... | collective-permute-start | bytes 165896 | tf_op jit(solution)/shard_map/ppermute | solution.py:51
  43.5 0.9 %copy.18 = bf16[4,16,32,128]{3,2,1,0:T(8,128)(2,1)} copy(bf16[4,16,32,128]{3,1,2,0:T(8,128)(2,1)S(1)} %slice_bitcast_fusion) | data formatting | bytes 1048576
  44.4 0.5 %collective-permute-done.10 = f32[216,64]{0,1:T(8,128)S(1)} collective-permute-done((f32[216,64]{0,1:T(8,128)S(1)}, f32[216,64]{0,1:T(8,128)S(1)}, u32[]{:S(2)}, u32[]{:S(2)}) %collective-permute-start.10) | collective-permute-done | bytes 55328 | tf_op jit(solution)/shard_map/ppermute | solution.py:51
  45.0 3.9 %collective-permute-done.8 = f32[216,64]{0,1:T(8,128)S(1)} collective-permute-done((f32[216,64]{0,1:T(8,128)S(1)}, f32[216,64]{0,1:T(8,128)S(1)}, u32[]{:S(2)}, u32[]{:S(2)}) %collective-permute-start.8) | collective-permute-done | bytes 55328 | tf_op jit(solution)/shard_map/ppermute | solution.py:51
  48.9 0.8 %maximum_multiply_fusion = f32[432,64]{0,1:T(8,128)} fusion(f32[216,64]{0,1:T(8,128)S(1)} %fusion.16, f32[216,64]{0,1:T(8,128)S(1)} %fusion.18), kind=kLoop, calls=%fused_computation.36 | loop fusion | flops 55296 | bytes 221184 | tf_op jit(solution)/shard_map/div | solution.py:125
  (59 shorter events, 2.1 us)
Async XLA Ops:
  0.6 26.9 %copy-start = (bf16[27,128,128]{2,1,0:T(8,128)(2,1)S(1)}, bf16[27,128,128]{2,1,0:T(8,128)(2,1)}, u32[]{:S(2)}) copy-start(bf16[27,128,128]{2,1,0:T(8,128)(2,1)} %param.5) | copy-start | bytes 2654212
  0.6 5.8 %copy-start.1 = (bf16[4,16,32,128]{3,2,1,0:T(8,128)(2,1)S(1)}, bf16[4,16,32,128]{3,2,1,0:T(8,128)(2,1)}, u32[]{:S(2)}) copy-start(bf16[4,16,32,128]{3,2,1,0:T(8,128)(2,1)} %param.4) | copy-start | bytes 1572868
  1.6 4.8 %collective-permute-start = (bf16[4,1,32,128]{3,2,1,0:T(8,128)(2,1)S(1)}, bf16[4,1,32,128]{3,2,1,0:T(8,128)(2,1)S(1)}, u32[]{:S(2)}, u32[]{:S(2)}) collective-permute-start(bf16[4,1,32,128]{3,2,1,0:T(8,128)(2,1)S(1)} %slice_select_fusion.2), channel_id=1, source_target_pairs={{0,2},{2,0},{1,3},{3,1},{4,6},{6,4},{5,7},{7,5},{8,10},{10,8},{9,1... | collective-permute-start | bytes 98312 | tf_op jit(solution)/shard_map/ppermute | solution.py:18
  6.5 8.6 %collective-permute-start.1 = (bf16[1,18,32,128]{3,2,1,0:T(8,128)(2,1)S(1)}, bf16[1,18,32,128]{3,2,1,0:T(8,128)(2,1)S(1)}, u32[]{:S(2)}, u32[]{:S(2)}) collective-permute-start(bf16[1,18,32,128]{3,2,1,0:T(8,128)(2,1)S(1)} %get-tuple-element.10), channel_id=1, source_target_pairs={{0,4},{4,8},{8,12},{12,0},{1,5},{5,9},{9,13},{13,1},{2,6},{6,10},{... | collective-permute-start | bytes 442376 | tf_op jit(solution)/shard_map/ppermute | solution.py:23
  8.6 7.4 %collective-permute-start.2 = (bf16[1,18,32,128]{3,2,1,0:T(8,128)(2,1)S(1)}, bf16[1,18,32,128]{3,2,1,0:T(8,128)(2,1)S(1)}, u32[]{:S(2)}, u32[]{:S(2)}) collective-permute-start(bf16[1,18,32,128]{3,2,1,0:T(8,128)(2,1)S(1)} %get-tuple-element.11), channel_id=1, source_target_pairs={{4,0},{8,4},{12,8},{0,12},{5,1},{9,5},{13,9},{1,13},{6,2},{10,6},{... | collective-permute-start | bytes 442376 | tf_op jit(solution)/shard_map/ppermute | solution.py:24
  17.4 1.0 %copy-start.2 = (bf16[4,16,32,128]{3,2,1,0:T(8,128)(2,1)S(1)}, bf16[4,16,32,128]{3,2,1,0:T(8,128)(2,1)}, u32[]{:S(2)}) copy-start(bf16[4,16,32,128]{3,2,1,0:T(8,128)(2,1)} %param.3) | copy-start | bytes 1572868
  25.2 7.9 %collective-permute-start.4 = (f32[4,216,64]{1,2,0:T(8,128)S(1)}, f32[4,216,64]{1,2,0:T(8,128)S(1)}, u32[]{:S(2)}, u32[]{:S(2)}) collective-permute-start(f32[4,216,64]{1,2,0:T(8,128)S(1)} %slice_select_fusion), channel_id=1, source_target_pairs={{0,2},{2,0},{1,3},{3,1},{4,6},{6,4},{5,7},{7,5},{8,10},{10,8},{9,1... | collective-permute-start | bytes 663560 | tf_op jit(solution)/shard_map/ppermute | solution.py:115
  27.3 0.7 %copy-start.3 = (pred[8,5]{0,1:T(8,128)(4,1)S(1)}, pred[8,5]{0,1:T(8,128)(4,1)}, u32[]{:S(2)}) copy-start(pred[8,5]{0,1:T(8,128)(4,1)} %constant.77) | copy-start | bytes 124
  33.3 6.4 %collective-permute-start.3 = (f32[4,216,64]{1,2,0:T(8,128)S(1)}, f32[4,216,64]{1,2,0:T(8,128)S(1)}, u32[]{:S(2)}, u32[]{:S(2)}) collective-permute-start(f32[4,216,64]{1,2,0:T(8,128)S(1)} %get-tuple-element.7), channel_id=1, source_target_pairs={{0,2},{2,0},{1,3},{3,1},{4,6},{6,4},{5,7},{7,5},{8,10},{10,8},{9,1... | collective-permute-start | bytes 663560 | tf_op jit(solution)/shard_map/ppermute | solution.py:115
  34.0 8.9 %collective-permute-start.5 = (f32[216,64]{0,1:T(8,128)S(1)}, f32[216,64]{0,1:T(8,128)S(1)}, u32[]{:S(2)}, u32[]{:S(2)}) collective-permute-start(f32[216,64]{0,1:T(8,128)S(1)} %get-tuple-element.14), channel_id=1, source_target_pairs={{0,4},{4,8},{8,12},{12,0},{1,5},{5,9},{9,13},{13,1},{2,6},{6,10},{... | collective-permute-start | bytes 165896 | tf_op jit(solution)/shard_map/ppermute | solution.py:51
  35.4 8.1 %collective-permute-start.6 = (f32[216,64]{0,1:T(8,128)S(1)}, f32[216,64]{0,1:T(8,128)S(1)}, u32[]{:S(2)}, u32[]{:S(2)}) collective-permute-start(f32[216,64]{0,1:T(8,128)S(1)} %get-tuple-element.16), channel_id=1, source_target_pairs={{0,8},{4,12},{8,0},{12,4},{1,9},{5,13},{9,1},{13,5},{2,10},{6,14},... | collective-permute-start | bytes 165896 | tf_op jit(solution)/shard_map/ppermute | solution.py:51
  37.5 6.0 %collective-permute-start.7 = (f32[216,64]{0,1:T(8,128)S(1)}, f32[216,64]{0,1:T(8,128)S(1)}, u32[]{:S(2)}, u32[]{:S(2)}) collective-permute-start(f32[216,64]{0,1:T(8,128)S(1)} %get-tuple-element.15), channel_id=1, source_target_pairs={{0,12},{4,0},{8,4},{12,8},{1,13},{5,1},{9,5},{13,9},{2,14},{6,2},{... | collective-permute-start | bytes 165896 | tf_op jit(solution)/shard_map/ppermute | solution.py:51
  39.9 5.0 %collective-permute-start.10 = (f32[216,64]{0,1:T(8,128)S(1)}, f32[216,64]{0,1:T(8,128)S(1)}, u32[]{:S(2)}, u32[]{:S(2)}) collective-permute-start(f32[216,64]{0,1:T(8,128)S(1)} %get-tuple-element.18), channel_id=1, source_target_pairs={{0,12},{4,0},{8,4},{12,8},{1,13},{5,1},{9,5},{13,9},{2,14},{6,2},{... | collective-permute-start | bytes 165896 | tf_op jit(solution)/shard_map/ppermute | solution.py:51
  42.8 6.1 %collective-permute-start.8 = (f32[216,64]{0,1:T(8,128)S(1)}, f32[216,64]{0,1:T(8,128)S(1)}, u32[]{:S(2)}, u32[]{:S(2)}) collective-permute-start(f32[216,64]{0,1:T(8,128)S(1)} %get-tuple-element.17), channel_id=1, source_target_pairs={{0,4},{4,8},{8,12},{12,0},{1,5},{5,9},{9,13},{13,1},{2,6},{6,10},{... | collective-permute-start | bytes 165896 | tf_op jit(solution)/shard_map/ppermute | solution.py:51
  42.9 6.1 %collective-permute-start.9 = (f32[216,64]{0,1:T(8,128)S(1)}, f32[216,64]{0,1:T(8,128)S(1)}, u32[]{:S(2)}, u32[]{:S(2)}) collective-permute-start(f32[216,64]{0,1:T(8,128)S(1)} %get-tuple-element.19), channel_id=1, source_target_pairs={{0,8},{4,12},{8,0},{12,4},{1,9},{5,13},{9,1},{13,5},{2,10},{6,14},... | collective-permute-start | bytes 165896 | tf_op jit(solution)/shard_map/ppermute | solution.py:51

commit v22 on v19

--- a/solution.py
+++ b/solution.py
@@ -80,14 +80,17 @@
         preferred_element_type=jnp.float32,
     )[0]
     grad_in = inner.astype(jnp.bfloat16)
-    if ncores == 1:
-        gshare = assemble(grad_out, got, 0, half)
-    else:
-        gshare = jnp.where(
-            lax.axis_index("col") == 0, assemble(grad_out, got, 0, half), assemble(grad_out, got, half, 2 * half)
-        )
-    gdeep = jnp.pad(gshare, ((0, 0), (0, 0), (1, 1), (0, 0)))
-    stack = jnp.concatenate([lax.slice_in_dim(gdeep, 2 - c, 2 - c + depth, axis=2) for c in range(3)], axis=3)
+    def share_stack(piece):
+        if ncores == 1:
+            mine = piece[..., :half]
+        else:
+            mine = lax.dynamic_slice_in_dim(piece, offset, half, 3)
+        deep = jnp.pad(mine, ((0, 0), (0, 0), (1, 1), (0, 0)))
+        return jnp.concatenate([lax.slice_in_dim(deep, 2 - c, 2 - c + depth, axis=2) for c in range(3)], axis=3)
+
+    stack = share_stack(grad_out)
+    for dim, low, high in got:
+        stack = jnp.concatenate([share_stack(low), stack, share_stack(high)], axis=dim)
     pieces = []
     for a in range(3):
         for b in range(3):

time: 49.9 us -> 50.4 us (1.010)
  waiting for transfers between devices: 11.4 us -> 8.2 us
  matrix products: 9.11 us -> 11.2 us
  starting transfers between devices: 17 us -> 18.3 us
  other arithmetic: 4.48 us -> 5.35 us
  local copies, waits for them, and re-layouts: 6.47 us -> 5.85 us
    ppermute x1, waiting for transfers between devices: 4.23 us -> 0.01 us  [halo_parts(): low = lax.ppermute(tail, axis, [(i, (i + 1) % count) for i in range(count)])]
    dot_general x9, matrix products: 4.15 us -> 6.45 us  [on_device(): lax.dot_general(x_act, window, (((0, 1, 2), (0, 1, 2)), ((), ())), prefer...]
    slice x5, local copies, waits for them, and re-layouts: 2.61 us -> 0.61 us  [share_stack(): lax.slice_in_dim(deep, 2 - c, 2 - c + depth, axis=2)]
    ppermute x1, waiting for transfers between devices: 0.84 us -> 2.78 us  [halo_parts(): lax.ppermute(head, axis, [((i + 1) % count, i) for i in range(count)])]
    dynamic_slice x0 -> x3, local copies, waits for them, and re-layouts: none -> 1.54 us  [share_stack(): mine = lax.dynamic_slice_in_dim(piece, offset, half, 3)]
    ppermute x6, starting transfers between devices: 7.65 us -> 9.18 us  [scatter_sum(): lax.ppermute(part, axis, [(j, (j + shift) % count) for j in range(count)])]
    concatenate x1 -> x2, other arithmetic: 0.86 us -> 2.28 us  [on_device(): jnp.concatenate([share_stack(low), stack, share_stack(high)], axis=dim)]
    ppermute x2, waiting for transfers between devices: 0.67 us -> 0.01 us  [on_device(): partial = keep + lax.ppermute(send, 'gy', [(0, 1), (1, 0)])]
  transfers between devices with their start and end apart: 11 -> 11, of which waited for: 6 -> 4; matrix products, arithmetic and copies ran while one was open for 18% -> 26% of each run, Pallas kernels for 0% -> 0%
where the time goes in v22:
time: 50.4 us; the launch traced here: 50.2 us
  starting transfers between devices  18.3 us (36%)
  matrix products  11.2 us (22%)
  waiting for transfers between devices  8.2 us (16%)
  local copies, waits for them, and re-layouts  5.85 us (12%)
  other arithmetic  5.35 us (11%)
  between operations  1.23 us (2%)
    ppermute x6, starting transfers between devices, scatter_sum(): lax.ppermute(part, axis, [(j, (j + shift) % count) for j in range(count)])  9.18 us
    dot_general x9, matrix products, on_device(): lax.dot_general(x_act, window, (((0, 1, 2), (0, 1, 2)), ((), ())), prefer...  6.45 us
    ppermute x6, waiting for transfers between devices, scatter_sum(): lax.ppermute(part, axis, [(j, (j + shift) % count) for j in range(count)])  5.41 us
    conv_general_dilated x1, matrix products, on_device(): lax.conv_general_dilated(gh[None], kflip, (1, 1, 1), pad, dimension_numbe...  4.75 us
    ppermute x1, starting transfers between devices, halo_parts(): recv = lax.ppermute(jnp.where(me == 0, tail, head), axis, [(0, 1), (1, 0)])  2.94 us
    ppermute x1, waiting for transfers between devices, halo_parts(): lax.ppermute(head, axis, [((i + 1) % count, i) for i in range(count)])  2.78 us
    ppermute x1, starting transfers between devices, halo_parts(): lax.ppermute(head, axis, [((i + 1) % count, i) for i in range(count)])  2.45 us
    concatenate x2, other arithmetic, on_device(): jnp.concatenate([share_stack(low), stack, share_stack(high)], axis=dim)  2.28 us
  transfers between devices with their start and end apart: 11, of which 4 were waited for; matrix products, arithmetic and copies ran while one was open for 26% of the time, Pallas kernels for 0%

profile of v22, /device:TPU:0, one launch (start us, length us, event | category | flops | bytes accessed | tf_op | source)
XLA Modules:
  0.0 50.2 jit_solution(7090717339898511916)
XLA Ops:
  0.7 0.9 %slice_select_fusion.2 = bf16[4,1,32,128]{3,2,1,0:T(8,128)(2,1)S(1)} fusion(bf16[4,16,32,128]{3,2,1,0:T(8,128)(2,1)} %param.4, pred[]{:T(512)S(6)} %eq.26), kind=kLoop, calls=%fused_computation.96 | loop fusion | flops 16384 | bytes 98305 | tf_op jit(solution)/shard_map/jit(_where)/select_n | solution.py:18
  1.5 2.9 %collective-permute-start = (bf16[4,1,32,128]{3,2,1,0:T(8,128)(2,1)S(1)}, bf16[4,1,32,128]{3,2,1,0:T(8,128)(2,1)S(1)}, u32[]{:S(2)}, u32[]{:S(2)}) collective-permute-start(bf16[4,1,32,128]{3,2,1,0:T(8,128)(2,1)S(1)} %slice_select_fusion.2), channel_id=1, source_target_pairs={{0,2},{2,0},{1,3},{3,1},{4,6},{6,4},{5,7},{7,5},{8,10},{10,8},{9,1... | collective-permute-start | bytes 98312 | tf_op jit(solution)/shard_map/ppermute | solution.py:18
  4.5 1.3 %constant_dynamic-slice_fusion.3 = bf16[4,16,32,64]{3,2,1,0:T(8,128)(2,1)S(1)} fusion(bf16[4,16,32,128]{3,2,1,0:T(8,128)(2,1)} %param.4, s32[]{:T(128)S(6)} %select_n.107), kind=kLoop, calls=%fused_computation.102 | loop fusion | bytes 524292 | tf_op jit(solution)/shard_map/dynamic_slice | solution.py:87
  5.8 0.4 pad_slice_fusion.1
  6.2 0.9 %fusion.38 = f32[192,128,1,1]{1,0,3,2:T(8,128)S(1)} fusion(bf16[4,16,32,128]{3,2,1,0:T(8,128)(2,1)S(1)} %copy-done.2, bf16[4,16,32,64]{3,2,1,0:T(8,128)(2,1)S(1)} %get-tuple-element.9, bf16[4,16,32,64]{3,2,1,0:T(8,128)(2,1)S(1)} %constant_dynamic-slice_fusion.3, bf16[4,16,32,64]{3,2,1,0:T(8,128)(2,1)S(1)} %get-tuple-element.8), kind=kOutput, calls=%fused_computation.36 | convolution fusion | flops 103022592 | bytes 1409024 | tf_op jit(solution)/shard_map/dot_general | solution.py:98
  7.3 0.1 constant_dynamic-slice_fusion.2
  7.4 1.6 %collective-permute-start.1 = (bf16[1,18,32,128]{3,2,1,0:T(8,128)(2,1)S(1)}, bf16[1,18,32,128]{3,2,1,0:T(8,128)(2,1)S(1)}, u32[]{:S(2)}, u32[]{:S(2)}) collective-permute-start(bf16[1,18,32,128]{3,2,1,0:T(8,128)(2,1)S(1)} %get-tuple-element.6), channel_id=1, source_target_pairs={{0,4},{4,8},{8,12},{12,0},{1,5},{5,9},{9,13},{13,1},{2,6},{6,10},{... | collective-permute-start | bytes 442376 | tf_op jit(solution)/shard_map/ppermute | solution.py:23
  9.1 2.0 %fusion.26 = f32[192,128,1,1]{1,0,3,2:T(8,128)S(1)} fusion(bf16[4,16,32,128]{3,2,1,0:T(8,128)(2,1)} %param.3, bf16[4,16,32,64]{3,2,1,0:T(8,128)(2,1)S(1)} %get-tuple-element.9, bf16[4,16,32,64]{3,2,1,0:T(8,128)(2,1)S(1)} %constant_dynamic-slice_fusion.3, bf16[4,16,32,64]{3,2,1,0:T(8,128)(2,1)S(1)} %get-tuple-element.8, ...), kind=kOutput, calls=%fused_computation.24 | convolution fusion | flops 105676800 | bytes 1458176 | tf_op jit(solution)/shard_map/dot_general | solution.py:98
  11.2 0.9 %fusion.14 = f32[192,128,1,1]{1,0,3,2:T(8,128)S(1)} fusion(bf16[4,16,32,128]{3,2,1,0:T(8,128)(2,1)S(1)} %copy-done.3, bf16[4,1,32,64]{3,2,1,0:T(8,128)(2,1)S(1)} %get-tuple-element.25, bf16[4,1,32,64]{3,2,1,0:T(8,128)(2,1)S(1)} %get-tuple-element.28, bf16[4,1,32,64]{3,2,1,0:T(8,128)(2,1)S(1)} %get-tuple-element.24, ...), kind=kOutput, calls=%fused_computation.12 | convolution fusion | flops 105676800 | bytes 1458176 | tf_op jit(solution)/shard_map/dot_general | solution.py:98
  12.1 0.1 maximum_bitcast_fusion.3
  12.5 2.5 %collective-permute-start.2 = (bf16[1,18,32,128]{3,2,1,0:T(8,128)(2,1)S(1)}, bf16[1,18,32,128]{3,2,1,0:T(8,128)(2,1)S(1)}, u32[]{:S(2)}, u32[]{:S(2)}) collective-permute-start(bf16[1,18,32,128]{3,2,1,0:T(8,128)(2,1)S(1)} %get-tuple-element.7), channel_id=1, source_target_pairs={{4,0},{8,4},{12,8},{0,12},{5,1},{9,5},{13,9},{1,13},{6,2},{10,6},{... | collective-permute-start | bytes 442376 | tf_op jit(solution)/shard_map/ppermute | solution.py:24
  14.9 0.1 maximum_bitcast_fusion.6
  15.0 2.8 %collective-permute-done.2 = bf16[1,18,32,128]{3,2,1,0:T(8,128)(2,1)S(1)} collective-permute-done((bf16[1,18,32,128]{3,2,1,0:T(8,128)(2,1)S(1)}, bf16[1,18,32,128]{3,2,1,0:T(8,128)(2,1)S(1)}, u32[]{:S(2)}, u32[]{:S(2)}) %collective-permute-start.2) | collective-permute-done | bytes 147488 | tf_op jit(solution)/shard_map/ppermute | solution.py:24
  17.8 0.2 constant_dynamic-slice_fusion
  18.1 1.2 %maximum_maximum_fusion = bf16[5,18,32,192]{3,2,1,0:T(8,128)(2,1)S(1)} fusion(bf16[1,18,32,64]{3,2,1,0:T(8,128)(2,1)S(1)} %get-tuple-element.17, bf16[1,18,32,64]{3,2,1,0:T(8,128)(2,1)S(1)} %get-tuple-element.31, bf16[1,18,32,64]{3,2,1,0:T(8,128)(2,1)S(1)} %get-tuple-element.16, bf16[4,1,32,64]{3,2,1,0:T(8,128)(2,1)S(1)} %get-tuple-element.25, ...), kind=kLoop, calls=%fused_computation.8 | loop fusion | flops 13271040 | bytes 2211840 | tf_op jit(solution)/shard_map/concatenate | solution.py:93
  19.3 0.5 fusion.57
  19.8 0.5 fusion.56
  20.2 0.5 fusion.58
  20.8 1.1 %maximum_maximum_fusion.1 = bf16[5,18,32,192]{3,2,1,0:T(8,128)(2,1)S(1)} fusion(bf16[4,1,32,64]{3,2,1,0:T(8,128)(2,1)S(1)} %get-tuple-element.25, bf16[4,1,32,64]{3,2,1,0:T(8,128)(2,1)S(1)} %get-tuple-element.28, bf16[4,1,32,64]{3,2,1,0:T(8,128)(2,1)S(1)} %get-tuple-element.24, bf16[4,16,32,64]{3,2,1,0:T(8,128)(2,1)S(1)} %get-tuple-element.9, ...), kind=kLoop, calls=%fused_computation.9 | loop fusion | flops 13271040 | bytes 2211840 | tf_op jit(solution)/shard_map/concatenate | solution.py:93
  21.9 0.5 fusion.59
  22.3 0.5 fusion.60
  23.2 0.5 fusion.61
  23.7 0.2 maximum_bitcast_fusion
  24.5 0.1 maximum_bitcast_fusion.4
  24.6 0.1 maximum_bitcast_fusion.5
  24.6 0.1 maximum_bitcast_fusion.7
  24.7 0.1 maximum_bitcast_fusion.8
  25.0 1.2 %collective-permute-start.3 = (f32[4,216,64]{1,2,0:T(8,128)S(1)}, f32[4,216,64]{1,2,0:T(8,128)S(1)}, u32[]{:S(2)}, u32[]{:S(2)}) collective-permute-start(f32[4,216,64]{1,2,0:T(8,128)S(1)} %slice_select_fusion.1), channel_id=1, source_target_pairs={{0,2},{2,0},{1,3},{3,1},{4,6},{6,4},{5,7},{7,5},{8,10},{10,8},{9,1... | collective-permute-start | bytes 663560 | tf_op jit(solution)/shard_map/ppermute | solution.py:118
  26.1 0.4 copy.28
  26.5 0.2 pad.23.clone
  26.8 0.1 copy.7
  26.9 0.1 slice.179
  27.1 0.4 copy-done.4
  27.5 4.7 %fusion.11 = bf16[4,16,8,5,128]{4,2,3,1,0:T(8,128)(2,1)S(1)} fusion(bf16[3,3,3,128,128]{4,3,2,1,0:T(8,128)(2,1)S(1)} %bitcast.198, bf16[6,18,1,7,2,128]{5,3,4,1,0,2:T(8,128)(2,1)S(1)} %slice.179, bf16[6,18,1,8,5,128]{5,3,4,1,0,2:T(8,128)(2,1)S(1)} %copy.7, pred[8,5]{0,1:T(8,128)(4,1)S(1)} %copy-done.4), kind=kOutput, calls=%fused_computation.11 | convolution fusion | flops 2270224384 | bytes 3033128 | tf_op jit(solution)/shard_map/conv_general_dilated | solution.py:77
  32.2 0.1 copy.8
  32.3 0.2 select_add_fusion.1
  32.6 1.0 %collective-permute-start.7 = (f32[4,216,64]{1,2,0:T(8,128)S(1)}, f32[4,216,64]{1,2,0:T(8,128)S(1)}, u32[]{:S(2)}, u32[]{:S(2)}) collective-permute-start(f32[4,216,64]{1,2,0:T(8,128)S(1)} %get-tuple-element.5), channel_id=1, source_target_pairs={{0,2},{2,0},{1,3},{3,1},{4,6},{6,4},{5,7},{7,5},{8,10},{10,8},{9,1... | collective-permute-start | bytes 663560 | tf_op jit(solution)/shard_map/ppermute | solution.py:118
  33.6 0.9 %copy.18 = bf16[4,16,32,128]{3,2,1,0:T(8,128)(2,1)} copy(bf16[4,16,32,128]{3,1,2,0:T(8,128)(2,1)S(1)} %slice_bitcast_fusion) | data formatting | bytes 1048576
  34.5 1.6 %collective-permute-start.4 = (f32[216,64]{0,1:T(8,128)S(1)}, f32[216,64]{0,1:T(8,128)S(1)}, u32[]{:S(2)}, u32[]{:S(2)}) collective-permute-start(f32[216,64]{0,1:T(8,128)S(1)} %get-tuple-element.10), channel_id=1, source_target_pairs={{0,4},{4,8},{8,12},{12,0},{1,5},{5,9},{9,13},{13,1},{2,6},{6,10},{... | collective-permute-start | bytes 165896 | tf_op jit(solution)/shard_map/ppermute | solution.py:51
  36.2 3.0 %collective-permute-start.5 = (f32[216,64]{0,1:T(8,128)S(1)}, f32[216,64]{0,1:T(8,128)S(1)}, u32[]{:S(2)}, u32[]{:S(2)}) collective-permute-start(f32[216,64]{0,1:T(8,128)S(1)} %get-tuple-element.12), channel_id=1, source_target_pairs={{0,8},{4,12},{8,0},{12,4},{1,9},{5,13},{9,1},{13,5},{2,10},{6,14},... | collective-permute-start | bytes 165896 | tf_op jit(solution)/shard_map/ppermute | solution.py:51
  39.2 0.9 %collective-permute-start.6 = (f32[216,64]{0,1:T(8,128)S(1)}, f32[216,64]{0,1:T(8,128)S(1)}, u32[]{:S(2)}, u32[]{:S(2)}) collective-permute-start(f32[216,64]{0,1:T(8,128)S(1)} %get-tuple-element.11), channel_id=1, source_target_pairs={{0,12},{4,0},{8,4},{12,8},{1,13},{5,1},{9,5},{13,9},{2,14},{6,2},{... | collective-permute-start | bytes 165896 | tf_op jit(solution)/shard_map/ppermute | solution.py:51
  40.1 0.2 select_add_fusion
  40.3 3.0 %collective-permute-start.10 = (f32[216,64]{0,1:T(8,128)S(1)}, f32[216,64]{0,1:T(8,128)S(1)}, u32[]{:S(2)}, u32[]{:S(2)}) collective-permute-start(f32[216,64]{0,1:T(8,128)S(1)} %get-tuple-element.14), channel_id=1, source_target_pairs={{0,12},{4,0},{8,4},{12,8},{1,13},{5,1},{9,5},{13,9},{2,14},{6,2},{... | collective-permute-start | bytes 165896 | tf_op jit(solution)/shard_map/ppermute | solution.py:51
  43.3 0.6 %collective-permute-start.9 = (f32[216,64]{0,1:T(8,128)S(1)}, f32[216,64]{0,1:T(8,128)S(1)}, u32[]{:S(2)}, u32[]{:S(2)}) collective-permute-start(f32[216,64]{0,1:T(8,128)S(1)} %get-tuple-element.15), channel_id=1, source_target_pairs={{0,8},{4,12},{8,0},{12,4},{1,9},{5,13},{9,1},{13,5},{2,10},{6,14},... | collective-permute-start | bytes 165896 | tf_op jit(solution)/shard_map/ppermute | solution.py:51
  44.0 0.9 %collective-permute-done.6 = f32[216,64]{0,1:T(8,128)S(1)} collective-permute-done((f32[216,64]{0,1:T(8,128)S(1)}, f32[216,64]{0,1:T(8,128)S(1)}, u32[]{:S(2)}, u32[]{:S(2)}) %collective-permute-start.6) | collective-permute-done | bytes 55328 | tf_op jit(solution)/shard_map/ppermute | solution.py:51
  44.9 0.9 %collective-permute-done.10 = f32[216,64]{0,1:T(8,128)S(1)} collective-permute-done((f32[216,64]{0,1:T(8,128)S(1)}, f32[216,64]{0,1:T(8,128)S(1)}, u32[]{:S(2)}, u32[]{:S(2)}) %collective-permute-start.10) | collective-permute-done | bytes 55328 | tf_op jit(solution)/shard_map/ppermute | solution.py:51
  45.8 3.6 %collective-permute-done.8 = f32[216,64]{0,1:T(8,128)S(1)} collective-permute-done((f32[216,64]{0,1:T(8,128)S(1)}, f32[216,64]{0,1:T(8,128)S(1)}, u32[]{:S(2)}, u32[]{:S(2)}) %collective-permute-start.8) | collective-permute-done | bytes 55328 | tf_op jit(solution)/shard_map/ppermute | solution.py:51
  49.4 0.8 %maximum_multiply_fusion = f32[432,64]{0,1:T(8,128)} fusion(f32[216,64]{0,1:T(8,128)S(1)} %fusion.46, f32[216,64]{0,1:T(8,128)S(1)} %fusion.48), kind=kLoop, calls=%fused_computation.70 | loop fusion | flops 55296 | bytes 221184 | tf_op jit(solution)/shard_map/div | solution.py:126
  (64 shorter events, 2.0 us)
Async XLA Ops:
  0.6 26.4 %copy-start = (bf16[27,128,128]{2,1,0:T(8,128)(2,1)S(1)}, bf16[27,128,128]{2,1,0:T(8,128)(2,1)}, u32[]{:S(2)}) copy-start(bf16[27,128,128]{2,1,0:T(8,128)(2,1)} %param.5) | copy-start | bytes 2654212
  1.5 5.7 %collective-permute-start = (bf16[4,1,32,128]{3,2,1,0:T(8,128)(2,1)S(1)}, bf16[4,1,32,128]{3,2,1,0:T(8,128)(2,1)S(1)}, u32[]{:S(2)}, u32[]{:S(2)}) collective-permute-start(bf16[4,1,32,128]{3,2,1,0:T(8,128)(2,1)S(1)} %slice_select_fusion.2), channel_id=1, source_target_pairs={{0,2},{2,0},{1,3},{3,1},{4,6},{6,4},{5,7},{7,5},{8,10},{10,8},{9,1... | collective-permute-start | bytes 98312 | tf_op jit(solution)/shard_map/ppermute | solution.py:18
  4.5 1.7 %copy-start.2 = (bf16[4,16,32,128]{3,2,1,0:T(8,128)(2,1)S(1)}, bf16[4,16,32,128]{3,2,1,0:T(8,128)(2,1)}, u32[]{:S(2)}) copy-start(bf16[4,16,32,128]{3,2,1,0:T(8,128)(2,1)} %param.3) | copy-start | bytes 1572868
  6.2 1.1 %copy-start.1 = (bf16[4,16,32,128]{3,2,1,0:T(8,128)(2,1)S(1)}, bf16[4,16,32,128]{3,2,1,0:T(8,128)(2,1)}, u32[]{:S(2)}) copy-start(bf16[4,16,32,128]{3,2,1,0:T(8,128)(2,1)} %param.4) | copy-start | bytes 1572868
  7.4 7.6 %collective-permute-start.1 = (bf16[1,18,32,128]{3,2,1,0:T(8,128)(2,1)S(1)}, bf16[1,18,32,128]{3,2,1,0:T(8,128)(2,1)S(1)}, u32[]{:S(2)}, u32[]{:S(2)}) collective-permute-start(bf16[1,18,32,128]{3,2,1,0:T(8,128)(2,1)S(1)} %get-tuple-element.6), channel_id=1, source_target_pairs={{0,4},{4,8},{8,12},{12,0},{1,5},{5,9},{9,13},{13,1},{2,6},{6,10},{... | collective-permute-start | bytes 442376 | tf_op jit(solution)/shard_map/ppermute | solution.py:23
  9.1 2.1 %copy-start.3 = (bf16[4,16,32,128]{3,2,1,0:T(8,128)(2,1)S(1)}, bf16[4,16,32,128]{3,2,1,0:T(8,128)(2,1)}, u32[]{:S(2)}) copy-start(bf16[4,16,32,128]{3,2,1,0:T(8,128)(2,1)} %param.3) | copy-start | bytes 1572868
  12.5 5.4 %collective-permute-start.2 = (bf16[1,18,32,128]{3,2,1,0:T(8,128)(2,1)S(1)}, bf16[1,18,32,128]{3,2,1,0:T(8,128)(2,1)S(1)}, u32[]{:S(2)}, u32[]{:S(2)}) collective-permute-start(bf16[1,18,32,128]{3,2,1,0:T(8,128)(2,1)S(1)} %get-tuple-element.7), channel_id=1, source_target_pairs={{4,0},{8,4},{12,8},{0,12},{5,1},{9,5},{13,9},{1,13},{6,2},{10,6},{... | collective-permute-start | bytes 442376 | tf_op jit(solution)/shard_map/ppermute | solution.py:24
  25.0 7.3 %collective-permute-start.3 = (f32[4,216,64]{1,2,0:T(8,128)S(1)}, f32[4,216,64]{1,2,0:T(8,128)S(1)}, u32[]{:S(2)}, u32[]{:S(2)}) collective-permute-start(f32[4,216,64]{1,2,0:T(8,128)S(1)} %slice_select_fusion.1), channel_id=1, source_target_pairs={{0,2},{2,0},{1,3},{3,1},{4,6},{6,4},{5,7},{7,5},{8,10},{10,8},{9,1... | collective-permute-start | bytes 663560 | tf_op jit(solution)/shard_map/ppermute | solution.py:118
  26.8 0.7 %copy-start.4 = (pred[8,5]{0,1:T(8,128)(4,1)S(1)}, pred[8,5]{0,1:T(8,128)(4,1)}, u32[]{:S(2)}) copy-start(pred[8,5]{0,1:T(8,128)(4,1)} %constant.89) | copy-start | bytes 124
  32.6 7.5 %collective-permute-start.7 = (f32[4,216,64]{1,2,0:T(8,128)S(1)}, f32[4,216,64]{1,2,0:T(8,128)S(1)}, u32[]{:S(2)}, u32[]{:S(2)}) collective-permute-start(f32[4,216,64]{1,2,0:T(8,128)S(1)} %get-tuple-element.5), channel_id=1, source_target_pairs={{0,2},{2,0},{1,3},{3,1},{4,6},{6,4},{5,7},{7,5},{8,10},{10,8},{9,1... | collective-permute-start | bytes 663560 | tf_op jit(solution)/shard_map/ppermute | solution.py:118
  34.5 8.8 %collective-permute-start.4 = (f32[216,64]{0,1:T(8,128)S(1)}, f32[216,64]{0,1:T(8,128)S(1)}, u32[]{:S(2)}, u32[]{:S(2)}) collective-permute-start(f32[216,64]{0,1:T(8,128)S(1)} %get-tuple-element.10), channel_id=1, source_target_pairs={{0,4},{4,8},{8,12},{12,0},{1,5},{5,9},{9,13},{13,1},{2,6},{6,10},{... | collective-permute-start | bytes 165896 | tf_op jit(solution)/shard_map/ppermute | solution.py:51
  36.2 7.8 %collective-permute-start.5 = (f32[216,64]{0,1:T(8,128)S(1)}, f32[216,64]{0,1:T(8,128)S(1)}, u32[]{:S(2)}, u32[]{:S(2)}) collective-permute-start(f32[216,64]{0,1:T(8,128)S(1)} %get-tuple-element.12), channel_id=1, source_target_pairs={{0,8},{4,12},{8,0},{12,4},{1,9},{5,13},{9,1},{13,5},{2,10},{6,14},... | collective-permute-start | bytes 165896 | tf_op jit(solution)/shard_map/ppermute | solution.py:51
  39.2 5.6 %collective-permute-start.6 = (f32[216,64]{0,1:T(8,128)S(1)}, f32[216,64]{0,1:T(8,128)S(1)}, u32[]{:S(2)}, u32[]{:S(2)}) collective-permute-start(f32[216,64]{0,1:T(8,128)S(1)} %get-tuple-element.11), channel_id=1, source_target_pairs={{0,12},{4,0},{8,4},{12,8},{1,13},{5,1},{9,5},{13,9},{2,14},{6,2},{... | collective-permute-start | bytes 165896 | tf_op jit(solution)/shard_map/ppermute | solution.py:51
  40.3 5.4 %collective-permute-start.10 = (f32[216,64]{0,1:T(8,128)S(1)}, f32[216,64]{0,1:T(8,128)S(1)}, u32[]{:S(2)}, u32[]{:S(2)}) collective-permute-start(f32[216,64]{0,1:T(8,128)S(1)} %get-tuple-element.14), channel_id=1, source_target_pairs={{0,12},{4,0},{8,4},{12,8},{1,13},{5,1},{9,5},{13,9},{2,14},{6,2},{... | collective-permute-start | bytes 165896 | tf_op jit(solution)/shard_map/ppermute | solution.py:51
  43.3 6.1 %collective-permute-start.8 = (f32[216,64]{0,1:T(8,128)S(1)}, f32[216,64]{0,1:T(8,128)S(1)}, u32[]{:S(2)}, u32[]{:S(2)}) collective-permute-start(f32[216,64]{0,1:T(8,128)S(1)} %get-tuple-element.13), channel_id=1, source_target_pairs={{0,4},{4,8},{8,12},{12,0},{1,5},{5,9},{9,13},{13,1},{2,6},{6,10},{... | collective-permute-start | bytes 165896 | tf_op jit(solution)/shard_map/ppermute | solution.py:51
  43.3 6.1 %collective-permute-start.9 = (f32[216,64]{0,1:T(8,128)S(1)}, f32[216,64]{0,1:T(8,128)S(1)}, u32[]{:S(2)}, u32[]{:S(2)}) collective-permute-start(f32[216,64]{0,1:T(8,128)S(1)} %get-tuple-element.15), channel_id=1, source_target_pairs={{0,8},{4,12},{8,0},{12,4},{1,9},{5,13},{9,1},{13,5},{2,10},{6,14},... | collective-permute-start | bytes 165896 | tf_op jit(solution)/shard_map/ppermute | solution.py:51

commit v23 on v19

--- a/solution.py
+++ b/solution.py
@@ -105,9 +105,10 @@
             jnp.stack([take_rows(pieces, (gx * 2 + y) * owned_rows, owned_rows) for gx in range(nx)])
             for y in range(2)
         ]
-        split = owned_rows // 2 if owned_rows % 16 == 0 else owned_rows
+        cuts = 3 if owned_rows % 24 == 0 else 1
+        bounds = [owned_rows * k // cuts for k in range(cuts + 1)]
         parts = []
-        for lo, hi in ((0, split), (split, owned_rows)):
+        for lo, hi in zip(bounds[:-1], bounds[1:]):
             if lo == hi:
                 continue
             keep = jnp.where(iy == 0, side[0][:, lo:hi], side[1][:, lo:hi])

time: 49.9 us -> 63.3 us (1.27)
  waiting for transfers between devices: 11.4 us -> 18 us
  starting transfers between devices: 17 us -> 23.4 us
    ppermute x2 -> x3, waiting for transfers between devices: 0.67 us -> 8.32 us  [on_device(): partial = keep + lax.ppermute(send, 'gy', [(0, 1), (1, 0)])]
    ppermute x6 -> x9, starting transfers between devices: 7.65 us -> 12.7 us  [scatter_sum(): lax.ppermute(part, axis, [(j, (j + shift) % count) for j in range(count)])]
    ppermute x2 -> x3, starting transfers between devices: 2.15 us -> 3.51 us  [on_device(): partial = keep + lax.ppermute(send, 'gy', [(0, 1), (1, 0)])]
    ppermute x6 -> x9, waiting for transfers between devices: 5.41 us -> 4.35 us  [scatter_sum(): lax.ppermute(part, axis, [(j, (j + shift) % count) for j in range(count)])]
  transfers between devices with their start and end apart: 11 -> 15, of which waited for: 6 -> 9; matrix products, arithmetic and copies ran while one was open for 18% -> 14% of each run, Pallas kernels for 0% -> 0%
where the time goes in v23:
time: 63.3 us; the launch traced here: 63.1 us
  starting transfers between devices  23.4 us (37%)
  waiting for transfers between devices  18 us (28%)
  matrix products  9.09 us (14%)
  local copies, waits for them, and re-layouts  6.49 us (10%)
  other arithmetic  4.79 us (8%)
  between operations  1.23 us (2%)
    ppermute x9, starting transfers between devices, scatter_sum(): lax.ppermute(part, axis, [(j, (j + shift) % count) for j in range(count)])  12.7 us
    ppermute x3, waiting for transfers between devices, on_device(): partial = keep + lax.ppermute(send, 'gy', [(0, 1), (1, 0)])  8.32 us
    conv_general_dilated x1, matrix products, on_device(): lax.conv_general_dilated(gh[None], kflip, (1, 1, 1), pad, dimension_numbe...  4.94 us
    ppermute x9, waiting for transfers between devices, scatter_sum(): lax.ppermute(part, axis, [(j, (j + shift) % count) for j in range(count)])  4.35 us
    ppermute x1, waiting for transfers between devices, halo_parts(): low = lax.ppermute(tail, axis, [(i, (i + 1) % count) for i in range(count)])  4.23 us
    dot_general x9, matrix products, on_device(): lax.dot_general(x_act, window, (((0, 1, 2), (0, 1, 2)), ((), ())), prefer...  4.15 us
    ppermute x3, starting transfers between devices, on_device(): partial = keep + lax.ppermute(send, 'gy', [(0, 1), (1, 0)])  3.51 us
    ppermute x1, starting transfers between devices, halo_parts(): recv = lax.ppermute(jnp.where(me == 0, tail, head), axis, [(0, 1), (1, 0)])  2.94 us
  transfers between devices with their start and end apart: 15, of which 9 were waited for; matrix products, arithmetic and copies ran while one was open for 14% of the time, Pallas kernels for 0%

profile of v23, /device:TPU:0, one launch (start us, length us, event | category | flops | bytes accessed | tf_op | source)
XLA Modules:
  0.0 63.1 jit_solution(9183438976970147763)
XLA Ops:
  0.7 0.9 %slice_select_fusion.3 = bf16[4,1,32,128]{3,2,1,0:T(8,128)(2,1)S(1)} fusion(bf16[4,16,32,128]{3,2,1,0:T(8,128)(2,1)} %param.4, pred[]{:T(512)S(6)} %eq.34), kind=kLoop, calls=%fused_computation.66 | loop fusion | flops 16384 | bytes 98305 | tf_op jit(solution)/shard_map/jit(_where)/select_n | solution.py:18
  1.6 2.9 %collective-permute-start = (bf16[4,1,32,128]{3,2,1,0:T(8,128)(2,1)S(1)}, bf16[4,1,32,128]{3,2,1,0:T(8,128)(2,1)S(1)}, u32[]{:S(2)}, u32[]{:S(2)}) collective-permute-start(bf16[4,1,32,128]{3,2,1,0:T(8,128)(2,1)S(1)} %slice_select_fusion.3), channel_id=1, source_target_pairs={{0,2},{2,0},{1,3},{3,1},{4,6},{6,4},{5,7},{7,5},{8,10},{10,8},{9,1... | collective-permute-start | bytes 98312 | tf_op jit(solution)/shard_map/ppermute | solution.py:18
  4.5 1.5 %fusion.24 = (bf16[4,16,32,64]{3,2,1,0:T(8,128)(2,1)S(1)}, bf16[4,16,32,64]{3,2,1,0:T(8,128)(2,1)S(1)}) fusion(bf16[4,16,32,128]{3,2,1,0:T(8,128)(2,1)} %param.4), kind=kLoop, calls=%fused_computation.72 | loop fusion | bytes 1048576 | tf_op jit(solution)/shard_map/slice | solution.py:33
  6.1 0.3 collective-permute-done
  6.5 2.2 %collective-permute-start.1 = (bf16[1,18,32,128]{3,2,1,0:T(8,128)(2,1)S(1)}, bf16[1,18,32,128]{3,2,1,0:T(8,128)(2,1)S(1)}, u32[]{:S(2)}, u32[]{:S(2)}) collective-permute-start(bf16[1,18,32,128]{3,2,1,0:T(8,128)(2,1)S(1)} %get-tuple-element.11), channel_id=1, source_target_pairs={{0,4},{4,8},{8,12},{12,0},{1,5},{5,9},{9,13},{13,1},{2,6},{6,10},{... | collective-permute-start | bytes 442376 | tf_op jit(solution)/shard_map/ppermute | solution.py:23
  8.6 2.1 %collective-permute-start.2 = (bf16[1,18,32,128]{3,2,1,0:T(8,128)(2,1)S(1)}, bf16[1,18,32,128]{3,2,1,0:T(8,128)(2,1)S(1)}, u32[]{:S(2)}, u32[]{:S(2)}) collective-permute-start(bf16[1,18,32,128]{3,2,1,0:T(8,128)(2,1)S(1)} %get-tuple-element.12), channel_id=1, source_target_pairs={{4,0},{8,4},{12,8},{0,12},{5,1},{9,5},{13,9},{1,13},{6,2},{10,6},{... | collective-permute-start | bytes 442376 | tf_op jit(solution)/shard_map/ppermute | solution.py:24
  10.8 4.2 %collective-permute-done.1 = bf16[1,18,32,128]{3,2,1,0:T(8,128)(2,1)S(1)} collective-permute-done((bf16[1,18,32,128]{3,2,1,0:T(8,128)(2,1)S(1)}, bf16[1,18,32,128]{3,2,1,0:T(8,128)(2,1)S(1)}, u32[]{:S(2)}, u32[]{:S(2)}) %collective-permute-start.1) | collective-permute-done | bytes 147488 | tf_op jit(solution)/shard_map/ppermute | solution.py:23
  15.2 0.8 %collective-permute-done.2 = bf16[1,18,32,128]{3,2,1,0:T(8,128)(2,1)S(1)} collective-permute-done((bf16[1,18,32,128]{3,2,1,0:T(8,128)(2,1)S(1)}, bf16[1,18,32,128]{3,2,1,0:T(8,128)(2,1)S(1)}, u32[]{:S(2)}, u32[]{:S(2)}) %collective-permute-start.2) | collective-permute-done | bytes 147488 | tf_op jit(solution)/shard_map/ppermute | solution.py:24
  16.1 0.5 maximum_select_fusion
  16.7 0.8 %pad_slice_fusion.1 = (bf16[6,18,32,64]{3,2,1,0:T(8,128)(2,1)S(1)}, bf16[6,18,32,64]{3,2,1,0:T(8,128)(2,1)S(1)}) fusion(bf16[6,18,32,64]{3,2,1,0:T(8,128)(2,1)S(1)} %maximum_select_fusion), kind=kLoop, calls=%fused_computation.12 | loop fusion | bytes 1327104 | tf_op jit(solution)/shard_map/slice | solution.py:90
  17.4 0.9 %pad_maximum_fusion = bf16[6,18,32,192]{3,2,1,0:T(8,128)(2,1)S(1)} fusion(bf16[6,18,32,64]{3,2,1,0:T(8,128)(2,1)S(1)} %get-tuple-element.10, bf16[6,18,32,64]{3,2,1,0:T(8,128)(2,1)S(1)} %maximum_select_fusion, bf16[6,18,32,64]{3,2,1,0:T(8,128)(2,1)S(1)} %get-tuple-element.9), kind=kLoop, calls=%fused_computation.2 | loop fusion | flops 3981312 | bytes 2654208 | tf_op jit(solution)/shard_map/concatenate | solution.py:90
  18.3 0.2 copy-done.2
  18.5 0.5 fusion.31
  18.9 0.5 fusion.30
  19.4 0.5 fusion.32
  19.9 0.5 fusion.33
  20.3 0.5 fusion.34
  20.8 0.5 fusion.35
  21.3 0.5 fusion.36
  21.7 0.5 fusion.37
  23.0 0.5 fusion.38
  23.5 0.2 maximum_bitcast_fusion
  25.2 1.5 %collective-permute-start.3 = (f32[4,144,64]{1,2,0:T(8,128)S(1)}, f32[4,144,64]{1,2,0:T(8,128)S(1)}, u32[]{:S(2)}, u32[]{:S(2)}) collective-permute-start(f32[4,144,64]{1,2,0:T(8,128)S(1)} %slice_select_fusion.2), channel_id=1, source_target_pairs={{0,2},{2,0},{1,3},{3,1},{4,6},{6,4},{5,7},{7,5},{8,10},{10,8},{9,1... | collective-permute-start | bytes 442376 | tf_op jit(solution)/shard_map/ppermute | solution.py:116
  26.6 0.4 copy.28
  27.0 0.2 pad.5.clone
  27.3 0.1 copy.7
  27.6 0.4 copy-done.3
  28.0 4.9 %fusion.11 = bf16[4,16,8,5,128]{4,2,3,1,0:T(8,128)(2,1)S(1)} fusion(bf16[3,3,3,128,128]{4,3,2,1,0:T(8,128)(2,1)S(1)} %bitcast.213, bf16[6,18,1,7,2,128]{5,3,4,1,0,2:T(8,128)(2,1)S(1)} %slice.189, bf16[6,18,1,8,5,128]{5,3,4,1,0,2:T(8,128)(2,1)S(1)} %copy.7, pred[8,5]{0,1:T(8,128)(4,1)S(1)} %copy-done.3), kind=kOutput, calls=%fused_computation.10 | convolution fusion | flops 2270224384 | bytes 3033128 | tf_op jit(solution)/shard_map/conv_general_dilated | solution.py:77
  33.0 0.4 select_add_fusion.2
  33.4 1.2 %collective-permute-start.4 = (f32[144,64]{0,1:T(8,128)S(1)}, f32[144,64]{0,1:T(8,128)S(1)}, u32[]{:S(2)}, u32[]{:S(2)}) collective-permute-start(f32[144,64]{0,1:T(8,128)S(1)} %get-tuple-element.15), channel_id=1, source_target_pairs={{0,4},{4,8},{8,12},{12,0},{1,5},{5,9},{9,13},{13,1},{2,6},{6,10},{... | collective-permute-start | bytes 110600 | tf_op jit(solution)/shard_map/ppermute | solution.py:51
  34.6 2.3 %collective-permute-start.5 = (f32[144,64]{0,1:T(8,128)S(1)}, f32[144,64]{0,1:T(8,128)S(1)}, u32[]{:S(2)}, u32[]{:S(2)}) collective-permute-start(f32[144,64]{0,1:T(8,128)S(1)} %get-tuple-element.17), channel_id=1, source_target_pairs={{0,8},{4,12},{8,0},{12,4},{1,9},{5,13},{9,1},{13,5},{2,10},{6,14},... | collective-permute-start | bytes 110600 | tf_op jit(solution)/shard_map/ppermute | solution.py:51
  36.9 0.7 %collective-permute-start.6 = (f32[144,64]{0,1:T(8,128)S(1)}, f32[144,64]{0,1:T(8,128)S(1)}, u32[]{:S(2)}, u32[]{:S(2)}) collective-permute-start(f32[144,64]{0,1:T(8,128)S(1)} %get-tuple-element.16), channel_id=1, source_target_pairs={{0,12},{4,0},{8,4},{12,8},{1,13},{5,1},{9,5},{13,9},{2,14},{6,2},{... | collective-permute-start | bytes 110600 | tf_op jit(solution)/shard_map/ppermute | solution.py:51
  37.6 0.9 %copy.18 = bf16[4,16,32,128]{3,2,1,0:T(8,128)(2,1)} copy(bf16[4,16,32,128]{3,1,2,0:T(8,128)(2,1)S(1)} %slice_bitcast_fusion) | data formatting | bytes 1048576
  38.5 0.6 collective-permute-start.11
  39.1 1.4 %collective-permute-start.7 = (f32[4,144,64]{1,2,0:T(8,128)S(1)}, f32[4,144,64]{1,2,0:T(8,128)S(1)}, u32[]{:S(2)}, u32[]{:S(2)}) collective-permute-start(f32[4,144,64]{1,2,0:T(8,128)S(1)} %get-tuple-element.5), channel_id=1, source_target_pairs={{0,2},{2,0},{1,3},{3,1},{4,6},{6,4},{5,7},{7,5},{8,10},{10,8},{9,1... | collective-permute-start | bytes 442376 | tf_op jit(solution)/shard_map/ppermute | solution.py:116
  40.5 0.4 collective-permute-done.5
  41.0 0.7 %collective-permute-done.6 = f32[144,64]{0,1:T(8,128)S(1)} collective-permute-done((f32[144,64]{0,1:T(8,128)S(1)}, f32[144,64]{0,1:T(8,128)S(1)}, u32[]{:S(2)}, u32[]{:S(2)}) %collective-permute-start.6) | collective-permute-done | bytes 36896 | tf_op jit(solution)/shard_map/ppermute | solution.py:51
  41.7 5.5 %collective-permute-done.11 = f32[4,144,64]{1,2,0:T(8,128)S(1)} collective-permute-done((f32[4,144,64]{1,2,0:T(8,128)S(1)}, f32[4,144,64]{1,2,0:T(8,128)S(1)}, u32[]{:S(2)}, u32[]{:S(2)}) %collective-permute-start.11) | collective-permute-done | bytes 147488 | tf_op jit(solution)/shard_map/ppermute | solution.py:116
  47.2 2.8 %collective-permute-done.7 = f32[4,144,64]{1,2,0:T(8,128)S(1)} collective-permute-done((f32[4,144,64]{1,2,0:T(8,128)S(1)}, f32[4,144,64]{1,2,0:T(8,128)S(1)}, u32[]{:S(2)}, u32[]{:S(2)}) %collective-permute-start.7) | collective-permute-done | bytes 147488 | tf_op jit(solution)/shard_map/ppermute | solution.py:116
  50.0 0.3 select_add_fusion.1
  50.4 1.7 %collective-permute-start.10 = (f32[144,64]{0,1:T(8,128)S(1)}, f32[144,64]{0,1:T(8,128)S(1)}, u32[]{:S(2)}, u32[]{:S(2)}) collective-permute-start(f32[144,64]{0,1:T(8,128)S(1)} %get-tuple-element.19), channel_id=1, source_target_pairs={{0,12},{4,0},{8,4},{12,8},{1,13},{5,1},{9,5},{13,9},{2,14},{6,2},{... | collective-permute-start | bytes 110600 | tf_op jit(solution)/shard_map/ppermute | solution.py:51
  52.1 0.4 collective-permute-start.8
  52.4 1.3 %collective-permute-start.9 = (f32[144,64]{0,1:T(8,128)S(1)}, f32[144,64]{0,1:T(8,128)S(1)}, u32[]{:S(2)}, u32[]{:S(2)}) collective-permute-start(f32[144,64]{0,1:T(8,128)S(1)} %get-tuple-element.20), channel_id=1, source_target_pairs={{0,8},{4,12},{8,0},{12,4},{1,9},{5,13},{9,1},{13,5},{2,10},{6,14},... | collective-permute-start | bytes 110600 | tf_op jit(solution)/shard_map/ppermute | solution.py:51
  53.8 2.7 %collective-permute-start.12 = (f32[144,64]{0,1:T(8,128)S(1)}, f32[144,64]{0,1:T(8,128)S(1)}, u32[]{:S(2)}, u32[]{:S(2)}) collective-permute-start(f32[144,64]{0,1:T(8,128)S(1)} %get-tuple-element.21), channel_id=1, source_target_pairs={{0,4},{4,8},{8,12},{12,0},{1,5},{5,9},{9,13},{13,1},{2,6},{6,10},{... | collective-permute-start | bytes 110600 | tf_op jit(solution)/shard_map/ppermute | solution.py:51
  56.5 2.4 %collective-permute-start.14 = (f32[144,64]{0,1:T(8,128)S(1)}, f32[144,64]{0,1:T(8,128)S(1)}, u32[]{:S(2)}, u32[]{:S(2)}) collective-permute-start(f32[144,64]{0,1:T(8,128)S(1)} %get-tuple-element.22), channel_id=1, source_target_pairs={{0,12},{4,0},{8,4},{12,8},{1,13},{5,1},{9,5},{13,9},{2,14},{6,2},{... | collective-permute-start | bytes 110600 | tf_op jit(solution)/shard_map/ppermute | solution.py:51
  59.0 1.4 %collective-permute-done.9 = f32[144,64]{0,1:T(8,128)S(1)} collective-permute-done((f32[144,64]{0,1:T(8,128)S(1)}, f32[144,64]{0,1:T(8,128)S(1)}, u32[]{:S(2)}, u32[]{:S(2)}) %collective-permute-start.9) | collective-permute-done | bytes 36896 | tf_op jit(solution)/shard_map/ppermute | solution.py:51
  60.4 1.8 %collective-permute-done.13 = f32[144,64]{0,1:T(8,128)S(1)} collective-permute-done((f32[144,64]{0,1:T(8,128)S(1)}, f32[144,64]{0,1:T(8,128)S(1)}, u32[]{:S(2)}, u32[]{:S(2)}) %collective-permute-start.13) | collective-permute-done | bytes 36896 | tf_op jit(solution)/shard_map/ppermute | solution.py:51
  62.3 0.8 %maximum_multiply_fusion = f32[432,64]{0,1:T(8,128)} fusion(f32[144,64]{0,1:T(8,128)S(1)} %fusion.16, f32[144,64]{0,1:T(8,128)S(1)} %fusion.18, f32[144,64]{0,1:T(8,128)S(1)} %fusion.20), kind=kLoop, calls=%fused_computation.38 | loop fusion | flops 82944 | bytes 221184 | tf_op jit(solution)/shard_map/div | solution.py:124
  (69 shorter events, 2.9 us)
Async XLA Ops:
  0.6 26.9 %copy-start = (bf16[27,128,128]{2,1,0:T(8,128)(2,1)S(1)}, bf16[27,128,128]{2,1,0:T(8,128)(2,1)}, u32[]{:S(2)}) copy-start(bf16[27,128,128]{2,1,0:T(8,128)(2,1)} %param.5) | copy-start | bytes 2654212
  0.6 5.8 %copy-start.1 = (bf16[4,16,32,128]{3,2,1,0:T(8,128)(2,1)S(1)}, bf16[4,16,32,128]{3,2,1,0:T(8,128)(2,1)}, u32[]{:S(2)}) copy-start(bf16[4,16,32,128]{3,2,1,0:T(8,128)(2,1)} %param.4) | copy-start | bytes 1572868
  1.6 4.8 %collective-permute-start = (bf16[4,1,32,128]{3,2,1,0:T(8,128)(2,1)S(1)}, bf16[4,1,32,128]{3,2,1,0:T(8,128)(2,1)S(1)}, u32[]{:S(2)}, u32[]{:S(2)}) collective-permute-start(bf16[4,1,32,128]{3,2,1,0:T(8,128)(2,1)S(1)} %slice_select_fusion.3), channel_id=1, source_target_pairs={{0,2},{2,0},{1,3},{3,1},{4,6},{6,4},{5,7},{7,5},{8,10},{10,8},{9,1... | collective-permute-start | bytes 98312 | tf_op jit(solution)/shard_map/ppermute | solution.py:18
  6.5 8.6 %collective-permute-start.1 = (bf16[1,18,32,128]{3,2,1,0:T(8,128)(2,1)S(1)}, bf16[1,18,32,128]{3,2,1,0:T(8,128)(2,1)S(1)}, u32[]{:S(2)}, u32[]{:S(2)}) collective-permute-start(bf16[1,18,32,128]{3,2,1,0:T(8,128)(2,1)S(1)} %get-tuple-element.11), channel_id=1, source_target_pairs={{0,4},{4,8},{8,12},{12,0},{1,5},{5,9},{9,13},{13,1},{2,6},{6,10},{... | collective-permute-start | bytes 442376 | tf_op jit(solution)/shard_map/ppermute | solution.py:23
  8.6 7.4 %collective-permute-start.2 = (bf16[1,18,32,128]{3,2,1,0:T(8,128)(2,1)S(1)}, bf16[1,18,32,128]{3,2,1,0:T(8,128)(2,1)S(1)}, u32[]{:S(2)}, u32[]{:S(2)}) collective-permute-start(bf16[1,18,32,128]{3,2,1,0:T(8,128)(2,1)S(1)} %get-tuple-element.12), channel_id=1, source_target_pairs={{4,0},{8,4},{12,8},{0,12},{5,1},{9,5},{13,9},{1,13},{6,2},{10,6},{... | collective-permute-start | bytes 442376 | tf_op jit(solution)/shard_map/ppermute | solution.py:24
  17.4 1.0 %copy-start.2 = (bf16[4,16,32,128]{3,2,1,0:T(8,128)(2,1)S(1)}, bf16[4,16,32,128]{3,2,1,0:T(8,128)(2,1)}, u32[]{:S(2)}) copy-start(bf16[4,16,32,128]{3,2,1,0:T(8,128)(2,1)} %param.3) | copy-start | bytes 1572868
  25.2 7.9 %collective-permute-start.3 = (f32[4,144,64]{1,2,0:T(8,128)S(1)}, f32[4,144,64]{1,2,0:T(8,128)S(1)}, u32[]{:S(2)}, u32[]{:S(2)}) collective-permute-start(f32[4,144,64]{1,2,0:T(8,128)S(1)} %slice_select_fusion.2), channel_id=1, source_target_pairs={{0,2},{2,0},{1,3},{3,1},{4,6},{6,4},{5,7},{7,5},{8,10},{10,8},{9,1... | collective-permute-start | bytes 442376 | tf_op jit(solution)/shard_map/ppermute | solution.py:116
  27.3 0.7 %copy-start.3 = (pred[8,5]{0,1:T(8,128)(4,1)S(1)}, pred[8,5]{0,1:T(8,128)(4,1)}, u32[]{:S(2)}) copy-start(pred[8,5]{0,1:T(8,128)(4,1)} %constant.91) | copy-start | bytes 124
  33.4 7.1 %collective-permute-start.4 = (f32[144,64]{0,1:T(8,128)S(1)}, f32[144,64]{0,1:T(8,128)S(1)}, u32[]{:S(2)}, u32[]{:S(2)}) collective-permute-start(f32[144,64]{0,1:T(8,128)S(1)} %get-tuple-element.15), channel_id=1, source_target_pairs={{0,4},{4,8},{8,12},{12,0},{1,5},{5,9},{9,13},{13,1},{2,6},{6,10},{... | collective-permute-start | bytes 110600 | tf_op jit(solution)/shard_map/ppermute | solution.py:51
  34.6 6.4 %collective-permute-start.5 = (f32[144,64]{0,1:T(8,128)S(1)}, f32[144,64]{0,1:T(8,128)S(1)}, u32[]{:S(2)}, u32[]{:S(2)}) collective-permute-start(f32[144,64]{0,1:T(8,128)S(1)} %get-tuple-element.17), channel_id=1, source_target_pairs={{0,8},{4,12},{8,0},{12,4},{1,9},{5,13},{9,1},{13,5},{2,10},{6,14},... | collective-permute-start | bytes 110600 | tf_op jit(solution)/shard_map/ppermute | solution.py:51
  36.9 4.8 %collective-permute-start.6 = (f32[144,64]{0,1:T(8,128)S(1)}, f32[144,64]{0,1:T(8,128)S(1)}, u32[]{:S(2)}, u32[]{:S(2)}) collective-permute-start(f32[144,64]{0,1:T(8,128)S(1)} %get-tuple-element.16), channel_id=1, source_target_pairs={{0,12},{4,0},{8,4},{12,8},{1,13},{5,1},{9,5},{13,9},{2,14},{6,2},{... | collective-permute-start | bytes 110600 | tf_op jit(solution)/shard_map/ppermute | solution.py:51
  38.5 8.7 %collective-permute-start.11 = (f32[4,144,64]{1,2,0:T(8,128)S(1)}, f32[4,144,64]{1,2,0:T(8,128)S(1)}, u32[]{:S(2)}, u32[]{:S(2)}) collective-permute-start(f32[4,144,64]{1,2,0:T(8,128)S(1)} %get-tuple-element.6), channel_id=1, source_target_pairs={{0,2},{2,0},{1,3},{3,1},{4,6},{6,4},{5,7},{7,5},{8,10},{10,8},{9,1... | collective-permute-start | bytes 442376 | tf_op jit(solution)/shard_map/ppermute | solution.py:116
  39.1 10.9 %collective-permute-start.7 = (f32[4,144,64]{1,2,0:T(8,128)S(1)}, f32[4,144,64]{1,2,0:T(8,128)S(1)}, u32[]{:S(2)}, u32[]{:S(2)}) collective-permute-start(f32[4,144,64]{1,2,0:T(8,128)S(1)} %get-tuple-element.5), channel_id=1, source_target_pairs={{0,2},{2,0},{1,3},{3,1},{4,6},{6,4},{5,7},{7,5},{8,10},{10,8},{9,1... | collective-permute-start | bytes 442376 | tf_op jit(solution)/shard_map/ppermute | solution.py:116
  50.4 6.2 %collective-permute-start.10 = (f32[144,64]{0,1:T(8,128)S(1)}, f32[144,64]{0,1:T(8,128)S(1)}, u32[]{:S(2)}, u32[]{:S(2)}) collective-permute-start(f32[144,64]{0,1:T(8,128)S(1)} %get-tuple-element.19), channel_id=1, source_target_pairs={{0,12},{4,0},{8,4},{12,8},{1,13},{5,1},{9,5},{13,9},{2,14},{6,2},{... | collective-permute-start | bytes 110600 | tf_op jit(solution)/shard_map/ppermute | solution.py:51
  52.1 6.9 %collective-permute-start.8 = (f32[144,64]{0,1:T(8,128)S(1)}, f32[144,64]{0,1:T(8,128)S(1)}, u32[]{:S(2)}, u32[]{:S(2)}) collective-permute-start(f32[144,64]{0,1:T(8,128)S(1)} %get-tuple-element.18), channel_id=1, source_target_pairs={{0,4},{4,8},{8,12},{12,0},{1,5},{5,9},{9,13},{13,1},{2,6},{6,10},{... | collective-permute-start | bytes 110600 | tf_op jit(solution)/shard_map/ppermute | solution.py:51
  52.4 8.0 %collective-permute-start.9 = (f32[144,64]{0,1:T(8,128)S(1)}, f32[144,64]{0,1:T(8,128)S(1)}, u32[]{:S(2)}, u32[]{:S(2)}) collective-permute-start(f32[144,64]{0,1:T(8,128)S(1)} %get-tuple-element.20), channel_id=1, source_target_pairs={{0,8},{4,12},{8,0},{12,4},{1,9},{5,13},{9,1},{13,5},{2,10},{6,14},... | collective-permute-start | bytes 110600 | tf_op jit(solution)/shard_map/ppermute | solution.py:51
  53.8 6.6 %collective-permute-start.12 = (f32[144,64]{0,1:T(8,128)S(1)}, f32[144,64]{0,1:T(8,128)S(1)}, u32[]{:S(2)}, u32[]{:S(2)}) collective-permute-start(f32[144,64]{0,1:T(8,128)S(1)} %get-tuple-element.21), channel_id=1, source_target_pairs={{0,4},{4,8},{8,12},{12,0},{1,5},{5,9},{9,13},{13,1},{2,6},{6,10},{... | collective-permute-start | bytes 110600 | tf_op jit(solution)/shard_map/ppermute | solution.py:51
  56.5 5.7 %collective-permute-start.13 = (f32[144,64]{0,1:T(8,128)S(1)}, f32[144,64]{0,1:T(8,128)S(1)}, u32[]{:S(2)}, u32[]{:S(2)}) collective-permute-start(f32[144,64]{0,1:T(8,128)S(1)} %get-tuple-element.23), channel_id=1, source_target_pairs={{0,8},{4,12},{8,0},{12,4},{1,9},{5,13},{9,1},{13,5},{2,10},{6,14},... | collective-permute-start | bytes 110600 | tf_op jit(solution)/shard_map/ppermute | solution.py:51
  56.5 5.7 %collective-permute-start.14 = (f32[144,64]{0,1:T(8,128)S(1)}, f32[144,64]{0,1:T(8,128)S(1)}, u32[]{:S(2)}, u32[]{:S(2)}) collective-permute-start(f32[144,64]{0,1:T(8,128)S(1)} %get-tuple-element.22), channel_id=1, source_target_pairs={{0,12},{4,0},{8,4},{12,8},{1,13},{5,1},{9,5},{13,9},{2,14},{6,2},{... | collective-permute-start | bytes 110600 | tf_op jit(solution)/shard_map/ppermute | solution.py:51

commit v24 on v19

--- a/solution.py
+++ b/solution.py
@@ -46,7 +46,7 @@
         return lax.psum_scatter(blocks, axis, scatter_dimension=dim, tiled=False)
     me = lax.axis_index(axis)
     total = lax.dynamic_index_in_dim(blocks, me, dim, keepdims=False)
-    for shift in range(1, count):
+    for shift in sorted(range(1, count), key=lambda s: -min(s, count - s)):
         part = lax.dynamic_index_in_dim(blocks, (me + shift) % count, dim, keepdims=False)
         total = total + lax.ppermute(part, axis, [(j, (j + shift) % count) for j in range(count)])
     return total

time: 49.9 us -> 50.2 us (level)
  starting transfers between devices: 17 us -> 17.7 us
    ppermute x6, starting transfers between devices: 7.65 us -> 8.33 us  [scatter_sum(): lax.ppermute(part, axis, [(j, (j + shift) % count) for j in range(count)])]
    ppermute x2, waiting for transfers between devices: 0.67 us -> 0.01 us  [on_device(): partial = keep + lax.ppermute(send, 'gy', [(0, 1), (1, 0)])]
where the time goes in v24:
time: 50.2 us; the launch traced here: 50 us
  starting transfers between devices  17.7 us (35%)
  waiting for transfers between devices  11 us (22%)
  matrix products  9.11 us (18%)
  local copies, waits for them, and re-layouts  6.47 us (13%)
  other arithmetic  4.48 us (9%)
  between operations  1.21 us (2%)
    ppermute x6, starting transfers between devices, scatter_sum(): lax.ppermute(part, axis, [(j, (j + shift) % count) for j in range(count)])  8.33 us
    ppermute x6, waiting for transfers between devices, scatter_sum(): lax.ppermute(part, axis, [(j, (j + shift) % count) for j in range(count)])  5.68 us
    conv_general_dilated x1, matrix products, on_device(): lax.conv_general_dilated(gh[None], kflip, (1, 1, 1), pad, dimension_numbe...  4.96 us
    ppermute x1, waiting for transfers between devices, halo_parts(): low = lax.ppermute(tail, axis, [(i, (i + 1) % count) for i in range(count)])  4.23 us
    dot_general x9, matrix products, on_device(): lax.dot_general(x_act, window, (((0, 1, 2), (0, 1, 2)), ((), ())), prefer...  4.15 us
    ppermute x1, starting transfers between devices, halo_parts(): recv = lax.ppermute(jnp.where(me == 0, tail, head), axis, [(0, 1), (1, 0)])  2.94 us
    ppermute x1, starting transfers between devices, halo_parts(): low = lax.ppermute(tail, axis, [(i, (i + 1) % count) for i in range(count)])  2.16 us
    ppermute x2, starting transfers between devices, on_device(): partial = keep + lax.ppermute(send, 'gy', [(0, 1), (1, 0)])  2.15 us
  transfers between devices with their start and end apart: 11, of which 6 were waited for; matrix products, arithmetic and copies ran while one was open for 18% of the time, Pallas kernels for 0%

profile of v24, /device:TPU:0, one launch (start us, length us, event | category | flops | bytes accessed | tf_op | source)
XLA Modules:
  0.0 50.0 jit_solution(16678183959157852971)
XLA Ops:
  0.7 0.9 %slice_select_fusion.2 = bf16[4,1,32,128]{3,2,1,0:T(8,128)(2,1)S(1)} fusion(bf16[4,16,32,128]{3,2,1,0:T(8,128)(2,1)} %param.4, pred[]{:T(512)S(6)} %eq.29), kind=kLoop, calls=%fused_computation.58 | loop fusion | flops 16384 | bytes 98305 | tf_op jit(solution)/shard_map/jit(_where)/select_n | solution.py:18
  1.6 2.9 %collective-permute-start = (bf16[4,1,32,128]{3,2,1,0:T(8,128)(2,1)S(1)}, bf16[4,1,32,128]{3,2,1,0:T(8,128)(2,1)S(1)}, u32[]{:S(2)}, u32[]{:S(2)}) collective-permute-start(bf16[4,1,32,128]{3,2,1,0:T(8,128)(2,1)S(1)} %slice_select_fusion.2), channel_id=1, source_target_pairs={{0,2},{2,0},{1,3},{3,1},{4,6},{6,4},{5,7},{7,5},{8,10},{10,8},{9,1... | collective-permute-start | bytes 98312 | tf_op jit(solution)/shard_map/ppermute | solution.py:18
  4.5 1.5 %fusion.22 = (bf16[4,16,32,64]{3,2,1,0:T(8,128)(2,1)S(1)}, bf16[4,16,32,64]{3,2,1,0:T(8,128)(2,1)S(1)}) fusion(bf16[4,16,32,128]{3,2,1,0:T(8,128)(2,1)} %param.4), kind=kLoop, calls=%fused_computation.64 | loop fusion | bytes 1048576 | tf_op jit(solution)/shard_map/slice | solution.py:33
  6.1 0.3 collective-permute-done
  6.5 2.2 %collective-permute-start.1 = (bf16[1,18,32,128]{3,2,1,0:T(8,128)(2,1)S(1)}, bf16[1,18,32,128]{3,2,1,0:T(8,128)(2,1)S(1)}, u32[]{:S(2)}, u32[]{:S(2)}) collective-permute-start(bf16[1,18,32,128]{3,2,1,0:T(8,128)(2,1)S(1)} %get-tuple-element.8), channel_id=1, source_target_pairs={{0,4},{4,8},{8,12},{12,0},{1,5},{5,9},{9,13},{13,1},{2,6},{6,10},{... | collective-permute-start | bytes 442376 | tf_op jit(solution)/shard_map/ppermute | solution.py:23
  8.6 2.1 %collective-permute-start.2 = (bf16[1,18,32,128]{3,2,1,0:T(8,128)(2,1)S(1)}, bf16[1,18,32,128]{3,2,1,0:T(8,128)(2,1)S(1)}, u32[]{:S(2)}, u32[]{:S(2)}) collective-permute-start(bf16[1,18,32,128]{3,2,1,0:T(8,128)(2,1)S(1)} %get-tuple-element.9), channel_id=1, source_target_pairs={{4,0},{8,4},{12,8},{0,12},{5,1},{9,5},{13,9},{1,13},{6,2},{10,6},{... | collective-permute-start | bytes 442376 | tf_op jit(solution)/shard_map/ppermute | solution.py:24
  10.8 4.2 %collective-permute-done.1 = bf16[1,18,32,128]{3,2,1,0:T(8,128)(2,1)S(1)} collective-permute-done((bf16[1,18,32,128]{3,2,1,0:T(8,128)(2,1)S(1)}, bf16[1,18,32,128]{3,2,1,0:T(8,128)(2,1)S(1)}, u32[]{:S(2)}, u32[]{:S(2)}) %collective-permute-start.1) | collective-permute-done | bytes 147488 | tf_op jit(solution)/shard_map/ppermute | solution.py:23
  15.1 0.1 fusion.23
  15.2 0.8 %collective-permute-done.2 = bf16[1,18,32,128]{3,2,1,0:T(8,128)(2,1)S(1)} collective-permute-done((bf16[1,18,32,128]{3,2,1,0:T(8,128)(2,1)S(1)}, bf16[1,18,32,128]{3,2,1,0:T(8,128)(2,1)S(1)}, u32[]{:S(2)}, u32[]{:S(2)}) %collective-permute-start.2) | collective-permute-done | bytes 147488 | tf_op jit(solution)/shard_map/ppermute | solution.py:24
  16.0 0.1 fusion.24
  16.1 0.5 %maximum_select_fusion = bf16[6,18,32,64]{3,2,1,0:T(8,128)(2,1)S(1)} fusion(bf16[1,18,32,64]{3,2,1,0:T(8,128)(2,1)S(1)} %get-tuple-element.21, bf16[4,1,32,64]{3,2,1,0:T(8,128)(2,1)S(1)} %get-tuple-element.30, bf16[4,16,32,64]{3,2,1,0:T(8,128)(2,1)S(1)} %get-tuple-element.11, bf16[4,1,32,64]{3,2,1,0:T(8,128)(2,1)S(1)} %get-tuple-element.25, ...), kind=kLoop, calls=%fused_computation.14 | loop fusion | flops 1990656 | bytes 1327105 | tf_op jit(solution)/shard_map/jit(_where)/select_n | solution.py:86
  16.7 0.8 %pad_slice_fusion.1 = (bf16[6,18,32,64]{3,2,1,0:T(8,128)(2,1)S(1)}, bf16[6,18,32,64]{3,2,1,0:T(8,128)(2,1)S(1)}) fusion(bf16[6,18,32,64]{3,2,1,0:T(8,128)(2,1)S(1)} %maximum_select_fusion), kind=kLoop, calls=%fused_computation.12 | loop fusion | bytes 1327104 | tf_op jit(solution)/shard_map/slice | solution.py:90
  17.4 0.9 %pad_maximum_fusion = bf16[6,18,32,192]{3,2,1,0:T(8,128)(2,1)S(1)} fusion(bf16[6,18,32,64]{3,2,1,0:T(8,128)(2,1)S(1)} %get-tuple-element.7, bf16[6,18,32,64]{3,2,1,0:T(8,128)(2,1)S(1)} %maximum_select_fusion, bf16[6,18,32,64]{3,2,1,0:T(8,128)(2,1)S(1)} %get-tuple-element.6), kind=kLoop, calls=%fused_computation.2 | loop fusion | flops 3981312 | bytes 2654208 | tf_op jit(solution)/shard_map/concatenate | solution.py:90
  18.3 0.2 copy-done.2
  18.5 0.5 fusion.29
  18.9 0.5 fusion.28
  19.4 0.5 fusion.30
  19.9 0.5 fusion.31
  20.3 0.5 fusion.32
  20.8 0.5 fusion.33
  21.3 0.5 fusion.34
  21.7 0.5 fusion.35
  23.0 0.5 fusion.36
  23.5 0.2 maximum_bitcast_fusion
  24.5 0.1 maximum_bitcast_fusion.4
  24.9 0.1 maximum_bitcast_fusion.8
  25.2 1.5 %collective-permute-start.3 = (f32[4,216,64]{1,2,0:T(8,128)S(1)}, f32[4,216,64]{1,2,0:T(8,128)S(1)}, u32[]{:S(2)}, u32[]{:S(2)}) collective-permute-start(f32[4,216,64]{1,2,0:T(8,128)S(1)} %slice_select_fusion.1), channel_id=1, source_target_pairs={{0,2},{2,0},{1,3},{3,1},{4,6},{6,4},{5,7},{7,5},{8,10},{10,8},{9,1... | collective-permute-start | bytes 663560 | tf_op jit(solution)/shard_map/ppermute | solution.py:115
  26.6 0.4 copy.28
  27.0 0.2 pad.5.clone
  27.3 0.1 copy.7
  27.4 0.1 slice.179
  27.6 0.4 copy-done.3
  28.0 5.0 %fusion.11 = bf16[4,16,8,5,128]{4,2,3,1,0:T(8,128)(2,1)S(1)} fusion(bf16[3,3,3,128,128]{4,3,2,1,0:T(8,128)(2,1)S(1)} %bitcast.201, bf16[6,18,1,7,2,128]{5,3,4,1,0,2:T(8,128)(2,1)S(1)} %slice.179, bf16[6,18,1,8,5,128]{5,3,4,1,0,2:T(8,128)(2,1)S(1)} %copy.7, pred[8,5]{0,1:T(8,128)(4,1)S(1)} %copy-done.3), kind=kOutput, calls=%fused_computation.10 | convolution fusion | flops 2270224384 | bytes 3033128 | tf_op jit(solution)/shard_map/conv_general_dilated | solution.py:77
  32.9 0.1 copy.8
  33.0 0.2 select_add_fusion.1
  33.3 0.7 %collective-permute-start.7 = (f32[4,216,64]{1,2,0:T(8,128)S(1)}, f32[4,216,64]{1,2,0:T(8,128)S(1)}, u32[]{:S(2)}, u32[]{:S(2)}) collective-permute-start(f32[4,216,64]{1,2,0:T(8,128)S(1)} %get-tuple-element.5), channel_id=1, source_target_pairs={{0,2},{2,0},{1,3},{3,1},{4,6},{6,4},{5,7},{7,5},{8,10},{10,8},{9,1... | collective-permute-start | bytes 663560 | tf_op jit(solution)/shard_map/ppermute | solution.py:115
  34.0 0.9 %copy.18 = bf16[4,16,32,128]{3,2,1,0:T(8,128)(2,1)} copy(bf16[4,16,32,128]{3,1,2,0:T(8,128)(2,1)S(1)} %slice_bitcast_fusion) | data formatting | bytes 1048576
  34.9 1.2 %collective-permute-start.4 = (f32[216,64]{0,1:T(8,128)S(1)}, f32[216,64]{0,1:T(8,128)S(1)}, u32[]{:S(2)}, u32[]{:S(2)}) collective-permute-start(f32[216,64]{0,1:T(8,128)S(1)} %get-tuple-element.12), channel_id=1, source_target_pairs={{0,8},{4,12},{8,0},{12,4},{1,9},{5,13},{9,1},{13,5},{2,10},{6,14},... | collective-permute-start | bytes 165896 | tf_op jit(solution)/shard_map/ppermute | solution.py:51
  36.1 2.3 %collective-permute-start.5 = (f32[216,64]{0,1:T(8,128)S(1)}, f32[216,64]{0,1:T(8,128)S(1)}, u32[]{:S(2)}, u32[]{:S(2)}) collective-permute-start(f32[216,64]{0,1:T(8,128)S(1)} %get-tuple-element.14), channel_id=1, source_target_pairs={{0,4},{4,8},{8,12},{12,0},{1,5},{5,9},{9,13},{13,1},{2,6},{6,10},{... | collective-permute-start | bytes 165896 | tf_op jit(solution)/shard_map/ppermute | solution.py:51
  38.4 1.5 %collective-permute-start.6 = (f32[216,64]{0,1:T(8,128)S(1)}, f32[216,64]{0,1:T(8,128)S(1)}, u32[]{:S(2)}, u32[]{:S(2)}) collective-permute-start(f32[216,64]{0,1:T(8,128)S(1)} %get-tuple-element.13), channel_id=1, source_target_pairs={{0,12},{4,0},{8,4},{12,8},{1,13},{5,1},{9,5},{13,9},{2,14},{6,2},{... | collective-permute-start | bytes 165896 | tf_op jit(solution)/shard_map/ppermute | solution.py:51
  40.0 0.2 select_add_fusion
  40.2 2.7 %collective-permute-start.10 = (f32[216,64]{0,1:T(8,128)S(1)}, f32[216,64]{0,1:T(8,128)S(1)}, u32[]{:S(2)}, u32[]{:S(2)}) collective-permute-start(f32[216,64]{0,1:T(8,128)S(1)} %get-tuple-element.16), channel_id=1, source_target_pairs={{0,12},{4,0},{8,4},{12,8},{1,13},{5,1},{9,5},{13,9},{2,14},{6,2},{... | collective-permute-start | bytes 165896 | tf_op jit(solution)/shard_map/ppermute | solution.py:51
  42.8 0.3 collective-permute-start.8
  43.1 0.4 collective-permute-start.9
  43.5 2.4 %collective-permute-done.10 = f32[216,64]{0,1:T(8,128)S(1)} collective-permute-done((f32[216,64]{0,1:T(8,128)S(1)}, f32[216,64]{0,1:T(8,128)S(1)}, u32[]{:S(2)}, u32[]{:S(2)}) %collective-permute-start.10) | collective-permute-done | bytes 55328 | tf_op jit(solution)/shard_map/ppermute | solution.py:51
  45.9 2.1 %collective-permute-done.8 = f32[216,64]{0,1:T(8,128)S(1)} collective-permute-done((f32[216,64]{0,1:T(8,128)S(1)}, f32[216,64]{0,1:T(8,128)S(1)}, u32[]{:S(2)}, u32[]{:S(2)}) %collective-permute-start.8) | collective-permute-done | bytes 55328 | tf_op jit(solution)/shard_map/ppermute | solution.py:51
  48.0 1.2 %collective-permute-done.9 = f32[216,64]{0,1:T(8,128)S(1)} collective-permute-done((f32[216,64]{0,1:T(8,128)S(1)}, f32[216,64]{0,1:T(8,128)S(1)}, u32[]{:S(2)}, u32[]{:S(2)}) %collective-permute-start.9) | collective-permute-done | bytes 55328 | tf_op jit(solution)/shard_map/ppermute | solution.py:51
  49.2 0.8 %maximum_multiply_fusion = f32[432,64]{0,1:T(8,128)} fusion(f32[216,64]{0,1:T(8,128)S(1)} %fusion.16, f32[216,64]{0,1:T(8,128)S(1)} %fusion.18), kind=kLoop, calls=%fused_computation.36 | loop fusion | flops 55296 | bytes 221184 | tf_op jit(solution)/shard_map/div | solution.py:123
  (59 shorter events, 2.2 us)
Async XLA Ops:
  0.6 26.9 %copy-start = (bf16[27,128,128]{2,1,0:T(8,128)(2,1)S(1)}, bf16[27,128,128]{2,1,0:T(8,128)(2,1)}, u32[]{:S(2)}) copy-start(bf16[27,128,128]{2,1,0:T(8,128)(2,1)} %param.5) | copy-start | bytes 2654212
  0.6 5.8 %copy-start.1 = (bf16[4,16,32,128]{3,2,1,0:T(8,128)(2,1)S(1)}, bf16[4,16,32,128]{3,2,1,0:T(8,128)(2,1)}, u32[]{:S(2)}) copy-start(bf16[4,16,32,128]{3,2,1,0:T(8,128)(2,1)} %param.4) | copy-start | bytes 1572868
  1.6 4.8 %collective-permute-start = (bf16[4,1,32,128]{3,2,1,0:T(8,128)(2,1)S(1)}, bf16[4,1,32,128]{3,2,1,0:T(8,128)(2,1)S(1)}, u32[]{:S(2)}, u32[]{:S(2)}) collective-permute-start(bf16[4,1,32,128]{3,2,1,0:T(8,128)(2,1)S(1)} %slice_select_fusion.2), channel_id=1, source_target_pairs={{0,2},{2,0},{1,3},{3,1},{4,6},{6,4},{5,7},{7,5},{8,10},{10,8},{9,1... | collective-permute-start | bytes 98312 | tf_op jit(solution)/shard_map/ppermute | solution.py:18
  6.5 8.6 %collective-permute-start.1 = (bf16[1,18,32,128]{3,2,1,0:T(8,128)(2,1)S(1)}, bf16[1,18,32,128]{3,2,1,0:T(8,128)(2,1)S(1)}, u32[]{:S(2)}, u32[]{:S(2)}) collective-permute-start(bf16[1,18,32,128]{3,2,1,0:T(8,128)(2,1)S(1)} %get-tuple-element.8), channel_id=1, source_target_pairs={{0,4},{4,8},{8,12},{12,0},{1,5},{5,9},{9,13},{13,1},{2,6},{6,10},{... | collective-permute-start | bytes 442376 | tf_op jit(solution)/shard_map/ppermute | solution.py:23
  8.6 7.4 %collective-permute-start.2 = (bf16[1,18,32,128]{3,2,1,0:T(8,128)(2,1)S(1)}, bf16[1,18,32,128]{3,2,1,0:T(8,128)(2,1)S(1)}, u32[]{:S(2)}, u32[]{:S(2)}) collective-permute-start(bf16[1,18,32,128]{3,2,1,0:T(8,128)(2,1)S(1)} %get-tuple-element.9), channel_id=1, source_target_pairs={{4,0},{8,4},{12,8},{0,12},{5,1},{9,5},{13,9},{1,13},{6,2},{10,6},{... | collective-permute-start | bytes 442376 | tf_op jit(solution)/shard_map/ppermute | solution.py:24
  17.4 1.0 %copy-start.2 = (bf16[4,16,32,128]{3,2,1,0:T(8,128)(2,1)S(1)}, bf16[4,16,32,128]{3,2,1,0:T(8,128)(2,1)}, u32[]{:S(2)}) copy-start(bf16[4,16,32,128]{3,2,1,0:T(8,128)(2,1)} %param.3) | copy-start | bytes 1572868
  25.2 7.9 %collective-permute-start.3 = (f32[4,216,64]{1,2,0:T(8,128)S(1)}, f32[4,216,64]{1,2,0:T(8,128)S(1)}, u32[]{:S(2)}, u32[]{:S(2)}) collective-permute-start(f32[4,216,64]{1,2,0:T(8,128)S(1)} %slice_select_fusion.1), channel_id=1, source_target_pairs={{0,2},{2,0},{1,3},{3,1},{4,6},{6,4},{5,7},{7,5},{8,10},{10,8},{9,1... | collective-permute-start | bytes 663560 | tf_op jit(solution)/shard_map/ppermute | solution.py:115
  27.3 0.7 %copy-start.3 = (pred[8,5]{0,1:T(8,128)(4,1)S(1)}, pred[8,5]{0,1:T(8,128)(4,1)}, u32[]{:S(2)}) copy-start(pred[8,5]{0,1:T(8,128)(4,1)} %constant.77) | copy-start | bytes 124
  33.3 6.7 %collective-permute-start.7 = (f32[4,216,64]{1,2,0:T(8,128)S(1)}, f32[4,216,64]{1,2,0:T(8,128)S(1)}, u32[]{:S(2)}, u32[]{:S(2)}) collective-permute-start(f32[4,216,64]{1,2,0:T(8,128)S(1)} %get-tuple-element.5), channel_id=1, source_target_pairs={{0,2},{2,0},{1,3},{3,1},{4,6},{6,4},{5,7},{7,5},{8,10},{10,8},{9,1... | collective-permute-start | bytes 663560 | tf_op jit(solution)/shard_map/ppermute | solution.py:115
  34.9 8.2 %collective-permute-start.4 = (f32[216,64]{0,1:T(8,128)S(1)}, f32[216,64]{0,1:T(8,128)S(1)}, u32[]{:S(2)}, u32[]{:S(2)}) collective-permute-start(f32[216,64]{0,1:T(8,128)S(1)} %get-tuple-element.12), channel_id=1, source_target_pairs={{0,8},{4,12},{8,0},{12,4},{1,9},{5,13},{9,1},{13,5},{2,10},{6,14},... | collective-permute-start | bytes 165896 | tf_op jit(solution)/shard_map/ppermute | solution.py:51
  36.1 7.4 %collective-permute-start.5 = (f32[216,64]{0,1:T(8,128)S(1)}, f32[216,64]{0,1:T(8,128)S(1)}, u32[]{:S(2)}, u32[]{:S(2)}) collective-permute-start(f32[216,64]{0,1:T(8,128)S(1)} %get-tuple-element.14), channel_id=1, source_target_pairs={{0,4},{4,8},{8,12},{12,0},{1,5},{5,9},{9,13},{13,1},{2,6},{6,10},{... | collective-permute-start | bytes 165896 | tf_op jit(solution)/shard_map/ppermute | solution.py:51
  38.4 5.1 %collective-permute-start.6 = (f32[216,64]{0,1:T(8,128)S(1)}, f32[216,64]{0,1:T(8,128)S(1)}, u32[]{:S(2)}, u32[]{:S(2)}) collective-permute-start(f32[216,64]{0,1:T(8,128)S(1)} %get-tuple-element.13), channel_id=1, source_target_pairs={{0,12},{4,0},{8,4},{12,8},{1,13},{5,1},{9,5},{13,9},{2,14},{6,2},{... | collective-permute-start | bytes 165896 | tf_op jit(solution)/shard_map/ppermute | solution.py:51
  40.2 5.7 %collective-permute-start.10 = (f32[216,64]{0,1:T(8,128)S(1)}, f32[216,64]{0,1:T(8,128)S(1)}, u32[]{:S(2)}, u32[]{:S(2)}) collective-permute-start(f32[216,64]{0,1:T(8,128)S(1)} %get-tuple-element.16), channel_id=1, source_target_pairs={{0,12},{4,0},{8,4},{12,8},{1,13},{5,1},{9,5},{13,9},{2,14},{6,2},{... | collective-permute-start | bytes 165896 | tf_op jit(solution)/shard_map/ppermute | solution.py:51
  42.8 5.2 %collective-permute-start.8 = (f32[216,64]{0,1:T(8,128)S(1)}, f32[216,64]{0,1:T(8,128)S(1)}, u32[]{:S(2)}, u32[]{:S(2)}) collective-permute-start(f32[216,64]{0,1:T(8,128)S(1)} %get-tuple-element.15), channel_id=1, source_target_pairs={{0,8},{4,12},{8,0},{12,4},{1,9},{5,13},{9,1},{13,5},{2,10},{6,14},... | collective-permute-start | bytes 165896 | tf_op jit(solution)/shard_map/ppermute | solution.py:51
  43.1 6.1 %collective-permute-start.9 = (f32[216,64]{0,1:T(8,128)S(1)}, f32[216,64]{0,1:T(8,128)S(1)}, u32[]{:S(2)}, u32[]{:S(2)}) collective-permute-start(f32[216,64]{0,1:T(8,128)S(1)} %get-tuple-element.17), channel_id=1, source_target_pairs={{0,4},{4,8},{8,12},{12,0},{1,5},{5,9},{9,13},{13,1},{2,6},{6,10},{... | collective-permute-start | bytes 165896 | tf_op jit(solution)/shard_map/ppermute | solution.py:51
